TPU v7x, 128 devices: a whole 4x4x4 slice. The times are simulated.
128 devices in a mesh: gx: 8 (over x, z_hi), gy: 16 (over y, z_lo, core).
Axes of the slice: x: 4, y: 4, z: 4 (z_hi: 2, z_lo: 2; z = z_hi * 2 + z_lo), core: 2. Of those that a mesh axis runs over, the one named last changes fastest.
Arguments:
- right_side: float32 [16, 1024, 1024], P(None, 'gy', 'gx'), may hold values from -8 to 8
- conduct: float32 [16, 1024, 1024], P(None, 'gy', 'gx'), may hold values from 0.3 to 3
- excavated: int32 [16, 1024, 1024], P(None, 'gy', 'gx'), may hold values 0 or 1
- vectors_x: float32 [1024, 1024], replicated, may hold values from -0.1875 to 0.1875
- mass_x: float32 [1024], P('gy'), may hold values from 0.5 to 2
- values_x: float32 [1024], replicated, may hold values from 0.05 to 5
- vectors_y: float32 [1024, 1024], replicated, may hold values from -0.1875 to 0.1875
- mass_y: float32 [1024], P('gx'), may hold values from 0.5 to 2
- values_y: float32 [1024], replicated, may hold values from 0.05 to 5
- vertical_diag: float32 [16], replicated, may hold values from 3.2 to 4.5
- vertical_coupling: float32 [15], replicated, may hold values from 0.5 to 1.5
Outputs:
- adjoint: float32 [16, 1024, 1024], P(None, 'gy', 'gx')
- residual: float32 [16, 1024, 1024], P(None, 'gy', 'gx')
All inputs are finite; a program needn't handle non-finite values. No bound on the sum of `excavated` on one device may be relied on, other than what follows from the above.
Results may differ from a plain program's by a relative error of at most 0.0001.
Values sent between devices are 32-bit elements; how exact they have to be, the bound alone decides.
No kernel may reach another device: no remote copies, remote signals or barrier semaphores. Data moves between devices by JAX's collectives and lax.ppermute only.
A program may use at most 64 MiB of HBM per device.

v0:
```python
import jax
import jax.numpy as jnp
from jax import lax
from jax.experimental import pallas as pl
from jax.experimental.pallas import tpu as pltpu
from jax.sharding import PartitionSpec as P

ITERS = 2


storage_term = 0.2


def edges(block):
    strips = []
    for axis, dim in (("gy", 1), ("gx", 2)):
        count = lax.axis_size(axis)
        forward = [(i, i + 1) for i in range(count - 1)]
        backward = [(target, source) for source, target in forward]
        last = lax.index_in_dim(block, block.shape[dim] - 1, axis=dim, keepdims=False)
        first = lax.index_in_dim(block, 0, axis=dim, keepdims=False)
        strips.append((lax.ppermute(last, axis, forward), lax.ppermute(first, axis, backward)))
    return strips


def harmonic(first, second):
    return 2.0 * first * second / (first + second)


def neighbours(center, strips):
    (x_low, x_high), (y_low, y_high) = strips
    zeros = jnp.zeros_like(center[:1])
    return [
        jnp.concatenate([center[1:], zeros], axis=0),
        jnp.concatenate([zeros, center[:-1]], axis=0),
        jnp.concatenate([center[:, 1:], x_high[:, None, :]], axis=1),
        jnp.concatenate([x_low[:, None, :], center[:, :-1]], axis=1),
        jnp.concatenate([center[:, :, 1:], y_high[:, :, None]], axis=2),
        jnp.concatenate([y_low[:, :, None], center[:, :, :-1]], axis=2),
    ]


def faces_from(center):
    return [harmonic(center, other) for other in neighbours(center, edges(center))]


def stencil(center, faces):
    result = storage_term * center
    for face, other in zip(faces, neighbours(center, edges(center))):
        result = result + face * (center - other)
    return result


def solve_kernel(diag_ref, coup_ref, shifts_ref, rhs_ref, out_ref, ratio_ref):
    count = rhs_ref.shape[0]
    shifts = shifts_ref[...]
    denom = diag_ref[0] + shifts
    ratio = -coup_ref[0] / denom
    ratio_ref[0] = ratio
    part = rhs_ref[0] / denom
    out_ref[0] = part
    for position in range(1, count):
        denom = diag_ref[position] + shifts + coup_ref[position - 1] * ratio
        if position < count - 1:
            ratio = -coup_ref[position] / denom
            ratio_ref[position] = ratio
        part = (rhs_ref[position] + coup_ref[position - 1] * part) / denom
        out_ref[position] = part
    solved = part
    for position in range(count - 2, -1, -1):
        solved = out_ref[position] - ratio_ref[position] * solved
        out_ref[position] = solved


def vertical_solve(rhs, diagonal, coupling, shifts):
    smem = pl.BlockSpec(memory_space=pltpu.SMEM)
    vmem = pl.BlockSpec(memory_space=pltpu.VMEM)
    return pl.pallas_call(
        solve_kernel,
        out_shape=jax.ShapeDtypeStruct(rhs.shape, rhs.dtype),
        in_specs=[smem, smem, vmem, vmem],
        out_specs=vmem,
        scratch_shapes=[pltpu.VMEM(rhs.shape, rhs.dtype)],
    )(diagonal, coupling, shifts, rhs)


def shards(
    right_side,
    conduct,
    excavated,
    vectors_x,
    mass_x,
    values_x,
    vectors_y,
    mass_y,
    values_y,
    vertical_diag,
    vertical_coupling,
):
    precision = lax.Precision.HIGH
    active = excavated.astype(jnp.float32)
    faces = faces_from(conduct)
    local_modes = vectors_x.shape[1] // (lax.axis_size("gx") * lax.axis_size("gy"))
    mode_start = (lax.axis_index("gx") * lax.axis_size("gy") + lax.axis_index("gy")) * local_modes
    local_values = lax.dynamic_slice_in_dim(values_x, mode_start, local_modes, 0)
    shifts = local_values[:, None] + values_y[None, :]
    adjoint = jnp.zeros_like(right_side)
    residual = right_side
    everyone = ("gx", "gy")
    blocks_y = lax.axis_size("gx")
    for iteration in range(ITERS):
        scaled = residual * mass_x[None, :, None] * mass_y[None, None, :]
        modes = jnp.einsum(
            "zxy,xi->ziy",
            lax.all_to_all(scaled, "gy", split_axis=0, concat_axis=1, tiled=True),
            vectors_x,
            precision=precision,
        )
        chunks = modes.reshape(-1, local_modes, modes.shape[2])
        chunks = lax.all_to_all(chunks, everyone, split_axis=0, concat_axis=0, tiled=True)
        chunks = chunks.reshape(blocks_y, -1, local_modes, chunks.shape[2])
        modes = jnp.einsum(
            "azil,alj->zij",
            chunks,
            vectors_y.reshape(blocks_y, -1, vectors_y.shape[1]),
            precision=precision,
        )
        solved = vertical_solve(modes, vertical_diag, vertical_coupling, shifts)
        chunks = jnp.einsum(
            "zij,alj->azil",
            solved,
            vectors_y.reshape(blocks_y, -1, vectors_y.shape[1]),
            precision=precision,
        )
        chunks = chunks.reshape(-1, local_modes, chunks.shape[3])
        chunks = lax.all_to_all(chunks, everyone, split_axis=0, concat_axis=0, tiled=True)
        solved = chunks.reshape(1, -1, chunks.shape[2])
        solved = jnp.einsum("ziy,xi->zxy", solved, vectors_x, precision=precision)
        update = lax.all_to_all(solved, "gy", split_axis=1, concat_axis=0, tiled=True)
        adjoint = adjoint + update
        masked = active * update
        image = stencil(masked, faces) + (1.0 - active) * update
        residual = residual - image
    return (adjoint, residual)


def solution(mesh):
    in_specs = (
        P(None, "gy", "gx"),
        P(None, "gy", "gx"),
        P(None, "gy", "gx"),
        P(),
        P("gy"),
        P(),
        P(),
        P("gx"),
        P(),
        P(),
        P(),
    )
    out_specs = (P(None, "gy", "gx"), P(None, "gy", "gx"))
    return jax.shard_map(shards, mesh=mesh, in_specs=in_specs, out_specs=out_specs, check_vma=False)
```

profile of v0, /device:TPU:3, one launch (start us, length us, event | category | flops | bytes accessed | tf_op | source)
XLA Modules:
  0.0 232.2 jit_solution(14763349041398346411)
XLA Ops:
  2.6 6.5 %all-to-all-start = ((f32[16,64,128]{2,1,0:T(8,128)}), f32[16,64,128]{2,1,0:T(8,128)S(1)}, u32[]{:S(2)}, u32[]{:S(2)}) async-start(f32[16,64,128]{2,1,0:T(8,128)} %multiply_multiply_fusion.1), calls=%async_computation | async-start | bytes 1048576 | tf_op jit(solution)/shard_map/all_to_all | solution.py:115
  9.1 5.4 %copy.83 = f32[1024,1024]{0,1:T(8,128)} copy(f32[1024,1024]{1,0:T(8,128)} %param.14) | data formatting | bytes 8388608 | tf_op args[3]
  14.5 4.3 %all-to-all-done = f32[16,64,128]{2,1,0:T(8,128)S(1)} async-done(((f32[16,64,128]{2,1,0:T(8,128)}), f32[16,64,128]{2,1,0:T(8,128)S(1)}, u32[]{:S(2)}, u32[]{:S(2)}) %all-to-all-start) | async-done | bytes 524320 | tf_op jit(solution)/shard_map/all_to_all | solution.py:115
  18.8 6.4 %fusion.4 = f32[128,8,128]{0,2,1:T(8,128)S(1)} fusion(f32[1024,128,1]{1,0,2:T(8,128)S(1)} %bitcast.110, f32[128,8,1024]{2,1,0:T(8,128)} %bitcast.102), kind=kOutput, calls=%fused_computation.4 | convolution fusion | flops 805306368 | bytes 5242880 | tf_op jit(solution)/shard_map/zxy,xi->ziy/dot_general | solution.py:113
  26.2 8.9 %all-to-all-start.1 = ((f32[128,8,128]{2,1,0:T(8,128)}), f32[128,8,128]{2,1,0:T(8,128)S(1)}, u32[]{:S(2)}, u32[]{:S(2)}) async-start(f32[128,8,128]{2,1,0:T(8,128)} %copy.86), calls=%async_computation.1 | async-start | bytes 1048576 | tf_op jit(solution)/shard_map/all_to_all | solution.py:120
  41.9 6.0 %all-to-all-done.1 = f32[128,8,128]{2,1,0:T(8,128)S(1)} async-done(((f32[128,8,128]{2,1,0:T(8,128)}), f32[128,8,128]{2,1,0:T(8,128)S(1)}, u32[]{:S(2)}, u32[]{:S(2)}) %all-to-all-start.1) | async-done | bytes 524320 | tf_op jit(solution)/shard_map/all_to_all | solution.py:120
  47.9 4.3 %convolution_bitcast_fusion.5.rhs_ref = f32[16,8,1024]{2,1,0:T(8,128)} fusion(f32[8,16,8,128]{3,2,1,0:T(8,128)S(1)} %bitcast.109, f32[8,128,1024,1]{2,1,3,0:T(8,128)} %bitcast.98), kind=kOutput, calls=%fused_computation.11 | convolution fusion | flops 805306368 | bytes 5242880 | tf_op jit(solution)/shard_map/azil,alj->zij/dot_general | solution.py:122
  54.4 4.6 %convolution_bitcast_fusion.4 = f32[8,16,8,128]{3,2,0,1:T(8,128)S(1)} fusion(f32[8,128,1024,1]{2,1,0,3:T(8,128)} %bitcast.99, f32[16,8,1024]{2,1,0:T(8,128)} %shard_map.122), kind=kOutput, calls=%fused_computation.10 | convolution fusion | flops 805306368 | bytes 5242880 | tf_op jit(solution)/shard_map/zij,alj->azil/dot_general | solution.py:129
  59.7 4.9 %all-to-all-start.2 = ((f32[128,8,128]{2,1,0:T(8,128)}), f32[128,8,128]{2,1,0:T(8,128)S(1)}, u32[]{:S(2)}, u32[]{:S(2)}) async-start(f32[128,8,128]{2,1,0:T(8,128)} %bitcast.13), calls=%async_computation.2 | async-start | bytes 1048576 | tf_op jit(solution)/shard_map/all_to_all | solution.py:136
  65.1 5.1 %collective-permute-start.6 = (f32[16,64]{1,0:T(8,128)S(1)}, f32[16,64]{1,0:T(8,128)S(1)}, u32[]{:S(2)}, u32[]{:S(2)}) collective-permute-start(f32[16,64]{1,0:T(8,128)S(1)} %bitcast.118), channel_id=1, source_target_pairs={{0,16},{16,32},{32,48},{48,64},{64,80},{80,96},{96,112},{1,17},{17... | collective-permute-start | bytes 12296 | tf_op jit(solution)/shard_map/ppermute | solution.py:22
  77.8 4.5 %convolution_bitcast_fusion.3 = f32[1,1024,128]{1,2,0:T(8,128)S(1)} fusion(f32[1024,1024]{1,0:T(8,128)} %param.14, f32[128,8,128]{2,1,0:T(8,128)S(1)} %all-to-all-done.2), kind=kOutput, calls=%fused_computation.9 | convolution fusion | flops 805306368 | bytes 5242880 | tf_op jit(solution)/shard_map/ziy,xi->zxy/dot_general | solution.py:138
  89.8 7.0 %all-to-all-done.3 = f32[1,1024,128]{2,0,1:T(1,128)S(1)} async-done(((f32[1,1024,128]{2,0,1:T(1,128)}), f32[1,1024,128]{2,0,1:T(1,128)S(1)}, u32[]{:S(2)}, u32[]{:S(2)}) %all-to-all-start.3) | async-done | bytes 524320 | tf_op jit(solution)/shard_map/all_to_all | solution.py:139
  99.6 4.2 %collective-permute-start.5 = (f32[16,64]{1,0:T(8,128)S(1)}, f32[16,64]{1,0:T(8,128)S(1)}, u32[]{:S(2)}, u32[]{:S(2)}) collective-permute-start(f32[16,64]{1,0:T(8,128)S(1)} %get-tuple-element.5), channel_id=1, source_target_pairs={{16,0},{32,16},{48,32},{64,48},{80,64},{96,80},{112,96},{17,1},{33... | collective-permute-start | bytes 12296 | tf_op jit(solution)/shard_map/ppermute | solution.py:22
  116.8 5.3 %multiply_multiply_fusion = (f32[16,64,128]{2,1,0:T(8,128)S(1)}, f32[16,64,128]{2,1,0:T(8,128)}) fusion(f32[128]{0:T(128)S(1)} %copy-done.7, f32[64]{0:T(128)S(1)} %copy-done.8, f32[16,64,128]{2,1,0:T(8,128)} %param.11, f32[16,64,128]{2,1,0:T(8,128)S(1)} %bitcast.105, f32[16,64,127]{2,1,0:T(8,128)} %get-tuple-element.35, f32[16,64,1]{2,1,0:T(8,128)} %copy.98, ...), kind=kLoop, calls=%fused_computation.52 | loop fusion | flops 7077888 | bytes 9306880 | tf_op jit(solution)/shard_map/mul | solution.py:112
  122.1 15.9 %all_to_all.62 = f32[16,64,128]{2,1,0:T(8,128)S(1)} all-to-all(f32[16,64,128]{2,1,0:T(8,128)S(1)} %get-tuple-element.6), channel_id=1, replica_groups=mesh['gx'=8,'gy'=16] {'gy'}, dimensions={0} | all-to-all | bytes 1048576 | tf_op jit(solution)/shard_map/all_to_all | solution.py:115
  138.0 4.3 %fusion.7 = f32[128,8,128]{0,2,1:T(8,128)S(1)} fusion(f32[1024,128,1]{1,0,2:T(8,128)S(1)} %bitcast.111, f32[128,8,1024]{2,1,0:T(8,128)S(1)} %bitcast.103), kind=kOutput, calls=%fused_computation.5 | convolution fusion | flops 805306368 | bytes 5242880 | tf_op jit(solution)/shard_map/zxy,xi->ziy/dot_general | solution.py:113
  143.3 18.0 %all_to_all.63 = f32[128,8,128]{2,1,0:T(8,128)S(1)} all-to-all(f32[128,8,128]{2,1,0:T(8,128)} %copy.101), channel_id=1, replica_groups=mesh['gx'=8,'gy'=16] {'gx','gy'}, dimensions={0} | all-to-all | bytes 1048576 | tf_op jit(solution)/shard_map/all_to_all | solution.py:120
  161.3 4.3 %convolution_bitcast_fusion.2.rhs_ref = f32[16,8,1024]{2,1,0:T(8,128)} fusion(f32[8,16,8,128]{3,2,1,0:T(8,128)S(1)} %bitcast.112, f32[8,128,1024,1]{2,1,3,0:T(8,128)} %bitcast.100), kind=kOutput, calls=%fused_computation.8 | convolution fusion | flops 805306368 | bytes 5242880 | tf_op jit(solution)/shard_map/azil,alj->zij/dot_general | solution.py:122
  167.7 4.7 %convolution_bitcast_fusion.1 = f32[8,16,8,128]{3,2,0,1:T(8,128)S(1)} fusion(f32[8,128,1024,1]{2,1,0,3:T(8,128)} %bitcast.101, f32[16,8,1024]{2,1,0:T(8,128)} %shard_map.123), kind=kOutput, calls=%fused_computation.7 | convolution fusion | flops 805306368 | bytes 5242880 | tf_op jit(solution)/shard_map/zij,alj->azil/dot_general | solution.py:129
  172.5 17.5 %all_to_all.64 = f32[128,8,128]{2,1,0:T(8,128)S(1)} all-to-all(f32[128,8,128]{2,1,0:T(8,128)S(1)} %bitcast.113), channel_id=1, replica_groups=mesh['gx'=8,'gy'=16] {'gx','gy'}, dimensions={0} | all-to-all | bytes 1048576 | tf_op jit(solution)/shard_map/all_to_all | solution.py:136
  193.4 13.4 %all_to_all.65 = f32[1,1024,128]{2,0,1:T(1,128)S(1)} all-to-all(f32[1,1024,128]{2,0,1:T(1,128)} %copy.103), channel_id=1, replica_groups=mesh['gx'=8,'gy'=16] {'gy'}, dimensions={1} | all-to-all | bytes 1048576 | tf_op jit(solution)/shard_map/all_to_all | solution.py:139
  213.8 4.3 %collective-permute-start.10 = (f32[16,64]{1,0:T(8,128)S(1)}, f32[16,64]{1,0:T(8,128)S(1)}, u32[]{:S(2)}, u32[]{:S(2)}) collective-permute-start(f32[16,64]{1,0:T(8,128)S(1)} %get-tuple-element.3), channel_id=1, source_target_pairs={{16,0},{32,16},{48,32},{64,48},{80,64},{96,80},{112,96},{17,1},{33... | collective-permute-start | bytes 12296 | tf_op jit(solution)/shard_map/ppermute | solution.py:22
  218.2 3.8 %collective-permute-start.8 = (f32[16,128]{1,0:T(8,128)S(1)}, f32[16,128]{1,0:T(8,128)S(1)}, u32[]{:S(2)}, u32[]{:S(2)}) collective-permute-start(f32[16,128]{1,0:T(8,128)S(1)} %bitcast.129), channel_id=1, source_target_pairs={{1,0},{2,1},{3,2},{4,3},{5,4},{6,5},{7,6},{8,7},{9,8},{10,9},{11,1... | collective-permute-start | bytes 24584 | tf_op jit(solution)/shard_map/ppermute | solution.py:22
  227.1 5.1 %fusion.26 = f32[16,64,128]{2,1,0:T(8,128)} fusion(f32[16,64,128]{2,1,0:T(8,128)} %get-tuple-element.7, f32[16,1,128]{2,1,0:T(1,128)S(1)} %bitcast.134, f32[16,63,128]{2,1,0:T(8,128)} %get-tuple-element.15, f32[16,63,128]{2,1,0:T(8,128)} %get-tuple-element.14, f32[16,1,128]{2,1,0:T(1,128)S(1)} %bitcast.135, f32[16,64,1]{2,1,0:T(8,128)} %copy.106, ...), kind=kLoop, calls=%fused_computation.41 | loop fusion | flops 6815744 | bytes 8781824 | tf_op jit(solution)/shard_map/sub | solution.py:143
  (77 shorter events, 62.4 us)
Async XLA Ops:
  2.6 16.1 %all-to-all-start = ((f32[16,64,128]{2,1,0:T(8,128)}), f32[16,64,128]{2,1,0:T(8,128)S(1)}, u32[]{:S(2)}, u32[]{:S(2)}) async-start(f32[16,64,128]{2,1,0:T(8,128)} %multiply_multiply_fusion.1), calls=%async_computation | async-start | bytes 1048576 | tf_op jit(solution)/shard_map/all_to_all | solution.py:115
  14.5 20.5 %copy-start = (f32[16,64,128]{2,1,0:T(8,128)S(1)}, f32[16,64,128]{2,1,0:T(8,128)}, u32[]{:S(2)}) copy-start(f32[16,64,128]{2,1,0:T(8,128)} %param.12) | copy-start | bytes 1572868
  14.5 26.7 %copy-start.6 = (f32[1024]{0:T(1024)S(1)}, f32[1024]{0:T(1024)}, u32[]{:S(2)}) copy-start(f32[1024]{0:T(1024)} %param.19) | copy-start | bytes 12292
  26.2 21.8 %all-to-all-start.1 = ((f32[128,8,128]{2,1,0:T(8,128)}), f32[128,8,128]{2,1,0:T(8,128)S(1)}, u32[]{:S(2)}, u32[]{:S(2)}) async-start(f32[128,8,128]{2,1,0:T(8,128)} %copy.86), calls=%async_computation.1 | async-start | bytes 1048576 | tf_op jit(solution)/shard_map/all_to_all | solution.py:120
  35.0 81.7 %collective-permute-start.2 = (f32[16,128]{1,0:T(8,128)S(1)}, f32[16,128]{1,0:T(8,128)S(1)}, u32[]{:S(2)}, u32[]{:S(2)}) collective-permute-start(f32[16,128]{1,0:T(8,128)S(1)} %bitcast.127), channel_id=1, source_target_pairs={{0,1},{1,2},{2,3},{3,4},{4,5},{5,6},{6,7},{7,8},{8,9},{9,10},{10,1... | collective-permute-start | bytes 24584 | tf_op jit(solution)/shard_map/ppermute | solution.py:22
  38.5 78.2 %collective-permute-start = (f32[16,128]{1,0:T(8,128)S(1)}, f32[16,128]{1,0:T(8,128)S(1)}, u32[]{:S(2)}, u32[]{:S(2)}) collective-permute-start(f32[16,128]{1,0:T(8,128)S(1)} %bitcast.126), channel_id=1, source_target_pairs={{1,0},{2,1},{3,2},{4,3},{5,4},{6,5},{7,6},{8,7},{9,8},{10,9},{11,1... | collective-permute-start | bytes 24584 | tf_op jit(solution)/shard_map/ppermute | solution.py:22
  59.7 18.0 %all-to-all-start.2 = ((f32[128,8,128]{2,1,0:T(8,128)}), f32[128,8,128]{2,1,0:T(8,128)S(1)}, u32[]{:S(2)}, u32[]{:S(2)}) async-start(f32[128,8,128]{2,1,0:T(8,128)} %bitcast.13), calls=%async_computation.2 | async-start | bytes 1048576 | tf_op jit(solution)/shard_map/all_to_all | solution.py:136
  65.1 24.4 %collective-permute-start.6 = (f32[16,64]{1,0:T(8,128)S(1)}, f32[16,64]{1,0:T(8,128)S(1)}, u32[]{:S(2)}, u32[]{:S(2)}) collective-permute-start(f32[16,64]{1,0:T(8,128)S(1)} %bitcast.118), channel_id=1, source_target_pairs={{0,16},{16,32},{32,48},{48,64},{64,80},{80,96},{96,112},{1,17},{17... | collective-permute-start | bytes 12296 | tf_op jit(solution)/shard_map/ppermute | solution.py:22
  70.5 18.8 %collective-permute-start.4 = (f32[16,64]{1,0:T(8,128)S(1)}, f32[16,64]{1,0:T(8,128)S(1)}, u32[]{:S(2)}, u32[]{:S(2)}) collective-permute-start(f32[16,64]{1,0:T(8,128)S(1)} %bitcast.121), channel_id=1, source_target_pairs={{16,0},{32,16},{48,32},{64,48},{80,64},{96,80},{112,96},{17,1},{33... | collective-permute-start | bytes 12296 | tf_op jit(solution)/shard_map/ppermute | solution.py:22
  74.1 42.6 %copy-start.4 = (f32[16,63,128]{2,1,0:T(8,128)}, f32[16,63,128]{2,1,0:T(8,128)S(1)}, u32[]{:S(2)}) copy-start(f32[16,63,128]{2,1,0:T(8,128)S(1)} %get-tuple-element.22) | copy-start | bytes 1548292
  83.3 13.5 %all-to-all-start.3 = ((f32[1,1024,128]{2,0,1:T(1,128)}), f32[1,1024,128]{2,0,1:T(1,128)S(1)}, u32[]{:S(2)}, u32[]{:S(2)}) async-start(f32[1,1024,128]{2,0,1:T(1,128)} %copy.88), calls=%async_computation.3 | async-start | bytes 1048576 | tf_op jit(solution)/shard_map/all_to_all | solution.py:139
  96.8 19.9 %copy-start.7 = (f32[128]{0:T(128)S(1)}, f32[128]{0:T(128)}, u32[]{:S(2)}) copy-start(f32[128]{0:T(128)} %param.18) | copy-start | bytes 1540
  96.8 19.9 %copy-start.8 = (f32[64]{0:T(128)S(1)}, f32[64]{0:T(128)}, u32[]{:S(2)}) copy-start(f32[64]{0:T(128)} %param.15) | copy-start | bytes 772
  99.6 9.1 %collective-permute-start.5 = (f32[16,64]{1,0:T(8,128)S(1)}, f32[16,64]{1,0:T(8,128)S(1)}, u32[]{:S(2)}, u32[]{:S(2)}) collective-permute-start(f32[16,64]{1,0:T(8,128)S(1)} %get-tuple-element.5), channel_id=1, source_target_pairs={{16,0},{32,16},{48,32},{64,48},{80,64},{96,80},{112,96},{17,1},{33... | collective-permute-start | bytes 12296 | tf_op jit(solution)/shard_map/ppermute | solution.py:22
  103.9 12.8 %collective-permute-start.3 = (f32[16,128]{1,0:T(8,128)S(1)}, f32[16,128]{1,0:T(8,128)S(1)}, u32[]{:S(2)}, u32[]{:S(2)}) collective-permute-start(f32[16,128]{1,0:T(8,128)S(1)} %bitcast.131), channel_id=1, source_target_pairs={{0,1},{1,2},{2,3},{3,4},{4,5},{5,6},{6,7},{7,8},{8,9},{9,10},{10,1... | collective-permute-start | bytes 24584 | tf_op jit(solution)/shard_map/ppermute | solution.py:22
  106.8 10.0 %collective-permute-start.1 = (f32[16,128]{1,0:T(8,128)S(1)}, f32[16,128]{1,0:T(8,128)S(1)}, u32[]{:S(2)}, u32[]{:S(2)}) collective-permute-start(f32[16,128]{1,0:T(8,128)S(1)} %bitcast.130), channel_id=1, source_target_pairs={{1,0},{2,1},{3,2},{4,3},{5,4},{6,5},{7,6},{8,7},{9,8},{10,9},{11,1... | collective-permute-start | bytes 24584 | tf_op jit(solution)/shard_map/ppermute | solution.py:22
  108.7 6.9 %collective-permute-start.7 = (f32[16,64]{1,0:T(8,128)S(1)}, f32[16,64]{1,0:T(8,128)S(1)}, u32[]{:S(2)}, u32[]{:S(2)}) collective-permute-start(f32[16,64]{1,0:T(8,128)S(1)} %get-tuple-element.4), channel_id=1, source_target_pairs={{0,16},{16,32},{32,48},{48,64},{64,80},{80,96},{96,112},{1,17},{17... | collective-permute-start | bytes 12296 | tf_op jit(solution)/shard_map/ppermute | solution.py:22
  116.8 21.2 %copy-start.2 = (f32[1024,1024]{0,1:T(8,128)S(1)}, f32[1024,1024]{0,1:T(8,128)}, u32[]{:S(2)}) copy-start(f32[1024,1024]{0,1:T(8,128)} %copy.83) | copy-start | bytes 12582916
  167.7 22.3 %copy-start.1 = (f32[1024,1024]{1,0:T(8,128)S(1)}, f32[1024,1024]{1,0:T(8,128)}, u32[]{:S(2)}) copy-start(f32[1024,1024]{1,0:T(8,128)} %param.14) | copy-start | bytes 12582916
  207.7 19.4 %copy-start.5 = (f32[16,63,128]{2,1,0:T(8,128)S(1)}, f32[16,63,128]{2,1,0:T(8,128)}, u32[]{:S(2)}) copy-start(f32[16,63,128]{2,1,0:T(8,128)} %copy-done.4) | copy-start | bytes 1548292
  210.5 15.6 %collective-permute-start.11 = (f32[16,64]{1,0:T(8,128)S(1)}, f32[16,64]{1,0:T(8,128)S(1)}, u32[]{:S(2)}, u32[]{:S(2)}) collective-permute-start(f32[16,64]{1,0:T(8,128)S(1)} %get-tuple-element.2), channel_id=1, source_target_pairs={{0,16},{16,32},{32,48},{48,64},{64,80},{80,96},{96,112},{1,17},{17... | collective-permute-start | bytes 12296 | tf_op jit(solution)/shard_map/ppermute | solution.py:22
  213.8 11.2 %collective-permute-start.10 = (f32[16,64]{1,0:T(8,128)S(1)}, f32[16,64]{1,0:T(8,128)S(1)}, u32[]{:S(2)}, u32[]{:S(2)}) collective-permute-start(f32[16,64]{1,0:T(8,128)S(1)} %get-tuple-element.3), channel_id=1, source_target_pairs={{16,0},{32,16},{48,32},{64,48},{80,64},{96,80},{112,96},{17,1},{33... | collective-permute-start | bytes 12296 | tf_op jit(solution)/shard_map/ppermute | solution.py:22
  218.2 8.9 %collective-permute-start.8 = (f32[16,128]{1,0:T(8,128)S(1)}, f32[16,128]{1,0:T(8,128)S(1)}, u32[]{:S(2)}, u32[]{:S(2)}) collective-permute-start(f32[16,128]{1,0:T(8,128)S(1)} %bitcast.129), channel_id=1, source_target_pairs={{1,0},{2,1},{3,2},{4,3},{5,4},{6,5},{7,6},{8,7},{9,8},{10,9},{11,1... | collective-permute-start | bytes 24584 | tf_op jit(solution)/shard_map/ppermute | solution.py:22
  222.0 5.1 %collective-permute-start.9 = (f32[16,128]{1,0:T(8,128)S(1)}, f32[16,128]{1,0:T(8,128)S(1)}, u32[]{:S(2)}, u32[]{:S(2)}) collective-permute-start(f32[16,128]{1,0:T(8,128)S(1)} %bitcast.128), channel_id=1, source_target_pairs={{0,1},{1,2},{2,3},{3,4},{4,5},{5,6},{6,7},{7,8},{8,9},{9,10},{10,1... | collective-permute-start | bytes 24584 | tf_op jit(solution)/shard_map/ppermute | solution.py:22
  (1 other events, 14.5 us)
where the time goes:
time: 234 us; the launch traced here: 232 us
  blocking collectives  64.9 us (28%)
  starting transfers between devices  63.6 us (27%)
  matrix products  35.4 us (15%)
  local copies, waits for them, and re-layouts  27.2 us (12%)
  waiting for transfers between devices  22 us (9%)
  other arithmetic  14.1 us (6%)
  Pallas kernels  4.14 us (2%)
    all_to_all x2, blocking collectives, shards(): lax.all_to_all(chunks, everyone, split_axis=0, concat_axis=0, tiled=True)  35.5 us
    ppermute x6, starting transfers between devices, edges(): lax.ppermute(last, axis, forward)  20.5 us
    ppermute x6, starting transfers between devices, edges(): lax.ppermute(first, axis, backward)  19 us
    all_to_all x1, blocking collectives, shards(): lax.all_to_all(scaled, 'gy', split_axis=0, concat_axis=1, tiled=True)  15.9 us
    all_to_all x2, starting transfers between devices, shards(): lax.all_to_all(chunks, everyone, split_axis=0, concat_axis=0, tiled=True)  13.8 us
    all_to_all x1, blocking collectives, shards(): lax.all_to_all(solved, 'gy', split_axis=1, concat_axis=0, tiled=True)  13.4 us
    dot_general x2, matrix products, shards(): jnp.einsum('zxy,xi->ziy', lax.all_to_all(scaled, 'gy', split_axis=0, conc...  10.7 us
    all_to_all x2, waiting for transfers between devices, shards(): lax.all_to_all(chunks, everyone, split_axis=0, concat_axis=0, tiled=True)  9.69 us
  transfers between devices with their start and end apart: 16, of which 5 were waited for; matrix products, arithmetic and copies ran while one was open for 15% of the time, Pallas kernels for 1%

commit v1 on v0

--- a/solution.py
+++ b/solution.py
@@ -84,6 +84,21 @@
     )(diagonal, coupling, shifts, rhs)
 
 
+def split_bf16(values):
+    rounded = lax.reduce_precision(values, exponent_bits=8, mantissa_bits=7)
+    return rounded.astype(jnp.bfloat16), (values - rounded).astype(jnp.bfloat16)
+
+
+def transform(spec, data, basis):
+    high, low = split_bf16(data)
+    basis_high, basis_low = basis
+
+    def product(first, second):
+        return jnp.einsum(spec, first, second, preferred_element_type=jnp.float32)
+
+    return product(high, basis_high) + (product(low, basis_high) + product(high, basis_low))
+
+
 def shards(
     right_side,
     conduct,
@@ -97,7 +112,6 @@
     vertical_diag,
     vertical_coupling,
 ):
-    precision = lax.Precision.HIGH
     active = excavated.astype(jnp.float32)
     faces = faces_from(conduct)
     local_modes = vectors_x.shape[1] // (lax.axis_size("gx") * lax.axis_size("gy"))
@@ -108,34 +122,25 @@
     residual = right_side
     everyone = ("gx", "gy")
     blocks_y = lax.axis_size("gx")
+    basis_x = split_bf16(vectors_x)
+    basis_y = tuple(piece.reshape(blocks_y, -1, vectors_y.shape[1]) for piece in split_bf16(vectors_y))
     for iteration in range(ITERS):
         scaled = residual * mass_x[None, :, None] * mass_y[None, None, :]
-        modes = jnp.einsum(
+        modes = transform(
             "zxy,xi->ziy",
             lax.all_to_all(scaled, "gy", split_axis=0, concat_axis=1, tiled=True),
-            vectors_x,
-            precision=precision,
+            basis_x,
         )
         chunks = modes.reshape(-1, local_modes, modes.shape[2])
         chunks = lax.all_to_all(chunks, everyone, split_axis=0, concat_axis=0, tiled=True)
         chunks = chunks.reshape(blocks_y, -1, local_modes, chunks.shape[2])
-        modes = jnp.einsum(
-            "azil,alj->zij",
-            chunks,
-            vectors_y.reshape(blocks_y, -1, vectors_y.shape[1]),
-            precision=precision,
-        )
+        modes = transform("azil,alj->zij", chunks, basis_y)
         solved = vertical_solve(modes, vertical_diag, vertical_coupling, shifts)
-        chunks = jnp.einsum(
-            "zij,alj->azil",
-            solved,
-            vectors_y.reshape(blocks_y, -1, vectors_y.shape[1]),
-            precision=precision,
-        )
+        chunks = transform("zij,alj->azil", solved, basis_y)
         chunks = chunks.reshape(-1, local_modes, chunks.shape[3])
         chunks = lax.all_to_all(chunks, everyone, split_axis=0, concat_axis=0, tiled=True)
         solved = chunks.reshape(1, -1, chunks.shape[2])
-        solved = jnp.einsum("ziy,xi->zxy", solved, vectors_x, precision=precision)
+        solved = transform("ziy,xi->zxy", solved, basis_x)
         update = lax.all_to_all(solved, "gy", split_axis=1, concat_axis=0, tiled=True)
         adjoint = adjoint + update
         masked = active * update

time: 234 us -> 237 us (1.013)
  other arithmetic: 14.1 us -> 25 us
  waiting for transfers between devices: 22 us -> 14.4 us
  matrix products: 35.4 us -> 28.6 us
  starting transfers between devices: 63.6 us -> 67.9 us
    convert_element_type x0 -> x6, other arithmetic: none -> 9.26 us  [the longest x2 8.92 us: split_bf16(): rounded.astype(jnp.bfloat16)]
    add x0 -> x6, local copies, waits for them, and re-layouts: none -> 7.1 us  [transform(): product(high, basis_high)]
    dot_general x8 -> x24, matrix products: 35.4 us -> 28.6 us  [product(): return jnp.einsum(spec, first, second, preferred_element_type=jnp.float32)]
    all_to_all x1, waiting for transfers between devices: 4.27 us -> 0.01 us  [shards(): lax.all_to_all(scaled, 'gy', split_axis=0, concat_axis=1, tiled=True)]
    transpose x4 -> x0, local copies, waits for them, and re-layouts: 2.93 us -> none  [the longest x2 2.07 us: shards(): solved = jnp.einsum('ziy,xi->zxy', solved, vectors_x, precision=precision)]
    unnamed x21 -> x38, local copies, waits for them, and re-layouts: 5.8 us -> 3.64 us
  transfers between devices with their start and end apart: 16 -> 16, of which waited for: 5 -> 4; matrix products, arithmetic and copies ran while one was open for 15% -> 21% of each run, Pallas kernels for 1% -> 1%
where the time goes in v1:
time: 237 us; the launch traced here: 235 us
  starting transfers between devices  67.9 us (29%)
  blocking collectives  65.2 us (28%)
  local copies, waits for them, and re-layouts  29.2 us (12%)
  matrix products  28.6 us (12%)
  other arithmetic  25 us (11%)
  waiting for transfers between devices  14.4 us (6%)
  Pallas kernels  4.14 us (2%)
    all_to_all x2, blocking collectives, shards(): lax.all_to_all(chunks, everyone, split_axis=0, concat_axis=0, tiled=True)  36.5 us
    dot_general x24, matrix products, product(): return jnp.einsum(spec, first, second, preferred_element_type=jnp.float32)  28.6 us
    ppermute x6, starting transfers between devices, edges(): lax.ppermute(last, axis, forward)  20.9 us
    ppermute x6, starting transfers between devices, edges(): lax.ppermute(first, axis, backward)  18.7 us
    all_to_all x2, starting transfers between devices, shards(): lax.all_to_all(chunks, everyone, split_axis=0, concat_axis=0, tiled=True)  16 us
    all_to_all x1, blocking collectives, shards(): lax.all_to_all(scaled, 'gy', split_axis=0, concat_axis=1, tiled=True)  15.9 us
    all_to_all x1, blocking collectives, shards(): lax.all_to_all(solved, 'gy', split_axis=1, concat_axis=0, tiled=True)  12.8 us
    convert_element_type x2, other arithmetic, split_bf16(): rounded.astype(jnp.bfloat16)  8.92 us
  transfers between devices with their start and end apart: 16, of which 4 were waited for; matrix products, arithmetic and copies ran while one was open for 21% of the time, Pallas kernels for 1%

profile of v1, /device:TPU:3, one launch (start us, length us, event | category | flops | bytes accessed | tf_op | source)
XLA Modules:
  0.0 235.5 jit_solution(8407025339606270997)
XLA Ops:
  2.7 6.5 %all-to-all-start = ((f32[16,64,128]{2,1,0:T(8,128)}), f32[16,64,128]{2,1,0:T(8,128)S(1)}, u32[]{:S(2)}, u32[]{:S(2)}) async-start(f32[16,64,128]{2,1,0:T(8,128)} %multiply_multiply_fusion.1), calls=%async_computation | async-start | bytes 1048576 | tf_op jit(solution)/shard_map/all_to_all | solution.py:131
  9.2 3.5 %collective-permute-start.2 = (f32[16,128]{1,0:T(8,128)S(1)}, f32[16,128]{1,0:T(8,128)S(1)}, u32[]{:S(2)}, u32[]{:S(2)}) collective-permute-start(f32[16,128]{1,0:T(8,128)S(1)} %bitcast.247), channel_id=1, source_target_pairs={{0,1},{1,2},{2,3},{3,4},{4,5},{5,6},{6,7},{7,8},{8,9},{9,10},{10,1... | collective-permute-start | bytes 24584 | tf_op jit(solution)/shard_map/ppermute | solution.py:22
  15.5 4.4 %reduce-precision_convert_fusion.1 = (bf16[1024,1024]{1,0:T(8,128)(2,1)S(1)}, bf16[1024,1024]{1,0:T(8,128)(2,1)}) fusion(f32[1024,1024]{1,0:T(8,128)} %param.14), kind=kLoop, calls=%fused_computation.3 | loop fusion | flops 4194304 | bytes 8388608 | tf_op jit(solution)/shard_map/convert_element_type | solution.py:89
  20.0 2.8 %fusion.76 = f32[1024,128]{0,1:T(8,128)S(1)} fusion(bf16[1024,1024]{1,0:T(8,128)(2,1)} %get-tuple-element.11, bf16[1024,128]{1,0:T(8,128)(2,1)S(1)} %get-tuple-element.47), kind=kOutput, calls=%fused_computation.135 | convolution fusion | flops 268435456 | bytes 2883584 | tf_op jit(solution)/shard_map/zxy,xi->ziy/dot_general | solution.py:97
  24.8 11.1 %all-to-all-start.1 = ((f32[128,8,128]{2,1,0:T(8,128)}), f32[128,8,128]{2,1,0:T(8,128)S(1)}, u32[]{:S(2)}, u32[]{:S(2)}) async-start(f32[128,8,128]{2,1,0:T(8,128)} %bitcast.3), calls=%async_computation.1 | async-start | bytes 1048576 | tf_op jit(solution)/shard_map/all_to_all | solution.py:135
  36.5 4.5 %reduce-precision_convert_fusion = (bf16[1024,1024]{1,0:T(8,128)(2,1)S(1)}, bf16[1024,1024]{1,0:T(8,128)(2,1)}) fusion(f32[1024,1024]{1,0:T(8,128)} %param.17), kind=kLoop, calls=%fused_computation.1 | loop fusion | flops 4194304 | bytes 8388608 | tf_op jit(solution)/shard_map/convert_element_type | solution.py:89
  41.0 7.8 %all-to-all-done.1 = f32[128,8,128]{2,1,0:T(8,128)S(1)} async-done(((f32[128,8,128]{2,1,0:T(8,128)}), f32[128,8,128]{2,1,0:T(8,128)S(1)}, u32[]{:S(2)}, u32[]{:S(2)}) %all-to-all-start.1) | async-done | bytes 524320 | tf_op jit(solution)/shard_map/all_to_all | solution.py:135
  59.7 5.0 %all-to-all-start.2 = ((f32[128,8,128]{2,1,0:T(8,128)}), f32[128,8,128]{2,1,0:T(8,128)S(1)}, u32[]{:S(2)}, u32[]{:S(2)}) async-start(f32[128,8,128]{2,1,0:T(8,128)} %bitcast.229), calls=%async_computation.2 | async-start | bytes 1048576 | tf_op jit(solution)/shard_map/all_to_all | solution.py:141
  67.0 5.1 %collective-permute-start.6 = (f32[16,64]{1,0:T(8,128)S(1)}, f32[16,64]{1,0:T(8,128)S(1)}, u32[]{:S(2)}, u32[]{:S(2)}) collective-permute-start(f32[16,64]{1,0:T(8,128)S(1)} %bitcast.238), channel_id=1, source_target_pairs={{0,16},{16,32},{32,48},{48,64},{64,80},{80,96},{96,112},{1,17},{17... | collective-permute-start | bytes 12296 | tf_op jit(solution)/shard_map/ppermute | solution.py:22
  77.7 2.6 %fusion.56 = f32[1024,128]{0,1:T(8,128)S(1)} fusion(bf16[1024,1024]{1,0:T(8,128)(2,1)} %get-tuple-element.11, f32[128,8,128]{2,1,0:T(8,128)S(1)} %all-to-all-done.2), kind=kOutput, calls=%fused_computation.119 | convolution fusion | flops 268697600 | bytes 3145728 | tf_op jit(solution)/shard_map/ziy,xi->zxy/dot_general | solution.py:97
  84.7 5.8 %all-to-all-start.3 = ((f32[1,1024,128]{2,0,1:T(1,128)}), f32[1,1024,128]{2,0,1:T(1,128)S(1)}, u32[]{:S(2)}, u32[]{:S(2)}) async-start(f32[1,1024,128]{2,0,1:T(1,128)} %copy.99), calls=%async_computation.3 | async-start | bytes 1048576 | tf_op jit(solution)/shard_map/all_to_all | solution.py:144
  95.0 5.2 %all-to-all-done.3 = f32[1,1024,128]{2,0,1:T(1,128)S(1)} async-done(((f32[1,1024,128]{2,0,1:T(1,128)}), f32[1,1024,128]{2,0,1:T(1,128)S(1)}, u32[]{:S(2)}, u32[]{:S(2)}) %all-to-all-start.3) | async-done | bytes 524320 | tf_op jit(solution)/shard_map/all_to_all | solution.py:144
  104.1 3.9 %collective-permute-start.5 = (f32[16,64]{1,0:T(8,128)S(1)}, f32[16,64]{1,0:T(8,128)S(1)}, u32[]{:S(2)}, u32[]{:S(2)}) collective-permute-start(f32[16,64]{1,0:T(8,128)S(1)} %get-tuple-element.5), channel_id=1, source_target_pairs={{16,0},{32,16},{48,32},{64,48},{80,64},{96,80},{112,96},{17,1},{33... | collective-permute-start | bytes 12296 | tf_op jit(solution)/shard_map/ppermute | solution.py:22
  108.0 2.9 %collective-permute-start.3 = (f32[16,128]{1,0:T(8,128)S(1)}, f32[16,128]{1,0:T(8,128)S(1)}, u32[]{:S(2)}, u32[]{:S(2)}) collective-permute-start(f32[16,128]{1,0:T(8,128)S(1)} %bitcast.251), channel_id=1, source_target_pairs={{0,1},{1,2},{2,3},{3,4},{4,5},{5,6},{6,7},{7,8},{8,9},{9,10},{10,1... | collective-permute-start | bytes 24584 | tf_op jit(solution)/shard_map/ppermute | solution.py:22
  112.8 4.3 %collective-permute-start.7 = (f32[16,64]{1,0:T(8,128)S(1)}, f32[16,64]{1,0:T(8,128)S(1)}, u32[]{:S(2)}, u32[]{:S(2)}) collective-permute-start(f32[16,64]{1,0:T(8,128)S(1)} %get-tuple-element.4), channel_id=1, source_target_pairs={{0,16},{16,32},{32,48},{48,64},{64,80},{80,96},{96,112},{1,17},{17... | collective-permute-start | bytes 12296 | tf_op jit(solution)/shard_map/ppermute | solution.py:22
  121.1 5.8 %multiply_multiply_fusion = (f32[16,64,128]{2,1,0:T(8,128)S(1)}, f32[16,64,128]{2,1,0:T(8,128)}) fusion(f32[128]{0:T(128)S(1)} %copy-done.16, f32[64]{0:T(128)S(1)} %copy-done.17, f32[16,64,128]{2,1,0:T(8,128)} %param.11, f32[16,64,128]{2,1,0:T(8,128)S(1)} %bitcast.221, f32[16,64,127]{2,1,0:T(8,128)} %get-tuple-element.43, f32[16,64,1]{2,1,0:T(8,128)} %copy.109, ...), kind=kLoop, calls=%fused_computation.104 | loop fusion | flops 7077888 | bytes 9306880 | tf_op jit(solution)/shard_map/mul | solution.py:128
  126.8 15.9 %all_to_all.68 = f32[16,64,128]{2,1,0:T(8,128)S(1)} all-to-all(f32[16,64,128]{2,1,0:T(8,128)S(1)} %get-tuple-element.6), channel_id=1, replica_groups=mesh['gx'=8,'gy'=16] {'gy'}, dimensions={0} | all-to-all | bytes 1048576 | tf_op jit(solution)/shard_map/all_to_all | solution.py:131
  148.2 19.0 %all_to_all.69 = f32[128,8,128]{2,1,0:T(8,128)S(1)} all-to-all(f32[128,8,128]{2,1,0:T(8,128)} %bitcast.230), channel_id=1, replica_groups=mesh['gx'=8,'gy'=16] {'gx','gy'}, dimensions={0} | all-to-all | bytes 1048576 | tf_op jit(solution)/shard_map/all_to_all | solution.py:135
  175.8 17.5 %all_to_all.70 = f32[128,8,128]{2,1,0:T(8,128)S(1)} all-to-all(f32[128,8,128]{2,1,0:T(8,128)S(1)} %bitcast.231), channel_id=1, replica_groups=mesh['gx'=8,'gy'=16] {'gx','gy'}, dimensions={0} | all-to-all | bytes 1048576 | tf_op jit(solution)/shard_map/all_to_all | solution.py:141
  198.0 12.8 %all_to_all.71 = f32[1,1024,128]{2,0,1:T(1,128)S(1)} all-to-all(f32[1,1024,128]{2,0,1:T(1,128)S(1)} %copy.114), channel_id=1, replica_groups=mesh['gx'=8,'gy'=16] {'gy'}, dimensions={1} | all-to-all | bytes 1048576 | tf_op jit(solution)/shard_map/all_to_all | solution.py:144
  214.5 3.1 %collective-permute-start.11 = (f32[16,64]{1,0:T(8,128)S(1)}, f32[16,64]{1,0:T(8,128)S(1)}, u32[]{:S(2)}, u32[]{:S(2)}) collective-permute-start(f32[16,64]{1,0:T(8,128)S(1)} %get-tuple-element.2), channel_id=1, source_target_pairs={{0,16},{16,32},{32,48},{48,64},{64,80},{80,96},{96,112},{1,17},{17... | collective-permute-start | bytes 12296 | tf_op jit(solution)/shard_map/ppermute | solution.py:22
  217.6 4.6 %collective-permute-start.10 = (f32[16,64]{1,0:T(8,128)S(1)}, f32[16,64]{1,0:T(8,128)S(1)}, u32[]{:S(2)}, u32[]{:S(2)}) collective-permute-start(f32[16,64]{1,0:T(8,128)S(1)} %get-tuple-element.3), channel_id=1, source_target_pairs={{16,0},{32,16},{48,32},{64,48},{80,64},{96,80},{112,96},{17,1},{33... | collective-permute-start | bytes 12296 | tf_op jit(solution)/shard_map/ppermute | solution.py:22
  222.2 3.8 %collective-permute-start.8 = (f32[16,128]{1,0:T(8,128)S(1)}, f32[16,128]{1,0:T(8,128)S(1)}, u32[]{:S(2)}, u32[]{:S(2)}) collective-permute-start(f32[16,128]{1,0:T(8,128)S(1)} %bitcast.249), channel_id=1, source_target_pairs={{1,0},{2,1},{3,2},{4,3},{5,4},{6,5},{7,6},{8,7},{9,8},{10,9},{11,1... | collective-permute-start | bytes 24584 | tf_op jit(solution)/shard_map/ppermute | solution.py:22
  230.3 5.1 %fusion.44 = f32[16,64,128]{2,1,0:T(8,128)} fusion(f32[16,64,128]{2,1,0:T(8,128)} %get-tuple-element.7, f32[16,1,128]{2,1,0:T(1,128)S(1)} %bitcast.254, f32[16,63,128]{2,1,0:T(8,128)} %get-tuple-element.19, f32[16,63,128]{2,1,0:T(8,128)} %get-tuple-element.18, f32[16,1,128]{2,1,0:T(1,128)S(1)} %bitcast.255, f32[16,64,1]{2,1,0:T(8,128)S(1)} %copy.117, ...), kind=kLoop, calls=%fused_computation.97 | loop fusion | flops 6815744 | bytes 8781824 | tf_op jit(solution)/shard_map/sub | solution.py:148
  (116 shorter events, 71.5 us)
Async XLA Ops:
  2.7 17.2 %all-to-all-start = ((f32[16,64,128]{2,1,0:T(8,128)}), f32[16,64,128]{2,1,0:T(8,128)S(1)}, u32[]{:S(2)}, u32[]{:S(2)}) async-start(f32[16,64,128]{2,1,0:T(8,128)} %multiply_multiply_fusion.1), calls=%async_computation | async-start | bytes 1048576 | tf_op jit(solution)/shard_map/all_to_all | solution.py:131
  9.2 111.8 %collective-permute-start.2 = (f32[16,128]{1,0:T(8,128)S(1)}, f32[16,128]{1,0:T(8,128)S(1)}, u32[]{:S(2)}, u32[]{:S(2)}) collective-permute-start(f32[16,128]{1,0:T(8,128)S(1)} %bitcast.247), channel_id=1, source_target_pairs={{0,1},{1,2},{2,3},{3,4},{4,5},{5,6},{6,7},{7,8},{8,9},{9,10},{10,1... | collective-permute-start | bytes 24584 | tf_op jit(solution)/shard_map/ppermute | solution.py:22
  12.8 108.3 %collective-permute-start = (f32[16,128]{1,0:T(8,128)S(1)}, f32[16,128]{1,0:T(8,128)S(1)}, u32[]{:S(2)}, u32[]{:S(2)}) collective-permute-start(f32[16,128]{1,0:T(8,128)S(1)} %bitcast.246), channel_id=1, source_target_pairs={{1,0},{2,1},{3,2},{4,3},{5,4},{6,5},{7,6},{8,7},{9,8},{10,9},{11,1... | collective-permute-start | bytes 24584 | tf_op jit(solution)/shard_map/ppermute | solution.py:22
  24.8 24.0 %all-to-all-start.1 = ((f32[128,8,128]{2,1,0:T(8,128)}), f32[128,8,128]{2,1,0:T(8,128)S(1)}, u32[]{:S(2)}, u32[]{:S(2)}) async-start(f32[128,8,128]{2,1,0:T(8,128)} %bitcast.3), calls=%async_computation.1 | async-start | bytes 1048576 | tf_op jit(solution)/shard_map/all_to_all | solution.py:135
  59.7 18.0 %all-to-all-start.2 = ((f32[128,8,128]{2,1,0:T(8,128)}), f32[128,8,128]{2,1,0:T(8,128)S(1)}, u32[]{:S(2)}, u32[]{:S(2)}) async-start(f32[128,8,128]{2,1,0:T(8,128)} %bitcast.229), calls=%async_computation.2 | async-start | bytes 1048576 | tf_op jit(solution)/shard_map/all_to_all | solution.py:141
  67.0 26.9 %collective-permute-start.6 = (f32[16,64]{1,0:T(8,128)S(1)}, f32[16,64]{1,0:T(8,128)S(1)}, u32[]{:S(2)}, u32[]{:S(2)}) collective-permute-start(f32[16,64]{1,0:T(8,128)S(1)} %bitcast.238), channel_id=1, source_target_pairs={{0,16},{16,32},{32,48},{48,64},{64,80},{80,96},{96,112},{1,17},{17... | collective-permute-start | bytes 12296 | tf_op jit(solution)/shard_map/ppermute | solution.py:22
  73.4 19.4 %collective-permute-start.4 = (f32[16,64]{1,0:T(8,128)S(1)}, f32[16,64]{1,0:T(8,128)S(1)}, u32[]{:S(2)}, u32[]{:S(2)}) collective-permute-start(f32[16,64]{1,0:T(8,128)S(1)} %bitcast.240), channel_id=1, source_target_pairs={{16,0},{32,16},{48,32},{64,48},{80,64},{96,80},{112,96},{17,1},{33... | collective-permute-start | bytes 12296 | tf_op jit(solution)/shard_map/ppermute | solution.py:22
  84.7 15.5 %all-to-all-start.3 = ((f32[1,1024,128]{2,0,1:T(1,128)}), f32[1,1024,128]{2,0,1:T(1,128)S(1)}, u32[]{:S(2)}, u32[]{:S(2)}) async-start(f32[1,1024,128]{2,0,1:T(1,128)} %copy.99), calls=%async_computation.3 | async-start | bytes 1048576 | tf_op jit(solution)/shard_map/all_to_all | solution.py:144
  102.9 18.1 %copy-start.16 = (f32[128]{0:T(128)S(1)}, f32[128]{0:T(128)}, u32[]{:S(2)}) copy-start(f32[128]{0:T(128)} %param.18) | copy-start | bytes 1540
  102.9 18.1 %copy-start.17 = (f32[64]{0:T(128)S(1)}, f32[64]{0:T(128)}, u32[]{:S(2)}) copy-start(f32[64]{0:T(128)} %param.15) | copy-start | bytes 772
  104.1 8.8 %collective-permute-start.5 = (f32[16,64]{1,0:T(8,128)S(1)}, f32[16,64]{1,0:T(8,128)S(1)}, u32[]{:S(2)}, u32[]{:S(2)}) collective-permute-start(f32[16,64]{1,0:T(8,128)S(1)} %get-tuple-element.5), channel_id=1, source_target_pairs={{16,0},{32,16},{48,32},{64,48},{80,64},{96,80},{112,96},{17,1},{33... | collective-permute-start | bytes 12296 | tf_op jit(solution)/shard_map/ppermute | solution.py:22
  108.0 13.0 %collective-permute-start.3 = (f32[16,128]{1,0:T(8,128)S(1)}, f32[16,128]{1,0:T(8,128)S(1)}, u32[]{:S(2)}, u32[]{:S(2)}) collective-permute-start(f32[16,128]{1,0:T(8,128)S(1)} %bitcast.251), channel_id=1, source_target_pairs={{0,1},{1,2},{2,3},{3,4},{4,5},{5,6},{6,7},{7,8},{8,9},{9,10},{10,1... | collective-permute-start | bytes 24584 | tf_op jit(solution)/shard_map/ppermute | solution.py:22
  110.9 10.1 %collective-permute-start.1 = (f32[16,128]{1,0:T(8,128)S(1)}, f32[16,128]{1,0:T(8,128)S(1)}, u32[]{:S(2)}, u32[]{:S(2)}) collective-permute-start(f32[16,128]{1,0:T(8,128)S(1)} %bitcast.250), channel_id=1, source_target_pairs={{1,0},{2,1},{3,2},{4,3},{5,4},{6,5},{7,6},{8,7},{9,8},{10,9},{11,1... | collective-permute-start | bytes 24584 | tf_op jit(solution)/shard_map/ppermute | solution.py:22
  112.8 7.1 %collective-permute-start.7 = (f32[16,64]{1,0:T(8,128)S(1)}, f32[16,64]{1,0:T(8,128)S(1)}, u32[]{:S(2)}, u32[]{:S(2)}) collective-permute-start(f32[16,64]{1,0:T(8,128)S(1)} %get-tuple-element.4), channel_id=1, source_target_pairs={{0,16},{16,32},{32,48},{48,64},{64,80},{80,96},{96,112},{1,17},{17... | collective-permute-start | bytes 12296 | tf_op jit(solution)/shard_map/ppermute | solution.py:22
  148.2 19.1 %copy-start.7 = (bf16[1024,1024]{1,0:T(8,128)(2,1)S(1)}, bf16[1024,1024]{1,0:T(8,128)(2,1)}, u32[]{:S(2)}) copy-start(bf16[1024,1024]{1,0:T(8,128)(2,1)} %get-tuple-element.9) | copy-start | bytes 6291460
  174.9 18.4 %copy-start.5 = (bf16[1024,1024]{1,0:T(8,128)(2,1)S(1)}, bf16[1024,1024]{1,0:T(8,128)(2,1)}, u32[]{:S(2)}) copy-start(bf16[1024,1024]{1,0:T(8,128)(2,1)} %get-tuple-element.11) | copy-start | bytes 6291460
  175.8 18.4 %copy-start.3 = (bf16[1024,1024]{1,0:T(8,128)(2,1)S(1)}, bf16[1024,1024]{1,0:T(8,128)(2,1)}, u32[]{:S(2)}) copy-start(bf16[1024,1024]{1,0:T(8,128)(2,1)} %copy-done) | copy-start | bytes 6291460
  213.4 16.9 %copy-start.11 = (f32[16,64,1]{2,1,0:T(8,128)S(1)}, f32[16,64,1]{2,1,0:T(8,128)}, u32[]{:S(2)}) copy-start(f32[16,64,1]{2,1,0:T(8,128)} %copy.105) | copy-start | bytes 12292
  213.4 16.9 %copy-start.12 = (f32[16,64,1]{2,1,0:T(8,128)S(1)}, f32[16,64,1]{2,1,0:T(8,128)}, u32[]{:S(2)}) copy-start(f32[16,64,1]{2,1,0:T(8,128)} %copy.108) | copy-start | bytes 12292
  213.4 16.9 %copy-start.14 = (f32[1,1024,128]{2,0,1:T(1,128)S(1)}, f32[1,1024,128]{2,0,1:T(1,128)}, u32[]{:S(2)}) copy-start(f32[1,1024,128]{2,0,1:T(1,128)} %copy-done.13) | copy-start | bytes 1572868
  214.5 14.8 %collective-permute-start.11 = (f32[16,64]{1,0:T(8,128)S(1)}, f32[16,64]{1,0:T(8,128)S(1)}, u32[]{:S(2)}, u32[]{:S(2)}) collective-permute-start(f32[16,64]{1,0:T(8,128)S(1)} %get-tuple-element.2), channel_id=1, source_target_pairs={{0,16},{16,32},{32,48},{48,64},{64,80},{80,96},{96,112},{1,17},{17... | collective-permute-start | bytes 12296 | tf_op jit(solution)/shard_map/ppermute | solution.py:22
  217.6 11.4 %collective-permute-start.10 = (f32[16,64]{1,0:T(8,128)S(1)}, f32[16,64]{1,0:T(8,128)S(1)}, u32[]{:S(2)}, u32[]{:S(2)}) collective-permute-start(f32[16,64]{1,0:T(8,128)S(1)} %get-tuple-element.3), channel_id=1, source_target_pairs={{16,0},{32,16},{48,32},{64,48},{80,64},{96,80},{112,96},{17,1},{33... | collective-permute-start | bytes 12296 | tf_op jit(solution)/shard_map/ppermute | solution.py:22
  222.2 8.1 %collective-permute-start.8 = (f32[16,128]{1,0:T(8,128)S(1)}, f32[16,128]{1,0:T(8,128)S(1)}, u32[]{:S(2)}, u32[]{:S(2)}) collective-permute-start(f32[16,128]{1,0:T(8,128)S(1)} %bitcast.249), channel_id=1, source_target_pairs={{1,0},{2,1},{3,2},{4,3},{5,4},{6,5},{7,6},{8,7},{9,8},{10,9},{11,1... | collective-permute-start | bytes 24584 | tf_op jit(solution)/shard_map/ppermute | solution.py:22
  226.0 4.3 %collective-permute-start.9 = (f32[16,128]{1,0:T(8,128)S(1)}, f32[16,128]{1,0:T(8,128)S(1)}, u32[]{:S(2)}, u32[]{:S(2)}) collective-permute-start(f32[16,128]{1,0:T(8,128)S(1)} %bitcast.248), channel_id=1, source_target_pairs={{0,1},{1,2},{2,3},{3,4},{4,5},{5,6},{6,7},{7,8},{8,9},{9,10},{10,1... | collective-permute-start | bytes 24584 | tf_op jit(solution)/shard_map/ppermute | solution.py:22
  (10 other events, 65.3 us)

commit v2 on v1

--- a/solution.py
+++ b/solution.py
@@ -11,16 +11,17 @@
 storage_term = 0.2
 
 
+def edge_pair(block, axis, dim):
+    count = lax.axis_size(axis)
+    forward = [(i, i + 1) for i in range(count - 1)]
+    backward = [(target, source) for source, target in forward]
+    last = lax.index_in_dim(block, block.shape[dim] - 1, axis=dim, keepdims=False)
+    first = lax.index_in_dim(block, 0, axis=dim, keepdims=False)
+    return lax.ppermute(last, axis, forward), lax.ppermute(first, axis, backward)
+
+
 def edges(block):
-    strips = []
-    for axis, dim in (("gy", 1), ("gx", 2)):
-        count = lax.axis_size(axis)
-        forward = [(i, i + 1) for i in range(count - 1)]
-        backward = [(target, source) for source, target in forward]
-        last = lax.index_in_dim(block, block.shape[dim] - 1, axis=dim, keepdims=False)
-        first = lax.index_in_dim(block, 0, axis=dim, keepdims=False)
-        strips.append((lax.ppermute(last, axis, forward), lax.ppermute(first, axis, backward)))
-    return strips
+    return [edge_pair(block, "gy", 1), edge_pair(block, "gx", 2)]
 
 
 def harmonic(first, second):
@@ -44,9 +45,9 @@
     return [harmonic(center, other) for other in neighbours(center, edges(center))]
 
 
-def stencil(center, faces):
+def stencil(center, faces, strips):
     result = storage_term * center
-    for face, other in zip(faces, neighbours(center, edges(center))):
+    for face, other in zip(faces, neighbours(center, strips)):
         result = result + face * (center - other)
     return result
 
@@ -123,6 +124,15 @@
     everyone = ("gx", "gy")
     blocks_y = lax.axis_size("gx")
     basis_x = split_bf16(vectors_x)
+    rows = right_side.shape[1]
+    framed_basis = []
+    for piece in basis_x:
+        blocks = piece.reshape(-1, rows, piece.shape[1])
+        zero = jnp.zeros_like(blocks[:1, :1])
+        below = jnp.concatenate([zero, blocks[:-1, -1:]], axis=0)
+        above = jnp.concatenate([blocks[1:, :1], zero], axis=0)
+        framed_basis.append(jnp.concatenate([below, blocks, above], axis=1))
+    active_x = edge_pair(active, "gy", 1)
     basis_y = tuple(piece.reshape(blocks_y, -1, vectors_y.shape[1]) for piece in split_bf16(vectors_y))
     for iteration in range(ITERS):
         scaled = residual * mass_x[None, :, None] * mass_y[None, None, :]
@@ -139,12 +149,15 @@
         chunks = transform("zij,alj->azil", solved, basis_y)
         chunks = chunks.reshape(-1, local_modes, chunks.shape[3])
         chunks = lax.all_to_all(chunks, everyone, split_axis=0, concat_axis=0, tiled=True)
-        solved = chunks.reshape(1, -1, chunks.shape[2])
-        solved = transform("ziy,xi->zxy", solved, basis_x)
-        update = lax.all_to_all(solved, "gy", split_axis=1, concat_axis=0, tiled=True)
+        solved = chunks.reshape(-1, chunks.shape[2])
+        framed = transform("iy,bri->bry", solved, framed_basis)
+        framed = lax.all_to_all(framed, "gy", split_axis=0, concat_axis=0, tiled=True)
+        update = framed[:, 1:-1]
         adjoint = adjoint + update
         masked = active * update
-        image = stencil(masked, faces) + (1.0 - active) * update
+        x_strips = (active_x[0] * framed[:, 0], active_x[1] * framed[:, -1])
+        strips = (x_strips, edge_pair(masked, "gx", 2))
+        image = stencil(masked, faces, strips) + (1.0 - active) * update
         residual = residual - image
     return (adjoint, residual)
 

time: 237 us -> 263 us (1.11)
  local copies, waits for them, and re-layouts: 29.2 us -> 42.4 us
  other arithmetic: 25 us -> 31.5 us
  starting transfers between devices: 67.9 us -> 61.9 us
  waiting for transfers between devices: 14.4 us -> 19.6 us
  blocking collectives: 65.2 us -> 68.5 us
    slice x6 -> x13, local copies, waits for them, and re-layouts: 2.2 us -> 11.9 us  [the longest x4 3.92 us: edge_pair(): first = lax.index_in_dim(block, 0, axis=dim, keepdims=False)]
    convert_element_type x4 -> x5, other arithmetic: 0.34 us -> 6.86 us  [split_bf16(): (values - rounded).astype(jnp.bfloat16)]
    all_to_all x2, waiting for transfers between devices: 8.42 us -> 14.6 us  [shards(): lax.all_to_all(chunks, everyone, split_axis=0, concat_axis=0, tiled=True)]
    ppermute x12 -> x10, starting transfers between devices: 39.5 us -> 33.9 us  [the longest x5 18.5 us: edge_pair(): lax.ppermute(last, axis, forward)]
    convert_element_type x2 -> x1, other arithmetic: 8.92 us -> 4.44 us  [split_bf16(): rounded.astype(jnp.bfloat16)]
    concatenate x0 -> x1, other arithmetic: none -> 4.38 us  [shards(): framed_basis.append(jnp.concatenate([below, blocks, above], axis=1))]
    unnamed x38 -> x49, local copies, waits for them, and re-layouts: 3.64 us -> 7.5 us
    all_to_all x1, waiting for transfers between devices: 5.22 us -> 2.35 us  [shards(): lax.all_to_all(framed, 'gy', split_axis=0, concat_axis=0, tiled=True)]
  transfers between devices with their start and end apart: 16 -> 14, of which waited for: 4 -> 5; matrix products, arithmetic and copies ran while one was open for 21% -> 25% of each run, Pallas kernels for 1% -> 1%
where the time goes in v2:
time: 263 us; the launch traced here: 260 us
  blocking collectives  68.5 us (26%)
  starting transfers between devices  61.9 us (24%)
  local copies, waits for them, and re-layouts  42.4 us (16%)
  other arithmetic  31.5 us (12%)
  matrix products  30.7 us (12%)
  waiting for transfers between devices  19.6 us (7%)
  Pallas kernels  4.14 us (2%)
    all_to_all x2, blocking collectives, shards(): lax.all_to_all(chunks, everyone, split_axis=0, concat_axis=0, tiled=True)  38.7 us
    dot_general x24, matrix products, product(): return jnp.einsum(spec, first, second, preferred_element_type=jnp.float32)  30.7 us
    ppermute x5, starting transfers between devices, edge_pair(): lax.ppermute(last, axis, forward)  18.5 us
    all_to_all x2, starting transfers between devices, shards(): lax.all_to_all(chunks, everyone, split_axis=0, concat_axis=0, tiled=True)  17.2 us
    ppermute x5, starting transfers between devices, edge_pair(): lax.ppermute(first, axis, backward)  15.4 us
    all_to_all x1, blocking collectives, shards(): lax.all_to_all(scaled, 'gy', split_axis=0, concat_axis=1, tiled=True)  15.2 us
    all_to_all x2, waiting for transfers between devices, shards(): lax.all_to_all(chunks, everyone, split_axis=0, concat_axis=0, tiled=True)  14.6 us
    all_to_all x1, blocking collectives, shards(): lax.all_to_all(framed, 'gy', split_axis=0, concat_axis=0, tiled=True)  14.6 us
  transfers between devices with their start and end apart: 14, of which 5 were waited for; matrix products, arithmetic and copies ran while one was open for 25% of the time, Pallas kernels for 1%

profile of v2, /device:TPU:3, one launch (start us, length us, event | category | flops | bytes accessed | tf_op | source)
XLA Modules:
  0.0 259.9 jit_solution(17961231161277639125)
XLA Ops:
  4.7 3.6 %collective-permute-start.2 = (f32[16,128]{1,0:T(8,128)S(1)}, f32[16,128]{1,0:T(8,128)S(1)}, u32[]{:S(2)}, u32[]{:S(2)}) collective-permute-start(f32[16,128]{1,0:T(8,128)S(1)} %get-tuple-element.45), channel_id=1, source_target_pairs={{0,1},{1,2},{2,3},{3,4},{4,5},{5,6},{6,7},{7,8},{8,9},{9,10},{10,1... | collective-permute-start | bytes 24584 | tf_op jit(solution)/shard_map/ppermute | solution.py:20
  10.6 6.4 %all-to-all-start = ((f32[16,64,128]{2,1,0:T(8,128)}), f32[16,64,128]{2,1,0:T(8,128)}, u32[]{:S(2)}, u32[]{:S(2)}) async-start(f32[16,64,128]{2,1,0:T(8,128)} %copy.151), calls=%async_computation | async-start | bytes 1048576 | tf_op jit(solution)/shard_map/all_to_all | solution.py:141
  19.8 5.2 %collective-permute-start.6 = (f32[16,64]{1,0:T(8,128)S(1)}, f32[16,64]{1,0:T(8,128)S(1)}, u32[]{:S(2)}, u32[]{:S(2)}) collective-permute-start(f32[16,64]{1,0:T(8,128)S(1)} %bitcast.246), channel_id=1, source_target_pairs={{0,16},{16,32},{32,48},{48,64},{64,80},{80,96},{96,112},{1,17},{17... | collective-permute-start | bytes 12296 | tf_op jit(solution)/shard_map/ppermute | solution.py:20
  27.7 4.4 %fusion.4 = (bf16[1024,1024]{1,0:T(8,128)(2,1)}, bf16[1024,1024]{1,0:T(8,128)(2,1)S(1)}) fusion(f32[1024,1024]{1,0:T(8,128)} %param.14), kind=kLoop, calls=%fused_computation.10 | loop fusion | flops 4194304 | bytes 8388608 | tf_op jit(solution)/shard_map/convert_element_type | solution.py:90
  41.1 11.2 %all-to-all-start.1 = ((f32[128,8,128]{2,1,0:T(8,128)}), f32[128,8,128]{2,1,0:T(8,128)}, u32[]{:S(2)}, u32[]{:S(2)}) async-start(f32[128,8,128]{2,1,0:T(8,128)} %bitcast.4), calls=%async_computation.1 | async-start | bytes 1048576 | tf_op jit(solution)/shard_map/all_to_all | solution.py:145
  53.0 4.4 %reduce-precision_convert_fusion = (bf16[1024,1024]{1,0:T(8,128)(2,1)S(1)}, bf16[1024,1024]{1,0:T(8,128)(2,1)}) fusion(f32[1024,1024]{1,0:T(8,128)} %param.17), kind=kLoop, calls=%fused_computation.1 | loop fusion | flops 4194304 | bytes 8388608 | tf_op jit(solution)/shard_map/convert_element_type | solution.py:90
  57.5 7.4 %all-to-all-done.1 = f32[128,8,128]{2,1,0:T(8,128)} async-done(((f32[128,8,128]{2,1,0:T(8,128)}), f32[128,8,128]{2,1,0:T(8,128)}, u32[]{:S(2)}, u32[]{:S(2)}) %all-to-all-start.1) | async-done | bytes 524320 | tf_op jit(solution)/shard_map/all_to_all | solution.py:145
  77.0 6.0 %all-to-all-start.2 = ((f32[128,8,128]{2,1,0:T(8,128)}), f32[128,8,128]{2,1,0:T(8,128)}, u32[]{:S(2)}, u32[]{:S(2)}) async-start(f32[128,8,128]{2,1,0:T(8,128)} %bitcast.233), calls=%async_computation.2 | async-start | bytes 1048576 | tf_op jit(solution)/shard_map/all_to_all | solution.py:151
  84.1 4.4 %fusion.7 = bf16[16,66,1024]{2,1,0:T(8,128)(2,1)} fusion(bf16[15,1,1024]{2,1,0:T(2,128)(2,1)S(1)} %get-tuple-element.19, bf16[15,1,1024]{2,1,0:T(2,128)(2,1)S(1)} %get-tuple-element.18, bf16[16,64,1024]{2,1,0:T(8,128)(2,1)} %bitcast.221), kind=kLoop, calls=%fused_computation.13 | loop fusion | flops 10813440 | bytes 4321280 | tf_op jit(solution)/shard_map/concatenate | solution.py:134
  88.5 7.1 %all-to-all-done.2 = f32[128,8,128]{2,1,0:T(8,128)} async-done(((f32[128,8,128]{2,1,0:T(8,128)}), f32[128,8,128]{2,1,0:T(8,128)}, u32[]{:S(2)}, u32[]{:S(2)}) %all-to-all-start.2) | async-done | bytes 524320 | tf_op jit(solution)/shard_map/all_to_all | solution.py:151
  95.7 2.7 %fusion.58 = f32[16,66,128]{2,1,0:T(8,128)S(1)} fusion(bf16[16,66,1024]{2,1,0:T(8,128)(2,1)} %fusion.7, f32[128,8,128]{2,1,0:T(8,128)} %all-to-all-done.2), kind=kOutput, calls=%fused_computation.120 | convolution fusion | flops 277217280 | bytes 3227648 | tf_op jit(solution)/shard_map/iy,bri->bry/dot_general | solution.py:98
  100.4 3.0 %fusion.11 = f32[16,66,128]{2,1,0:T(8,128)} fusion(f32[16,66,128]{2,1,0:T(8,128)S(1)} %fusion.70, f32[16,66,128]{2,1,0:T(8,128)S(1)} %fusion.58, f32[128,8,128]{2,1,0:T(8,128)} %all-to-all-done.2, bf16[15,1,1024]{2,1,0:T(2,128)(2,1)S(1)} %get-tuple-element.17, bf16[15,1,1024]{2,1,0:T(2,128)(2,1)S(1)} %get-tuple-element.16, ...), kind=kOutput, calls=%fused_computation.19 | convolution fusion | flops 288169984 | bytes 4304896 | tf_op jit(solution)/shard_map/iy,bri->bry/dot_general | solution.py:98
  103.4 4.4 %all-to-all-start.3 = ((f32[16,66,128]{2,1,0:T(8,128)}), f32[16,66,128]{2,1,0:T(8,128)}, u32[]{:S(2)}, u32[]{:S(2)}) async-start(f32[16,66,128]{2,1,0:T(8,128)} %fusion.11), calls=%async_computation.3 | async-start | bytes 1179648 | tf_op jit(solution)/shard_map/all_to_all | solution.py:154
  109.9 3.5 %collective-permute-start.3 = (f32[16,128]{1,0:T(8,128)S(1)}, f32[16,128]{1,0:T(8,128)S(1)}, u32[]{:S(2)}, u32[]{:S(2)}) collective-permute-start(f32[16,128]{1,0:T(8,128)S(1)} %get-tuple-element.49), channel_id=1, source_target_pairs={{0,1},{1,2},{2,3},{3,4},{4,5},{5,6},{6,7},{7,8},{8,9},{9,10},{10,1... | collective-permute-start | bytes 24584 | tf_op jit(solution)/shard_map/ppermute | solution.py:20
  125.4 3.4 %collective-permute-start.7 = (f32[16,64]{1,0:T(8,128)S(1)}, f32[16,64]{1,0:T(8,128)S(1)}, u32[]{:S(2)}, u32[]{:S(2)}) collective-permute-start(f32[16,64]{1,0:T(8,128)S(1)} %bitcast.250), channel_id=1, source_target_pairs={{0,16},{16,32},{32,48},{48,64},{64,80},{80,96},{96,112},{1,17},{17... | collective-permute-start | bytes 12296 | tf_op jit(solution)/shard_map/ppermute | solution.py:20
  131.0 4.3 %collective-permute-start.5 = (f32[16,64]{1,0:T(8,128)S(1)}, f32[16,64]{1,0:T(8,128)S(1)}, u32[]{:S(2)}, u32[]{:S(2)}) collective-permute-start(f32[16,64]{1,0:T(8,128)S(1)} %bitcast.256), channel_id=1, source_target_pairs={{16,0},{32,16},{48,32},{64,48},{80,64},{96,80},{112,96},{17,1},{33... | collective-permute-start | bytes 12296 | tf_op jit(solution)/shard_map/ppermute | solution.py:20
  139.0 6.2 %multiply_multiply_fusion = (f32[16,64,128]{2,0,1:T(8,128)S(1)}, f32[16,64,128]{2,0,1:T(8,128)}) fusion(f32[128]{0:T(128)S(1)} %copy-done.20, f32[64]{0:T(128)S(1)} %copy-done.21, f32[16,64,127]{2,0,1:T(8,128)} %get-tuple-element.55, f32[16,64,1]{2,0,1:T(8,128)} %copy.180, f32[16,64,127]{2,0,1:T(8,128)} %get-tuple-element.51, f32[16,64,1]{2,0,1:T(8,128)} %copy.177, ...), kind=kLoop, calls=%fused_computation.105 | loop fusion | flops 7077888 | bytes 9306880 | tf_op jit(solution)/shard_map/mul | solution.py:138
  145.4 15.2 %all_to_all.54 = f32[16,64,128]{2,1,0:T(8,128)S(1)} all-to-all(f32[16,64,128]{2,1,0:T(8,128)S(1)} %copy.182), channel_id=1, replica_groups=mesh['gx'=8,'gy'=16] {'gy'}, dimensions={0} | all-to-all | bytes 1048576 | tf_op jit(solution)/shard_map/all_to_all | solution.py:141
  166.1 21.2 %all_to_all.55 = f32[128,8,128]{2,1,0:T(8,128)S(1)} all-to-all(f32[128,8,128]{2,1,0:T(8,128)} %bitcast.234), channel_id=1, replica_groups=mesh['gx'=8,'gy'=16] {'gx','gy'}, dimensions={0} | all-to-all | bytes 1048576 | tf_op jit(solution)/shard_map/all_to_all | solution.py:145
  196.0 17.5 %all_to_all.56 = f32[128,8,128]{2,1,0:T(8,128)S(1)} all-to-all(f32[128,8,128]{2,1,0:T(8,128)S(1)} %bitcast.235), channel_id=1, replica_groups=mesh['gx'=8,'gy'=16] {'gx','gy'}, dimensions={0} | all-to-all | bytes 1048576 | tf_op jit(solution)/shard_map/all_to_all | solution.py:151
  217.0 14.6 %all_to_all.57 = f32[16,66,128]{2,1,0:T(8,128)S(1)} all-to-all(f32[16,66,128]{2,1,0:T(8,128)S(1)} %fusion.10), channel_id=1, replica_groups=mesh['gx'=8,'gy'=16] {'gy'}, dimensions={0} | all-to-all | bytes 1081344 | tf_op jit(solution)/shard_map/all_to_all | solution.py:154
  241.1 3.9 %collective-permute-start.8 = (f32[16,64]{1,0:T(8,128)S(1)}, f32[16,64]{1,0:T(8,128)S(1)}, u32[]{:S(2)}, u32[]{:S(2)}) collective-permute-start(f32[16,64]{1,0:T(8,128)S(1)} %bitcast.252), channel_id=1, source_target_pairs={{16,0},{32,16},{48,32},{64,48},{80,64},{96,80},{112,96},{17,1},{33... | collective-permute-start | bytes 12296 | tf_op jit(solution)/shard_map/ppermute | solution.py:20
  245.1 2.8 %collective-permute-start.9 = (f32[16,64]{1,0:T(8,128)S(1)}, f32[16,64]{1,0:T(8,128)S(1)}, u32[]{:S(2)}, u32[]{:S(2)}) collective-permute-start(f32[16,64]{1,0:T(8,128)S(1)} %bitcast.254), channel_id=1, source_target_pairs={{0,16},{16,32},{32,48},{48,64},{64,80},{80,96},{96,112},{1,17},{17... | collective-permute-start | bytes 12296 | tf_op jit(solution)/shard_map/ppermute | solution.py:20
  254.0 4.9 %fusion.48 = f32[16,64,128]{2,0,1:T(8,128)S(1)} fusion(f32[16,64,128]{2,0,1:T(8,128)} %get-tuple-element.11, f32[16,1,128]{2,0,1:T(8,128)S(1)} %get-tuple-element.63, f32[16,63,128]{2,0,1:T(8,128)} %get-tuple-element.31, f32[16,63,128]{2,0,1:T(8,128)} %get-tuple-element.30, f32[16,1,128]{2,0,1:T(8,128)S(1)} %get-tuple-element.62, f32[16,64,1]{2,0,1:T(8,128)} %copy.190, ...), kind=kLoop, calls=%fused_computation.97 | loop fusion | flops 6815744 | bytes 8781824 | tf_op jit(solution)/shard_map/sub | solution.py:161
  (137 shorter events, 90.8 us)
Async XLA Ops:
  0.6 16.3 %copy-start.8 = (s32[16,64,128]{2,1,0:T(8,128)S(1)}, s32[16,64,128]{2,1,0:T(8,128)}, u32[]{:S(2)}) copy-start(s32[16,64,128]{2,1,0:T(8,128)} %param.13) | copy-start | bytes 1572868
  2.1 137.0 %collective-permute-start = (f32[16,128]{1,0:T(8,128)S(1)}, f32[16,128]{1,0:T(8,128)S(1)}, u32[]{:S(2)}, u32[]{:S(2)}) collective-permute-start(f32[16,128]{1,0:T(8,128)S(1)} %get-tuple-element.44), channel_id=1, source_target_pairs={{1,0},{2,1},{3,2},{4,3},{5,4},{6,5},{7,6},{8,7},{9,8},{10,9},{11,1... | collective-permute-start | bytes 24584 | tf_op jit(solution)/shard_map/ppermute | solution.py:20
  4.7 134.4 %collective-permute-start.2 = (f32[16,128]{1,0:T(8,128)S(1)}, f32[16,128]{1,0:T(8,128)S(1)}, u32[]{:S(2)}, u32[]{:S(2)}) collective-permute-start(f32[16,128]{1,0:T(8,128)S(1)} %get-tuple-element.45), channel_id=1, source_target_pairs={{0,1},{1,2},{2,3},{3,4},{4,5},{5,6},{6,7},{7,8},{8,9},{9,10},{10,1... | collective-permute-start | bytes 24584 | tf_op jit(solution)/shard_map/ppermute | solution.py:20
  10.6 23.5 %all-to-all-start = ((f32[16,64,128]{2,1,0:T(8,128)}), f32[16,64,128]{2,1,0:T(8,128)}, u32[]{:S(2)}, u32[]{:S(2)}) async-start(f32[16,64,128]{2,1,0:T(8,128)} %copy.151), calls=%async_computation | async-start | bytes 1048576 | tf_op jit(solution)/shard_map/all_to_all | solution.py:141
  17.3 113.7 %collective-permute-start.1 = (f32[16,128]{1,0:T(8,128)S(1)}, f32[16,128]{1,0:T(8,128)S(1)}, u32[]{:S(2)}, u32[]{:S(2)}) collective-permute-start(f32[16,128]{1,0:T(8,128)S(1)} %get-tuple-element.48), channel_id=1, source_target_pairs={{1,0},{2,1},{3,2},{4,3},{5,4},{6,5},{7,6},{8,7},{9,8},{10,9},{11,1... | collective-permute-start | bytes 24584 | tf_op jit(solution)/shard_map/ppermute | solution.py:20
  19.8 94.8 %collective-permute-start.6 = (f32[16,64]{1,0:T(8,128)S(1)}, f32[16,64]{1,0:T(8,128)S(1)}, u32[]{:S(2)}, u32[]{:S(2)}) collective-permute-start(f32[16,64]{1,0:T(8,128)S(1)} %bitcast.246), channel_id=1, source_target_pairs={{0,16},{16,32},{32,48},{48,64},{64,80},{80,96},{96,112},{1,17},{17... | collective-permute-start | bytes 12296 | tf_op jit(solution)/shard_map/ppermute | solution.py:20
  25.2 84.7 %collective-permute-start.4 = (f32[16,64]{1,0:T(8,128)S(1)}, f32[16,64]{1,0:T(8,128)S(1)}, u32[]{:S(2)}, u32[]{:S(2)}) collective-permute-start(f32[16,64]{1,0:T(8,128)S(1)} %bitcast.249), channel_id=1, source_target_pairs={{16,0},{32,16},{48,32},{64,48},{80,64},{96,80},{112,96},{17,1},{33... | collective-permute-start | bytes 12296 | tf_op jit(solution)/shard_map/ppermute | solution.py:20
  41.1 23.8 %all-to-all-start.1 = ((f32[128,8,128]{2,1,0:T(8,128)}), f32[128,8,128]{2,1,0:T(8,128)}, u32[]{:S(2)}, u32[]{:S(2)}) async-start(f32[128,8,128]{2,1,0:T(8,128)} %bitcast.4), calls=%async_computation.1 | async-start | bytes 1048576 | tf_op jit(solution)/shard_map/all_to_all | solution.py:145
  77.0 18.7 %all-to-all-start.2 = ((f32[128,8,128]{2,1,0:T(8,128)}), f32[128,8,128]{2,1,0:T(8,128)}, u32[]{:S(2)}, u32[]{:S(2)}) async-start(f32[128,8,128]{2,1,0:T(8,128)} %bitcast.233), calls=%async_computation.2 | async-start | bytes 1048576 | tf_op jit(solution)/shard_map/all_to_all | solution.py:151
  103.4 14.7 %all-to-all-start.3 = ((f32[16,66,128]{2,1,0:T(8,128)}), f32[16,66,128]{2,1,0:T(8,128)}, u32[]{:S(2)}, u32[]{:S(2)}) async-start(f32[16,66,128]{2,1,0:T(8,128)} %fusion.11), calls=%async_computation.3 | async-start | bytes 1179648 | tf_op jit(solution)/shard_map/all_to_all | solution.py:154
  109.9 25.4 %collective-permute-start.3 = (f32[16,128]{1,0:T(8,128)S(1)}, f32[16,128]{1,0:T(8,128)S(1)}, u32[]{:S(2)}, u32[]{:S(2)}) collective-permute-start(f32[16,128]{1,0:T(8,128)S(1)} %get-tuple-element.49), channel_id=1, source_target_pairs={{0,1},{1,2},{2,3},{3,4},{4,5},{5,6},{6,7},{7,8},{8,9},{9,10},{10,1... | collective-permute-start | bytes 24584 | tf_op jit(solution)/shard_map/ppermute | solution.py:20
  123.0 16.0 %copy-start.10 = (f32[16,64,128]{2,1,0:T(8,128)S(1)}, f32[16,64,128]{2,1,0:T(8,128)}, u32[]{:S(2)}) copy-start(f32[16,64,128]{2,1,0:T(8,128)} %param.12) | copy-start | bytes 1572868
  123.0 16.0 %copy-start.20 = (f32[128]{0:T(128)S(1)}, f32[128]{0:T(128)}, u32[]{:S(2)}) copy-start(f32[128]{0:T(128)} %param.18) | copy-start | bytes 1540
  123.0 16.0 %copy-start.21 = (f32[64]{0:T(128)S(1)}, f32[64]{0:T(128)}, u32[]{:S(2)}) copy-start(f32[64]{0:T(128)} %param.15) | copy-start | bytes 772
  125.4 12.5 %collective-permute-start.7 = (f32[16,64]{1,0:T(8,128)S(1)}, f32[16,64]{1,0:T(8,128)S(1)}, u32[]{:S(2)}, u32[]{:S(2)}) collective-permute-start(f32[16,64]{1,0:T(8,128)S(1)} %bitcast.250), channel_id=1, source_target_pairs={{0,16},{16,32},{32,48},{48,64},{64,80},{80,96},{96,112},{1,17},{17... | collective-permute-start | bytes 12296 | tf_op jit(solution)/shard_map/ppermute | solution.py:20
  131.0 5.9 %collective-permute-start.5 = (f32[16,64]{1,0:T(8,128)S(1)}, f32[16,64]{1,0:T(8,128)S(1)}, u32[]{:S(2)}, u32[]{:S(2)}) collective-permute-start(f32[16,64]{1,0:T(8,128)S(1)} %bitcast.256), channel_id=1, source_target_pairs={{16,0},{32,16},{48,32},{64,48},{80,64},{96,80},{112,96},{17,1},{33... | collective-permute-start | bytes 12296 | tf_op jit(solution)/shard_map/ppermute | solution.py:20
  145.3 15.5 %copy-start.5 = (bf16[1024,1024]{1,0:T(8,128)(2,1)S(1)}, bf16[1024,1024]{1,0:T(8,128)(2,1)}, u32[]{:S(2)}) copy-start(bf16[1024,1024]{1,0:T(8,128)(2,1)} %get-tuple-element.14) | copy-start | bytes 6291460
  166.1 21.3 %copy-start.7 = (bf16[1024,1024]{1,0:T(8,128)(2,1)S(1)}, bf16[1024,1024]{1,0:T(8,128)(2,1)}, u32[]{:S(2)}) copy-start(bf16[1024,1024]{1,0:T(8,128)(2,1)} %get-tuple-element.13) | copy-start | bytes 6291460
  195.1 18.4 %copy-start.3 = (bf16[16,66,1024]{2,1,0:T(8,128)(2,1)S(1)}, bf16[16,66,1024]{2,1,0:T(8,128)(2,1)}, u32[]{:S(2)}) copy-start(bf16[16,66,1024]{2,1,0:T(8,128)(2,1)} %fusion.7) | copy-start | bytes 6488068
  238.4 15.6 %copy-start.15 = (f32[16,64,1]{2,0,1:T(8,128)S(1)}, f32[16,64,1]{2,0,1:T(8,128)}, u32[]{:S(2)}) copy-start(f32[16,64,1]{2,0,1:T(8,128)} %copy.171) | copy-start | bytes 12292
  238.4 15.6 %copy-start.16 = (f32[16,64,1]{2,0,1:T(8,128)S(1)}, f32[16,64,1]{2,0,1:T(8,128)}, u32[]{:S(2)}) copy-start(f32[16,64,1]{2,0,1:T(8,128)} %copy.177) | copy-start | bytes 12292
  238.4 15.6 %copy-start.17 = (f32[15,64,128]{2,0,1:T(8,128)S(1)}, f32[15,64,128]{2,0,1:T(8,128)}, u32[]{:S(2)}) copy-start(f32[15,64,128]{2,0,1:T(8,128)} %get-tuple-element.38) | copy-start | bytes 1474564
  241.1 11.8 %collective-permute-start.8 = (f32[16,64]{1,0:T(8,128)S(1)}, f32[16,64]{1,0:T(8,128)S(1)}, u32[]{:S(2)}, u32[]{:S(2)}) collective-permute-start(f32[16,64]{1,0:T(8,128)S(1)} %bitcast.252), channel_id=1, source_target_pairs={{16,0},{32,16},{48,32},{64,48},{80,64},{96,80},{112,96},{17,1},{33... | collective-permute-start | bytes 12296 | tf_op jit(solution)/shard_map/ppermute | solution.py:20
  245.1 6.8 %collective-permute-start.9 = (f32[16,64]{1,0:T(8,128)S(1)}, f32[16,64]{1,0:T(8,128)S(1)}, u32[]{:S(2)}, u32[]{:S(2)}) collective-permute-start(f32[16,64]{1,0:T(8,128)S(1)} %bitcast.254), channel_id=1, source_target_pairs={{0,16},{16,32},{32,48},{48,64},{64,80},{80,96},{96,112},{1,17},{17... | collective-permute-start | bytes 12296 | tf_op jit(solution)/shard_map/ppermute | solution.py:20
  (12 other events, 66.9 us)

commit v3 on v1

--- a/solution.py
+++ b/solution.py
@@ -27,26 +27,36 @@
     return 2.0 * first * second / (first + second)
 
 
-def neighbours(center, strips):
+def framed(center, strips):
     (x_low, x_high), (y_low, y_high) = strips
-    zeros = jnp.zeros_like(center[:1])
+    rows = jnp.concatenate([x_low[:, None, :], center, x_high[:, None, :]], axis=1)
+    corner = jnp.zeros_like(center[:, :1, :1])
+    low = jnp.concatenate([corner, y_low[:, :, None], corner], axis=1)
+    high = jnp.concatenate([corner, y_high[:, :, None], corner], axis=1)
+    block = jnp.concatenate([low, rows, high], axis=2)
+    return jnp.pad(block, ((1, 1), (0, 0), (0, 0)))
+
+
+def neighbours(padded):
     return [
-        jnp.concatenate([center[1:], zeros], axis=0),
-        jnp.concatenate([zeros, center[:-1]], axis=0),
-        jnp.concatenate([center[:, 1:], x_high[:, None, :]], axis=1),
-        jnp.concatenate([x_low[:, None, :], center[:, :-1]], axis=1),
-        jnp.concatenate([center[:, :, 1:], y_high[:, :, None]], axis=2),
-        jnp.concatenate([y_low[:, :, None], center[:, :, :-1]], axis=2),
+        padded[2:, 1:-1, 1:-1],
+        padded[:-2, 1:-1, 1:-1],
+        padded[1:-1, 2:, 1:-1],
+        padded[1:-1, :-2, 1:-1],
+        padded[1:-1, 1:-1, 2:],
+        padded[1:-1, 1:-1, :-2],
     ]
 
 
 def faces_from(center):
-    return [harmonic(center, other) for other in neighbours(center, edges(center))]
+    padded = framed(center, edges(center))
+    return [harmonic(center, other) for other in neighbours(padded)]
 
 
 def stencil(center, faces):
+    padded = framed(center, edges(center))
     result = storage_term * center
-    for face, other in zip(faces, neighbours(center, edges(center))):
+    for face, other in zip(faces, neighbours(padded)):
         result = result + face * (center - other)
     return result
 

time: 237 us -> 249 us (1.051)
  blocking collectives: 65.2 us -> 82.1 us
  other arithmetic: 25 us -> 33.8 us
  starting transfers between devices: 67.9 us -> 60.2 us
  matrix products: 28.6 us -> 25.3 us
  local copies, waits for them, and re-layouts: 29.2 us -> 26.3 us
    all_to_all x2 -> x3, blocking collectives: 36.5 us -> 53 us  [shards(): lax.all_to_all(chunks, everyone, split_axis=0, concat_axis=0, tiled=True)]
    slice x9 -> x2, local copies, waits for them, and re-layouts: 9.98 us -> 1.77 us  [neighbours(): padded[2:, 1:-1, 1:-1]]
    concatenate x0 -> x9, local copies, waits for them, and re-layouts: none -> 7.44 us  [the longest x4 3.71 us: framed(): low = jnp.concatenate([corner, y_low[:, :, None], corner], axis=1)]
    all_to_all x2 -> x1, starting transfers between devices: 16 us -> 8.85 us  [shards(): lax.all_to_all(chunks, everyone, split_axis=0, concat_axis=0, tiled=True)]
    concatenate x0 -> x6, other arithmetic: none -> 5.71 us  [the longest x3 4.27 us: framed(): block = jnp.concatenate([low, rows, high], axis=2)]
    broadcast_in_dim x6 -> x0, local copies, waits for them, and re-layouts: 5.5 us -> none  [the longest x3 3.16 us: neighbours(): y_low[:, :, None]]
    all_to_all x1, waiting for transfers between devices: 5.22 us -> 0.01 us  [shards(): lax.all_to_all(solved, 'gy', split_axis=1, concat_axis=0, tiled=True)]
    all_to_all x1, waiting for transfers between devices: 0.01 us -> 4.42 us  [shards(): lax.all_to_all(scaled, 'gy', split_axis=0, concat_axis=1, tiled=True)]
  transfers between devices with their start and end apart: 16 -> 15, of which waited for: 4 -> 3; matrix products, arithmetic and copies ran while one was open for 21% -> 14% of each run, Pallas kernels for 1% -> 0%
where the time goes in v3:
time: 249 us; the launch traced here: 248 us
  blocking collectives  82.1 us (33%)
  starting transfers between devices  60.2 us (24%)
  other arithmetic  33.8 us (14%)
  local copies, waits for them, and re-layouts  26.3 us (11%)
  matrix products  25.3 us (10%)
  waiting for transfers between devices  14.5 us (6%)
  Pallas kernels  4.14 us (2%)
    all_to_all x3, blocking collectives, shards(): lax.all_to_all(chunks, everyone, split_axis=0, concat_axis=0, tiled=True)  53 us
    dot_general x24, matrix products, product(): return jnp.einsum(spec, first, second, preferred_element_type=jnp.float32)  25.3 us
    ppermute x6, starting transfers between devices, edges(): lax.ppermute(last, axis, forward)  20.5 us
    ppermute x6, starting transfers between devices, edges(): lax.ppermute(first, axis, backward)  20 us
    all_to_all x1, blocking collectives, shards(): lax.all_to_all(scaled, 'gy', split_axis=0, concat_axis=1, tiled=True)  16.3 us
    all_to_all x1, blocking collectives, shards(): lax.all_to_all(solved, 'gy', split_axis=1, concat_axis=0, tiled=True)  12.8 us
    convert_element_type x2, other arithmetic, split_bf16(): rounded.astype(jnp.bfloat16)  8.92 us
    all_to_all x1, starting transfers between devices, shards(): lax.all_to_all(chunks, everyone, split_axis=0, concat_axis=0, tiled=True)  8.85 us
  transfers between devices with their start and end apart: 15, of which 3 were waited for; matrix products, arithmetic and copies ran while one was open for 14% of the time, Pallas kernels for 0%

profile of v3, /device:TPU:3, one launch (start us, length us, event | category | flops | bytes accessed | tf_op | source)
XLA Modules:
  0.0 247.9 jit_solution(12053381213445954515)
XLA Ops:
  2.6 6.5 %all-to-all-start = ((f32[16,64,128]{2,1,0:T(8,128)}), f32[16,64,128]{2,1,0:T(8,128)S(1)}, u32[]{:S(2)}, u32[]{:S(2)}) async-start(f32[16,64,128]{2,1,0:T(8,128)} %multiply_multiply_fusion.1), calls=%async_computation | async-start | bytes 1048576 | tf_op jit(solution)/shard_map/all_to_all | solution.py:141
  9.9 4.4 %reduce-precision_convert_fusion.1 = (bf16[1024,1024]{1,0:T(8,128)(2,1)S(1)}, bf16[1024,1024]{1,0:T(8,128)(2,1)}) fusion(f32[1024,1024]{1,0:T(8,128)} %param.14), kind=kLoop, calls=%fused_computation.3 | loop fusion | flops 4194304 | bytes 8388608 | tf_op jit(solution)/shard_map/convert_element_type | solution.py:99
  14.3 4.4 %all-to-all-done = f32[16,64,128]{2,1,0:T(8,128)S(1)} async-done(((f32[16,64,128]{2,1,0:T(8,128)}), f32[16,64,128]{2,1,0:T(8,128)S(1)}, u32[]{:S(2)}, u32[]{:S(2)}) %all-to-all-start) | async-done | bytes 524320 | tf_op jit(solution)/shard_map/all_to_all | solution.py:141
  22.9 8.8 %all-to-all-start.1 = ((f32[128,8,128]{2,1,0:T(8,128)}), f32[128,8,128]{2,1,0:T(8,128)S(1)}, u32[]{:S(2)}, u32[]{:S(2)}) async-start(f32[128,8,128]{2,1,0:T(8,128)} %bitcast.3), calls=%async_computation.1 | async-start | bytes 1048576 | tf_op jit(solution)/shard_map/all_to_all | solution.py:145
  32.5 4.5 %reduce-precision_convert_fusion = (bf16[1024,1024]{1,0:T(8,128)(2,1)S(1)}, bf16[1024,1024]{1,0:T(8,128)(2,1)}) fusion(f32[1024,1024]{1,0:T(8,128)} %param.17), kind=kLoop, calls=%fused_computation.1 | loop fusion | flops 4194304 | bytes 8388608 | tf_op jit(solution)/shard_map/convert_element_type | solution.py:99
  36.9 7.8 %all-to-all-done.1 = f32[128,8,128]{2,1,0:T(8,128)S(1)} async-done(((f32[128,8,128]{2,1,0:T(8,128)}), f32[128,8,128]{2,1,0:T(8,128)S(1)}, u32[]{:S(2)}, u32[]{:S(2)}) %all-to-all-start.1) | async-done | bytes 524320 | tf_op jit(solution)/shard_map/all_to_all | solution.py:145
  50.6 2.5 %convolution_bitcast_fusion.12 = f32[8,16,8,128]{3,2,0,1:T(8,128)S(1)} fusion(bf16[8,128,1024,1]{2,1,0,3:T(8,128)(2,1)} %bitcast.215, f32[16,8,1024]{2,1,0:T(8,128)} %shard_map.122), kind=kOutput, calls=%fused_computation.34 | convolution fusion | flops 268697600 | bytes 3145728 | tf_op jit(solution)/shard_map/zij,alj->azil/dot_general | solution.py:107
  54.9 17.5 %all_to_all.68 = f32[128,8,128]{2,1,0:T(8,128)S(1)} all-to-all(f32[128,8,128]{2,1,0:T(8,128)S(1)} %bitcast.224), channel_id=1, replica_groups=mesh['gx'=8,'gy'=16] {'gx','gy'}, dimensions={0} | all-to-all | bytes 1048576 | tf_op jit(solution)/shard_map/all_to_all | solution.py:151
  76.0 4.4 %all-to-all-start.3 = ((f32[1,1024,128]{2,0,1:T(1,128)}), f32[1,1024,128]{2,0,1:T(1,128)}, u32[]{:S(2)}, u32[]{:S(2)}) async-start(f32[1,1024,128]{2,0,1:T(1,128)} %copy.156), calls=%async_computation.3 | async-start | bytes 1048576 | tf_op jit(solution)/shard_map/all_to_all | solution.py:154
  82.7 3.4 %collective-permute-start = (f32[16,64]{1,0:T(8,128)S(1)}, f32[16,64]{1,0:T(8,128)S(1)}, u32[]{:S(2)}, u32[]{:S(2)}) collective-permute-start(f32[16,64]{1,0:T(8,128)S(1)} %bitcast.245), channel_id=1, source_target_pairs={{0,16},{16,32},{32,48},{48,64},{64,80},{80,96},{96,112},{1,17},{17... | collective-permute-start | bytes 12296 | tf_op jit(solution)/shard_map/ppermute | solution.py:22
  87.4 4.3 %collective-permute-start.3 = (f32[16,64]{1,0:T(8,128)S(1)}, f32[16,64]{1,0:T(8,128)S(1)}, u32[]{:S(2)}, u32[]{:S(2)}) collective-permute-start(f32[16,64]{1,0:T(8,128)S(1)} %bitcast.244), channel_id=1, source_target_pairs={{16,0},{32,16},{48,32},{64,48},{80,64},{96,80},{112,96},{17,1},{33... | collective-permute-start | bytes 12296 | tf_op jit(solution)/shard_map/ppermute | solution.py:22
  92.0 4.1 %collective-permute-start.1 = (f32[16,128]{1,0:T(8,128)S(1)}, f32[16,128]{1,0:T(8,128)S(1)}, u32[]{:S(2)}, u32[]{:S(2)}) collective-permute-start(f32[16,128]{1,0:T(8,128)S(1)} %get-tuple-element.25), channel_id=1, source_target_pairs={{0,1},{1,2},{2,3},{3,4},{4,5},{5,6},{6,7},{7,8},{8,9},{9,10},{10,1... | collective-permute-start | bytes 24584 | tf_op jit(solution)/shard_map/ppermute | solution.py:22
  105.8 5.4 %collective-permute-start.7 = (f32[16,64]{1,0:T(8,128)S(1)}, f32[16,64]{1,0:T(8,128)S(1)}, u32[]{:S(2)}, u32[]{:S(2)}) collective-permute-start(f32[16,64]{1,0:T(8,128)S(1)} %bitcast.246), channel_id=1, source_target_pairs={{16,0},{32,16},{48,32},{64,48},{80,64},{96,80},{112,96},{17,1},{33... | collective-permute-start | bytes 12296 | tf_op jit(solution)/shard_map/ppermute | solution.py:22
  114.1 3.6 %collective-permute-start.5 = (f32[16,128]{1,0:T(8,128)S(1)}, f32[16,128]{1,0:T(8,128)S(1)}, u32[]{:S(2)}, u32[]{:S(2)}) collective-permute-start(f32[16,128]{1,0:T(8,128)S(1)} %get-tuple-element.27), channel_id=1, source_target_pairs={{0,1},{1,2},{2,3},{3,4},{4,5},{5,6},{6,7},{7,8},{8,9},{9,10},{10,1... | collective-permute-start | bytes 24584 | tf_op jit(solution)/shard_map/ppermute | solution.py:22
  122.1 3.0 %select_maximum_fusion.6 = f32[18,66,130]{2,1,0:T(8,128)} fusion(f32[16,66,1]{2,1,0:T(8,128)} %copy.164, f32[16,66,1]{2,1,0:T(8,128)} %copy.163, f32[16,1,128]{2,1,0:T(1,128)S(1)} %bitcast.232, f32[16,64,128]{2,1,0:T(8,128)S(1)} %copy-done.7, f32[16,1,128]{2,1,0:T(1,128)S(1)} %bitcast.229), kind=kLoop, calls=%fused_computation.17 | loop fusion | flops 1853280 | bytes 1166880 | tf_op jit(solution)/shard_map/concatenate | solution.py:36
  135.4 4.2 %multiply_multiply_fusion = (f32[16,64,128]{2,1,0:T(8,128)S(1)}, f32[16,64,128]{2,1,0:T(8,128)}) fusion(f32[128]{0:T(128)S(1)} %copy-done.36, f32[64]{0:T(128)S(1)} %copy-done.37, f32[16,64,128]{2,1,0:T(8,128)S(1)} %copy-done.33, f32[16,64,128]{2,1,0:T(8,128)} %bitcast.31, s32[16,64,128]{2,1,0:T(8,128)S(1)} %copy-done.14, f32[16,64,128]{2,1,0:T(8,128)S(1)} %copy-done.24, ...), kind=kLoop, calls=%fused_computation.160 | loop fusion | flops 6684672 | bytes 5817600 | tf_op jit(solution)/shard_map/mul | solution.py:138
  139.6 16.3 %all_to_all.69 = f32[16,64,128]{2,1,0:T(8,128)S(1)} all-to-all(f32[16,64,128]{2,1,0:T(8,128)S(1)} %get-tuple-element.4), channel_id=1, replica_groups=mesh['gx'=8,'gy'=16] {'gy'}, dimensions={0} | all-to-all | bytes 1048576 | tf_op jit(solution)/shard_map/all_to_all | solution.py:141
  160.6 17.9 %all_to_all.70 = f32[128,8,128]{2,1,0:T(8,128)S(1)} all-to-all(f32[128,8,128]{2,1,0:T(8,128)S(1)} %bitcast.225), channel_id=1, replica_groups=mesh['gx'=8,'gy'=16] {'gx','gy'}, dimensions={0} | all-to-all | bytes 1048576 | tf_op jit(solution)/shard_map/all_to_all | solution.py:145
  187.2 17.5 %all_to_all.71 = f32[128,8,128]{2,1,0:T(8,128)S(1)} all-to-all(f32[128,8,128]{2,1,0:T(8,128)S(1)} %bitcast.226), channel_id=1, replica_groups=mesh['gx'=8,'gy'=16] {'gx','gy'}, dimensions={0} | all-to-all | bytes 1048576 | tf_op jit(solution)/shard_map/all_to_all | solution.py:151
  209.3 12.8 %all_to_all.72 = f32[1,1024,128]{2,0,1:T(1,128)S(1)} all-to-all(f32[1,1024,128]{2,0,1:T(1,128)S(1)} %copy.190), channel_id=1, replica_groups=mesh['gx'=8,'gy'=16] {'gy'}, dimensions={1} | all-to-all | bytes 1048576 | tf_op jit(solution)/shard_map/all_to_all | solution.py:154
  225.0 3.1 %collective-permute-start.8 = (f32[16,64]{1,0:T(8,128)S(1)}, f32[16,64]{1,0:T(8,128)S(1)}, u32[]{:S(2)}, u32[]{:S(2)}) collective-permute-start(f32[16,64]{1,0:T(8,128)S(1)} %get-tuple-element.3), channel_id=1, source_target_pairs={{0,16},{16,32},{32,48},{48,64},{64,80},{80,96},{96,112},{1,17},{17... | collective-permute-start | bytes 12296 | tf_op jit(solution)/shard_map/ppermute | solution.py:22
  228.1 4.6 %collective-permute-start.11 = (f32[16,64]{1,0:T(8,128)S(1)}, f32[16,64]{1,0:T(8,128)S(1)}, u32[]{:S(2)}, u32[]{:S(2)}) collective-permute-start(f32[16,64]{1,0:T(8,128)S(1)} %get-tuple-element.2), channel_id=1, source_target_pairs={{16,0},{32,16},{48,32},{64,48},{80,64},{96,80},{112,96},{17,1},{33... | collective-permute-start | bytes 12296 | tf_op jit(solution)/shard_map/ppermute | solution.py:22
  232.7 3.8 %collective-permute-start.9 = (f32[16,128]{1,0:T(8,128)S(1)}, f32[16,128]{1,0:T(8,128)S(1)}, u32[]{:S(2)}, u32[]{:S(2)}) collective-permute-start(f32[16,128]{1,0:T(8,128)S(1)} %get-tuple-element.12), channel_id=1, source_target_pairs={{0,1},{1,2},{2,3},{3,4},{4,5},{5,6},{6,7},{7,8},{8,9},{9,10},{10,1... | collective-permute-start | bytes 24584 | tf_op jit(solution)/shard_map/ppermute | solution.py:22
  244.0 3.9 %fusion.34 = f32[16,64,128]{2,1,0:T(8,128)} fusion(f32[16,64,128]{2,1,0:T(8,128)S(1)} %copy-done.34, f32[16,64,128]{2,1,0:T(8,128)S(1)} %get-tuple-element.14, f32[16,66,1]{2,1,0:T(8,128)S(1)} %copy-done.17, f32[16,1,128]{2,1,0:T(1,128)S(1)} %bitcast.241, f32[16,1,128]{2,1,0:T(1,128)S(1)} %bitcast.239, f32[16,66,1]{2,1,0:T(8,128)S(1)} %copy-done.19, ...), kind=kLoop, calls=%fused_computation.90 | loop fusion | flops 6815744 | bytes 4768256 | tf_op jit(solution)/shard_map/sub | solution.py:158
  (167 shorter events, 77.7 us)
Async XLA Ops:
  2.6 16.1 %all-to-all-start = ((f32[16,64,128]{2,1,0:T(8,128)}), f32[16,64,128]{2,1,0:T(8,128)S(1)}, u32[]{:S(2)}, u32[]{:S(2)}) async-start(f32[16,64,128]{2,1,0:T(8,128)} %multiply_multiply_fusion.1), calls=%async_computation | async-start | bytes 1048576 | tf_op jit(solution)/shard_map/all_to_all | solution.py:141
  21.4 10.3 %copy-start.35 = (f32[1024]{0:T(1024)S(1)}, f32[1024]{0:T(1024)}, u32[]{:S(2)}) copy-start(f32[1024]{0:T(1024)} %param.19) | copy-start | bytes 12292
  22.9 21.8 %all-to-all-start.1 = ((f32[128,8,128]{2,1,0:T(8,128)}), f32[128,8,128]{2,1,0:T(8,128)S(1)}, u32[]{:S(2)}, u32[]{:S(2)}) async-start(f32[128,8,128]{2,1,0:T(8,128)} %bitcast.3), calls=%async_computation.1 | async-start | bytes 1048576 | tf_op jit(solution)/shard_map/all_to_all | solution.py:145
  54.0 18.4 %copy-start.4 = (bf16[1024,1024]{1,0:T(8,128)(2,1)S(1)}, bf16[1024,1024]{1,0:T(8,128)(2,1)}, u32[]{:S(2)}) copy-start(bf16[1024,1024]{1,0:T(8,128)(2,1)} %get-tuple-element.9) | copy-start | bytes 6291460
  54.9 18.4 %copy-start.1 = (bf16[1024,1024]{1,0:T(8,128)(2,1)S(1)}, bf16[1024,1024]{1,0:T(8,128)(2,1)}, u32[]{:S(2)}) copy-start(bf16[1024,1024]{1,0:T(8,128)(2,1)} %copy-done) | copy-start | bytes 6291460
  76.0 21.8 %all-to-all-start.3 = ((f32[1,1024,128]{2,0,1:T(1,128)}), f32[1,1024,128]{2,0,1:T(1,128)}, u32[]{:S(2)}, u32[]{:S(2)}) async-start(f32[1,1024,128]{2,0,1:T(1,128)} %copy.156), calls=%async_computation.3 | async-start | bytes 1048576 | tf_op jit(solution)/shard_map/all_to_all | solution.py:154
  80.4 15.8 %copy-start.13 = (s32[16,64,128]{2,1,0:T(8,128)S(1)}, s32[16,64,128]{2,1,0:T(8,128)}, u32[]{:S(2)}) copy-start(s32[16,64,128]{2,1,0:T(8,128)} %param.13) | copy-start | bytes 1572868
  82.7 29.4 %collective-permute-start = (f32[16,64]{1,0:T(8,128)S(1)}, f32[16,64]{1,0:T(8,128)S(1)}, u32[]{:S(2)}, u32[]{:S(2)}) collective-permute-start(f32[16,64]{1,0:T(8,128)S(1)} %bitcast.245), channel_id=1, source_target_pairs={{0,16},{16,32},{32,48},{48,64},{64,80},{80,96},{96,112},{1,17},{17... | collective-permute-start | bytes 12296 | tf_op jit(solution)/shard_map/ppermute | solution.py:22
  87.4 26.7 %collective-permute-start.3 = (f32[16,64]{1,0:T(8,128)S(1)}, f32[16,64]{1,0:T(8,128)S(1)}, u32[]{:S(2)}, u32[]{:S(2)}) collective-permute-start(f32[16,64]{1,0:T(8,128)S(1)} %bitcast.244), channel_id=1, source_target_pairs={{16,0},{32,16},{48,32},{64,48},{80,64},{96,80},{112,96},{17,1},{33... | collective-permute-start | bytes 12296 | tf_op jit(solution)/shard_map/ppermute | solution.py:22
  92.0 30.0 %collective-permute-start.1 = (f32[16,128]{1,0:T(8,128)S(1)}, f32[16,128]{1,0:T(8,128)S(1)}, u32[]{:S(2)}, u32[]{:S(2)}) collective-permute-start(f32[16,128]{1,0:T(8,128)S(1)} %get-tuple-element.25), channel_id=1, source_target_pairs={{0,1},{1,2},{2,3},{3,4},{4,5},{5,6},{6,7},{7,8},{8,9},{9,10},{10,1... | collective-permute-start | bytes 24584 | tf_op jit(solution)/shard_map/ppermute | solution.py:22
  102.0 15.7 %collective-permute-start.4 = (f32[16,64]{1,0:T(8,128)S(1)}, f32[16,64]{1,0:T(8,128)S(1)}, u32[]{:S(2)}, u32[]{:S(2)}) collective-permute-start(f32[16,64]{1,0:T(8,128)S(1)} %bitcast.247), channel_id=1, source_target_pairs={{0,16},{16,32},{32,48},{48,64},{64,80},{80,96},{96,112},{1,17},{17... | collective-permute-start | bytes 12296 | tf_op jit(solution)/shard_map/ppermute | solution.py:22
  105.8 13.9 %collective-permute-start.7 = (f32[16,64]{1,0:T(8,128)S(1)}, f32[16,64]{1,0:T(8,128)S(1)}, u32[]{:S(2)}, u32[]{:S(2)}) collective-permute-start(f32[16,64]{1,0:T(8,128)S(1)} %bitcast.246), channel_id=1, source_target_pairs={{16,0},{32,16},{48,32},{64,48},{80,64},{96,80},{112,96},{17,1},{33... | collective-permute-start | bytes 12296 | tf_op jit(solution)/shard_map/ppermute | solution.py:22
  112.1 9.9 %collective-permute-start.2 = (f32[16,128]{1,0:T(8,128)S(1)}, f32[16,128]{1,0:T(8,128)S(1)}, u32[]{:S(2)}, u32[]{:S(2)}) collective-permute-start(f32[16,128]{1,0:T(8,128)S(1)} %get-tuple-element.26), channel_id=1, source_target_pairs={{1,0},{2,1},{3,2},{4,3},{5,4},{6,5},{7,6},{8,7},{9,8},{10,9},{11,1... | collective-permute-start | bytes 24584 | tf_op jit(solution)/shard_map/ppermute | solution.py:22
  114.1 17.0 %collective-permute-start.5 = (f32[16,128]{1,0:T(8,128)S(1)}, f32[16,128]{1,0:T(8,128)S(1)}, u32[]{:S(2)}, u32[]{:S(2)}) collective-permute-start(f32[16,128]{1,0:T(8,128)S(1)} %get-tuple-element.27), channel_id=1, source_target_pairs={{0,1},{1,2},{2,3},{3,4},{4,5},{5,6},{6,7},{7,8},{8,9},{9,10},{10,1... | collective-permute-start | bytes 24584 | tf_op jit(solution)/shard_map/ppermute | solution.py:22
  117.7 13.3 %collective-permute-start.6 = (f32[16,128]{1,0:T(8,128)S(1)}, f32[16,128]{1,0:T(8,128)S(1)}, u32[]{:S(2)}, u32[]{:S(2)}) collective-permute-start(f32[16,128]{1,0:T(8,128)S(1)} %get-tuple-element.28), channel_id=1, source_target_pairs={{1,0},{2,1},{3,2},{4,3},{5,4},{6,5},{7,6},{8,7},{9,8},{10,9},{11,1... | collective-permute-start | bytes 24584 | tf_op jit(solution)/shard_map/ppermute | solution.py:22
  139.6 16.4 %copy-start.5 = (bf16[1024,1024]{1,0:T(8,128)(2,1)S(1)}, bf16[1024,1024]{1,0:T(8,128)(2,1)}, u32[]{:S(2)}) copy-start(bf16[1024,1024]{1,0:T(8,128)(2,1)} %get-tuple-element.9) | copy-start | bytes 6291460
  160.6 18.0 %copy-start.8 = (bf16[1024,1024]{1,0:T(8,128)(2,1)S(1)}, bf16[1024,1024]{1,0:T(8,128)(2,1)}, u32[]{:S(2)}) copy-start(bf16[1024,1024]{1,0:T(8,128)(2,1)} %get-tuple-element.7) | copy-start | bytes 6291460
  186.3 18.4 %copy-start.6 = (bf16[1024,1024]{1,0:T(8,128)(2,1)S(1)}, bf16[1024,1024]{1,0:T(8,128)(2,1)}, u32[]{:S(2)}) copy-start(bf16[1024,1024]{1,0:T(8,128)(2,1)} %get-tuple-element.9) | copy-start | bytes 6291460
  187.2 18.4 %copy-start.3 = (bf16[1024,1024]{1,0:T(8,128)(2,1)S(1)}, bf16[1024,1024]{1,0:T(8,128)(2,1)}, u32[]{:S(2)}) copy-start(bf16[1024,1024]{1,0:T(8,128)(2,1)} %copy-done) | copy-start | bytes 6291460
  206.4 15.7 %copy-start.15 = (s32[16,64,128]{2,1,0:T(8,128)S(1)}, s32[16,64,128]{2,1,0:T(8,128)}, u32[]{:S(2)}) copy-start(s32[16,64,128]{2,1,0:T(8,128)} %param.13) | copy-start | bytes 1572868
  225.0 13.4 %collective-permute-start.8 = (f32[16,64]{1,0:T(8,128)S(1)}, f32[16,64]{1,0:T(8,128)S(1)}, u32[]{:S(2)}, u32[]{:S(2)}) collective-permute-start(f32[16,64]{1,0:T(8,128)S(1)} %get-tuple-element.3), channel_id=1, source_target_pairs={{0,16},{16,32},{32,48},{48,64},{64,80},{80,96},{96,112},{1,17},{17... | collective-permute-start | bytes 12296 | tf_op jit(solution)/shard_map/ppermute | solution.py:22
  228.1 10.3 %collective-permute-start.11 = (f32[16,64]{1,0:T(8,128)S(1)}, f32[16,64]{1,0:T(8,128)S(1)}, u32[]{:S(2)}, u32[]{:S(2)}) collective-permute-start(f32[16,64]{1,0:T(8,128)S(1)} %get-tuple-element.2), channel_id=1, source_target_pairs={{16,0},{32,16},{48,32},{64,48},{80,64},{96,80},{112,96},{17,1},{33... | collective-permute-start | bytes 12296 | tf_op jit(solution)/shard_map/ppermute | solution.py:22
  232.7 6.5 %collective-permute-start.9 = (f32[16,128]{1,0:T(8,128)S(1)}, f32[16,128]{1,0:T(8,128)S(1)}, u32[]{:S(2)}, u32[]{:S(2)}) collective-permute-start(f32[16,128]{1,0:T(8,128)S(1)} %get-tuple-element.12), channel_id=1, source_target_pairs={{0,1},{1,2},{2,3},{3,4},{4,5},{5,6},{6,7},{7,8},{8,9},{9,10},{10,1... | collective-permute-start | bytes 24584 | tf_op jit(solution)/shard_map/ppermute | solution.py:22
  236.5 5.0 %collective-permute-start.10 = (f32[16,128]{1,0:T(8,128)S(1)}, f32[16,128]{1,0:T(8,128)S(1)}, u32[]{:S(2)}, u32[]{:S(2)}) collective-permute-start(f32[16,128]{1,0:T(8,128)S(1)} %get-tuple-element.13), channel_id=1, source_target_pairs={{1,0},{2,1},{3,2},{4,3},{5,4},{6,5},{7,6},{8,7},{9,8},{10,9},{11,1... | collective-permute-start | bytes 24584 | tf_op jit(solution)/shard_map/ppermute | solution.py:22
  (29 other events, 69.1 us)

commit v4 on v1

--- a/solution.py
+++ b/solution.py
@@ -44,11 +44,59 @@
     return [harmonic(center, other) for other in neighbours(center, edges(center))]
 
 
-def stencil(center, faces):
-    result = storage_term * center
-    for face, other in zip(faces, neighbours(center, edges(center))):
-        result = result + face * (center - other)
-    return result
+def stencil_kernel(
+    update_ref, active_ref, residual_ref, faces_ref, x_low_ref, x_high_ref,
+    y_low_ref, y_high_ref, mass_x_ref, mass_y_ref, out_ref, scaled_ref,
+):
+    planes, rows, cols = update_ref.shape
+    row = lax.broadcasted_iota(jnp.int32, (rows, cols), 0)
+    col = lax.broadcasted_iota(jnp.int32, (rows, cols), 1)
+    row_forward = pltpu.roll(row, 1, 0) == jnp.where(row == 0, rows - 1, row - 1)
+    col_forward = pltpu.roll(col, 1, 1) == jnp.where(col == 0, cols - 1, col - 1)
+
+    def before(plane, axis, count, forward):
+        return jnp.where(forward, pltpu.roll(plane, 1, axis), pltpu.roll(plane, count - 1, axis))
+
+    def after(plane, axis, count, forward):
+        return jnp.where(forward, pltpu.roll(plane, count - 1, axis), pltpu.roll(plane, 1, axis))
+
+    zeros = jnp.zeros((rows, cols), jnp.float32)
+    masked = [active_ref[z] * update_ref[z] for z in range(planes)]
+    for z in range(planes):
+        center = masked[z]
+        x_low = jnp.broadcast_to(x_low_ref[pl.ds(z, 1), :], (rows, cols))
+        x_high = jnp.broadcast_to(x_high_ref[pl.ds(z, 1), :], (rows, cols))
+        others = [
+            masked[z + 1] if z + 1 < planes else zeros,
+            masked[z - 1] if z > 0 else zeros,
+            jnp.where(row == rows - 1, x_high, after(center, 0, rows, row_forward)),
+            jnp.where(row == 0, x_low, before(center, 0, rows, row_forward)),
+            jnp.where(col == cols - 1, y_high_ref[z], after(center, 1, cols, col_forward)),
+            jnp.where(col == 0, y_low_ref[z], before(center, 1, cols, col_forward)),
+        ]
+        result = storage_term * center
+        for face, other in enumerate(others):
+            result = result + faces_ref[face, z] * (center - other)
+        update = update_ref[z]
+        image = result + (1.0 - active_ref[z]) * update
+        residual = residual_ref[z] - image
+        out_ref[z] = residual
+        scaled_ref[z] = residual * mass_x_ref[...] * mass_y_ref[...]
+
+
+def fused_stencil(update, active, residual, faces, x_strips, y_strips, mass_x, mass_y):
+    planes, rows, cols = update.shape
+    y_low, y_high = (jnp.broadcast_to(s[:, :, None], update.shape) for s in y_strips)
+    mass_x = jnp.broadcast_to(mass_x[:, None], (rows, cols))
+    mass_y = jnp.broadcast_to(mass_y[None, :], (rows, cols))
+    vmem = pl.BlockSpec(memory_space=pltpu.VMEM)
+    shape = jax.ShapeDtypeStruct(update.shape, update.dtype)
+    return pl.pallas_call(
+        stencil_kernel,
+        out_shape=(shape, shape),
+        in_specs=[vmem] * 10,
+        out_specs=(vmem, vmem),
+    )(update, active, residual, faces, x_strips[0], x_strips[1], y_low, y_high, mass_x, mass_y)
 
 
 def solve_kernel(diag_ref, coup_ref, shifts_ref, rhs_ref, out_ref, ratio_ref):
@@ -124,8 +172,9 @@
     blocks_y = lax.axis_size("gx")
     basis_x = split_bf16(vectors_x)
     basis_y = tuple(piece.reshape(blocks_y, -1, vectors_y.shape[1]) for piece in split_bf16(vectors_y))
+    faces = jnp.stack(faces)
+    scaled = residual * mass_x[None, :, None] * mass_y[None, None, :]
     for iteration in range(ITERS):
-        scaled = residual * mass_x[None, :, None] * mass_y[None, None, :]
         modes = transform(
             "zxy,xi->ziy",
             lax.all_to_all(scaled, "gy", split_axis=0, concat_axis=1, tiled=True),
@@ -143,9 +192,8 @@
         solved = transform("ziy,xi->zxy", solved, basis_x)
         update = lax.all_to_all(solved, "gy", split_axis=1, concat_axis=0, tiled=True)
         adjoint = adjoint + update
-        masked = active * update
-        image = stencil(masked, faces) + (1.0 - active) * update
-        residual = residual - image
+        x_strips, y_strips = edges(active * update)
+        residual, scaled = fused_stencil(update, active, residual, faces, x_strips, y_strips, mass_x, mass_y)
     return (adjoint, residual)
 
 

time: 237 us -> 246 us (1.038)
  Pallas kernels: 4.14 us -> 12.7 us
  local copies, waits for them, and re-layouts: 29.2 us -> 24 us
  other arithmetic: 25 us -> 28.6 us
  waiting for transfers between devices: 14.4 us -> 17.8 us
    unnamed x0 -> x5, other arithmetic: none -> 10 us
    pallas_call x0 -> x2, Pallas kernels: none -> 8.55 us  [fused_stencil(): pl.pallas_call(stencil_kernel, out_shape=(shape, shape), in_specs=[vmem]...]
    slice x7 -> x1, local copies, waits for them, and re-layouts: 7.76 us -> 1.13 us  [neighbours(): center[:-1]]
    mul x2 -> x1, other arithmetic: 7.83 us -> 1.99 us  [shards(): scaled = residual * mass_x[None, :, None] * mass_y[None, None, :]]
    broadcast_in_dim x0 -> x6, local copies, waits for them, and re-layouts: none -> 5.28 us  [the longest x4 3.99 us: fused_stencil(): jnp.broadcast_to(s[:, :, None], update.shape)]
    sub x1 -> x0, other arithmetic: 5.12 us -> none  [shards(): residual = residual - image]
    ppermute x6, starting transfers between devices: 18.7 us -> 23.3 us  [edges(): lax.ppermute(first, axis, backward)]
    ppermute x6, starting transfers between devices: 20.9 us -> 16.6 us  [edges(): lax.ppermute(last, axis, forward)]
  transfers between devices with their start and end apart: 16 -> 16, of which waited for: 4 -> 4; matrix products, arithmetic and copies ran while one was open for 21% -> 24% of each run, Pallas kernels for 1% -> 1%
where the time goes in v4:
time: 246 us; the launch traced here: 242 us
  starting transfers between devices  66.1 us (27%)
  blocking collectives  65 us (26%)
  other arithmetic  28.6 us (12%)
  matrix products  27 us (11%)
  local copies, waits for them, and re-layouts  24 us (10%)
  waiting for transfers between devices  17.8 us (7%)
  Pallas kernels  12.7 us (5%)
    all_to_all x2, blocking collectives, shards(): lax.all_to_all(chunks, everyone, split_axis=0, concat_axis=0, tiled=True)  38.1 us
    dot_general x24, matrix products, product(): return jnp.einsum(spec, first, second, preferred_element_type=jnp.float32)  27 us
    ppermute x6, starting transfers between devices, edges(): lax.ppermute(first, axis, backward)  23.3 us
    ppermute x6, starting transfers between devices, edges(): lax.ppermute(last, axis, forward)  16.6 us
    all_to_all x2, starting transfers between devices, shards(): lax.all_to_all(chunks, everyone, split_axis=0, concat_axis=0, tiled=True)  16.1 us
    all_to_all x1, blocking collectives, shards(): lax.all_to_all(scaled, 'gy', split_axis=0, concat_axis=1, tiled=True)  14.2 us
    all_to_all x1, blocking collectives, shards(): lax.all_to_all(solved, 'gy', split_axis=1, concat_axis=0, tiled=True)  12.8 us
    all_to_all x2, waiting for transfers between devices, shards(): lax.all_to_all(chunks, everyone, split_axis=0, concat_axis=0, tiled=True)  11.8 us
  transfers between devices with their start and end apart: 16, of which 4 were waited for; matrix products, arithmetic and copies ran while one was open for 24% of the time, Pallas kernels for 1%

profile of v4, /device:TPU:3, one launch (start us, length us, event | category | flops | bytes accessed | tf_op | source)
XLA Modules:
  0.0 242.3 jit_solution(7456257887068957546)
XLA Ops:
  4.2 3.4 %collective-permute-start.1 = (f32[16,128]{1,0:T(8,128)S(1)}, f32[16,128]{1,0:T(8,128)S(1)}, u32[]{:S(2)}, u32[]{:S(2)}) collective-permute-start(f32[16,128]{1,0:T(8,128)S(1)} %bitcast.249), channel_id=1, source_target_pairs={{0,1},{1,2},{2,3},{3,4},{4,5},{5,6},{6,7},{7,8},{8,9},{9,10},{10,1... | collective-permute-start | bytes 24584 | tf_op jit(solution)/shard_map/ppermute | solution.py:22
  9.6 6.4 %all-to-all-start = ((f32[16,64,128]{2,1,0:T(8,128)}), f32[16,64,128]{2,1,0:T(8,128)S(1)}, u32[]{:S(2)}, u32[]{:S(2)}) async-start(f32[16,64,128]{2,1,0:T(8,128)} %multiply_multiply_fusion), calls=%async_computation | async-start | bytes 1048576 | tf_op jit(solution)/shard_map/all_to_all | solution.py:180
  16.4 5.2 %collective-permute-start.2 = (f32[16,64]{1,0:T(8,128)S(1)}, f32[16,64]{1,0:T(8,128)S(1)}, u32[]{:S(2)}, u32[]{:S(2)}) collective-permute-start(f32[16,64]{1,0:T(8,128)S(1)} %bitcast.241), channel_id=1, source_target_pairs={{16,0},{32,16},{48,32},{64,48},{80,64},{96,80},{112,96},{17,1},{33... | collective-permute-start | bytes 12296 | tf_op jit(solution)/shard_map/ppermute | solution.py:22
  29.0 4.5 %reduce-precision_convert_fusion.1 = (bf16[1024,1024]{1,0:T(8,128)(2,1)S(1)}, bf16[1024,1024]{1,0:T(8,128)(2,1)}) fusion(f32[1024,1024]{1,0:T(8,128)} %param.14), kind=kLoop, calls=%fused_computation.3 | loop fusion | flops 4194304 | bytes 8388608 | tf_op jit(solution)/shard_map/convert_element_type | solution.py:137
  33.6 2.8 %fusion.49 = f32[1024,128]{0,1:T(8,128)S(1)} fusion(bf16[1024,1024]{1,0:T(8,128)(2,1)} %get-tuple-element.13, bf16[1024,128]{1,0:T(8,128)(2,1)S(1)} %get-tuple-element.39), kind=kOutput, calls=%fused_computation.100 | convolution fusion | flops 268435456 | bytes 2883584 | tf_op jit(solution)/shard_map/zxy,xi->ziy/dot_general | solution.py:145
  38.3 11.1 %all-to-all-start.1 = ((f32[128,8,128]{2,1,0:T(8,128)}), f32[128,8,128]{2,1,0:T(8,128)S(1)}, u32[]{:S(2)}, u32[]{:S(2)}) async-start(f32[128,8,128]{2,1,0:T(8,128)} %bitcast.3), calls=%async_computation.1 | async-start | bytes 1048576 | tf_op jit(solution)/shard_map/all_to_all | solution.py:184
  50.1 4.5 %reduce-precision_convert_fusion = (bf16[1024,1024]{1,0:T(8,128)(2,1)S(1)}, bf16[1024,1024]{1,0:T(8,128)(2,1)}) fusion(f32[1024,1024]{1,0:T(8,128)} %param.17), kind=kLoop, calls=%fused_computation.1 | loop fusion | flops 4194304 | bytes 8388608 | tf_op jit(solution)/shard_map/convert_element_type | solution.py:137
  54.6 7.7 %all-to-all-done.1 = f32[128,8,128]{2,1,0:T(8,128)S(1)} async-done(((f32[128,8,128]{2,1,0:T(8,128)}), f32[128,8,128]{2,1,0:T(8,128)S(1)}, u32[]{:S(2)}, u32[]{:S(2)}) %all-to-all-start.1) | async-done | bytes 524320 | tf_op jit(solution)/shard_map/all_to_all | solution.py:184
  73.4 4.9 %all-to-all-start.2 = ((f32[128,8,128]{2,1,0:T(8,128)}), f32[128,8,128]{2,1,0:T(8,128)S(1)}, u32[]{:S(2)}, u32[]{:S(2)}) async-start(f32[128,8,128]{2,1,0:T(8,128)} %bitcast.234), calls=%async_computation.2 | async-start | bytes 1048576 | tf_op jit(solution)/shard_map/all_to_all | solution.py:190
  87.3 4.1 %all-to-all-done.2 = f32[128,8,128]{2,1,0:T(8,128)S(1)} async-done(((f32[128,8,128]{2,1,0:T(8,128)}), f32[128,8,128]{2,1,0:T(8,128)S(1)}, u32[]{:S(2)}, u32[]{:S(2)}) %all-to-all-start.2) | async-done | bytes 524320 | tf_op jit(solution)/shard_map/all_to_all | solution.py:190
  98.4 3.8 %all-to-all-start.3 = ((f32[1,1024,128]{2,0,1:T(1,128)}), f32[1,1024,128]{2,0,1:T(1,128)S(1)}, u32[]{:S(2)}, u32[]{:S(2)}) async-start(f32[1,1024,128]{2,0,1:T(1,128)} %copy.74), calls=%async_computation.3 | async-start | bytes 1048576 | tf_op jit(solution)/shard_map/all_to_all | solution.py:193
  106.3 5.5 %all-to-all-done.3 = f32[1,1024,128]{2,0,1:T(1,128)S(1)} async-done(((f32[1,1024,128]{2,0,1:T(1,128)}), f32[1,1024,128]{2,0,1:T(1,128)S(1)}, u32[]{:S(2)}, u32[]{:S(2)}) %all-to-all-start.3) | async-done | bytes 524320 | tf_op jit(solution)/shard_map/all_to_all | solution.py:193
  114.8 3.4 %collective-permute-start.5 = (f32[16,128]{1,0:T(8,128)S(1)}, f32[16,128]{1,0:T(8,128)S(1)}, u32[]{:S(2)}, u32[]{:S(2)}) collective-permute-start(f32[16,128]{1,0:T(8,128)S(1)} %get-tuple-element.24), channel_id=1, source_target_pairs={{1,0},{2,1},{3,2},{4,3},{5,4},{6,5},{7,6},{8,7},{9,8},{10,9},{11,1... | collective-permute-start | bytes 24584 | tf_op jit(solution)/shard_map/ppermute | solution.py:22
  123.0 3.4 %collective-permute-start.6 = (f32[16,64]{1,0:T(8,128)S(1)}, f32[16,64]{1,0:T(8,128)S(1)}, u32[]{:S(2)}, u32[]{:S(2)}) collective-permute-start(f32[16,64]{1,0:T(8,128)S(1)} %bitcast.247), channel_id=1, source_target_pairs={{0,16},{16,32},{32,48},{48,64},{64,80},{80,96},{96,112},{1,17},{17... | collective-permute-start | bytes 12296 | tf_op jit(solution)/shard_map/ppermute | solution.py:22
  126.4 4.3 %collective-permute-start.7 = (f32[16,64]{1,0:T(8,128)S(1)}, f32[16,64]{1,0:T(8,128)S(1)}, u32[]{:S(2)}, u32[]{:S(2)}) collective-permute-start(f32[16,64]{1,0:T(8,128)S(1)} %bitcast.245), channel_id=1, source_target_pairs={{16,0},{32,16},{48,32},{64,48},{80,64},{96,80},{112,96},{17,1},{33... | collective-permute-start | bytes 12296 | tf_op jit(solution)/shard_map/ppermute | solution.py:22
  136.3 4.3 %shard_map.123 = (f32[16,64,128]{2,1,0:T(8,128)}, f32[16,64,128]{2,1,0:T(8,128)}) custom-call(f32[16,64,128]{2,1,0:T(8,128)} %bitcast.225, f32[16,64,128]{2,1,0:T(8,128)} %copy.85.active_ref, f32[16,64,128]{2,1,0:T(8,128)} %residual_ref.1, f32[6,16,64,128]{3,2,1,0:T(8,128)} %bitcast_dynamic-update-slice_fusion.faces_ref, f32[16,128]{1,0:T(8,128)} %copy-done.19, ...), custom_call_target="tpu_custom_call" | custom-call | tf_op jit(solution)/shard_map/pallas_call | solution.py:94
  140.6 14.2 %all_to_all.68 = f32[16,64,128]{2,1,0:T(8,128)S(1)} all-to-all(f32[16,64,128]{2,1,0:T(8,128)} %get-tuple-element.5), channel_id=1, replica_groups=mesh['gx'=8,'gy'=16] {'gy'}, dimensions={0} | all-to-all | bytes 1048576 | tf_op jit(solution)/shard_map/all_to_all | solution.py:180
  157.6 20.6 %all_to_all.69 = f32[128,8,128]{2,1,0:T(8,128)S(1)} all-to-all(f32[128,8,128]{2,1,0:T(8,128)S(1)} %bitcast.235), channel_id=1, replica_groups=mesh['gx'=8,'gy'=16] {'gx','gy'}, dimensions={0} | all-to-all | bytes 1048576 | tf_op jit(solution)/shard_map/all_to_all | solution.py:184
  186.8 17.5 %all_to_all.70 = f32[128,8,128]{2,1,0:T(8,128)S(1)} all-to-all(f32[128,8,128]{2,1,0:T(8,128)S(1)} %bitcast.236), channel_id=1, replica_groups=mesh['gx'=8,'gy'=16] {'gx','gy'}, dimensions={0} | all-to-all | bytes 1048576 | tf_op jit(solution)/shard_map/all_to_all | solution.py:190
  207.2 12.8 %all_to_all.71 = f32[1,1024,128]{2,0,1:T(1,128)S(1)} all-to-all(f32[1,1024,128]{2,0,1:T(1,128)S(1)} %copy.90), channel_id=1, replica_groups=mesh['gx'=8,'gy'=16] {'gy'}, dimensions={1} | all-to-all | bytes 1048576 | tf_op jit(solution)/shard_map/all_to_all | solution.py:193
  220.6 3.2 %collective-permute-start.9 = (f32[16,128]{1,0:T(8,128)S(1)}, f32[16,128]{1,0:T(8,128)S(1)}, u32[]{:S(2)}, u32[]{:S(2)}) collective-permute-start(f32[16,128]{1,0:T(8,128)S(1)} %get-tuple-element.16), channel_id=1, source_target_pairs={{1,0},{2,1},{3,2},{4,3},{5,4},{6,5},{7,6},{8,7},{9,8},{10,9},{11,1... | collective-permute-start | bytes 24584 | tf_op jit(solution)/shard_map/ppermute | solution.py:22
  226.9 3.2 %collective-permute-start.10 = (f32[16,64]{1,0:T(8,128)S(1)}, f32[16,64]{1,0:T(8,128)S(1)}, u32[]{:S(2)}, u32[]{:S(2)}) collective-permute-start(f32[16,64]{1,0:T(8,128)S(1)} %bitcast.248), channel_id=1, source_target_pairs={{0,16},{16,32},{32,48},{48,64},{64,80},{80,96},{96,112},{1,17},{17... | collective-permute-start | bytes 12296 | tf_op jit(solution)/shard_map/ppermute | solution.py:22
  230.1 4.5 %collective-permute-start.11 = (f32[16,64]{1,0:T(8,128)S(1)}, f32[16,64]{1,0:T(8,128)S(1)}, u32[]{:S(2)}, u32[]{:S(2)}) collective-permute-start(f32[16,64]{1,0:T(8,128)S(1)} %bitcast.246), channel_id=1, source_target_pairs={{16,0},{32,16},{48,32},{64,48},{80,64},{96,80},{112,96},{17,1},{33... | collective-permute-start | bytes 12296 | tf_op jit(solution)/shard_map/ppermute | solution.py:22
  238.0 4.3 %shard_map.125 = (f32[16,64,128]{2,1,0:T(8,128)}, f32[16,64,128]{2,1,0:T(8,128)}) custom-call(f32[16,64,128]{2,1,0:T(8,128)} %bitcast.229, f32[16,64,128]{2,1,0:T(8,128)} %copy.85.active_ref, f32[16,64,128]{2,1,0:T(8,128)} %get-tuple-element.6.residual_ref, f32[6,16,64,128]{3,2,1,0:T(8,128)} %bitcast_dynamic-update-slice_fusion.faces_ref, ...), custom_call_target="tpu_custom_call" | custom-call | tf_op jit(solution)/shard_map/pallas_call | solution.py:94
  (135 shorter events, 81.6 us)
Async XLA Ops:
  0.6 15.4 %copy-start.4 = (f32[16,64,128]{2,1,0:T(8,128)S(1)}, f32[16,64,128]{2,1,0:T(8,128)}, u32[]{:S(2)}) copy-start(f32[16,64,128]{2,1,0:T(8,128)} %param.12) | copy-start | bytes 1572868
  1.6 83.8 %collective-permute-start = (f32[16,128]{1,0:T(8,128)S(1)}, f32[16,128]{1,0:T(8,128)S(1)}, u32[]{:S(2)}, u32[]{:S(2)}) collective-permute-start(f32[16,128]{1,0:T(8,128)S(1)} %bitcast.250), channel_id=1, source_target_pairs={{1,0},{2,1},{3,2},{4,3},{5,4},{6,5},{7,6},{8,7},{9,8},{10,9},{11,1... | collective-permute-start | bytes 24584 | tf_op jit(solution)/shard_map/ppermute | solution.py:22
  4.2 98.0 %collective-permute-start.1 = (f32[16,128]{1,0:T(8,128)S(1)}, f32[16,128]{1,0:T(8,128)S(1)}, u32[]{:S(2)}, u32[]{:S(2)}) collective-permute-start(f32[16,128]{1,0:T(8,128)S(1)} %bitcast.249), channel_id=1, source_target_pairs={{0,1},{1,2},{2,3},{3,4},{4,5},{5,6},{6,7},{7,8},{8,9},{9,10},{10,1... | collective-permute-start | bytes 24584 | tf_op jit(solution)/shard_map/ppermute | solution.py:22
  9.6 23.9 %all-to-all-start = ((f32[16,64,128]{2,1,0:T(8,128)}), f32[16,64,128]{2,1,0:T(8,128)S(1)}, u32[]{:S(2)}, u32[]{:S(2)}) async-start(f32[16,64,128]{2,1,0:T(8,128)} %multiply_multiply_fusion), calls=%async_computation | async-start | bytes 1048576 | tf_op jit(solution)/shard_map/all_to_all | solution.py:180
  16.4 67.9 %collective-permute-start.2 = (f32[16,64]{1,0:T(8,128)S(1)}, f32[16,64]{1,0:T(8,128)S(1)}, u32[]{:S(2)}, u32[]{:S(2)}) collective-permute-start(f32[16,64]{1,0:T(8,128)S(1)} %bitcast.241), channel_id=1, source_target_pairs={{16,0},{32,16},{48,32},{64,48},{80,64},{96,80},{112,96},{17,1},{33... | collective-permute-start | bytes 12296 | tf_op jit(solution)/shard_map/ppermute | solution.py:22
  21.8 61.4 %collective-permute-start.3 = (f32[16,64]{1,0:T(8,128)S(1)}, f32[16,64]{1,0:T(8,128)S(1)}, u32[]{:S(2)}, u32[]{:S(2)}) collective-permute-start(f32[16,64]{1,0:T(8,128)S(1)} %bitcast.243), channel_id=1, source_target_pairs={{0,16},{16,32},{32,48},{48,64},{64,80},{80,96},{96,112},{1,17},{17... | collective-permute-start | bytes 12296 | tf_op jit(solution)/shard_map/ppermute | solution.py:22
  38.3 24.1 %all-to-all-start.1 = ((f32[128,8,128]{2,1,0:T(8,128)}), f32[128,8,128]{2,1,0:T(8,128)S(1)}, u32[]{:S(2)}, u32[]{:S(2)}) async-start(f32[128,8,128]{2,1,0:T(8,128)} %bitcast.3), calls=%async_computation.1 | async-start | bytes 1048576 | tf_op jit(solution)/shard_map/all_to_all | solution.py:184
  73.4 18.0 %all-to-all-start.2 = ((f32[128,8,128]{2,1,0:T(8,128)}), f32[128,8,128]{2,1,0:T(8,128)S(1)}, u32[]{:S(2)}, u32[]{:S(2)}) async-start(f32[128,8,128]{2,1,0:T(8,128)} %bitcast.234), calls=%async_computation.2 | async-start | bytes 1048576 | tf_op jit(solution)/shard_map/all_to_all | solution.py:190
  98.4 13.4 %all-to-all-start.3 = ((f32[1,1024,128]{2,0,1:T(1,128)}), f32[1,1024,128]{2,0,1:T(1,128)S(1)}, u32[]{:S(2)}, u32[]{:S(2)}) async-start(f32[1,1024,128]{2,0,1:T(1,128)} %copy.74), calls=%async_computation.3 | async-start | bytes 1048576 | tf_op jit(solution)/shard_map/all_to_all | solution.py:193
  114.8 18.3 %copy-start.21 = (f32[64]{0:T(128)S(1)}, f32[64]{0:T(128)}, u32[]{:S(2)}) copy-start(f32[64]{0:T(128)} %param.15) | copy-start | bytes 772
  114.8 19.0 %copy-start.22 = (f32[128]{0:T(128)S(1)}, f32[128]{0:T(128)}, u32[]{:S(2)}) copy-start(f32[128]{0:T(128)} %param.18) | copy-start | bytes 1540
  114.8 18.2 %collective-permute-start.5 = (f32[16,128]{1,0:T(8,128)S(1)}, f32[16,128]{1,0:T(8,128)S(1)}, u32[]{:S(2)}, u32[]{:S(2)}) collective-permute-start(f32[16,128]{1,0:T(8,128)S(1)} %get-tuple-element.24), channel_id=1, source_target_pairs={{1,0},{2,1},{3,2},{4,3},{5,4},{6,5},{7,6},{8,7},{9,8},{10,9},{11,1... | collective-permute-start | bytes 24584 | tf_op jit(solution)/shard_map/ppermute | solution.py:22
  118.1 14.8 %collective-permute-start.4 = (f32[16,128]{1,0:T(8,128)S(1)}, f32[16,128]{1,0:T(8,128)S(1)}, u32[]{:S(2)}, u32[]{:S(2)}) collective-permute-start(f32[16,128]{1,0:T(8,128)S(1)} %get-tuple-element.25), channel_id=1, source_target_pairs={{0,1},{1,2},{2,3},{3,4},{4,5},{5,6},{6,7},{7,8},{8,9},{9,10},{10,1... | collective-permute-start | bytes 24584 | tf_op jit(solution)/shard_map/ppermute | solution.py:22
  123.0 9.9 %collective-permute-start.6 = (f32[16,64]{1,0:T(8,128)S(1)}, f32[16,64]{1,0:T(8,128)S(1)}, u32[]{:S(2)}, u32[]{:S(2)}) collective-permute-start(f32[16,64]{1,0:T(8,128)S(1)} %bitcast.247), channel_id=1, source_target_pairs={{0,16},{16,32},{32,48},{48,64},{64,80},{80,96},{96,112},{1,17},{17... | collective-permute-start | bytes 12296 | tf_op jit(solution)/shard_map/ppermute | solution.py:22
  126.4 6.5 %collective-permute-start.7 = (f32[16,64]{1,0:T(8,128)S(1)}, f32[16,64]{1,0:T(8,128)S(1)}, u32[]{:S(2)}, u32[]{:S(2)}) collective-permute-start(f32[16,64]{1,0:T(8,128)S(1)} %bitcast.245), channel_id=1, source_target_pairs={{16,0},{32,16},{48,32},{64,48},{80,64},{96,80},{112,96},{17,1},{33... | collective-permute-start | bytes 12296 | tf_op jit(solution)/shard_map/ppermute | solution.py:22
  157.6 20.7 %copy-start.7 = (bf16[1024,1024]{1,0:T(8,128)(2,1)S(1)}, bf16[1024,1024]{1,0:T(8,128)(2,1)}, u32[]{:S(2)}) copy-start(bf16[1024,1024]{1,0:T(8,128)(2,1)} %get-tuple-element.11) | copy-start | bytes 6291460
  185.9 18.4 %copy-start.6 = (bf16[1024,1024]{1,0:T(8,128)(2,1)S(1)}, bf16[1024,1024]{1,0:T(8,128)(2,1)}, u32[]{:S(2)}) copy-start(bf16[1024,1024]{1,0:T(8,128)(2,1)} %get-tuple-element.13) | copy-start | bytes 6291460
  186.8 18.4 %copy-start.3 = (bf16[1024,1024]{1,0:T(8,128)(2,1)S(1)}, bf16[1024,1024]{1,0:T(8,128)(2,1)}, u32[]{:S(2)}) copy-start(bf16[1024,1024]{1,0:T(8,128)(2,1)} %copy-done) | copy-start | bytes 6291460
  220.0 14.6 %copy-start.10 = (f32[1,1024,128]{2,0,1:T(1,128)}, f32[1,1024,128]{2,0,1:T(1,128)S(1)}, u32[]{:S(2)}) copy-start(f32[1,1024,128]{2,0,1:T(1,128)S(1)} %all_to_all.71) | copy-start | bytes 1572868
  220.0 14.6 %copy-start.9 = (f32[1,1024,128]{2,0,1:T(1,128)S(1)}, f32[1,1024,128]{2,0,1:T(1,128)}, u32[]{:S(2)}) copy-start(f32[1,1024,128]{2,0,1:T(1,128)} %copy-done.8) | copy-start | bytes 1572868
  220.6 15.4 %collective-permute-start.9 = (f32[16,128]{1,0:T(8,128)S(1)}, f32[16,128]{1,0:T(8,128)S(1)}, u32[]{:S(2)}, u32[]{:S(2)}) collective-permute-start(f32[16,128]{1,0:T(8,128)S(1)} %get-tuple-element.16), channel_id=1, source_target_pairs={{1,0},{2,1},{3,2},{4,3},{5,4},{6,5},{7,6},{8,7},{9,8},{10,9},{11,1... | collective-permute-start | bytes 24584 | tf_op jit(solution)/shard_map/ppermute | solution.py:22
  223.8 12.1 %collective-permute-start.8 = (f32[16,128]{1,0:T(8,128)S(1)}, f32[16,128]{1,0:T(8,128)S(1)}, u32[]{:S(2)}, u32[]{:S(2)}) collective-permute-start(f32[16,128]{1,0:T(8,128)S(1)} %get-tuple-element.17), channel_id=1, source_target_pairs={{0,1},{1,2},{2,3},{3,4},{4,5},{5,6},{6,7},{7,8},{8,9},{9,10},{10,1... | collective-permute-start | bytes 24584 | tf_op jit(solution)/shard_map/ppermute | solution.py:22
  226.9 8.6 %collective-permute-start.10 = (f32[16,64]{1,0:T(8,128)S(1)}, f32[16,64]{1,0:T(8,128)S(1)}, u32[]{:S(2)}, u32[]{:S(2)}) collective-permute-start(f32[16,64]{1,0:T(8,128)S(1)} %bitcast.248), channel_id=1, source_target_pairs={{0,16},{16,32},{32,48},{48,64},{64,80},{80,96},{96,112},{1,17},{17... | collective-permute-start | bytes 12296 | tf_op jit(solution)/shard_map/ppermute | solution.py:22
  230.1 5.9 %collective-permute-start.11 = (f32[16,64]{1,0:T(8,128)S(1)}, f32[16,64]{1,0:T(8,128)S(1)}, u32[]{:S(2)}, u32[]{:S(2)}) collective-permute-start(f32[16,64]{1,0:T(8,128)S(1)} %bitcast.246), channel_id=1, source_target_pairs={{16,0},{32,16},{48,32},{64,48},{80,64},{96,80},{112,96},{17,1},{33... | collective-permute-start | bytes 12296 | tf_op jit(solution)/shard_map/ppermute | solution.py:22
  (15 other events, 80.2 us)

commit v5 on v1

--- a/solution.py
+++ b/solution.py
@@ -44,11 +44,55 @@
     return [harmonic(center, other) for other in neighbours(center, edges(center))]
 
 
-def stencil(center, faces):
-    result = storage_term * center
-    for face, other in zip(faces, neighbours(center, edges(center))):
-        result = result + face * (center - other)
-    return result
+def stencil_kernel(update_ref, active_ref, residual_ref, *refs):
+    face_refs, out_ref = refs[:-1], refs[-1]
+    planes, rows, cols = update_ref.shape
+    row = lax.broadcasted_iota(jnp.int32, (rows, cols), 0)
+    col = lax.broadcasted_iota(jnp.int32, (rows, cols), 1)
+    row_forward = pltpu.roll(row, 1, 0) == jnp.where(row == 0, rows - 1, row - 1)
+    col_forward = pltpu.roll(col, 1, 1) == jnp.where(col == 0, cols - 1, col - 1)
+
+    def before(plane, axis, count, forward):
+        return jnp.where(forward, pltpu.roll(plane, 1, axis), pltpu.roll(plane, count - 1, axis))
+
+    def after(plane, axis, count, forward):
+        return jnp.where(forward, pltpu.roll(plane, count - 1, axis), pltpu.roll(plane, 1, axis))
+
+    zeros = jnp.zeros((rows, cols), jnp.float32)
+    masked = [active_ref[z] * update_ref[z] for z in range(planes)]
+    for z in range(planes):
+        center = masked[z]
+        others = [
+            masked[z + 1] if z + 1 < planes else zeros,
+            masked[z - 1] if z > 0 else zeros,
+            jnp.where(row == rows - 1, zeros, after(center, 0, rows, row_forward)),
+            jnp.where(row == 0, zeros, before(center, 0, rows, row_forward)),
+            jnp.where(col == cols - 1, zeros, after(center, 1, cols, col_forward)),
+            jnp.where(col == 0, zeros, before(center, 1, cols, col_forward)),
+        ]
+        result = storage_term * center
+        for face_ref, other in zip(face_refs, others):
+            result = result + face_ref[z] * (center - other)
+        update = update_ref[z]
+        out_ref[z] = residual_ref[z] - (result + (1.0 - active_ref[z]) * update)
+
+
+def fused_stencil(update, active, residual, faces):
+    vmem = pl.BlockSpec(memory_space=pltpu.VMEM)
+    return pl.pallas_call(
+        stencil_kernel,
+        out_shape=jax.ShapeDtypeStruct(update.shape, update.dtype),
+        in_specs=[vmem] * (3 + len(faces)),
+        out_specs=vmem,
+    )(update, active, residual, *faces)
+
+
+def add_halo_terms(residual, faces, strips):
+    (x_low, x_high), (y_low, y_high) = strips
+    residual = residual.at[:, 0, :].add(faces[3][:, 0, :] * x_low)
+    residual = residual.at[:, -1, :].add(faces[2][:, -1, :] * x_high)
+    residual = residual.at[:, :, 0].add(faces[5][:, :, 0] * y_low)
+    return residual.at[:, :, -1].add(faces[4][:, :, -1] * y_high)
 
 
 def solve_kernel(diag_ref, coup_ref, shifts_ref, rhs_ref, out_ref, ratio_ref):
@@ -143,9 +187,8 @@
         solved = transform("ziy,xi->zxy", solved, basis_x)
         update = lax.all_to_all(solved, "gy", split_axis=1, concat_axis=0, tiled=True)
         adjoint = adjoint + update
-        masked = active * update
-        image = stencil(masked, faces) + (1.0 - active) * update
-        residual = residual - image
+        strips = edges(active * update)
+        residual = add_halo_terms(fused_stencil(update, active, residual, faces), faces, strips)
     return (adjoint, residual)
 
 

time: 237 us -> 267 us (1.13)
  local copies, waits for them, and re-layouts: 29.2 us -> 45.2 us
  waiting for transfers between devices: 14.4 us -> 28.3 us
  blocking collectives: 65.2 us -> 52 us
  Pallas kernels: 4.14 us -> 11.6 us
    scatter-add x0 -> x5, local copies, waits for them, and re-layouts: none -> 15.4 us  [the longest x3 12.5 us: add_halo_terms(): return residual.at[:, :, -1].add(faces[4][:, :, -1] * y_high)]
    all_to_all x1 -> x0, blocking collectives: 12.8 us -> none  [shards(): lax.all_to_all(solved, 'gy', split_axis=1, concat_axis=0, tiled=True)]
    all_to_all x1 -> x2, waiting for transfers between devices: 5.22 us -> 14.9 us  [shards(): lax.all_to_all(solved, 'gy', split_axis=1, concat_axis=0, tiled=True)]
    pallas_call x0 -> x2, Pallas kernels: none -> 7.47 us  [fused_stencil(): pl.pallas_call(stencil_kernel, out_shape=jax.ShapeDtypeStruct(update.shap...]
    mul x2, other arithmetic: 7.83 us -> 1.51 us  [shards(): scaled = residual * mass_x[None, :, None] * mass_y[None, None, :]]
    div x0 -> x2, other arithmetic: none -> 5.79 us  [harmonic(): return 2.0 * first * second / (first + second)]
    sub x1 -> x0, other arithmetic: 5.12 us -> none  [shards(): residual = residual - image]
    slice x6 -> x4, local copies, waits for them, and re-layouts: 6.63 us -> 1.74 us  [the longest x1 1.13 us: neighbours(): center[:-1]]
  transfers between devices with their start and end apart: 16 -> 17, of which waited for: 4 -> 6; matrix products, arithmetic and copies ran while one was open for 21% -> 22% of each run, Pallas kernels for 1% -> 4%
where the time goes in v5:
time: 267 us; the launch traced here: 263 us
  starting transfers between devices  70.4 us (26%)
  blocking collectives  52 us (19%)
  local copies, waits for them, and re-layouts  45.2 us (17%)
  waiting for transfers between devices  28.3 us (11%)
  matrix products  27.8 us (10%)
  other arithmetic  26.5 us (10%)
  Pallas kernels  11.6 us (4%)
    all_to_all x2, blocking collectives, shards(): lax.all_to_all(chunks, everyone, split_axis=0, concat_axis=0, tiled=True)  38.3 us
    dot_general x24, matrix products, product(): return jnp.einsum(spec, first, second, preferred_element_type=jnp.float32)  27.8 us
    ppermute x6, starting transfers between devices, edges(): lax.ppermute(first, axis, backward)  22.2 us
    ppermute x6, starting transfers between devices, edges(): lax.ppermute(last, axis, forward)  18.3 us
    all_to_all x2, starting transfers between devices, shards(): lax.all_to_all(chunks, everyone, split_axis=0, concat_axis=0, tiled=True)  16.1 us
    all_to_all x2, waiting for transfers between devices, shards(): lax.all_to_all(solved, 'gy', split_axis=1, concat_axis=0, tiled=True)  14.9 us
    all_to_all x1, blocking collectives, shards(): lax.all_to_all(scaled, 'gy', split_axis=0, concat_axis=1, tiled=True)  13.8 us
    scatter-add x3, local copies, waits for them, and re-layouts, add_halo_terms(): return residual.at[:, :, -1].add(faces[4][:, :, -1] * y_high)  12.5 us
  transfers between devices with their start and end apart: 17, of which 6 were waited for; matrix products, arithmetic and copies ran while one was open for 22% of the time, Pallas kernels for 4%

profile of v5, /device:TPU:3, one launch (start us, length us, event | category | flops | bytes accessed | tf_op | source)
XLA Modules:
  0.0 263.1 jit_solution(4010712413719726370)
XLA Ops:
  2.1 4.1 %collective-permute-start.1 = (f32[16,128]{1,0:T(8,128)S(1)}, f32[16,128]{1,0:T(8,128)S(1)}, u32[]{:S(2)}, u32[]{:S(2)}) collective-permute-start(f32[16,128]{1,0:T(8,128)S(1)} %get-tuple-element.142), channel_id=1, source_target_pairs={{0,1},{1,2},{2,3},{3,4},{4,5},{5,6},{6,7},{7,8},{8,9},{9,10},{10,1... | collective-permute-start | bytes 24584 | tf_op jit(solution)/shard_map/ppermute | solution.py:22
  10.5 6.0 %all-to-all-start = ((f32[16,64,128]{2,1,0:T(8,128)}), f32[16,64,128]{2,1,0:T(8,128)S(1)}, u32[]{:S(2)}, u32[]{:S(2)}) async-start(f32[16,64,128]{2,1,0:T(8,128)} %copy.419), calls=%async_computation | async-start | bytes 1048576 | tf_op jit(solution)/shard_map/all_to_all | solution.py:175
  16.9 5.2 %collective-permute-start.2 = (f32[16,64]{1,0:T(8,128)S(1)}, f32[16,64]{1,0:T(8,128)S(1)}, u32[]{:S(2)}, u32[]{:S(2)}) collective-permute-start(f32[16,64]{1,0:T(8,128)S(1)} %bitcast.253), channel_id=1, source_target_pairs={{16,0},{32,16},{48,32},{64,48},{80,64},{96,80},{112,96},{17,1},{33... | collective-permute-start | bytes 12296 | tf_op jit(solution)/shard_map/ppermute | solution.py:22
  27.3 4.5 %reduce-precision_convert_fusion.1 = (bf16[1024,1024]{1,0:T(8,128)(2,1)S(1)}, bf16[1024,1024]{1,0:T(8,128)(2,1)}) fusion(f32[1024,1024]{1,0:T(8,128)} %param.30), kind=kLoop, calls=%fused_computation.3 | loop fusion | flops 4194304 | bytes 8388608 | tf_op jit(solution)/shard_map/convert_element_type | solution.py:133
  36.6 11.1 %all-to-all-start.1 = ((f32[128,8,128]{2,1,0:T(8,128)}), f32[128,8,128]{2,1,0:T(8,128)S(1)}, u32[]{:S(2)}, u32[]{:S(2)}) async-start(f32[128,8,128]{2,1,0:T(8,128)} %bitcast.3), calls=%async_computation.1 | async-start | bytes 1048576 | tf_op jit(solution)/shard_map/all_to_all | solution.py:179
  48.5 4.5 %reduce-precision_convert_fusion = (bf16[1024,1024]{1,0:T(8,128)(2,1)S(1)}, bf16[1024,1024]{1,0:T(8,128)(2,1)}) fusion(f32[1024,1024]{1,0:T(8,128)} %param.33), kind=kLoop, calls=%fused_computation.1 | loop fusion | flops 4194304 | bytes 8388608 | tf_op jit(solution)/shard_map/convert_element_type | solution.py:133
  52.9 7.8 %all-to-all-done.1 = f32[128,8,128]{2,1,0:T(8,128)S(1)} async-done(((f32[128,8,128]{2,1,0:T(8,128)}), f32[128,8,128]{2,1,0:T(8,128)S(1)}, u32[]{:S(2)}, u32[]{:S(2)}) %all-to-all-start.1) | async-done | bytes 524320 | tf_op jit(solution)/shard_map/all_to_all | solution.py:179
  71.7 5.0 %all-to-all-start.2 = ((f32[128,8,128]{2,1,0:T(8,128)}), f32[128,8,128]{2,1,0:T(8,128)S(1)}, u32[]{:S(2)}, u32[]{:S(2)}) async-start(f32[128,8,128]{2,1,0:T(8,128)} %bitcast.245), calls=%async_computation.2 | async-start | bytes 1048576 | tf_op jit(solution)/shard_map/all_to_all | solution.py:185
  82.9 3.9 %add_divide_fusion = (f32[16,64,128]{2,1,0:T(8,128)}, f32[16,64,128]{2,1,0:T(8,128)S(1)}, f32[16,64,128]{2,1,0:T(8,128)}, f32[16,64,128]{2,1,0:T(8,128)}, f32[16,64,128]{2,1,0:T(8,128)}, /*index=5*/f32[16,64,128]{2,1,0:T(8,128)}) fusion(f32[16,64,128]{2,1,0:T(8,128)S(1)} %copy-done.6, f32[16,64,127]{2,1,0:T(8,128)} %get-tuple-element.140, ...), kind=kLoop, calls=%fused_computation.86 | loop fusion | flops 2490368 | bytes 6225920 | tf_op jit(solution)/shard_map/div | solution.py:27
  96.7 3.9 %all-to-all-start.3 = ((f32[1,1024,128]{2,0,1:T(1,128)}), f32[1,1024,128]{2,0,1:T(1,128)S(1)}, u32[]{:S(2)}, u32[]{:S(2)}) async-start(f32[1,1024,128]{2,0,1:T(1,128)} %copy.424), calls=%async_computation.3 | async-start | bytes 1048576 | tf_op jit(solution)/shard_map/all_to_all | solution.py:188
  104.1 6.1 %all-to-all-done.3 = f32[1,1024,128]{2,0,1:T(1,128)S(1)} async-done(((f32[1,1024,128]{2,0,1:T(1,128)}), f32[1,1024,128]{2,0,1:T(1,128)S(1)}, u32[]{:S(2)}, u32[]{:S(2)}) %all-to-all-start.3) | async-done | bytes 524320 | tf_op jit(solution)/shard_map/all_to_all | solution.py:188
  114.5 4.8 %collective-permute-start.6 = (f32[16,64]{1,0:T(8,128)S(1)}, f32[16,64]{1,0:T(8,128)S(1)}, u32[]{:S(2)}, u32[]{:S(2)}) collective-permute-start(f32[16,64]{1,0:T(8,128)S(1)} %bitcast.258), channel_id=1, source_target_pairs={{0,16},{16,32},{32,48},{48,64},{64,80},{80,96},{96,112},{1,17},{17... | collective-permute-start | bytes 12296 | tf_op jit(solution)/shard_map/ppermute | solution.py:22
  119.3 3.5 %collective-permute-start.5 = (f32[16,128]{1,0:T(8,128)S(1)}, f32[16,128]{1,0:T(8,128)S(1)}, u32[]{:S(2)}, u32[]{:S(2)}) collective-permute-start(f32[16,128]{1,0:T(8,128)S(1)} %get-tuple-element.130), channel_id=1, source_target_pairs={{1,0},{2,1},{3,2},{4,3},{5,4},{6,5},{7,6},{8,7},{9,8},{10,9},{11,1... | collective-permute-start | bytes 24584 | tf_op jit(solution)/shard_map/ppermute | solution.py:22
  124.9 3.8 %shard_map.123 = f32[16,64,128]{2,1,0:T(8,128)} custom-call(f32[16,64,128]{2,1,0:T(8,128)} %bitcast.236, f32[16,64,128]{2,1,0:T(8,128)} %copy.435.active_ref, f32[16,64,128]{2,1,0:T(8,128)} %residual_ref.1, f32[16,64,128]{2,1,0:T(8,128)} %get-tuple-element.136.refs_0_, f32[16,64,128]{2,1,0:T(8,128)} %get-tuple-element.135.refs_1_, ...), custom_call_target="tpu_custom_call" | custom-call | tf_op jit(solution)/shard_map/pallas_call | solution.py:82
  143.0 6.2 %scatter-add.31 = f32[16,64,128]{2,0,1:T(8,128)S(1)} dynamic-update-slice(f32[16,64,128]{2,0,1:T(8,128)S(1)} %scatter-add.30, f32[16,64,1]{2,0,1:T(8,128)} %slice_add_fusion.2, s32[]{:T(128)} %constant.202.clone.1, s32[]{:T(128)} %constant.202.clone.1, s32[]{:T(128)} %constant.207.clone.1) | dynamic-update-slice | bytes 8196 | tf_op jit(solution)/shard_map/scatter-add | solution.py:95
  149.5 13.8 %all_to_all.68 = f32[16,64,128]{2,1,0:T(8,128)S(1)} all-to-all(f32[16,64,128]{2,1,0:T(8,128)S(1)} %copy.444), channel_id=1, replica_groups=mesh['gx'=8,'gy'=16] {'gy'}, dimensions={0} | all-to-all | bytes 1048576 | tf_op jit(solution)/shard_map/all_to_all | solution.py:175
  168.0 20.7 %all_to_all.69 = f32[128,8,128]{2,1,0:T(8,128)S(1)} all-to-all(f32[128,8,128]{2,1,0:T(8,128)S(1)} %bitcast.246), channel_id=1, replica_groups=mesh['gx'=8,'gy'=16] {'gx','gy'}, dimensions={0} | all-to-all | bytes 1048576 | tf_op jit(solution)/shard_map/all_to_all | solution.py:179
  197.4 17.5 %all_to_all.70 = f32[128,8,128]{2,1,0:T(8,128)S(1)} all-to-all(f32[128,8,128]{2,1,0:T(8,128)S(1)} %bitcast.247), channel_id=1, replica_groups=mesh['gx'=8,'gy'=16] {'gx','gy'}, dimensions={0} | all-to-all | bytes 1048576 | tf_op jit(solution)/shard_map/all_to_all | solution.py:185
  218.5 3.8 %all-to-all-start.7 = ((f32[1,1024,128]{2,0,1:T(1,128)}), f32[1,1024,128]{2,0,1:T(1,128)S(1)}, u32[]{:S(2)}, u32[]{:S(2)}) async-start(f32[1,1024,128]{2,0,1:T(1,128)} %copy.449), calls=%async_computation.7 | async-start | bytes 1048576 | tf_op jit(solution)/shard_map/all_to_all | solution.py:188
  223.2 8.7 %all-to-all-done.7 = f32[1,1024,128]{2,0,1:T(1,128)S(1)} async-done(((f32[1,1024,128]{2,0,1:T(1,128)}), f32[1,1024,128]{2,0,1:T(1,128)S(1)}, u32[]{:S(2)}, u32[]{:S(2)}) %all-to-all-start.7) | async-done | bytes 524320 | tf_op jit(solution)/shard_map/all_to_all | solution.py:188
  237.2 3.7 %shard_map.125 = f32[16,64,128]{2,1,0:T(8,128)} custom-call(f32[16,64,128]{2,1,0:T(8,128)} %bitcast.240, f32[16,64,128]{2,1,0:T(8,128)} %copy.435.active_ref, f32[16,64,128]{2,1,0:T(8,128)} %copy.451.residual_ref, f32[16,64,128]{2,1,0:T(8,128)} %get-tuple-element.136.refs_0_, f32[16,64,128]{2,1,0:T(8,128)} %get-tuple-element.135.refs_1_, ...), custom_call_target="tpu_custom_call" | custom-call | tf_op jit(solution)/shard_map/pallas_call | solution.py:82
  242.3 3.5 %collective-permute-start.9 = (f32[16,128]{1,0:T(8,128)S(1)}, f32[16,128]{1,0:T(8,128)S(1)}, u32[]{:S(2)}, u32[]{:S(2)}) collective-permute-start(f32[16,128]{1,0:T(8,128)S(1)} %get-tuple-element.122), channel_id=1, source_target_pairs={{1,0},{2,1},{3,2},{4,3},{5,4},{6,5},{7,6},{8,7},{9,8},{10,9},{11,1... | collective-permute-start | bytes 24584 | tf_op jit(solution)/shard_map/ppermute | solution.py:22
  248.1 4.7 %collective-permute-start.11 = (f32[16,64]{1,0:T(8,128)S(1)}, f32[16,64]{1,0:T(8,128)S(1)}, u32[]{:S(2)}, u32[]{:S(2)}) collective-permute-start(f32[16,64]{1,0:T(8,128)S(1)} %bitcast.259), channel_id=1, source_target_pairs={{16,0},{32,16},{48,32},{64,48},{80,64},{96,80},{112,96},{17,1},{33... | collective-permute-start | bytes 12296 | tf_op jit(solution)/shard_map/ppermute | solution.py:22
  256.8 5.4 %scatter-add.39 = f32[16,64,128]{2,0,1:T(8,128)S(1)} dynamic-update-slice(f32[16,64,128]{2,0,1:T(8,128)S(1)} %scatter-add.36, f32[16,64,1]{2,0,1:T(8,128)S(1)} %slice_add_fusion, s32[]{:T(128)} %constant.202.clone.1, s32[]{:T(128)} %constant.202.clone.1, s32[]{:T(128)} %constant.207.clone.1) | dynamic-update-slice | bytes 8196 | tf_op jit(solution)/shard_map/scatter-add | solution.py:95
  (158 shorter events, 99.5 us)
Async XLA Ops:
  0.6 15.9 %copy-start.6 = (f32[16,64,128]{2,1,0:T(8,128)S(1)}, f32[16,64,128]{2,1,0:T(8,128)}, u32[]{:S(2)}) copy-start(f32[16,64,128]{2,1,0:T(8,128)} %param.28) | copy-start | bytes 1572868
  2.1 14.7 %copy-start.18 = (f32[16,64,128]{2,0,1:T(8,128)}, f32[16,64,128]{2,0,1:T(8,128)S(1)}, u32[]{:S(2)}) copy-start(f32[16,64,128]{2,0,1:T(8,128)S(1)} %copy.426) | copy-start | bytes 1572868
  2.1 80.8 %collective-permute-start.1 = (f32[16,128]{1,0:T(8,128)S(1)}, f32[16,128]{1,0:T(8,128)S(1)}, u32[]{:S(2)}, u32[]{:S(2)}) collective-permute-start(f32[16,128]{1,0:T(8,128)S(1)} %get-tuple-element.142), channel_id=1, source_target_pairs={{0,1},{1,2},{2,3},{3,4},{4,5},{5,6},{6,7},{7,8},{8,9},{9,10},{10,1... | collective-permute-start | bytes 24584 | tf_op jit(solution)/shard_map/ppermute | solution.py:22
  6.2 94.5 %collective-permute-start = (f32[16,128]{1,0:T(8,128)S(1)}, f32[16,128]{1,0:T(8,128)S(1)}, u32[]{:S(2)}, u32[]{:S(2)}) collective-permute-start(f32[16,128]{1,0:T(8,128)S(1)} %get-tuple-element.143), channel_id=1, source_target_pairs={{1,0},{2,1},{3,2},{4,3},{5,4},{6,5},{7,6},{8,7},{9,8},{10,9},{11,1... | collective-permute-start | bytes 24584 | tf_op jit(solution)/shard_map/ppermute | solution.py:22
  10.5 21.4 %all-to-all-start = ((f32[16,64,128]{2,1,0:T(8,128)}), f32[16,64,128]{2,1,0:T(8,128)S(1)}, u32[]{:S(2)}, u32[]{:S(2)}) async-start(f32[16,64,128]{2,1,0:T(8,128)} %copy.419), calls=%async_computation | async-start | bytes 1048576 | tf_op jit(solution)/shard_map/all_to_all | solution.py:175
  16.9 64.9 %collective-permute-start.2 = (f32[16,64]{1,0:T(8,128)S(1)}, f32[16,64]{1,0:T(8,128)S(1)}, u32[]{:S(2)}, u32[]{:S(2)}) collective-permute-start(f32[16,64]{1,0:T(8,128)S(1)} %bitcast.253), channel_id=1, source_target_pairs={{16,0},{32,16},{48,32},{64,48},{80,64},{96,80},{112,96},{17,1},{33... | collective-permute-start | bytes 12296 | tf_op jit(solution)/shard_map/ppermute | solution.py:22
  22.3 58.5 %collective-permute-start.3 = (f32[16,64]{1,0:T(8,128)S(1)}, f32[16,64]{1,0:T(8,128)S(1)}, u32[]{:S(2)}, u32[]{:S(2)}) collective-permute-start(f32[16,64]{1,0:T(8,128)S(1)} %bitcast.255), channel_id=1, source_target_pairs={{0,16},{16,32},{32,48},{48,64},{64,80},{80,96},{96,112},{1,17},{17... | collective-permute-start | bytes 12296 | tf_op jit(solution)/shard_map/ppermute | solution.py:22
  36.6 24.1 %all-to-all-start.1 = ((f32[128,8,128]{2,1,0:T(8,128)}), f32[128,8,128]{2,1,0:T(8,128)S(1)}, u32[]{:S(2)}, u32[]{:S(2)}) async-start(f32[128,8,128]{2,1,0:T(8,128)} %bitcast.3), calls=%async_computation.1 | async-start | bytes 1048576 | tf_op jit(solution)/shard_map/all_to_all | solution.py:179
  71.7 18.0 %all-to-all-start.2 = ((f32[128,8,128]{2,1,0:T(8,128)}), f32[128,8,128]{2,1,0:T(8,128)S(1)}, u32[]{:S(2)}, u32[]{:S(2)}) async-start(f32[128,8,128]{2,1,0:T(8,128)} %bitcast.245), calls=%async_computation.2 | async-start | bytes 1048576 | tf_op jit(solution)/shard_map/all_to_all | solution.py:185
  96.7 13.6 %all-to-all-start.3 = ((f32[1,1024,128]{2,0,1:T(1,128)}), f32[1,1024,128]{2,0,1:T(1,128)S(1)}, u32[]{:S(2)}, u32[]{:S(2)}) async-start(f32[1,1024,128]{2,0,1:T(1,128)} %copy.424), calls=%async_computation.3 | async-start | bytes 1048576 | tf_op jit(solution)/shard_map/all_to_all | solution.py:188
  114.5 19.1 %collective-permute-start.6 = (f32[16,64]{1,0:T(8,128)S(1)}, f32[16,64]{1,0:T(8,128)S(1)}, u32[]{:S(2)}, u32[]{:S(2)}) collective-permute-start(f32[16,64]{1,0:T(8,128)S(1)} %bitcast.258), channel_id=1, source_target_pairs={{0,16},{16,32},{32,48},{48,64},{64,80},{80,96},{96,112},{1,17},{17... | collective-permute-start | bytes 12296 | tf_op jit(solution)/shard_map/ppermute | solution.py:22
  119.3 18.3 %collective-permute-start.5 = (f32[16,128]{1,0:T(8,128)S(1)}, f32[16,128]{1,0:T(8,128)S(1)}, u32[]{:S(2)}, u32[]{:S(2)}) collective-permute-start(f32[16,128]{1,0:T(8,128)S(1)} %get-tuple-element.130), channel_id=1, source_target_pairs={{1,0},{2,1},{3,2},{4,3},{5,4},{6,5},{7,6},{8,7},{9,8},{10,9},{11,1... | collective-permute-start | bytes 24584 | tf_op jit(solution)/shard_map/ppermute | solution.py:22
  122.8 14.7 %collective-permute-start.4 = (f32[16,128]{1,0:T(8,128)S(1)}, f32[16,128]{1,0:T(8,128)S(1)}, u32[]{:S(2)}, u32[]{:S(2)}) collective-permute-start(f32[16,128]{1,0:T(8,128)S(1)} %get-tuple-element.131), channel_id=1, source_target_pairs={{0,1},{1,2},{2,3},{3,4},{4,5},{5,6},{6,7},{7,8},{8,9},{9,10},{10,1... | collective-permute-start | bytes 24584 | tf_op jit(solution)/shard_map/ppermute | solution.py:22
  130.3 5.9 %collective-permute-start.7 = (f32[16,64]{1,0:T(8,128)S(1)}, f32[16,64]{1,0:T(8,128)S(1)}, u32[]{:S(2)}, u32[]{:S(2)}) collective-permute-start(f32[16,64]{1,0:T(8,128)S(1)} %bitcast.260), channel_id=1, source_target_pairs={{16,0},{32,16},{48,32},{64,48},{80,64},{96,80},{112,96},{17,1},{33... | collective-permute-start | bytes 12296 | tf_op jit(solution)/shard_map/ppermute | solution.py:22
  149.2 14.2 %copy-start.4 = (bf16[1024,1024]{1,0:T(8,128)(2,1)S(1)}, bf16[1024,1024]{1,0:T(8,128)(2,1)}, u32[]{:S(2)}) copy-start(bf16[1024,1024]{1,0:T(8,128)(2,1)} %get-tuple-element.119) | copy-start | bytes 6291460
  168.0 20.8 %copy-start.7 = (bf16[1024,1024]{1,0:T(8,128)(2,1)S(1)}, bf16[1024,1024]{1,0:T(8,128)(2,1)}, u32[]{:S(2)}) copy-start(bf16[1024,1024]{1,0:T(8,128)(2,1)} %get-tuple-element.117) | copy-start | bytes 6291460
  196.4 18.5 %copy-start.5 = (bf16[1024,1024]{1,0:T(8,128)(2,1)S(1)}, bf16[1024,1024]{1,0:T(8,128)(2,1)}, u32[]{:S(2)}) copy-start(bf16[1024,1024]{1,0:T(8,128)(2,1)} %get-tuple-element.119) | copy-start | bytes 6291460
  197.3 18.4 %copy-start.3 = (bf16[1024,1024]{1,0:T(8,128)(2,1)S(1)}, bf16[1024,1024]{1,0:T(8,128)(2,1)}, u32[]{:S(2)}) copy-start(bf16[1024,1024]{1,0:T(8,128)(2,1)} %copy-done) | copy-start | bytes 6291460
  217.4 14.5 %copy-start.16 = (s32[16,64,128]{2,1,0:T(8,128)S(1)}, s32[16,64,128]{2,1,0:T(8,128)}, u32[]{:S(2)}) copy-start(s32[16,64,128]{2,1,0:T(8,128)} %param.29) | copy-start | bytes 1572868
  218.5 13.4 %all-to-all-start.7 = ((f32[1,1024,128]{2,0,1:T(1,128)}), f32[1,1024,128]{2,0,1:T(1,128)S(1)}, u32[]{:S(2)}, u32[]{:S(2)}) async-start(f32[1,1024,128]{2,0,1:T(1,128)} %copy.449), calls=%async_computation.7 | async-start | bytes 1048576 | tf_op jit(solution)/shard_map/all_to_all | solution.py:188
  233.0 19.9 %collective-permute-start.10 = (f32[16,64]{1,0:T(8,128)S(1)}, f32[16,64]{1,0:T(8,128)S(1)}, u32[]{:S(2)}, u32[]{:S(2)}) collective-permute-start(f32[16,64]{1,0:T(8,128)S(1)} %bitcast.257), channel_id=1, source_target_pairs={{0,16},{16,32},{32,48},{48,64},{64,80},{80,96},{96,112},{1,17},{17... | collective-permute-start | bytes 12296 | tf_op jit(solution)/shard_map/ppermute | solution.py:22
  242.3 12.4 %collective-permute-start.9 = (f32[16,128]{1,0:T(8,128)S(1)}, f32[16,128]{1,0:T(8,128)S(1)}, u32[]{:S(2)}, u32[]{:S(2)}) collective-permute-start(f32[16,128]{1,0:T(8,128)S(1)} %get-tuple-element.122), channel_id=1, source_target_pairs={{1,0},{2,1},{3,2},{4,3},{5,4},{6,5},{7,6},{8,7},{9,8},{10,9},{11,1... | collective-permute-start | bytes 24584 | tf_op jit(solution)/shard_map/ppermute | solution.py:22
  245.8 8.8 %collective-permute-start.8 = (f32[16,128]{1,0:T(8,128)S(1)}, f32[16,128]{1,0:T(8,128)S(1)}, u32[]{:S(2)}, u32[]{:S(2)}) collective-permute-start(f32[16,128]{1,0:T(8,128)S(1)} %get-tuple-element.123), channel_id=1, source_target_pairs={{0,1},{1,2},{2,3},{3,4},{4,5},{5,6},{6,7},{7,8},{8,9},{9,10},{10,1... | collective-permute-start | bytes 24584 | tf_op jit(solution)/shard_map/ppermute | solution.py:22
  248.1 5.9 %collective-permute-start.11 = (f32[16,64]{1,0:T(8,128)S(1)}, f32[16,64]{1,0:T(8,128)S(1)}, u32[]{:S(2)}, u32[]{:S(2)}) collective-permute-start(f32[16,64]{1,0:T(8,128)S(1)} %bitcast.259), channel_id=1, source_target_pairs={{16,0},{32,16},{48,32},{64,48},{80,64},{96,80},{112,96},{17,1},{33... | collective-permute-start | bytes 12296 | tf_op jit(solution)/shard_map/ppermute | solution.py:22
  (16 other events, 69.4 us)

commit v6 on v2

--- a/solution.py
+++ b/solution.py
@@ -45,11 +45,55 @@
     return [harmonic(center, other) for other in neighbours(center, edges(center))]
 
 
-def stencil(center, faces, strips):
-    result = storage_term * center
-    for face, other in zip(faces, neighbours(center, strips)):
-        result = result + face * (center - other)
-    return result
+def framed_kernel(
+    framed_ref, active_ref, residual_ref, adjoint_ref, x_low_ref, x_high_ref, y_low_ref, y_high_ref, *refs
+):
+    face_refs, residual_out, adjoint_out = refs[:-2], refs[-2], refs[-1]
+    planes, rows, cols = active_ref.shape
+    row = lax.broadcasted_iota(jnp.int32, (rows, cols), 0)
+    col = lax.broadcasted_iota(jnp.int32, (rows, cols), 1)
+    row_forward = pltpu.roll(row, 1, 0) == jnp.where(row == 0, rows - 1, row - 1)
+    col_forward = pltpu.roll(col, 1, 1) == jnp.where(col == 0, cols - 1, col - 1)
+
+    def before(plane, axis, count, forward):
+        return jnp.where(forward, pltpu.roll(plane, 1, axis), pltpu.roll(plane, count - 1, axis))
+
+    def after(plane, axis, count, forward):
+        return jnp.where(forward, pltpu.roll(plane, count - 1, axis), pltpu.roll(plane, 1, axis))
+
+    zeros = jnp.zeros((rows, cols), jnp.float32)
+    updates = [framed_ref[z, pl.ds(1, rows), :] for z in range(planes)]
+    masked = [active_ref[z] * updates[z] for z in range(planes)]
+    for z in range(planes):
+        center = masked[z]
+        x_low = x_low_ref[pl.ds(z, 1), :] * framed_ref[z, pl.ds(0, 1), :]
+        x_high = x_high_ref[pl.ds(z, 1), :] * framed_ref[z, pl.ds(rows + 1, 1), :]
+        others = [
+            masked[z + 1] if z + 1 < planes else zeros,
+            masked[z - 1] if z > 0 else zeros,
+            jnp.where(row == rows - 1, jnp.broadcast_to(x_high, (rows, cols)), after(center, 0, rows, row_forward)),
+            jnp.where(row == 0, jnp.broadcast_to(x_low, (rows, cols)), before(center, 0, rows, row_forward)),
+            jnp.where(col == cols - 1, y_high_ref[z], after(center, 1, cols, col_forward)),
+            jnp.where(col == 0, y_low_ref[z], before(center, 1, cols, col_forward)),
+        ]
+        result = storage_term * center
+        for face_ref, other in zip(face_refs, others):
+            result = result + face_ref[z] * (center - other)
+        update = updates[z]
+        residual_out[z] = residual_ref[z] - (result + (1.0 - active_ref[z]) * update)
+        adjoint_out[z] = adjoint_ref[z] + update
+
+
+def framed_stencil(framed, active, residual, adjoint, x_strips, y_strips, faces):
+    vmem = pl.BlockSpec(memory_space=pltpu.VMEM)
+    shape = jax.ShapeDtypeStruct(active.shape, active.dtype)
+    y_low, y_high = (jnp.broadcast_to(strip[:, :, None], active.shape) for strip in y_strips)
+    return pl.pallas_call(
+        framed_kernel,
+        out_shape=(shape, shape),
+        in_specs=[vmem] * (8 + len(faces)),
+        out_specs=(vmem, vmem),
+    )(framed, active, residual, adjoint, x_strips[0], x_strips[1], y_low, y_high, *faces)
 
 
 def solve_kernel(diag_ref, coup_ref, shifts_ref, rhs_ref, out_ref, ratio_ref):
@@ -132,7 +176,10 @@
         below = jnp.concatenate([zero, blocks[:-1, -1:]], axis=0)
         above = jnp.concatenate([blocks[1:, :1], zero], axis=0)
         framed_basis.append(jnp.concatenate([below, blocks, above], axis=1))
-    active_x = edge_pair(active, "gy", 1)
+    active_x, active_y = edges(active)
+    count_y = lax.axis_size("gx")
+    forward_y = [(i, i + 1) for i in range(count_y - 1)]
+    backward_y = [(target, source) for source, target in forward_y]
     basis_y = tuple(piece.reshape(blocks_y, -1, vectors_y.shape[1]) for piece in split_bf16(vectors_y))
     for iteration in range(ITERS):
         scaled = residual * mass_x[None, :, None] * mass_y[None, None, :]
@@ -151,14 +198,13 @@
         chunks = lax.all_to_all(chunks, everyone, split_axis=0, concat_axis=0, tiled=True)
         solved = chunks.reshape(-1, chunks.shape[2])
         framed = transform("iy,bri->bry", solved, framed_basis)
+        from_left = lax.ppermute(framed[:, 1:-1, -1], "gx", forward_y)
+        from_right = lax.ppermute(framed[:, 1:-1, 0], "gx", backward_y)
+        halo_row = jnp.concatenate([from_left, from_right], axis=1)[:, None, :]
+        framed = jnp.concatenate([framed, halo_row], axis=1)
         framed = lax.all_to_all(framed, "gy", split_axis=0, concat_axis=0, tiled=True)
-        update = framed[:, 1:-1]
-        adjoint = adjoint + update
-        masked = active * update
-        x_strips = (active_x[0] * framed[:, 0], active_x[1] * framed[:, -1])
-        strips = (x_strips, edge_pair(masked, "gx", 2))
-        image = stencil(masked, faces, strips) + (1.0 - active) * update
-        residual = residual - image
+        y_strips = (active_y[0] * framed[:, -1, :rows], active_y[1] * framed[:, -1, rows:])
+        residual, adjoint = framed_stencil(framed, active, residual, adjoint, active_x, y_strips, faces)
     return (adjoint, residual)
 
 

time: 263 us -> 262 us (level)
  Pallas kernels: 4.14 us -> 12.7 us
  local copies, waits for them, and re-layouts: 42.4 us -> 34.5 us
  starting transfers between devices: 61.9 us -> 68.7 us
  waiting for transfers between devices: 19.6 us -> 16 us
    ppermute x0 -> x4, starting transfers between devices: none -> 14.5 us  [the longest x2 8.49 us: shards(): from_right = lax.ppermute(framed[:, 1:-1, 0], 'gx', backward_y)]
    pallas_call x0 -> x2, Pallas kernels: none -> 8.54 us  [framed_stencil(): pl.pallas_call(framed_kernel, out_shape=(shape, shape), in_specs=[vmem] *...]
    slice x11 -> x4, local copies, waits for them, and re-layouts: 10.4 us -> 3.31 us  [the longest x1 1.15 us: shards(): from_left = lax.ppermute(framed[:, 1:-1, -1], 'gx', forward_y)]
    sub x1 -> x0, other arithmetic: 4.94 us -> none  [shards(): residual = residual - image]
    broadcast_in_dim x0 -> x5, local copies, waits for them, and re-layouts: none -> 4.82 us  [the longest x4 3.97 us: framed_stencil(): jnp.broadcast_to(strip[:, :, None], active.shape)]
    div x0 -> x1, other arithmetic: none -> 4.4 us  [harmonic(): return 2.0 * first * second / (first + second)]
    mul x2, other arithmetic: 7.58 us -> 3.3 us  [shards(): scaled = residual * mass_x[None, :, None] * mass_y[None, None, :]]
    ppermute x5 -> x4, starting transfers between devices: 15.4 us -> 11.6 us  [edge_pair(): lax.ppermute(first, axis, backward)]
  transfers between devices with their start and end apart: 14 -> 16, of which waited for: 5 -> 4; matrix products, arithmetic and copies ran while one was open for 25% -> 26% of each run, Pallas kernels for 1% -> 1%
where the time goes in v6:
time: 262 us; the launch traced here: 259 us
  starting transfers between devices  68.7 us (26%)
  blocking collectives  67.4 us (26%)
  local copies, waits for them, and re-layouts  34.5 us (13%)
  other arithmetic  29.1 us (11%)
  matrix products  29 us (11%)
  waiting for transfers between devices  16 us (6%)
  Pallas kernels  12.7 us (5%)
    all_to_all x2, blocking collectives, shards(): lax.all_to_all(chunks, everyone, split_axis=0, concat_axis=0, tiled=True)  36.8 us
    dot_general x24, matrix products, product(): return jnp.einsum(spec, first, second, preferred_element_type=jnp.float32)  29 us
    all_to_all x1, blocking collectives, shards(): lax.all_to_all(framed, 'gy', split_axis=0, concat_axis=0, tiled=True)  16.4 us
    all_to_all x2, starting transfers between devices, shards(): lax.all_to_all(chunks, everyone, split_axis=0, concat_axis=0, tiled=True)  15.5 us
    ppermute x4, starting transfers between devices, edge_pair(): lax.ppermute(last, axis, forward)  14.8 us
    all_to_all x2, waiting for transfers between devices, shards(): lax.all_to_all(chunks, everyone, split_axis=0, concat_axis=0, tiled=True)  14.6 us
    all_to_all x1, blocking collectives, shards(): lax.all_to_all(scaled, 'gy', split_axis=0, concat_axis=1, tiled=True)  14.2 us
    ppermute x4, starting transfers between devices, edge_pair(): lax.ppermute(first, axis, backward)  11.6 us
  transfers between devices with their start and end apart: 16, of which 4 were waited for; matrix products, arithmetic and copies ran while one was open for 26% of the time, Pallas kernels for 1%

profile of v6, /device:TPU:3, one launch (start us, length us, event | category | flops | bytes accessed | tf_op | source)
XLA Modules:
  0.0 258.7 jit_solution(14080628440545692659)
XLA Ops:
  4.1 3.4 %collective-permute-start.7 = (f32[16,128]{1,0:T(8,128)S(1)}, f32[16,128]{1,0:T(8,128)S(1)}, u32[]{:S(2)}, u32[]{:S(2)}) collective-permute-start(f32[16,128]{1,0:T(8,128)S(1)} %bitcast.246), channel_id=1, source_target_pairs={{0,1},{1,2},{2,3},{3,4},{4,5},{5,6},{6,7},{7,8},{8,9},{9,10},{10,1... | collective-permute-start | bytes 24584 | tf_op jit(solution)/shard_map/ppermute | solution.py:20
  13.0 6.9 %all-to-all-start = ((f32[16,64,128]{2,1,0:T(8,128)}), f32[16,64,128]{2,1,0:T(8,128)}, u32[]{:S(2)}, u32[]{:S(2)}) async-start(f32[16,64,128]{2,1,0:T(8,128)} %multiply_multiply_fusion.1), calls=%async_computation | async-start | bytes 1048576 | tf_op jit(solution)/shard_map/all_to_all | solution.py:188
  22.1 4.5 %fusion.4 = (bf16[1024,1024]{1,0:T(8,128)(2,1)}, bf16[1024,1024]{1,0:T(8,128)(2,1)S(1)}) fusion(f32[1024,1024]{1,0:T(8,128)} %param.14), kind=kLoop, calls=%fused_computation.10 | loop fusion | flops 4194304 | bytes 8388608 | tf_op jit(solution)/shard_map/convert_element_type | solution.py:134
  36.7 9.5 %all-to-all-start.1 = ((f32[128,8,128]{2,1,0:T(8,128)}), f32[128,8,128]{2,1,0:T(8,128)}, u32[]{:S(2)}, u32[]{:S(2)}) async-start(f32[128,8,128]{2,1,0:T(8,128)} %bitcast.4), calls=%async_computation.1 | async-start | bytes 1048576 | tf_op jit(solution)/shard_map/all_to_all | solution.py:192
  46.8 4.5 %reduce-precision_convert_fusion = (bf16[1024,1024]{1,0:T(8,128)(2,1)S(1)}, bf16[1024,1024]{1,0:T(8,128)(2,1)}) fusion(f32[1024,1024]{1,0:T(8,128)} %param.17), kind=kLoop, calls=%fused_computation.1 | loop fusion | flops 4194304 | bytes 8388608 | tf_op jit(solution)/shard_map/convert_element_type | solution.py:134
  51.4 7.4 %all-to-all-done.1 = f32[128,8,128]{2,1,0:T(8,128)} async-done(((f32[128,8,128]{2,1,0:T(8,128)}), f32[128,8,128]{2,1,0:T(8,128)}, u32[]{:S(2)}, u32[]{:S(2)}) %all-to-all-start.1) | async-done | bytes 524320 | tf_op jit(solution)/shard_map/all_to_all | solution.py:192
  70.8 6.0 %all-to-all-start.2 = ((f32[128,8,128]{2,1,0:T(8,128)}), f32[128,8,128]{2,1,0:T(8,128)}, u32[]{:S(2)}, u32[]{:S(2)}) async-start(f32[128,8,128]{2,1,0:T(8,128)} %bitcast.227), calls=%async_computation.2 | async-start | bytes 1048576 | tf_op jit(solution)/shard_map/all_to_all | solution.py:198
  77.9 4.3 %fusion.7 = bf16[16,66,1024]{2,1,0:T(8,128)(2,1)} fusion(bf16[15,1,1024]{2,1,0:T(2,128)(2,1)S(1)} %get-tuple-element.17, bf16[15,1,1024]{2,1,0:T(2,128)(2,1)S(1)} %get-tuple-element.16, bf16[16,64,1024]{2,1,0:T(8,128)(2,1)} %bitcast.215), kind=kLoop, calls=%fused_computation.13 | loop fusion | flops 10813440 | bytes 4321280 | tf_op jit(solution)/shard_map/concatenate | solution.py:178
  82.2 7.3 %all-to-all-done.2 = f32[128,8,128]{2,1,0:T(8,128)} async-done(((f32[128,8,128]{2,1,0:T(8,128)}), f32[128,8,128]{2,1,0:T(8,128)}, u32[]{:S(2)}, u32[]{:S(2)}) %all-to-all-start.2) | async-done | bytes 524320 | tf_op jit(solution)/shard_map/all_to_all | solution.py:198
  100.8 3.3 %collective-permute-start.1 = (f32[16,64]{1,0:T(8,128)S(1)}, f32[16,64]{1,0:T(8,128)S(1)}, u32[]{:S(2)}, u32[]{:S(2)}) collective-permute-start(f32[16,64]{1,0:T(8,128)S(1)} %bitcast.245), channel_id=1, source_target_pairs={{16,0},{32,16},{48,32},{64,48},{80,64},{96,80},{112,96},{17,1},{33... | collective-permute-start | bytes 12296 | tf_op jit(solution)/shard_map/ppermute | solution.py:202
  104.1 3.5 %collective-permute-start = (f32[16,64]{1,0:T(8,128)S(1)}, f32[16,64]{1,0:T(8,128)S(1)}, u32[]{:S(2)}, u32[]{:S(2)}) collective-permute-start(f32[16,64]{1,0:T(8,128)S(1)} %bitcast.244), channel_id=1, source_target_pairs={{0,16},{16,32},{32,48},{48,64},{64,80},{80,96},{96,112},{1,17},{17... | collective-permute-start | bytes 12296 | tf_op jit(solution)/shard_map/ppermute | solution.py:201
  111.2 4.2 %collective-permute-start.8 = (f32[16,64]{1,0:T(8,128)S(1)}, f32[16,64]{1,0:T(8,128)S(1)}, u32[]{:S(2)}, u32[]{:S(2)}) collective-permute-start(f32[16,64]{1,0:T(8,128)S(1)} %bitcast.240), channel_id=1, source_target_pairs={{16,0},{32,16},{48,32},{64,48},{80,64},{96,80},{112,96},{17,1},{33... | collective-permute-start | bytes 12296 | tf_op jit(solution)/shard_map/ppermute | solution.py:20
  120.1 5.5 %all-to-all-start.3 = ((f32[16,67,128]{2,1,0:T(8,128)}), f32[16,67,128]{2,1,0:T(8,128)}, u32[]{:S(2)}, u32[]{:S(2)}) async-start(f32[16,67,128]{2,1,0:T(8,128)} %pad_maximum_fusion), calls=%async_computation.3 | async-start | bytes 1179648 | tf_op jit(solution)/shard_map/all_to_all | solution.py:205
  130.2 3.5 %collective-permute-start.2 = (f32[16,128]{1,0:T(8,128)S(1)}, f32[16,128]{1,0:T(8,128)S(1)}, u32[]{:S(2)}, u32[]{:S(2)}) collective-permute-start(f32[16,128]{1,0:T(8,128)S(1)} %get-tuple-element.49), channel_id=1, source_target_pairs={{0,1},{1,2},{2,3},{3,4},{4,5},{5,6},{6,7},{7,8},{8,9},{9,10},{10,1... | collective-permute-start | bytes 24584 | tf_op jit(solution)/shard_map/ppermute | solution.py:20
  134.0 5.2 %collective-permute-start.4 = (f32[16,64]{1,0:T(8,128)S(1)}, f32[16,64]{1,0:T(8,128)S(1)}, u32[]{:S(2)}, u32[]{:S(2)}) collective-permute-start(f32[16,64]{1,0:T(8,128)S(1)} %bitcast.238), channel_id=1, source_target_pairs={{0,16},{16,32},{32,48},{48,64},{64,80},{80,96},{96,112},{1,17},{17... | collective-permute-start | bytes 12296 | tf_op jit(solution)/shard_map/ppermute | solution.py:20
  140.2 2.8 %collective-permute-start.5 = (f32[16,64]{1,0:T(8,128)S(1)}, f32[16,64]{1,0:T(8,128)S(1)}, u32[]{:S(2)}, u32[]{:S(2)}) collective-permute-start(f32[16,64]{1,0:T(8,128)S(1)} %bitcast.239), channel_id=1, source_target_pairs={{16,0},{32,16},{48,32},{64,48},{80,64},{96,80},{112,96},{17,1},{33... | collective-permute-start | bytes 12296 | tf_op jit(solution)/shard_map/ppermute | solution.py:20
  143.0 4.4 %add_divide_fusion = (f32[16,64,128]{2,1,0:T(8,128)}, f32[16,64,128]{2,1,0:T(8,128)}, f32[16,64,128]{2,1,0:T(8,128)}, f32[16,64,128]{2,1,0:T(8,128)}, f32[16,64,128]{2,1,0:T(8,128)}, /*index=5*/f32[16,64,128]{2,1,0:T(8,128)}) fusion(f32[16,64,128]{2,1,0:T(8,128)S(1)} %copy-done.8, f32[16,64,127]{2,1,0:T(8,128)} %get-tuple-element.38, ...), kind=kLoop, calls=%fused_computation.79 | loop fusion | flops 3014656 | bytes 6750208 | tf_op jit(solution)/shard_map/div | solution.py:28
  151.3 4.3 %shard_map.123 = (f32[16,64,128]{2,1,0:T(8,128)}, f32[16,64,128]{2,1,0:T(8,128)}) custom-call(f32[16,67,128]{2,1,0:T(8,128)} %all-to-all-done.3.framed_ref, f32[16,64,128]{2,1,0:T(8,128)} %copy.150.active_ref, f32[16,64,128]{2,1,0:T(8,128)} %residual_ref.1, f32[16,64,128]{2,1,0:T(8,128)} %broadcast_in_dim.23.adjoint_ref, f32[16,128]{1,0:T(8,128)} %copy-done.16, ...), custom_call_target="tpu_custom_call" | custom-call | tf_op jit(solution)/shard_map/pallas_call | solution.py:91
  157.0 14.2 %all_to_all.54 = f32[16,64,128]{2,1,0:T(8,128)S(1)} all-to-all(f32[16,64,128]{2,1,0:T(8,128)S(1)} %multiply_multiply_fusion), channel_id=1, replica_groups=mesh['gx'=8,'gy'=16] {'gy'}, dimensions={0} | all-to-all | bytes 1048576 | tf_op jit(solution)/shard_map/all_to_all | solution.py:188
  174.0 19.3 %all_to_all.55 = f32[128,8,128]{2,1,0:T(8,128)S(1)} all-to-all(f32[128,8,128]{2,1,0:T(8,128)S(1)} %bitcast.228), channel_id=1, replica_groups=mesh['gx'=8,'gy'=16] {'gx','gy'}, dimensions={0} | all-to-all | bytes 1048576 | tf_op jit(solution)/shard_map/all_to_all | solution.py:192
  201.9 17.5 %all_to_all.56 = f32[128,8,128]{2,1,0:T(8,128)S(1)} all-to-all(f32[128,8,128]{2,1,0:T(8,128)S(1)} %bitcast.229), channel_id=1, replica_groups=mesh['gx'=8,'gy'=16] {'gx','gy'}, dimensions={0} | all-to-all | bytes 1048576 | tf_op jit(solution)/shard_map/all_to_all | solution.py:198
  229.9 5.2 %collective-permute-start.11 = (f32[16,64]{1,0:T(8,128)S(1)}, f32[16,64]{1,0:T(8,128)S(1)}, u32[]{:S(2)}, u32[]{:S(2)}) collective-permute-start(f32[16,64]{1,0:T(8,128)S(1)} %get-tuple-element.19), channel_id=1, source_target_pairs={{16,0},{32,16},{48,32},{64,48},{80,64},{96,80},{112,96},{17,1},{33... | collective-permute-start | bytes 12296 | tf_op jit(solution)/shard_map/ppermute | solution.py:202
  236.0 16.4 %all_to_all.57.framed_ref = f32[16,67,128]{2,1,0:T(8,128)S(1)} all-to-all(f32[16,67,128]{2,1,0:T(8,128)S(1)} %pad_maximum_fusion.1), channel_id=1, replica_groups=mesh['gx'=8,'gy'=16] {'gy'}, dimensions={0} | all-to-all | bytes 1097728 | tf_op jit(solution)/shard_map/all_to_all | solution.py:205
  254.5 4.2 %shard_map.125 = (f32[16,64,128]{2,1,0:T(8,128)}, f32[16,64,128]{2,1,0:T(8,128)}) custom-call(f32[16,67,128]{2,1,0:T(8,128)} %copy-done.14, f32[16,64,128]{2,1,0:T(8,128)} %copy.150.active_ref, f32[16,64,128]{2,1,0:T(8,128)} %get-tuple-element.6.residual_ref, f32[16,64,128]{2,1,0:T(8,128)} %get-tuple-element.7.adjoint_ref, f32[16,128]{1,0:T(8,128)} %copy-done.16, ...), custom_call_target="tpu_custom_call" | custom-call | tf_op jit(solution)/shard_map/pallas_call | solution.py:91
  (137 shorter events, 90.3 us)
Async XLA Ops:
  1.5 138.7 %collective-permute-start.6 = (f32[16,128]{1,0:T(8,128)S(1)}, f32[16,128]{1,0:T(8,128)S(1)}, u32[]{:S(2)}, u32[]{:S(2)}) collective-permute-start(f32[16,128]{1,0:T(8,128)S(1)} %bitcast.247), channel_id=1, source_target_pairs={{1,0},{2,1},{3,2},{4,3},{5,4},{6,5},{7,6},{8,7},{9,8},{10,9},{11,1... | collective-permute-start | bytes 24584 | tf_op jit(solution)/shard_map/ppermute | solution.py:20
  4.1 138.9 %collective-permute-start.7 = (f32[16,128]{1,0:T(8,128)S(1)}, f32[16,128]{1,0:T(8,128)S(1)}, u32[]{:S(2)}, u32[]{:S(2)}) collective-permute-start(f32[16,128]{1,0:T(8,128)S(1)} %bitcast.246), channel_id=1, source_target_pairs={{0,1},{1,2},{2,3},{3,4},{4,5},{5,6},{6,7},{7,8},{8,9},{9,10},{10,1... | collective-permute-start | bytes 24584 | tf_op jit(solution)/shard_map/ppermute | solution.py:20
  8.9 12.2 %copy-start.8 = (f32[16,64,128]{2,1,0:T(8,128)S(1)}, f32[16,64,128]{2,1,0:T(8,128)}, u32[]{:S(2)}) copy-start(f32[16,64,128]{2,1,0:T(8,128)} %param.12) | copy-start | bytes 1572868
  8.9 139.5 %collective-permute-start.3 = (f32[16,128]{1,0:T(8,128)S(1)}, f32[16,128]{1,0:T(8,128)S(1)}, u32[]{:S(2)}, u32[]{:S(2)}) collective-permute-start(f32[16,128]{1,0:T(8,128)S(1)} %get-tuple-element.48), channel_id=1, source_target_pairs={{1,0},{2,1},{3,2},{4,3},{5,4},{6,5},{7,6},{8,7},{9,8},{10,9},{11,1... | collective-permute-start | bytes 24584 | tf_op jit(solution)/shard_map/ppermute | solution.py:20
  13.0 16.7 %all-to-all-start = ((f32[16,64,128]{2,1,0:T(8,128)}), f32[16,64,128]{2,1,0:T(8,128)}, u32[]{:S(2)}, u32[]{:S(2)}) async-start(f32[16,64,128]{2,1,0:T(8,128)} %multiply_multiply_fusion.1), calls=%async_computation | async-start | bytes 1048576 | tf_op jit(solution)/shard_map/all_to_all | solution.py:188
  26.6 6.7 %copy-start = (bf16[1024,1024]{1,0:T(8,128)(2,1)}, bf16[1024,1024]{1,0:T(8,128)(2,1)S(1)}, u32[]{:S(2)}) copy-start(bf16[1024,1024]{1,0:T(8,128)(2,1)S(1)} %get-tuple-element.13) | copy-start | bytes 6291460
  33.4 12.8 %copy-start.17 = (f32[1024]{0:T(1024)S(1)}, f32[1024]{0:T(1024)}, u32[]{:S(2)}) copy-start(f32[1024]{0:T(1024)} %param.19) | copy-start | bytes 12292
  36.7 22.0 %all-to-all-start.1 = ((f32[128,8,128]{2,1,0:T(8,128)}), f32[128,8,128]{2,1,0:T(8,128)}, u32[]{:S(2)}, u32[]{:S(2)}) async-start(f32[128,8,128]{2,1,0:T(8,128)} %bitcast.4), calls=%async_computation.1 | async-start | bytes 1048576 | tf_op jit(solution)/shard_map/all_to_all | solution.py:192
  70.8 18.7 %all-to-all-start.2 = ((f32[128,8,128]{2,1,0:T(8,128)}), f32[128,8,128]{2,1,0:T(8,128)}, u32[]{:S(2)}, u32[]{:S(2)}) async-start(f32[128,8,128]{2,1,0:T(8,128)} %bitcast.227), calls=%async_computation.2 | async-start | bytes 1048576 | tf_op jit(solution)/shard_map/all_to_all | solution.py:198
  100.8 10.4 %collective-permute-start.1 = (f32[16,64]{1,0:T(8,128)S(1)}, f32[16,64]{1,0:T(8,128)S(1)}, u32[]{:S(2)}, u32[]{:S(2)}) collective-permute-start(f32[16,64]{1,0:T(8,128)S(1)} %bitcast.245), channel_id=1, source_target_pairs={{16,0},{32,16},{48,32},{64,48},{80,64},{96,80},{112,96},{17,1},{33... | collective-permute-start | bytes 12296 | tf_op jit(solution)/shard_map/ppermute | solution.py:202
  104.1 11.3 %collective-permute-start = (f32[16,64]{1,0:T(8,128)S(1)}, f32[16,64]{1,0:T(8,128)S(1)}, u32[]{:S(2)}, u32[]{:S(2)}) collective-permute-start(f32[16,64]{1,0:T(8,128)S(1)} %bitcast.244), channel_id=1, source_target_pairs={{0,16},{16,32},{32,48},{48,64},{64,80},{80,96},{96,112},{1,17},{17... | collective-permute-start | bytes 12296 | tf_op jit(solution)/shard_map/ppermute | solution.py:201
  111.2 22.7 %collective-permute-start.8 = (f32[16,64]{1,0:T(8,128)S(1)}, f32[16,64]{1,0:T(8,128)S(1)}, u32[]{:S(2)}, u32[]{:S(2)}) collective-permute-start(f32[16,64]{1,0:T(8,128)S(1)} %bitcast.240), channel_id=1, source_target_pairs={{16,0},{32,16},{48,32},{64,48},{80,64},{96,80},{112,96},{17,1},{33... | collective-permute-start | bytes 12296 | tf_op jit(solution)/shard_map/ppermute | solution.py:20
  115.4 14.8 %collective-permute-start.9 = (f32[16,64]{1,0:T(8,128)S(1)}, f32[16,64]{1,0:T(8,128)S(1)}, u32[]{:S(2)}, u32[]{:S(2)}) collective-permute-start(f32[16,64]{1,0:T(8,128)S(1)} %bitcast.242), channel_id=1, source_target_pairs={{0,16},{16,32},{32,48},{48,64},{64,80},{80,96},{96,112},{1,17},{17... | collective-permute-start | bytes 12296 | tf_op jit(solution)/shard_map/ppermute | solution.py:20
  120.1 27.3 %all-to-all-start.3 = ((f32[16,67,128]{2,1,0:T(8,128)}), f32[16,67,128]{2,1,0:T(8,128)}, u32[]{:S(2)}, u32[]{:S(2)}) async-start(f32[16,67,128]{2,1,0:T(8,128)} %pad_maximum_fusion), calls=%async_computation.3 | async-start | bytes 1179648 | tf_op jit(solution)/shard_map/all_to_all | solution.py:205
  130.2 18.3 %collective-permute-start.2 = (f32[16,128]{1,0:T(8,128)S(1)}, f32[16,128]{1,0:T(8,128)S(1)}, u32[]{:S(2)}, u32[]{:S(2)}) collective-permute-start(f32[16,128]{1,0:T(8,128)S(1)} %get-tuple-element.49), channel_id=1, source_target_pairs={{0,1},{1,2},{2,3},{3,4},{4,5},{5,6},{6,7},{7,8},{8,9},{9,10},{10,1... | collective-permute-start | bytes 24584 | tf_op jit(solution)/shard_map/ppermute | solution.py:20
  134.0 14.4 %collective-permute-start.4 = (f32[16,64]{1,0:T(8,128)S(1)}, f32[16,64]{1,0:T(8,128)S(1)}, u32[]{:S(2)}, u32[]{:S(2)}) collective-permute-start(f32[16,64]{1,0:T(8,128)S(1)} %bitcast.238), channel_id=1, source_target_pairs={{0,16},{16,32},{32,48},{48,64},{64,80},{80,96},{96,112},{1,17},{17... | collective-permute-start | bytes 12296 | tf_op jit(solution)/shard_map/ppermute | solution.py:20
  140.2 8.2 %collective-permute-start.5 = (f32[16,64]{1,0:T(8,128)S(1)}, f32[16,64]{1,0:T(8,128)S(1)}, u32[]{:S(2)}, u32[]{:S(2)}) collective-permute-start(f32[16,64]{1,0:T(8,128)S(1)} %bitcast.239), channel_id=1, source_target_pairs={{16,0},{32,16},{48,32},{64,48},{80,64},{96,80},{112,96},{17,1},{33... | collective-permute-start | bytes 12296 | tf_op jit(solution)/shard_map/ppermute | solution.py:20
  151.3 4.3 %copy-start.18 = (f32[128]{0:T(128)S(1)}, f32[128]{0:T(128)}, u32[]{:S(2)}) copy-start(f32[128]{0:T(128)} %param.18) | copy-start | bytes 1540
  151.3 4.3 %copy-start.19 = (f32[64]{0:T(128)S(1)}, f32[64]{0:T(128)}, u32[]{:S(2)}) copy-start(f32[64]{0:T(128)} %param.15) | copy-start | bytes 772
  155.6 15.6 %copy-start.6 = (bf16[1024,1024]{1,0:T(8,128)(2,1)S(1)}, bf16[1024,1024]{1,0:T(8,128)(2,1)}, u32[]{:S(2)}) copy-start(bf16[1024,1024]{1,0:T(8,128)(2,1)} %get-tuple-element.12) | copy-start | bytes 6291460
  174.0 19.4 %copy-start.9 = (bf16[1024,1024]{1,0:T(8,128)(2,1)S(1)}, bf16[1024,1024]{1,0:T(8,128)(2,1)}, u32[]{:S(2)}) copy-start(bf16[1024,1024]{1,0:T(8,128)(2,1)} %get-tuple-element.11) | copy-start | bytes 6291460
  201.0 18.4 %copy-start.3 = (bf16[16,66,1024]{2,1,0:T(8,128)(2,1)S(1)}, bf16[16,66,1024]{2,1,0:T(8,128)(2,1)}, u32[]{:S(2)}) copy-start(bf16[16,66,1024]{2,1,0:T(8,128)(2,1)} %fusion.7) | copy-start | bytes 6488068
  227.4 8.2 %collective-permute-start.10 = (f32[16,64]{1,0:T(8,128)S(1)}, f32[16,64]{1,0:T(8,128)S(1)}, u32[]{:S(2)}, u32[]{:S(2)}) collective-permute-start(f32[16,64]{1,0:T(8,128)S(1)} %get-tuple-element.18), channel_id=1, source_target_pairs={{0,16},{16,32},{32,48},{48,64},{64,80},{80,96},{96,112},{1,17},{17... | collective-permute-start | bytes 12296 | tf_op jit(solution)/shard_map/ppermute | solution.py:201
  229.9 6.0 %collective-permute-start.11 = (f32[16,64]{1,0:T(8,128)S(1)}, f32[16,64]{1,0:T(8,128)S(1)}, u32[]{:S(2)}, u32[]{:S(2)}) collective-permute-start(f32[16,64]{1,0:T(8,128)S(1)} %get-tuple-element.19), channel_id=1, source_target_pairs={{16,0},{32,16},{48,32},{64,48},{80,64},{96,80},{112,96},{17,1},{33... | collective-permute-start | bytes 12296 | tf_op jit(solution)/shard_map/ppermute | solution.py:202
  (12 other events, 25.7 us)

commit v7 on v6

--- a/solution.py
+++ b/solution.py
@@ -21,7 +21,7 @@
 
 
 def edges(block):
-    return [edge_pair(block, "gy", 1), edge_pair(block, "gx", 2)]
+    return [edge_pair(block, "gy", block.ndim - 2), edge_pair(block, "gx", block.ndim - 1)]
 
 
 def harmonic(first, second):
@@ -41,8 +41,8 @@
     ]
 
 
-def faces_from(center):
-    return [harmonic(center, other) for other in neighbours(center, edges(center))]
+def faces_from(center, strips):
+    return [harmonic(center, other) for other in neighbours(center, strips)]
 
 
 def framed_kernel(
@@ -158,7 +158,9 @@
     vertical_coupling,
 ):
     active = excavated.astype(jnp.float32)
-    faces = faces_from(conduct)
+    both = edges(jnp.stack([conduct, active]))
+    faces = faces_from(conduct, [(low[0], high[0]) for low, high in both])
+    active_x, active_y = [(low[1], high[1]) for low, high in both]
     local_modes = vectors_x.shape[1] // (lax.axis_size("gx") * lax.axis_size("gy"))
     mode_start = (lax.axis_index("gx") * lax.axis_size("gy") + lax.axis_index("gy")) * local_modes
     local_values = lax.dynamic_slice_in_dim(values_x, mode_start, local_modes, 0)
@@ -176,7 +178,6 @@
         below = jnp.concatenate([zero, blocks[:-1, -1:]], axis=0)
         above = jnp.concatenate([blocks[1:, :1], zero], axis=0)
         framed_basis.append(jnp.concatenate([below, blocks, above], axis=1))
-    active_x, active_y = edges(active)
     count_y = lax.axis_size("gx")
     forward_y = [(i, i + 1) for i in range(count_y - 1)]
     backward_y = [(target, source) for source, target in forward_y]

time: 262 us -> 242 us (0.924)
  starting transfers between devices: 68.7 us -> 56.8 us
  local copies, waits for them, and re-layouts: 34.5 us -> 24.9 us
  waiting for transfers between devices: 16 us -> 25.5 us
  matrix products: 29 us -> 25.9 us
  other arithmetic: 29.1 us -> 26.2 us
    ppermute x4 -> x2, starting transfers between devices: 14.8 us -> 5.49 us  [edge_pair(): lax.ppermute(last, axis, forward)]
    all_to_all x1, waiting for transfers between devices: 0.01 us -> 5 us  [shards(): lax.all_to_all(framed, 'gy', split_axis=0, concat_axis=0, tiled=True)]
    slice x5 -> x2, local copies, waits for them, and re-layouts: 5.78 us -> 1.2 us  [shards(): faces = faces_from(conduct, [(low[0], high[0]) for low, high in both])]
    ppermute x4 -> x2, starting transfers between devices: 11.6 us -> 7.1 us  [edge_pair(): lax.ppermute(first, axis, backward)]
    dot_general x24, matrix products: 29 us -> 25.9 us  [product(): return jnp.einsum(spec, first, second, preferred_element_type=jnp.float32)]
    all_to_all x2, waiting for transfers between devices: 14.6 us -> 17.5 us  [shards(): lax.all_to_all(chunks, everyone, split_axis=0, concat_axis=0, tiled=True)]
    unnamed x44 -> x42, local copies, waits for them, and re-layouts: 7.63 us -> 4.86 us
    ppermute x2, waiting for transfers between devices: 0.01 us -> 2.66 us  [shards(): from_left = lax.ppermute(framed[:, 1:-1, -1], 'gx', forward_y)]
  transfers between devices with their start and end apart: 16 -> 12, of which waited for: 4 -> 5; matrix products, arithmetic and copies ran while one was open for 26% -> 21% of each run, Pallas kernels for 1% -> 1%
where the time goes in v7:
time: 242 us; the launch traced here: 239 us
  blocking collectives  65.4 us (27%)
  starting transfers between devices  56.8 us (23%)
  other arithmetic  26.2 us (11%)
  matrix products  25.9 us (11%)
  waiting for transfers between devices  25.5 us (11%)
  local copies, waits for them, and re-layouts  24.9 us (10%)
  Pallas kernels  12.7 us (5%)
    all_to_all x2, blocking collectives, shards(): lax.all_to_all(chunks, everyone, split_axis=0, concat_axis=0, tiled=True)  35.4 us
    dot_general x24, matrix products, product(): return jnp.einsum(spec, first, second, preferred_element_type=jnp.float32)  25.9 us
    all_to_all x2, waiting for transfers between devices, shards(): lax.all_to_all(chunks, everyone, split_axis=0, concat_axis=0, tiled=True)  17.5 us
    all_to_all x2, starting transfers between devices, shards(): lax.all_to_all(chunks, everyone, split_axis=0, concat_axis=0, tiled=True)  17.1 us
    all_to_all x1, blocking collectives, shards(): lax.all_to_all(framed, 'gy', split_axis=0, concat_axis=0, tiled=True)  16.4 us
    all_to_all x1, blocking collectives, shards(): lax.all_to_all(scaled, 'gy', split_axis=0, concat_axis=1, tiled=True)  13.7 us
    pallas_call x2, Pallas kernels, framed_stencil(): pl.pallas_call(framed_kernel, out_shape=(shape, shape), in_specs=[vmem] *...  8.54 us
    ppermute x2, starting transfers between devices, shards(): from_right = lax.ppermute(framed[:, 1:-1, 0], 'gx', backward_y)  8.49 us
  transfers between devices with their start and end apart: 12, of which 5 were waited for; matrix products, arithmetic and copies ran while one was open for 21% of the time, Pallas kernels for 1%

profile of v7, /device:TPU:3, one launch (start us, length us, event | category | flops | bytes accessed | tf_op | source)
XLA Modules:
  0.0 238.6 jit_solution(12934275658563271943)
XLA Ops:
  2.7 6.5 %all-to-all-start = ((f32[16,64,128]{2,1,0:T(8,128)}), f32[16,64,128]{2,1,0:T(8,128)S(1)}, u32[]{:S(2)}, u32[]{:S(2)}) async-start(f32[16,64,128]{2,1,0:T(8,128)} %multiply_multiply_fusion.1), calls=%async_computation | async-start | bytes 1048576 | tf_op jit(solution)/shard_map/all_to_all | solution.py:189
  10.2 3.5 %collective-permute-start.2 = (f32[2,16,128]{2,1,0:T(8,128)S(1)}, f32[2,16,128]{2,1,0:T(8,128)S(1)}, u32[]{:S(2)}, u32[]{:S(2)}) collective-permute-start(f32[2,16,128]{2,1,0:T(8,128)S(1)} %bitcast.252), channel_id=1, source_target_pairs={{0,1},{1,2},{2,3},{3,4},{4,5},{5,6},{6,7},{7,8},{8,9},{9,10},{10,1... | collective-permute-start | bytes 49160 | tf_op jit(solution)/shard_map/ppermute | solution.py:20
  16.6 5.2 %collective-permute-start.5 = (f32[2,16,64]{2,1,0:T(8,128)S(1)}, f32[2,16,64]{2,1,0:T(8,128)S(1)}, u32[]{:S(2)}, u32[]{:S(2)}) collective-permute-start(f32[2,16,64]{2,1,0:T(8,128)S(1)} %get-tuple-element.10), channel_id=1, source_target_pairs={{16,0},{32,16},{48,32},{64,48},{80,64},{96,80},{112,96},{17,1},{33... | collective-permute-start | bytes 24584 | tf_op jit(solution)/shard_map/ppermute | solution.py:20
  27.0 4.4 %fusion.4 = (bf16[1024,1024]{1,0:T(8,128)(2,1)}, bf16[1024,1024]{1,0:T(8,128)(2,1)S(1)}) fusion(f32[1024,1024]{1,0:T(8,128)} %param.14), kind=kLoop, calls=%fused_computation.10 | loop fusion | flops 4194304 | bytes 8388608 | tf_op jit(solution)/shard_map/convert_element_type | solution.py:134
  32.2 2.8 %fusion.7 = bf16[16,66,1024]{2,1,0:T(8,128)(2,1)} fusion(bf16[15,1,1024]{2,1,0:T(2,128)(2,1)S(1)} %get-tuple-element.19, bf16[15,1,1024]{2,1,0:T(2,128)(2,1)S(1)} %get-tuple-element.18, bf16[16,64,1024]{2,1,0:T(8,128)(2,1)S(1)} %bitcast.224), kind=kLoop, calls=%fused_computation.13 | loop fusion | flops 10813440 | bytes 4321280 | tf_op jit(solution)/shard_map/concatenate | solution.py:180
  39.1 12.2 %all-to-all-start.1 = ((f32[128,8,128]{2,1,0:T(8,128)}), f32[128,8,128]{2,1,0:T(8,128)S(1)}, u32[]{:S(2)}, u32[]{:S(2)}) async-start(f32[128,8,128]{2,1,0:T(8,128)} %bitcast.4), calls=%async_computation.1 | async-start | bytes 1048576 | tf_op jit(solution)/shard_map/all_to_all | solution.py:193
  52.0 4.5 %reduce-precision_convert_fusion = (bf16[1024,1024]{1,0:T(8,128)(2,1)S(1)}, bf16[1024,1024]{1,0:T(8,128)(2,1)}) fusion(f32[1024,1024]{1,0:T(8,128)} %param.17), kind=kLoop, calls=%fused_computation.1 | loop fusion | flops 4194304 | bytes 8388608 | tf_op jit(solution)/shard_map/convert_element_type | solution.py:134
  56.5 7.8 %all-to-all-done.1 = f32[128,8,128]{2,1,0:T(8,128)S(1)} async-done(((f32[128,8,128]{2,1,0:T(8,128)}), f32[128,8,128]{2,1,0:T(8,128)S(1)}, u32[]{:S(2)}, u32[]{:S(2)}) %all-to-all-start.1) | async-done | bytes 524320 | tf_op jit(solution)/shard_map/all_to_all | solution.py:193
  75.2 5.0 %all-to-all-start.2 = ((f32[128,8,128]{2,1,0:T(8,128)}), f32[128,8,128]{2,1,0:T(8,128)S(1)}, u32[]{:S(2)}, u32[]{:S(2)}) async-start(f32[128,8,128]{2,1,0:T(8,128)} %bitcast.238), calls=%async_computation.2 | async-start | bytes 1048576 | tf_op jit(solution)/shard_map/all_to_all | solution.py:199
  83.5 9.8 %all-to-all-done.2 = f32[128,8,128]{2,1,0:T(8,128)S(1)} async-done(((f32[128,8,128]{2,1,0:T(8,128)}), f32[128,8,128]{2,1,0:T(8,128)S(1)}, u32[]{:S(2)}, u32[]{:S(2)}) %all-to-all-start.2) | async-done | bytes 524320 | tf_op jit(solution)/shard_map/all_to_all | solution.py:199
  93.3 2.6 %fusion.38 = f32[16,66,128]{2,1,0:T(8,128)S(1)} fusion(bf16[16,66,1024]{2,1,0:T(8,128)(2,1)} %fusion.7, f32[128,8,128]{2,1,0:T(8,128)S(1)} %all-to-all-done.2), kind=kOutput, calls=%fused_computation.92 | convolution fusion | flops 277217280 | bytes 3227648 | tf_op jit(solution)/shard_map/iy,bri->bry/dot_general | solution.py:142
  101.9 3.3 %collective-permute-start.1 = (f32[16,64]{1,0:T(8,128)S(1)}, f32[16,64]{1,0:T(8,128)S(1)}, u32[]{:S(2)}, u32[]{:S(2)}) collective-permute-start(f32[16,64]{1,0:T(8,128)S(1)} %bitcast.254), channel_id=1, source_target_pairs={{16,0},{32,16},{48,32},{64,48},{80,64},{96,80},{112,96},{17,1},{33... | collective-permute-start | bytes 12296 | tf_op jit(solution)/shard_map/ppermute | solution.py:203
  105.2 3.5 %collective-permute-start = (f32[16,64]{1,0:T(8,128)S(1)}, f32[16,64]{1,0:T(8,128)S(1)}, u32[]{:S(2)}, u32[]{:S(2)}) collective-permute-start(f32[16,64]{1,0:T(8,128)S(1)} %bitcast.253), channel_id=1, source_target_pairs={{0,16},{16,32},{32,48},{48,64},{64,80},{80,96},{96,112},{1,17},{17... | collective-permute-start | bytes 12296 | tf_op jit(solution)/shard_map/ppermute | solution.py:202
  109.3 2.7 %collective-permute-done = f32[16,64]{1,0:T(8,128)S(1)} collective-permute-done((f32[16,64]{1,0:T(8,128)S(1)}, f32[16,64]{1,0:T(8,128)S(1)}, u32[]{:S(2)}, u32[]{:S(2)}) %collective-permute-start) | collective-permute-done | bytes 4128 | tf_op jit(solution)/shard_map/ppermute | solution.py:202
  114.0 6.1 %all-to-all-start.3 = ((f32[16,67,128]{2,1,0:T(8,128)}), f32[16,67,128]{2,1,0:T(8,128)S(1)}, u32[]{:S(2)}, u32[]{:S(2)}) async-start(f32[16,67,128]{2,1,0:T(8,128)} %pad_maximum_fusion.1), calls=%async_computation.3 | async-start | bytes 1179648 | tf_op jit(solution)/shard_map/all_to_all | solution.py:206
  120.7 4.6 %add_divide_fusion = (f32[16,64,128]{2,1,0:T(8,128)}, f32[16,64,128]{2,1,0:T(8,128)}, f32[16,64,128]{2,1,0:T(8,128)}, f32[16,64,128]{2,1,0:T(8,128)}, f32[16,64,128]{2,1,0:T(8,128)}, /*index=5*/f32[16,64,128]{2,1,0:T(8,128)}) fusion(f32[16,64,128]{2,1,0:T(8,128)S(1)} %copy-done.8, f32[16,64,127]{2,1,0:T(8,128)} %get-tuple-element.40, ...), kind=kLoop, calls=%fused_computation.81 | loop fusion | flops 3014656 | bytes 6750208 | tf_op jit(solution)/shard_map/div | solution.py:28
  125.3 5.0 %all-to-all-done.3.framed_ref = f32[16,67,128]{2,1,0:T(8,128)S(1)} async-done(((f32[16,67,128]{2,1,0:T(8,128)}), f32[16,67,128]{2,1,0:T(8,128)S(1)}, u32[]{:S(2)}, u32[]{:S(2)}) %all-to-all-start.3) | async-done | bytes 548896 | tf_op jit(solution)/shard_map/all_to_all | solution.py:206
  133.3 4.3 %shard_map.123 = (f32[16,64,128]{2,1,0:T(8,128)}, f32[16,64,128]{2,1,0:T(8,128)}) custom-call(f32[16,67,128]{2,1,0:T(8,128)} %copy-done.14, f32[16,64,128]{2,1,0:T(8,128)} %get-tuple-element.47.active_ref, f32[16,64,128]{2,1,0:T(8,128)} %residual_ref.1, f32[16,64,128]{2,1,0:T(8,128)} %broadcast_in_dim.15.adjoint_ref, f32[16,128]{1,0:T(8,128)} %get-tuple-element.53.x_low_ref, ...), custom_call_target="tpu_custom_call" | custom-call | tf_op jit(solution)/shard_map/pallas_call | solution.py:91
  138.9 13.7 %all_to_all.54 = f32[16,64,128]{2,1,0:T(8,128)S(1)} all-to-all(f32[16,64,128]{2,1,0:T(8,128)S(1)} %multiply_multiply_fusion), channel_id=1, replica_groups=mesh['gx'=8,'gy'=16] {'gy'}, dimensions={0} | all-to-all | bytes 1048576 | tf_op jit(solution)/shard_map/all_to_all | solution.py:189
  155.4 17.9 %all_to_all.55 = f32[128,8,128]{2,1,0:T(8,128)S(1)} all-to-all(f32[128,8,128]{2,1,0:T(8,128)S(1)} %bitcast.239), channel_id=1, replica_groups=mesh['gx'=8,'gy'=16] {'gx','gy'}, dimensions={0} | all-to-all | bytes 1048576 | tf_op jit(solution)/shard_map/all_to_all | solution.py:193
  181.9 17.5 %all_to_all.56 = f32[128,8,128]{2,1,0:T(8,128)S(1)} all-to-all(f32[128,8,128]{2,1,0:T(8,128)S(1)} %bitcast.240), channel_id=1, replica_groups=mesh['gx'=8,'gy'=16] {'gx','gy'}, dimensions={0} | all-to-all | bytes 1048576 | tf_op jit(solution)/shard_map/all_to_all | solution.py:199
  209.8 5.2 %collective-permute-start.7 = (f32[16,64]{1,0:T(8,128)S(1)}, f32[16,64]{1,0:T(8,128)S(1)}, u32[]{:S(2)}, u32[]{:S(2)}) collective-permute-start(f32[16,64]{1,0:T(8,128)S(1)} %get-tuple-element.21), channel_id=1, source_target_pairs={{16,0},{32,16},{48,32},{64,48},{80,64},{96,80},{112,96},{17,1},{33... | collective-permute-start | bytes 12296 | tf_op jit(solution)/shard_map/ppermute | solution.py:203
  215.9 16.4 %all_to_all.57.framed_ref = f32[16,67,128]{2,1,0:T(8,128)S(1)} all-to-all(f32[16,67,128]{2,1,0:T(8,128)S(1)} %pad_maximum_fusion.2), channel_id=1, replica_groups=mesh['gx'=8,'gy'=16] {'gy'}, dimensions={0} | all-to-all | bytes 1097728 | tf_op jit(solution)/shard_map/all_to_all | solution.py:206
  234.4 4.2 %shard_map.125 = (f32[16,64,128]{2,1,0:T(8,128)}, f32[16,64,128]{2,1,0:T(8,128)}) custom-call(f32[16,67,128]{2,1,0:T(8,128)} %copy-done.15, f32[16,64,128]{2,1,0:T(8,128)} %get-tuple-element.47.active_ref, f32[16,64,128]{2,1,0:T(8,128)} %get-tuple-element.6.residual_ref, f32[16,64,128]{2,1,0:T(8,128)} %get-tuple-element.7.adjoint_ref, ...), custom_call_target="tpu_custom_call" | custom-call | tf_op jit(solution)/shard_map/pallas_call | solution.py:91
  (126 shorter events, 68.9 us)
Async XLA Ops:
  0.6 8.6 %copy-start.16 = (s32[16,64,128]{2,1,0:T(8,128)S(1)}, s32[16,64,128]{2,1,0:T(8,128)}, u32[]{:S(2)}) copy-start(s32[16,64,128]{2,1,0:T(8,128)} %param.13) | copy-start | bytes 1572868
  0.6 9.5 %copy-start.8 = (f32[16,64,128]{2,1,0:T(8,128)S(1)}, f32[16,64,128]{2,1,0:T(8,128)}, u32[]{:S(2)}) copy-start(f32[16,64,128]{2,1,0:T(8,128)} %param.12) | copy-start | bytes 1572868
  2.7 32.3 %all-to-all-start = ((f32[16,64,128]{2,1,0:T(8,128)}), f32[16,64,128]{2,1,0:T(8,128)S(1)}, u32[]{:S(2)}, u32[]{:S(2)}) async-start(f32[16,64,128]{2,1,0:T(8,128)} %multiply_multiply_fusion.1), calls=%async_computation | async-start | bytes 1048576 | tf_op jit(solution)/shard_map/all_to_all | solution.py:189
  10.2 98.5 %collective-permute-start.2 = (f32[2,16,128]{2,1,0:T(8,128)S(1)}, f32[2,16,128]{2,1,0:T(8,128)S(1)}, u32[]{:S(2)}, u32[]{:S(2)}) collective-permute-start(f32[2,16,128]{2,1,0:T(8,128)S(1)} %bitcast.252), channel_id=1, source_target_pairs={{0,1},{1,2},{2,3},{3,4},{4,5},{5,6},{6,7},{7,8},{8,9},{9,10},{10,1... | collective-permute-start | bytes 49160 | tf_op jit(solution)/shard_map/ppermute | solution.py:20
  13.7 106.4 %collective-permute-start.3 = (f32[2,16,128]{2,1,0:T(8,128)S(1)}, f32[2,16,128]{2,1,0:T(8,128)S(1)}, u32[]{:S(2)}, u32[]{:S(2)}) collective-permute-start(f32[2,16,128]{2,1,0:T(8,128)S(1)} %bitcast.251), channel_id=1, source_target_pairs={{1,0},{2,1},{3,2},{4,3},{5,4},{6,5},{7,6},{8,7},{9,8},{10,9},{11,1... | collective-permute-start | bytes 49160 | tf_op jit(solution)/shard_map/ppermute | solution.py:20
  16.6 65.9 %collective-permute-start.5 = (f32[2,16,64]{2,1,0:T(8,128)S(1)}, f32[2,16,64]{2,1,0:T(8,128)S(1)}, u32[]{:S(2)}, u32[]{:S(2)}) collective-permute-start(f32[2,16,64]{2,1,0:T(8,128)S(1)} %get-tuple-element.10), channel_id=1, source_target_pairs={{16,0},{32,16},{48,32},{64,48},{80,64},{96,80},{112,96},{17,1},{33... | collective-permute-start | bytes 24584 | tf_op jit(solution)/shard_map/ppermute | solution.py:20
  21.8 59.6 %collective-permute-start.4 = (f32[2,16,64]{2,1,0:T(8,128)S(1)}, f32[2,16,64]{2,1,0:T(8,128)S(1)}, u32[]{:S(2)}, u32[]{:S(2)}) collective-permute-start(f32[2,16,64]{2,1,0:T(8,128)S(1)} %get-tuple-element.11), channel_id=1, source_target_pairs={{0,16},{16,32},{32,48},{48,64},{64,80},{80,96},{96,112},{1,17},{17... | collective-permute-start | bytes 24584 | tf_op jit(solution)/shard_map/ppermute | solution.py:20
  31.4 6.3 %copy-start = (bf16[1024,1024]{1,0:T(8,128)(2,1)}, bf16[1024,1024]{1,0:T(8,128)(2,1)S(1)}, u32[]{:S(2)}) copy-start(bf16[1024,1024]{1,0:T(8,128)(2,1)S(1)} %get-tuple-element.15) | copy-start | bytes 6291460
  37.7 13.7 %copy-start.17 = (f32[1024]{0:T(1024)S(1)}, f32[1024]{0:T(1024)}, u32[]{:S(2)}) copy-start(f32[1024]{0:T(1024)} %param.19) | copy-start | bytes 12292
  39.1 25.1 %all-to-all-start.1 = ((f32[128,8,128]{2,1,0:T(8,128)}), f32[128,8,128]{2,1,0:T(8,128)S(1)}, u32[]{:S(2)}, u32[]{:S(2)}) async-start(f32[128,8,128]{2,1,0:T(8,128)} %bitcast.4), calls=%async_computation.1 | async-start | bytes 1048576 | tf_op jit(solution)/shard_map/all_to_all | solution.py:193
  70.1 2.6 %copy-start.11 = (f32[16,8,1024]{2,1,0:T(8,128)S(1)}, f32[16,8,1024]{2,1,0:T(8,128)}, u32[]{:S(2)}) copy-start(f32[16,8,1024]{2,1,0:T(8,128)} %shard_map.122) | copy-start | bytes 1572868
  75.2 18.0 %all-to-all-start.2 = ((f32[128,8,128]{2,1,0:T(8,128)}), f32[128,8,128]{2,1,0:T(8,128)S(1)}, u32[]{:S(2)}, u32[]{:S(2)}) async-start(f32[128,8,128]{2,1,0:T(8,128)} %bitcast.238), calls=%async_computation.2 | async-start | bytes 1048576 | tf_op jit(solution)/shard_map/all_to_all | solution.py:199
  93.3 2.6 %copy-start.2 = (bf16[16,66,1024]{2,1,0:T(8,128)(2,1)S(1)}, bf16[16,66,1024]{2,1,0:T(8,128)(2,1)}, u32[]{:S(2)}) copy-start(bf16[16,66,1024]{2,1,0:T(8,128)(2,1)} %fusion.7) | copy-start | bytes 6488068
  101.9 7.4 %collective-permute-start.1 = (f32[16,64]{1,0:T(8,128)S(1)}, f32[16,64]{1,0:T(8,128)S(1)}, u32[]{:S(2)}, u32[]{:S(2)}) collective-permute-start(f32[16,64]{1,0:T(8,128)S(1)} %bitcast.254), channel_id=1, source_target_pairs={{16,0},{32,16},{48,32},{64,48},{80,64},{96,80},{112,96},{17,1},{33... | collective-permute-start | bytes 12296 | tf_op jit(solution)/shard_map/ppermute | solution.py:203
  105.2 6.8 %collective-permute-start = (f32[16,64]{1,0:T(8,128)S(1)}, f32[16,64]{1,0:T(8,128)S(1)}, u32[]{:S(2)}, u32[]{:S(2)}) collective-permute-start(f32[16,64]{1,0:T(8,128)S(1)} %bitcast.253), channel_id=1, source_target_pairs={{0,16},{16,32},{32,48},{48,64},{64,80},{80,96},{96,112},{1,17},{17... | collective-permute-start | bytes 12296 | tf_op jit(solution)/shard_map/ppermute | solution.py:202
  114.0 16.4 %all-to-all-start.3 = ((f32[16,67,128]{2,1,0:T(8,128)}), f32[16,67,128]{2,1,0:T(8,128)S(1)}, u32[]{:S(2)}, u32[]{:S(2)}) async-start(f32[16,67,128]{2,1,0:T(8,128)} %pad_maximum_fusion.1), calls=%async_computation.3 | async-start | bytes 1179648 | tf_op jit(solution)/shard_map/all_to_all | solution.py:206
  130.3 2.9 %copy-start.14 = (f32[16,67,128]{2,1,0:T(8,128)}, f32[16,67,128]{2,1,0:T(8,128)S(1)}, u32[]{:S(2)}) copy-start(f32[16,67,128]{2,1,0:T(8,128)S(1)} %all-to-all-done.3.framed_ref) | copy-start | bytes 1646596
  133.3 4.3 %copy-start.18 = (f32[128]{0:T(128)S(1)}, f32[128]{0:T(128)}, u32[]{:S(2)}) copy-start(f32[128]{0:T(128)} %param.18) | copy-start | bytes 1540
  133.3 4.3 %copy-start.19 = (f32[64]{0:T(128)S(1)}, f32[64]{0:T(128)}, u32[]{:S(2)}) copy-start(f32[64]{0:T(128)} %param.15) | copy-start | bytes 772
  137.6 15.1 %copy-start.6 = (bf16[1024,1024]{1,0:T(8,128)(2,1)S(1)}, bf16[1024,1024]{1,0:T(8,128)(2,1)}, u32[]{:S(2)}) copy-start(bf16[1024,1024]{1,0:T(8,128)(2,1)} %get-tuple-element.14) | copy-start | bytes 6291460
  155.4 18.0 %copy-start.9 = (bf16[1024,1024]{1,0:T(8,128)(2,1)S(1)}, bf16[1024,1024]{1,0:T(8,128)(2,1)}, u32[]{:S(2)}) copy-start(bf16[1024,1024]{1,0:T(8,128)(2,1)} %get-tuple-element.13) | copy-start | bytes 6291460
  181.0 18.4 %copy-start.3 = (bf16[16,66,1024]{2,1,0:T(8,128)(2,1)S(1)}, bf16[16,66,1024]{2,1,0:T(8,128)(2,1)}, u32[]{:S(2)}) copy-start(bf16[16,66,1024]{2,1,0:T(8,128)(2,1)} %fusion.7) | copy-start | bytes 6488068
  207.3 8.2 %collective-permute-start.6 = (f32[16,64]{1,0:T(8,128)S(1)}, f32[16,64]{1,0:T(8,128)S(1)}, u32[]{:S(2)}, u32[]{:S(2)}) collective-permute-start(f32[16,64]{1,0:T(8,128)S(1)} %get-tuple-element.20), channel_id=1, source_target_pairs={{0,16},{16,32},{32,48},{48,64},{64,80},{80,96},{96,112},{1,17},{17... | collective-permute-start | bytes 12296 | tf_op jit(solution)/shard_map/ppermute | solution.py:202
  209.8 6.0 %collective-permute-start.7 = (f32[16,64]{1,0:T(8,128)S(1)}, f32[16,64]{1,0:T(8,128)S(1)}, u32[]{:S(2)}, u32[]{:S(2)}) collective-permute-start(f32[16,64]{1,0:T(8,128)S(1)} %get-tuple-element.21), channel_id=1, source_target_pairs={{16,0},{32,16},{48,32},{64,48},{80,64},{96,80},{112,96},{17,1},{33... | collective-permute-start | bytes 12296 | tf_op jit(solution)/shard_map/ppermute | solution.py:203
  (8 other events, 14.3 us)

commit v8 on v7

--- a/solution.py
+++ b/solution.py
@@ -198,9 +198,11 @@
         chunks = chunks.reshape(-1, local_modes, chunks.shape[3])
         chunks = lax.all_to_all(chunks, everyone, split_axis=0, concat_axis=0, tiled=True)
         solved = chunks.reshape(-1, chunks.shape[2])
+        sides = jnp.concatenate([solved[:, :1], solved[:, -1:]], axis=1)
+        sides = transform("iy,bri->bry", sides, framed_basis)
+        from_left = lax.ppermute(sides[:, 1:-1, 1], "gx", forward_y)
+        from_right = lax.ppermute(sides[:, 1:-1, 0], "gx", backward_y)
         framed = transform("iy,bri->bry", solved, framed_basis)
-        from_left = lax.ppermute(framed[:, 1:-1, -1], "gx", forward_y)
-        from_right = lax.ppermute(framed[:, 1:-1, 0], "gx", backward_y)
         halo_row = jnp.concatenate([from_left, from_right], axis=1)[:, None, :]
         framed = jnp.concatenate([framed, halo_row], axis=1)
         framed = lax.all_to_all(framed, "gy", split_axis=0, concat_axis=0, tiled=True)

time: 242 us -> 246 us (1.017)
  matrix products: 25.9 us -> 31.4 us
  waiting for transfers between devices: 25.5 us -> 20.3 us
  other arithmetic: 26.2 us -> 29.9 us
    dot_general x24 -> x30, matrix products: 25.9 us -> 31.4 us  [product(): return jnp.einsum(spec, first, second, preferred_element_type=jnp.float32)]
    slice x1 -> x6, local copies, waits for them, and re-layouts: 1.01 us -> 5.91 us  [shards(): sides = jnp.concatenate([solved[:, :1], solved[:, -1:]], axis=1)]
    ppermute x4, waiting for transfers between devices: 2.98 us -> 0.01 us  [the longest x2 0.01 us: shards(): from_left = lax.ppermute(sides[:, 1:-1, 1], 'gx', forward_y)]
    concatenate x1 -> x2, other arithmetic: 2.75 us -> 5.61 us  [shards(): framed_basis.append(jnp.concatenate([below, blocks, above], axis=1))]
    all_to_all x2, blocking collectives: 35.4 us -> 38.1 us  [shards(): lax.all_to_all(chunks, everyone, split_axis=0, concat_axis=0, tiled=True)]
    unnamed x42, local copies, waits for them, and re-layouts: 4.86 us -> 2.33 us
  transfers between devices with their start and end apart: 12 -> 12, of which waited for: 5 -> 3; matrix products, arithmetic and copies ran while one was open for 21% -> 24% of each run, Pallas kernels for 1% -> 1%
where the time goes in v8:
time: 246 us; the launch traced here: 244 us
  blocking collectives  66.7 us (27%)
  starting transfers between devices  56.1 us (23%)
  matrix products  31.4 us (13%)
  other arithmetic  29.9 us (12%)
  local copies, waits for them, and re-layouts  25.3 us (10%)
  waiting for transfers between devices  20.3 us (8%)
  Pallas kernels  12.7 us (5%)
    all_to_all x2, blocking collectives, shards(): lax.all_to_all(chunks, everyone, split_axis=0, concat_axis=0, tiled=True)  38.1 us
    dot_general x30, matrix products, product(): return jnp.einsum(spec, first, second, preferred_element_type=jnp.float32)  31.4 us
    all_to_all x2, starting transfers between devices, shards(): lax.all_to_all(chunks, everyone, split_axis=0, concat_axis=0, tiled=True)  17.3 us
    all_to_all x2, waiting for transfers between devices, shards(): lax.all_to_all(chunks, everyone, split_axis=0, concat_axis=0, tiled=True)  15.9 us
    all_to_all x1, blocking collectives, shards(): lax.all_to_all(framed, 'gy', split_axis=0, concat_axis=0, tiled=True)  15 us
    all_to_all x1, blocking collectives, shards(): lax.all_to_all(scaled, 'gy', split_axis=0, concat_axis=1, tiled=True)  13.7 us
    ppermute x2, starting transfers between devices, shards(): from_right = lax.ppermute(sides[:, 1:-1, 0], 'gx', backward_y)  10.4 us
    pallas_call x2, Pallas kernels, framed_stencil(): pl.pallas_call(framed_kernel, out_shape=(shape, shape), in_specs=[vmem] *...  8.56 us
  transfers between devices with their start and end apart: 12, of which 3 were waited for; matrix products, arithmetic and copies ran while one was open for 24% of the time, Pallas kernels for 1%

profile of v8, /device:TPU:3, one launch (start us, length us, event | category | flops | bytes accessed | tf_op | source)
XLA Modules:
  0.0 243.6 jit_solution(10962230784673014471)
XLA Ops:
  2.7 6.5 %all-to-all-start = ((f32[16,64,128]{2,1,0:T(8,128)}), f32[16,64,128]{2,1,0:T(8,128)S(1)}, u32[]{:S(2)}, u32[]{:S(2)}) async-start(f32[16,64,128]{2,1,0:T(8,128)} %multiply_multiply_fusion.1), calls=%async_computation | async-start | bytes 1048576 | tf_op jit(solution)/shard_map/all_to_all | solution.py:189
  10.8 3.5 %collective-permute-start.2 = (f32[2,16,128]{2,1,0:T(8,128)}, f32[2,16,128]{2,1,0:T(8,128)}, u32[]{:S(2)}, u32[]{:S(2)}) collective-permute-start(f32[2,16,128]{2,1,0:T(8,128)} %bitcast.39), channel_id=1, source_target_pairs={{0,1},{1,2},{2,3},{3,4},{4,5},{5,6},{6,7},{7,8},{8,9},{9,10},{10,1... | collective-permute-start | bytes 49160 | tf_op jit(solution)/shard_map/ppermute | solution.py:20
  17.8 5.2 %collective-permute-start.5 = (f32[2,16,64]{2,1,0:T(8,128)}, f32[2,16,64]{2,1,0:T(8,128)S(1)}, u32[]{:S(2)}, u32[]{:S(2)}) collective-permute-start(f32[2,16,64]{2,1,0:T(8,128)} %get-tuple-element.10), channel_id=1, source_target_pairs={{16,0},{32,16},{48,32},{64,48},{80,64},{96,80},{112,96},{17,1},{33... | collective-permute-start | bytes 24584 | tf_op jit(solution)/shard_map/ppermute | solution.py:20
  28.2 4.5 %fusion.4 = (bf16[1024,1024]{1,0:T(8,128)(2,1)}, bf16[1024,1024]{1,0:T(8,128)(2,1)S(1)}) fusion(f32[1024,1024]{1,0:T(8,128)} %param.14), kind=kLoop, calls=%fused_computation.10 | loop fusion | flops 4194304 | bytes 8388608 | tf_op jit(solution)/shard_map/convert_element_type | solution.py:134
  34.0 2.9 %fusion.7 = bf16[16,66,1024]{2,1,0:T(8,128)(2,1)S(1)} fusion(bf16[15,1,1024]{2,1,0:T(2,128)(2,1)S(1)} %get-tuple-element.19, bf16[15,1,1024]{2,1,0:T(2,128)(2,1)S(1)} %get-tuple-element.18, bf16[16,64,1024]{2,1,0:T(8,128)(2,1)} %bitcast.254), kind=kLoop, calls=%fused_computation.13 | loop fusion | flops 10813440 | bytes 4321280 | tf_op jit(solution)/shard_map/concatenate | solution.py:180
  37.0 2.7 %fusion.9 = bf16[16,66,1024]{2,1,0:T(8,128)(2,1)} fusion(bf16[15,1,1024]{2,1,0:T(2,128)(2,1)S(1)} %get-tuple-element.17, bf16[15,1,1024]{2,1,0:T(2,128)(2,1)S(1)} %get-tuple-element.16, bf16[16,64,1024]{2,1,0:T(8,128)(2,1)S(1)} %bitcast.256), kind=kLoop, calls=%fused_computation.15 | loop fusion | flops 10813440 | bytes 4321280 | tf_op jit(solution)/shard_map/concatenate | solution.py:180
  44.0 12.2 %all-to-all-start.1 = ((f32[128,8,128]{2,1,0:T(8,128)}), f32[128,8,128]{2,1,0:T(8,128)S(1)}, u32[]{:S(2)}, u32[]{:S(2)}) async-start(f32[128,8,128]{2,1,0:T(8,128)} %bitcast.270), calls=%async_computation.1 | async-start | bytes 1048576 | tf_op jit(solution)/shard_map/all_to_all | solution.py:193
  56.9 5.2 %reduce-precision_convert_fusion = (bf16[1024,1024]{1,0:T(8,128)(2,1)}, bf16[1024,1024]{1,0:T(8,128)(2,1)}) fusion(f32[1024,1024]{1,0:T(8,128)} %param.17), kind=kLoop, calls=%fused_computation.1 | loop fusion | flops 4194304 | bytes 8388608 | tf_op jit(solution)/shard_map/convert_element_type | solution.py:134
  62.1 7.0 %all-to-all-done.1 = f32[128,8,128]{2,1,0:T(8,128)S(1)} async-done(((f32[128,8,128]{2,1,0:T(8,128)}), f32[128,8,128]{2,1,0:T(8,128)S(1)}, u32[]{:S(2)}, u32[]{:S(2)}) %all-to-all-start.1) | async-done | bytes 524320 | tf_op jit(solution)/shard_map/all_to_all | solution.py:193
  75.2 2.6 %convolution_bitcast_fusion.8 = f32[8,16,8,128]{3,2,0,1:T(8,128)S(1)} fusion(bf16[8,128,1024,1]{2,1,0,3:T(8,128)(2,1)} %bitcast.260, f32[16,8,1024]{2,1,0:T(8,128)} %shard_map.122), kind=kOutput, calls=%fused_computation.28 | convolution fusion | flops 268697600 | bytes 3145728 | tf_op jit(solution)/shard_map/zij,alj->azil/dot_general | solution.py:142
  80.3 5.1 %all-to-all-start.2 = ((f32[128,8,128]{2,1,0:T(8,128)}), f32[128,8,128]{2,1,0:T(8,128)S(1)}, u32[]{:S(2)}, u32[]{:S(2)}) async-start(f32[128,8,128]{2,1,0:T(8,128)} %bitcast.269), calls=%async_computation.2 | async-start | bytes 1048576 | tf_op jit(solution)/shard_map/all_to_all | solution.py:199
  89.6 8.9 %all-to-all-done.2 = f32[128,8,128]{2,1,0:T(8,128)S(1)} async-done(((f32[128,8,128]{2,1,0:T(8,128)}), f32[128,8,128]{2,1,0:T(8,128)S(1)}, u32[]{:S(2)}, u32[]{:S(2)}) %all-to-all-start.2) | async-done | bytes 524320 | tf_op jit(solution)/shard_map/all_to_all | solution.py:199
  107.6 5.2 %collective-permute-start.1 = (f32[16,64]{1,0:T(8,128)S(1)}, f32[16,64]{1,0:T(8,128)S(1)}, u32[]{:S(2)}, u32[]{:S(2)}) collective-permute-start(f32[16,64]{1,0:T(8,128)S(1)} %get-tuple-element.59), channel_id=1, source_target_pairs={{16,0},{32,16},{48,32},{64,48},{80,64},{96,80},{112,96},{17,1},{33... | collective-permute-start | bytes 12296 | tf_op jit(solution)/shard_map/ppermute | solution.py:204
  116.1 4.4 %all-to-all-start.3 = ((f32[16,67,128]{2,1,0:T(8,128)}), f32[16,67,128]{2,1,0:T(8,128)S(1)}, u32[]{:S(2)}, u32[]{:S(2)}) async-start(f32[16,67,128]{2,1,0:T(8,128)} %pad_maximum_fusion.1), calls=%async_computation.3 | async-start | bytes 1179648 | tf_op jit(solution)/shard_map/all_to_all | solution.py:208
  121.8 4.6 %add_divide_fusion = (f32[16,64,128]{2,1,0:T(8,128)}, f32[16,64,128]{2,1,0:T(8,128)}, f32[16,64,128]{2,1,0:T(8,128)}, f32[16,64,128]{2,1,0:T(8,128)}, f32[16,64,128]{2,1,0:T(8,128)}, /*index=5*/f32[16,64,128]{2,1,0:T(8,128)}) fusion(f32[16,64,128]{2,1,0:T(8,128)S(1)} %copy-done.11, f32[16,64,127]{2,1,0:T(8,128)} %get-tuple-element.38, ...), kind=kLoop, calls=%fused_computation.82 | loop fusion | flops 3014656 | bytes 6750208 | tf_op jit(solution)/shard_map/div | solution.py:28
  126.4 4.3 %all-to-all-done.3.framed_ref = f32[16,67,128]{2,1,0:T(8,128)S(1)} async-done(((f32[16,67,128]{2,1,0:T(8,128)}), f32[16,67,128]{2,1,0:T(8,128)S(1)}, u32[]{:S(2)}, u32[]{:S(2)}) %all-to-all-start.3) | async-done | bytes 548896 | tf_op jit(solution)/shard_map/all_to_all | solution.py:208
  134.4 4.3 %shard_map.123 = (f32[16,64,128]{2,1,0:T(8,128)}, f32[16,64,128]{2,1,0:T(8,128)}) custom-call(f32[16,67,128]{2,1,0:T(8,128)} %copy-done.15, f32[16,64,128]{2,1,0:T(8,128)} %get-tuple-element.45.active_ref, f32[16,64,128]{2,1,0:T(8,128)} %residual_ref.1, f32[16,64,128]{2,1,0:T(8,128)} %broadcast_in_dim.15.adjoint_ref, f32[16,128]{1,0:T(8,128)} %get-tuple-element.55.x_low_ref, ...), custom_call_target="tpu_custom_call" | custom-call | tf_op jit(solution)/shard_map/pallas_call | solution.py:91
  140.1 13.7 %all_to_all.54 = f32[16,64,128]{2,1,0:T(8,128)S(1)} all-to-all(f32[16,64,128]{2,1,0:T(8,128)S(1)} %multiply_multiply_fusion), channel_id=1, replica_groups=mesh['gx'=8,'gy'=16] {'gy'}, dimensions={0} | all-to-all | bytes 1048576 | tf_op jit(solution)/shard_map/all_to_all | solution.py:189
  156.6 20.6 %all_to_all.55 = f32[128,8,128]{2,1,0:T(8,128)S(1)} all-to-all(f32[128,8,128]{2,1,0:T(8,128)S(1)} %bitcast.271), channel_id=1, replica_groups=mesh['gx'=8,'gy'=16] {'gx','gy'}, dimensions={0} | all-to-all | bytes 1048576 | tf_op jit(solution)/shard_map/all_to_all | solution.py:193
  181.5 2.6 %convolution_bitcast_fusion = f32[8,16,8,128]{3,2,0,1:T(8,128)S(1)} fusion(bf16[8,128,1024,1]{2,1,0,3:T(8,128)(2,1)} %bitcast.261, f32[16,8,1024]{2,1,0:T(8,128)} %shard_map.124), kind=kOutput, calls=%fused_computation.20 | convolution fusion | flops 268697600 | bytes 3145728 | tf_op jit(solution)/shard_map/zij,alj->azil/dot_general | solution.py:142
  185.9 17.5 %all_to_all.56 = f32[128,8,128]{2,1,0:T(8,128)S(1)} all-to-all(f32[128,8,128]{2,1,0:T(8,128)S(1)} %bitcast.272), channel_id=1, replica_groups=mesh['gx'=8,'gy'=16] {'gx','gy'}, dimensions={0} | all-to-all | bytes 1048576 | tf_op jit(solution)/shard_map/all_to_all | solution.py:199
  212.9 5.2 %collective-permute-start.7 = (f32[16,64]{1,0:T(8,128)S(1)}, f32[16,64]{1,0:T(8,128)S(1)}, u32[]{:S(2)}, u32[]{:S(2)}) collective-permute-start(f32[16,64]{1,0:T(8,128)S(1)} %get-tuple-element.53), channel_id=1, source_target_pairs={{16,0},{32,16},{48,32},{64,48},{80,64},{96,80},{112,96},{17,1},{33... | collective-permute-start | bytes 12296 | tf_op jit(solution)/shard_map/ppermute | solution.py:204
  221.5 15.0 %all_to_all.57.framed_ref = f32[16,67,128]{2,1,0:T(8,128)S(1)} all-to-all(f32[16,67,128]{2,1,0:T(8,128)S(1)} %pad_maximum_fusion.2), channel_id=1, replica_groups=mesh['gx'=8,'gy'=16] {'gy'}, dimensions={0} | all-to-all | bytes 1097728 | tf_op jit(solution)/shard_map/all_to_all | solution.py:208
  239.3 4.2 %shard_map.125 = (f32[16,64,128]{2,1,0:T(8,128)}, f32[16,64,128]{2,1,0:T(8,128)}) custom-call(f32[16,67,128]{2,1,0:T(8,128)} %copy-done.16, f32[16,64,128]{2,1,0:T(8,128)} %get-tuple-element.45.active_ref, f32[16,64,128]{2,1,0:T(8,128)} %get-tuple-element.6.residual_ref, f32[16,64,128]{2,1,0:T(8,128)} %get-tuple-element.7.adjoint_ref, ...), custom_call_target="tpu_custom_call" | custom-call | tf_op jit(solution)/shard_map/pallas_call | solution.py:91
  (136 shorter events, 74.4 us)
Async XLA Ops:
  0.6 8.6 %copy-start.17 = (s32[16,64,128]{2,1,0:T(8,128)S(1)}, s32[16,64,128]{2,1,0:T(8,128)}, u32[]{:S(2)}) copy-start(s32[16,64,128]{2,1,0:T(8,128)} %param.13) | copy-start | bytes 1572868
  0.6 9.5 %copy-start.11 = (f32[16,64,128]{2,1,0:T(8,128)S(1)}, f32[16,64,128]{2,1,0:T(8,128)}, u32[]{:S(2)}) copy-start(f32[16,64,128]{2,1,0:T(8,128)} %param.12) | copy-start | bytes 1572868
  2.7 37.0 %all-to-all-start = ((f32[16,64,128]{2,1,0:T(8,128)}), f32[16,64,128]{2,1,0:T(8,128)S(1)}, u32[]{:S(2)}, u32[]{:S(2)}) async-start(f32[16,64,128]{2,1,0:T(8,128)} %multiply_multiply_fusion.1), calls=%async_computation | async-start | bytes 1048576 | tf_op jit(solution)/shard_map/all_to_all | solution.py:189
  10.8 77.5 %collective-permute-start.2 = (f32[2,16,128]{2,1,0:T(8,128)}, f32[2,16,128]{2,1,0:T(8,128)}, u32[]{:S(2)}, u32[]{:S(2)}) collective-permute-start(f32[2,16,128]{2,1,0:T(8,128)} %bitcast.39), channel_id=1, source_target_pairs={{0,1},{1,2},{2,3},{3,4},{4,5},{5,6},{6,7},{7,8},{8,9},{9,10},{10,1... | collective-permute-start | bytes 49160 | tf_op jit(solution)/shard_map/ppermute | solution.py:20
  14.3 106.2 %collective-permute-start.3 = (f32[2,16,128]{2,1,0:T(8,128)}, f32[2,16,128]{2,1,0:T(8,128)}, u32[]{:S(2)}, u32[]{:S(2)}) collective-permute-start(f32[2,16,128]{2,1,0:T(8,128)} %bitcast.41), channel_id=1, source_target_pairs={{1,0},{2,1},{3,2},{4,3},{5,4},{6,5},{7,6},{8,7},{9,8},{10,9},{11,1... | collective-permute-start | bytes 49160 | tf_op jit(solution)/shard_map/ppermute | solution.py:20
  17.8 67.7 %collective-permute-start.5 = (f32[2,16,64]{2,1,0:T(8,128)}, f32[2,16,64]{2,1,0:T(8,128)S(1)}, u32[]{:S(2)}, u32[]{:S(2)}) collective-permute-start(f32[2,16,64]{2,1,0:T(8,128)} %get-tuple-element.10), channel_id=1, source_target_pairs={{16,0},{32,16},{48,32},{64,48},{80,64},{96,80},{112,96},{17,1},{33... | collective-permute-start | bytes 24584 | tf_op jit(solution)/shard_map/ppermute | solution.py:20
  22.9 62.5 %collective-permute-start.4 = (f32[2,16,64]{2,1,0:T(8,128)}, f32[2,16,64]{2,1,0:T(8,128)}, u32[]{:S(2)}, u32[]{:S(2)}) collective-permute-start(f32[2,16,64]{2,1,0:T(8,128)} %get-tuple-element.11), channel_id=1, source_target_pairs={{0,16},{16,32},{32,48},{48,64},{64,80},{80,96},{96,112},{1,17},{17... | collective-permute-start | bytes 24584 | tf_op jit(solution)/shard_map/ppermute | solution.py:20
  32.7 4.2 %copy-start.7 = (bf16[1024,1024]{1,0:T(8,128)(2,1)S(1)}, bf16[1024,1024]{1,0:T(8,128)(2,1)}, u32[]{:S(2)}) copy-start(bf16[1024,1024]{1,0:T(8,128)(2,1)} %get-tuple-element.14) | copy-start | bytes 6291460
  42.5 13.7 %copy-start.18 = (f32[1024]{0:T(1024)S(1)}, f32[1024]{0:T(1024)}, u32[]{:S(2)}) copy-start(f32[1024]{0:T(1024)} %param.19) | copy-start | bytes 12292
  44.0 25.1 %all-to-all-start.1 = ((f32[128,8,128]{2,1,0:T(8,128)}), f32[128,8,128]{2,1,0:T(8,128)S(1)}, u32[]{:S(2)}, u32[]{:S(2)}) async-start(f32[128,8,128]{2,1,0:T(8,128)} %bitcast.270), calls=%async_computation.1 | async-start | bytes 1048576 | tf_op jit(solution)/shard_map/all_to_all | solution.py:193
  80.3 18.2 %all-to-all-start.2 = ((f32[128,8,128]{2,1,0:T(8,128)}), f32[128,8,128]{2,1,0:T(8,128)S(1)}, u32[]{:S(2)}, u32[]{:S(2)}) async-start(f32[128,8,128]{2,1,0:T(8,128)} %bitcast.269), calls=%async_computation.2 | async-start | bytes 1048576 | tf_op jit(solution)/shard_map/all_to_all | solution.py:199
  105.1 10.1 %collective-permute-start = (f32[16,64]{1,0:T(8,128)S(1)}, f32[16,64]{1,0:T(8,128)S(1)}, u32[]{:S(2)}, u32[]{:S(2)}) collective-permute-start(f32[16,64]{1,0:T(8,128)S(1)} %get-tuple-element.58), channel_id=1, source_target_pairs={{0,16},{16,32},{32,48},{48,64},{64,80},{80,96},{96,112},{1,17},{17... | collective-permute-start | bytes 12296 | tf_op jit(solution)/shard_map/ppermute | solution.py:203
  107.6 7.6 %collective-permute-start.1 = (f32[16,64]{1,0:T(8,128)S(1)}, f32[16,64]{1,0:T(8,128)S(1)}, u32[]{:S(2)}, u32[]{:S(2)}) collective-permute-start(f32[16,64]{1,0:T(8,128)S(1)} %get-tuple-element.59), channel_id=1, source_target_pairs={{16,0},{32,16},{48,32},{64,48},{80,64},{96,80},{112,96},{17,1},{33... | collective-permute-start | bytes 12296 | tf_op jit(solution)/shard_map/ppermute | solution.py:204
  116.1 14.6 %all-to-all-start.3 = ((f32[16,67,128]{2,1,0:T(8,128)}), f32[16,67,128]{2,1,0:T(8,128)S(1)}, u32[]{:S(2)}, u32[]{:S(2)}) async-start(f32[16,67,128]{2,1,0:T(8,128)} %pad_maximum_fusion.1), calls=%async_computation.3 | async-start | bytes 1179648 | tf_op jit(solution)/shard_map/all_to_all | solution.py:208
  130.7 3.7 %copy-start.15 = (f32[16,67,128]{2,1,0:T(8,128)}, f32[16,67,128]{2,1,0:T(8,128)S(1)}, u32[]{:S(2)}) copy-start(f32[16,67,128]{2,1,0:T(8,128)S(1)} %all-to-all-done.3.framed_ref) | copy-start | bytes 1646596
  134.4 4.3 %copy-start.19 = (f32[128]{0:T(128)S(1)}, f32[128]{0:T(128)}, u32[]{:S(2)}) copy-start(f32[128]{0:T(128)} %param.18) | copy-start | bytes 1540
  134.4 4.3 %copy-start.20 = (f32[64]{0:T(128)S(1)}, f32[64]{0:T(128)}, u32[]{:S(2)}) copy-start(f32[64]{0:T(128)} %param.15) | copy-start | bytes 772
  138.7 15.1 %copy-start.8 = (bf16[1024,1024]{1,0:T(8,128)(2,1)S(1)}, bf16[1024,1024]{1,0:T(8,128)(2,1)}, u32[]{:S(2)}) copy-start(bf16[1024,1024]{1,0:T(8,128)(2,1)} %get-tuple-element.14) | copy-start | bytes 6291460
  156.6 20.7 %copy-start.12 = (bf16[1024,1024]{1,0:T(8,128)(2,1)S(1)}, bf16[1024,1024]{1,0:T(8,128)(2,1)}, u32[]{:S(2)}) copy-start(bf16[1024,1024]{1,0:T(8,128)(2,1)} %get-tuple-element.13) | copy-start | bytes 6291460
  156.6 21.1 %copy-start.2 = (bf16[1024,1024]{1,0:T(8,128)(2,1)S(1)}, bf16[1024,1024]{1,0:T(8,128)(2,1)}, u32[]{:S(2)}) copy-start(bf16[1024,1024]{1,0:T(8,128)(2,1)} %get-tuple-element.12) | copy-start | bytes 6291460
  181.5 2.7 %copy-start.13 = (f32[16,8,1024]{2,1,0:T(8,128)S(1)}, f32[16,8,1024]{2,1,0:T(8,128)}, u32[]{:S(2)}) copy-start(f32[16,8,1024]{2,1,0:T(8,128)} %shard_map.124) | copy-start | bytes 1572868
  210.4 11.0 %collective-permute-start.6 = (f32[16,64]{1,0:T(8,128)S(1)}, f32[16,64]{1,0:T(8,128)S(1)}, u32[]{:S(2)}, u32[]{:S(2)}) collective-permute-start(f32[16,64]{1,0:T(8,128)S(1)} %get-tuple-element.52), channel_id=1, source_target_pairs={{0,16},{16,32},{32,48},{48,64},{64,80},{80,96},{96,112},{1,17},{17... | collective-permute-start | bytes 12296 | tf_op jit(solution)/shard_map/ppermute | solution.py:203
  212.9 8.5 %collective-permute-start.7 = (f32[16,64]{1,0:T(8,128)S(1)}, f32[16,64]{1,0:T(8,128)S(1)}, u32[]{:S(2)}, u32[]{:S(2)}) collective-permute-start(f32[16,64]{1,0:T(8,128)S(1)} %get-tuple-element.53), channel_id=1, source_target_pairs={{16,0},{32,16},{48,32},{64,48},{80,64},{96,80},{112,96},{17,1},{33... | collective-permute-start | bytes 12296 | tf_op jit(solution)/shard_map/ppermute | solution.py:204
  236.5 2.8 %copy-start.16 = (f32[16,67,128]{2,1,0:T(8,128)}, f32[16,67,128]{2,1,0:T(8,128)S(1)}, u32[]{:S(2)}) copy-start(f32[16,67,128]{2,1,0:T(8,128)S(1)} %all_to_all.57.framed_ref) | copy-start | bytes 1646596
  (9 other events, 19.0 us)

commit v9 on v7

--- a/solution.py
+++ b/solution.py
@@ -171,13 +171,6 @@
     blocks_y = lax.axis_size("gx")
     basis_x = split_bf16(vectors_x)
     rows = right_side.shape[1]
-    framed_basis = []
-    for piece in basis_x:
-        blocks = piece.reshape(-1, rows, piece.shape[1])
-        zero = jnp.zeros_like(blocks[:1, :1])
-        below = jnp.concatenate([zero, blocks[:-1, -1:]], axis=0)
-        above = jnp.concatenate([blocks[1:, :1], zero], axis=0)
-        framed_basis.append(jnp.concatenate([below, blocks, above], axis=1))
     count_y = lax.axis_size("gx")
     forward_y = [(i, i + 1) for i in range(count_y - 1)]
     backward_y = [(target, source) for source, target in forward_y]
@@ -198,11 +191,15 @@
         chunks = chunks.reshape(-1, local_modes, chunks.shape[3])
         chunks = lax.all_to_all(chunks, everyone, split_axis=0, concat_axis=0, tiled=True)
         solved = chunks.reshape(-1, chunks.shape[2])
-        framed = transform("iy,bri->bry", solved, framed_basis)
-        from_left = lax.ppermute(framed[:, 1:-1, -1], "gx", forward_y)
-        from_right = lax.ppermute(framed[:, 1:-1, 0], "gx", backward_y)
+        plane = transform("iy,xi->xy", solved, basis_x)
+        blocks = plane.reshape(-1, rows, plane.shape[1])
+        from_left = lax.ppermute(blocks[:, :, -1], "gx", forward_y)
+        from_right = lax.ppermute(blocks[:, :, 0], "gx", backward_y)
+        zero = jnp.zeros_like(blocks[:1, :1])
+        below = jnp.concatenate([zero, blocks[:-1, -1:]], axis=0)
+        above = jnp.concatenate([blocks[1:, :1], zero], axis=0)
         halo_row = jnp.concatenate([from_left, from_right], axis=1)[:, None, :]
-        framed = jnp.concatenate([framed, halo_row], axis=1)
+        framed = jnp.concatenate([below, blocks, above, halo_row], axis=1)
         framed = lax.all_to_all(framed, "gy", split_axis=0, concat_axis=0, tiled=True)
         y_strips = (active_y[0] * framed[:, -1, :rows], active_y[1] * framed[:, -1, rows:])
         residual, adjoint = framed_stencil(framed, active, residual, adjoint, active_x, y_strips, faces)

time: 242 us -> 235 us (0.971); the launches traced: 239 us -> 234 us
  other arithmetic: 26.2 us -> 21 us
  waiting for transfers between devices: 25.5 us -> 29.5 us
  local copies, waits for them, and re-layouts: 24.9 us -> 21.3 us
    convert_element_type x1 -> x2, other arithmetic: 4.48 us -> 8.92 us  [split_bf16(): rounded.astype(jnp.bfloat16)]
    convert_element_type x5 -> x4, other arithmetic: 4.75 us -> 0.34 us  [split_bf16(): (values - rounded).astype(jnp.bfloat16)]
    concatenate x3 -> x2, other arithmetic: 4.74 us -> 0.96 us  [shards(): framed = jnp.concatenate([below, blocks, above, halo_row], axis=1)]
    ppermute x4, waiting for transfers between devices: 2.98 us -> 6.49 us  [the longest x2 6.48 us: shards(): from_left = lax.ppermute(blocks[:, :, -1], 'gx', forward_y)]
    unnamed x42 -> x36, local copies, waits for them, and re-layouts: 4.86 us -> 4.08 us
  transfers between devices with their start and end apart: 12 -> 12, of which waited for: 5 -> 5; matrix products, arithmetic and copies ran while one was open for 21% -> 20% of each run, Pallas kernels for 1% -> 1%
where the time goes in v9:
time: 235 us; the launch traced here: 234 us
  blocking collectives  65.6 us (28%)
  starting transfers between devices  56.1 us (24%)
  waiting for transfers between devices  29.5 us (13%)
  matrix products  26.9 us (11%)
  local copies, waits for them, and re-layouts  21.3 us (9%)
  other arithmetic  21 us (9%)
  Pallas kernels  12.6 us (5%)
    all_to_all x2, blocking collectives, shards(): lax.all_to_all(chunks, everyone, split_axis=0, concat_axis=0, tiled=True)  35.4 us
    dot_general x24, matrix products, product(): return jnp.einsum(spec, first, second, preferred_element_type=jnp.float32)  26.9 us
    all_to_all x2, waiting for transfers between devices, shards(): lax.all_to_all(chunks, everyone, split_axis=0, concat_axis=0, tiled=True)  18.1 us
    all_to_all x2, starting transfers between devices, shards(): lax.all_to_all(chunks, everyone, split_axis=0, concat_axis=0, tiled=True)  17.1 us
    all_to_all x1, blocking collectives, shards(): lax.all_to_all(framed, 'gy', split_axis=0, concat_axis=0, tiled=True)  16.5 us
    all_to_all x1, blocking collectives, shards(): lax.all_to_all(scaled, 'gy', split_axis=0, concat_axis=1, tiled=True)  13.7 us
    convert_element_type x2, other arithmetic, split_bf16(): rounded.astype(jnp.bfloat16)  8.92 us
    pallas_call x2, Pallas kernels, framed_stencil(): pl.pallas_call(framed_kernel, out_shape=(shape, shape), in_specs=[vmem] *...  8.51 us
  transfers between devices with their start and end apart: 12, of which 5 were waited for; matrix products, arithmetic and copies ran while one was open for 20% of the time, Pallas kernels for 1%

profile of v9, /device:TPU:3, one launch (start us, length us, event | category | flops | bytes accessed | tf_op | source)
XLA Modules:
  0.0 234.3 jit_solution(13496554708293501692)
XLA Ops:
  2.7 6.5 %all-to-all-start = ((f32[16,64,128]{2,1,0:T(8,128)}), f32[16,64,128]{2,1,0:T(8,128)S(1)}, u32[]{:S(2)}, u32[]{:S(2)}) async-start(f32[16,64,128]{2,1,0:T(8,128)} %multiply_multiply_fusion.1), calls=%async_computation | async-start | bytes 1048576 | tf_op jit(solution)/shard_map/all_to_all | solution.py:182
  10.2 3.5 %collective-permute-start.2 = (f32[2,16,128]{2,1,0:T(8,128)S(1)}, f32[2,16,128]{2,1,0:T(8,128)S(1)}, u32[]{:S(2)}, u32[]{:S(2)}) collective-permute-start(f32[2,16,128]{2,1,0:T(8,128)S(1)} %bitcast.247), channel_id=1, source_target_pairs={{0,1},{1,2},{2,3},{3,4},{4,5},{5,6},{6,7},{7,8},{8,9},{9,10},{10,1... | collective-permute-start | bytes 49160 | tf_op jit(solution)/shard_map/ppermute | solution.py:20
  16.6 5.2 %collective-permute-start.5 = (f32[2,16,64]{2,1,0:T(8,128)S(1)}, f32[2,16,64]{2,1,0:T(8,128)S(1)}, u32[]{:S(2)}, u32[]{:S(2)}) collective-permute-start(f32[2,16,64]{2,1,0:T(8,128)S(1)} %get-tuple-element.10), channel_id=1, source_target_pairs={{16,0},{32,16},{48,32},{64,48},{80,64},{96,80},{112,96},{17,1},{33... | collective-permute-start | bytes 24584 | tf_op jit(solution)/shard_map/ppermute | solution.py:20
  27.8 4.4 %reduce-precision_convert_fusion.1 = (bf16[1024,1024]{1,0:T(8,128)(2,1)S(1)}, bf16[1024,1024]{1,0:T(8,128)(2,1)}) fusion(f32[1024,1024]{1,0:T(8,128)} %param.14), kind=kLoop, calls=%fused_computation.3 | loop fusion | flops 4194304 | bytes 8388608 | tf_op jit(solution)/shard_map/convert_element_type | solution.py:134
  37.1 12.2 %all-to-all-start.1 = ((f32[128,8,128]{2,1,0:T(8,128)}), f32[128,8,128]{2,1,0:T(8,128)S(1)}, u32[]{:S(2)}, u32[]{:S(2)}) async-start(f32[128,8,128]{2,1,0:T(8,128)} %bitcast.3), calls=%async_computation.1 | async-start | bytes 1048576 | tf_op jit(solution)/shard_map/all_to_all | solution.py:186
  49.9 4.5 %reduce-precision_convert_fusion = (bf16[1024,1024]{1,0:T(8,128)(2,1)S(1)}, bf16[1024,1024]{1,0:T(8,128)(2,1)}) fusion(f32[1024,1024]{1,0:T(8,128)} %param.17), kind=kLoop, calls=%fused_computation.1 | loop fusion | flops 4194304 | bytes 8388608 | tf_op jit(solution)/shard_map/convert_element_type | solution.py:134
  54.4 7.8 %all-to-all-done.1 = f32[128,8,128]{2,1,0:T(8,128)S(1)} async-done(((f32[128,8,128]{2,1,0:T(8,128)}), f32[128,8,128]{2,1,0:T(8,128)S(1)}, u32[]{:S(2)}, u32[]{:S(2)}) %all-to-all-start.1) | async-done | bytes 524320 | tf_op jit(solution)/shard_map/all_to_all | solution.py:186
  73.2 4.9 %all-to-all-start.2 = ((f32[128,8,128]{2,1,0:T(8,128)}), f32[128,8,128]{2,1,0:T(8,128)S(1)}, u32[]{:S(2)}, u32[]{:S(2)}) async-start(f32[128,8,128]{2,1,0:T(8,128)} %bitcast.233), calls=%async_computation.2 | async-start | bytes 1048576 | tf_op jit(solution)/shard_map/all_to_all | solution.py:192
  80.8 10.3 %all-to-all-done.2 = f32[128,8,128]{2,1,0:T(8,128)S(1)} async-done(((f32[128,8,128]{2,1,0:T(8,128)}), f32[128,8,128]{2,1,0:T(8,128)S(1)}, u32[]{:S(2)}, u32[]{:S(2)}) %all-to-all-start.2) | async-done | bytes 524320 | tf_op jit(solution)/shard_map/all_to_all | solution.py:192
  101.1 3.3 %collective-permute-start.1 = (f32[16,64]{1,0:T(8,128)S(1)}, f32[16,64]{1,0:T(8,128)S(1)}, u32[]{:S(2)}, u32[]{:S(2)}) collective-permute-start(f32[16,64]{1,0:T(8,128)S(1)} %bitcast.250), channel_id=1, source_target_pairs={{16,0},{32,16},{48,32},{64,48},{80,64},{96,80},{112,96},{17,1},{33... | collective-permute-start | bytes 12296 | tf_op jit(solution)/shard_map/ppermute | solution.py:197
  104.4 3.5 %collective-permute-start = (f32[16,64]{1,0:T(8,128)S(1)}, f32[16,64]{1,0:T(8,128)S(1)}, u32[]{:S(2)}, u32[]{:S(2)}) collective-permute-start(f32[16,64]{1,0:T(8,128)S(1)} %bitcast.248), channel_id=1, source_target_pairs={{0,16},{16,32},{32,48},{48,64},{64,80},{80,96},{96,112},{1,17},{17... | collective-permute-start | bytes 12296 | tf_op jit(solution)/shard_map/ppermute | solution.py:196
  107.9 3.2 %collective-permute-done = f32[16,64]{1,0:T(8,128)S(1)} collective-permute-done((f32[16,64]{1,0:T(8,128)S(1)}, f32[16,64]{1,0:T(8,128)S(1)}, u32[]{:S(2)}, u32[]{:S(2)}) %collective-permute-start) | collective-permute-done | bytes 4128 | tf_op jit(solution)/shard_map/ppermute | solution.py:196
  112.2 6.3 %all-to-all-start.3 = ((f32[16,67,128]{2,1,0:T(8,128)}), f32[16,67,128]{2,1,0:T(8,128)S(1)}, u32[]{:S(2)}, u32[]{:S(2)}) async-start(f32[16,67,128]{2,1,0:T(8,128)} %fusion.23), calls=%async_computation.3 | async-start | bytes 1179648 | tf_op jit(solution)/shard_map/all_to_all | solution.py:203
  119.1 4.7 %add_divide_fusion = (f32[16,64,128]{2,1,0:T(8,128)}, f32[16,64,128]{2,1,0:T(8,128)}, f32[16,64,128]{2,1,0:T(8,128)}, f32[16,64,128]{2,1,0:T(8,128)}, f32[16,64,128]{2,1,0:T(8,128)}, /*index=5*/f32[16,64,128]{2,1,0:T(8,128)}) fusion(f32[16,64,128]{2,1,0:T(8,128)S(1)} %copy-done.6, f32[16,64,127]{2,1,0:T(8,128)} %get-tuple-element.36, ...), kind=kLoop, calls=%fused_computation.85 | loop fusion | flops 3014656 | bytes 6750208 | tf_op jit(solution)/shard_map/div | solution.py:28
  123.7 4.9 %all-to-all-done.3.framed_ref = f32[16,67,128]{2,1,0:T(8,128)S(1)} async-done(((f32[16,67,128]{2,1,0:T(8,128)}), f32[16,67,128]{2,1,0:T(8,128)S(1)}, u32[]{:S(2)}, u32[]{:S(2)}) %all-to-all-start.3) | async-done | bytes 548896 | tf_op jit(solution)/shard_map/all_to_all | solution.py:203
  131.7 4.3 %shard_map.123 = (f32[16,64,128]{2,1,0:T(8,128)}, f32[16,64,128]{2,1,0:T(8,128)}) custom-call(f32[16,67,128]{2,1,0:T(8,128)} %copy-done.10, f32[16,64,128]{2,1,0:T(8,128)} %get-tuple-element.43.active_ref, f32[16,64,128]{2,1,0:T(8,128)} %residual_ref.1, f32[16,64,128]{2,1,0:T(8,128)} %broadcast_in_dim.15.adjoint_ref, f32[16,128]{1,0:T(8,128)} %get-tuple-element.53.x_low_ref, ...), custom_call_target="tpu_custom_call" | custom-call | tf_op jit(solution)/shard_map/pallas_call | solution.py:91
  137.3 13.7 %all_to_all.54 = f32[16,64,128]{2,1,0:T(8,128)S(1)} all-to-all(f32[16,64,128]{2,1,0:T(8,128)S(1)} %multiply_multiply_fusion), channel_id=1, replica_groups=mesh['gx'=8,'gy'=16] {'gy'}, dimensions={0} | all-to-all | bytes 1048576 | tf_op jit(solution)/shard_map/all_to_all | solution.py:182
  153.8 17.9 %all_to_all.55 = f32[128,8,128]{2,1,0:T(8,128)S(1)} all-to-all(f32[128,8,128]{2,1,0:T(8,128)S(1)} %bitcast.234), channel_id=1, replica_groups=mesh['gx'=8,'gy'=16] {'gx','gy'}, dimensions={0} | all-to-all | bytes 1048576 | tf_op jit(solution)/shard_map/all_to_all | solution.py:186
  180.2 17.5 %all_to_all.56 = f32[128,8,128]{2,1,0:T(8,128)S(1)} all-to-all(f32[128,8,128]{2,1,0:T(8,128)S(1)} %bitcast.235), channel_id=1, replica_groups=mesh['gx'=8,'gy'=16] {'gx','gy'}, dimensions={0} | all-to-all | bytes 1048576 | tf_op jit(solution)/shard_map/all_to_all | solution.py:192
  201.1 3.3 %collective-permute-start.7 = (f32[16,64]{1,0:T(8,128)S(1)}, f32[16,64]{1,0:T(8,128)S(1)}, u32[]{:S(2)}, u32[]{:S(2)}) collective-permute-start(f32[16,64]{1,0:T(8,128)S(1)} %bitcast.251), channel_id=1, source_target_pairs={{16,0},{32,16},{48,32},{64,48},{80,64},{96,80},{112,96},{17,1},{33... | collective-permute-start | bytes 12296 | tf_op jit(solution)/shard_map/ppermute | solution.py:197
  204.4 3.5 %collective-permute-start.6 = (f32[16,64]{1,0:T(8,128)S(1)}, f32[16,64]{1,0:T(8,128)S(1)}, u32[]{:S(2)}, u32[]{:S(2)}) collective-permute-start(f32[16,64]{1,0:T(8,128)S(1)} %bitcast.249), channel_id=1, source_target_pairs={{0,16},{16,32},{32,48},{48,64},{64,80},{80,96},{96,112},{1,17},{17... | collective-permute-start | bytes 12296 | tf_op jit(solution)/shard_map/ppermute | solution.py:196
  208.0 3.2 %collective-permute-done.6 = f32[16,64]{1,0:T(8,128)S(1)} collective-permute-done((f32[16,64]{1,0:T(8,128)S(1)}, f32[16,64]{1,0:T(8,128)S(1)}, u32[]{:S(2)}, u32[]{:S(2)}) %collective-permute-start.6) | collective-permute-done | bytes 4128 | tf_op jit(solution)/shard_map/ppermute | solution.py:196
  211.4 16.5 %all_to_all.57.framed_ref = f32[16,67,128]{2,1,0:T(8,128)S(1)} all-to-all(f32[16,67,128]{2,1,0:T(8,128)S(1)} %fusion.19), channel_id=1, replica_groups=mesh['gx'=8,'gy'=16] {'gy'}, dimensions={0} | all-to-all | bytes 1097728 | tf_op jit(solution)/shard_map/all_to_all | solution.py:203
  230.0 4.2 %shard_map.125 = (f32[16,64,128]{2,1,0:T(8,128)}, f32[16,64,128]{2,1,0:T(8,128)}) custom-call(f32[16,67,128]{2,1,0:T(8,128)} %copy-done.11, f32[16,64,128]{2,1,0:T(8,128)} %get-tuple-element.43.active_ref, f32[16,64,128]{2,1,0:T(8,128)} %get-tuple-element.6.residual_ref, f32[16,64,128]{2,1,0:T(8,128)} %get-tuple-element.7.adjoint_ref, ...), custom_call_target="tpu_custom_call" | custom-call | tf_op jit(solution)/shard_map/pallas_call | solution.py:91
  (116 shorter events, 63.6 us)
Async XLA Ops:
  0.6 8.6 %copy-start.12 = (s32[16,64,128]{2,1,0:T(8,128)S(1)}, s32[16,64,128]{2,1,0:T(8,128)}, u32[]{:S(2)}) copy-start(s32[16,64,128]{2,1,0:T(8,128)} %param.13) | copy-start | bytes 1572868
  0.6 9.5 %copy-start.6 = (f32[16,64,128]{2,1,0:T(8,128)S(1)}, f32[16,64,128]{2,1,0:T(8,128)}, u32[]{:S(2)}) copy-start(f32[16,64,128]{2,1,0:T(8,128)} %param.12) | copy-start | bytes 1572868
  2.7 29.5 %all-to-all-start = ((f32[16,64,128]{2,1,0:T(8,128)}), f32[16,64,128]{2,1,0:T(8,128)S(1)}, u32[]{:S(2)}, u32[]{:S(2)}) async-start(f32[16,64,128]{2,1,0:T(8,128)} %multiply_multiply_fusion.1), calls=%async_computation | async-start | bytes 1048576 | tf_op jit(solution)/shard_map/all_to_all | solution.py:182
  10.2 70.0 %collective-permute-start.2 = (f32[2,16,128]{2,1,0:T(8,128)S(1)}, f32[2,16,128]{2,1,0:T(8,128)S(1)}, u32[]{:S(2)}, u32[]{:S(2)}) collective-permute-start(f32[2,16,128]{2,1,0:T(8,128)S(1)} %bitcast.247), channel_id=1, source_target_pairs={{0,1},{1,2},{2,3},{3,4},{4,5},{5,6},{6,7},{7,8},{8,9},{9,10},{10,1... | collective-permute-start | bytes 49160 | tf_op jit(solution)/shard_map/ppermute | solution.py:20
  13.8 104.7 %collective-permute-start.3 = (f32[2,16,128]{2,1,0:T(8,128)S(1)}, f32[2,16,128]{2,1,0:T(8,128)S(1)}, u32[]{:S(2)}, u32[]{:S(2)}) collective-permute-start(f32[2,16,128]{2,1,0:T(8,128)S(1)} %bitcast.246), channel_id=1, source_target_pairs={{1,0},{2,1},{3,2},{4,3},{5,4},{6,5},{7,6},{8,7},{9,8},{10,9},{11,1... | collective-permute-start | bytes 49160 | tf_op jit(solution)/shard_map/ppermute | solution.py:20
  16.6 61.5 %collective-permute-start.5 = (f32[2,16,64]{2,1,0:T(8,128)S(1)}, f32[2,16,64]{2,1,0:T(8,128)S(1)}, u32[]{:S(2)}, u32[]{:S(2)}) collective-permute-start(f32[2,16,64]{2,1,0:T(8,128)S(1)} %get-tuple-element.10), channel_id=1, source_target_pairs={{16,0},{32,16},{48,32},{64,48},{80,64},{96,80},{112,96},{17,1},{33... | collective-permute-start | bytes 24584 | tf_op jit(solution)/shard_map/ppermute | solution.py:20
  21.8 56.4 %collective-permute-start.4 = (f32[2,16,64]{2,1,0:T(8,128)S(1)}, f32[2,16,64]{2,1,0:T(8,128)S(1)}, u32[]{:S(2)}, u32[]{:S(2)}) collective-permute-start(f32[2,16,64]{2,1,0:T(8,128)S(1)} %get-tuple-element.11), channel_id=1, source_target_pairs={{0,16},{16,32},{32,48},{48,64},{64,80},{80,96},{96,112},{1,17},{17... | collective-permute-start | bytes 24584 | tf_op jit(solution)/shard_map/ppermute | solution.py:20
  32.2 3.3 %copy-start = (bf16[1024,1024]{1,0:T(8,128)(2,1)}, bf16[1024,1024]{1,0:T(8,128)(2,1)S(1)}, u32[]{:S(2)}) copy-start(bf16[1024,1024]{1,0:T(8,128)(2,1)S(1)} %get-tuple-element.14) | copy-start | bytes 6291460
  35.6 13.7 %copy-start.13 = (f32[1024]{0:T(1024)S(1)}, f32[1024]{0:T(1024)}, u32[]{:S(2)}) copy-start(f32[1024]{0:T(1024)} %param.19) | copy-start | bytes 12292
  37.1 25.1 %all-to-all-start.1 = ((f32[128,8,128]{2,1,0:T(8,128)}), f32[128,8,128]{2,1,0:T(8,128)S(1)}, u32[]{:S(2)}, u32[]{:S(2)}) async-start(f32[128,8,128]{2,1,0:T(8,128)} %bitcast.3), calls=%async_computation.1 | async-start | bytes 1048576 | tf_op jit(solution)/shard_map/all_to_all | solution.py:186
  73.2 18.0 %all-to-all-start.2 = ((f32[128,8,128]{2,1,0:T(8,128)}), f32[128,8,128]{2,1,0:T(8,128)S(1)}, u32[]{:S(2)}, u32[]{:S(2)}) async-start(f32[128,8,128]{2,1,0:T(8,128)} %bitcast.233), calls=%async_computation.2 | async-start | bytes 1048576 | tf_op jit(solution)/shard_map/all_to_all | solution.py:192
  91.2 2.6 %copy-start.1 = (bf16[1024,1024]{1,0:T(8,128)(2,1)S(1)}, bf16[1024,1024]{1,0:T(8,128)(2,1)}, u32[]{:S(2)}) copy-start(bf16[1024,1024]{1,0:T(8,128)(2,1)} %copy-done) | copy-start | bytes 6291460
  101.1 6.8 %collective-permute-start.1 = (f32[16,64]{1,0:T(8,128)S(1)}, f32[16,64]{1,0:T(8,128)S(1)}, u32[]{:S(2)}, u32[]{:S(2)}) collective-permute-start(f32[16,64]{1,0:T(8,128)S(1)} %bitcast.250), channel_id=1, source_target_pairs={{16,0},{32,16},{48,32},{64,48},{80,64},{96,80},{112,96},{17,1},{33... | collective-permute-start | bytes 12296 | tf_op jit(solution)/shard_map/ppermute | solution.py:197
  104.4 6.8 %collective-permute-start = (f32[16,64]{1,0:T(8,128)S(1)}, f32[16,64]{1,0:T(8,128)S(1)}, u32[]{:S(2)}, u32[]{:S(2)}) collective-permute-start(f32[16,64]{1,0:T(8,128)S(1)} %bitcast.248), channel_id=1, source_target_pairs={{0,16},{16,32},{32,48},{48,64},{64,80},{80,96},{96,112},{1,17},{17... | collective-permute-start | bytes 12296 | tf_op jit(solution)/shard_map/ppermute | solution.py:196
  112.2 16.5 %all-to-all-start.3 = ((f32[16,67,128]{2,1,0:T(8,128)}), f32[16,67,128]{2,1,0:T(8,128)S(1)}, u32[]{:S(2)}, u32[]{:S(2)}) async-start(f32[16,67,128]{2,1,0:T(8,128)} %fusion.23), calls=%async_computation.3 | async-start | bytes 1179648 | tf_op jit(solution)/shard_map/all_to_all | solution.py:203
  128.7 3.0 %copy-start.10 = (f32[16,67,128]{2,1,0:T(8,128)}, f32[16,67,128]{2,1,0:T(8,128)S(1)}, u32[]{:S(2)}) copy-start(f32[16,67,128]{2,1,0:T(8,128)S(1)} %all-to-all-done.3.framed_ref) | copy-start | bytes 1646596
  131.6 4.3 %copy-start.14 = (f32[128]{0:T(128)S(1)}, f32[128]{0:T(128)}, u32[]{:S(2)}) copy-start(f32[128]{0:T(128)} %param.18) | copy-start | bytes 1540
  131.7 4.3 %copy-start.15 = (f32[64]{0:T(128)S(1)}, f32[64]{0:T(128)}, u32[]{:S(2)}) copy-start(f32[64]{0:T(128)} %param.15) | copy-start | bytes 772
  135.9 15.1 %copy-start.4 = (bf16[1024,1024]{1,0:T(8,128)(2,1)S(1)}, bf16[1024,1024]{1,0:T(8,128)(2,1)}, u32[]{:S(2)}) copy-start(bf16[1024,1024]{1,0:T(8,128)(2,1)} %get-tuple-element.15) | copy-start | bytes 6291460
  153.7 18.0 %copy-start.7 = (bf16[1024,1024]{1,0:T(8,128)(2,1)S(1)}, bf16[1024,1024]{1,0:T(8,128)(2,1)}, u32[]{:S(2)}) copy-start(bf16[1024,1024]{1,0:T(8,128)(2,1)} %get-tuple-element.13) | copy-start | bytes 6291460
  179.3 18.4 %copy-start.5 = (bf16[1024,1024]{1,0:T(8,128)(2,1)S(1)}, bf16[1024,1024]{1,0:T(8,128)(2,1)}, u32[]{:S(2)}) copy-start(bf16[1024,1024]{1,0:T(8,128)(2,1)} %get-tuple-element.15) | copy-start | bytes 6291460
  180.2 18.4 %copy-start.3 = (bf16[1024,1024]{1,0:T(8,128)(2,1)S(1)}, bf16[1024,1024]{1,0:T(8,128)(2,1)}, u32[]{:S(2)}) copy-start(bf16[1024,1024]{1,0:T(8,128)(2,1)} %copy-done) | copy-start | bytes 6291460
  201.1 6.8 %collective-permute-start.7 = (f32[16,64]{1,0:T(8,128)S(1)}, f32[16,64]{1,0:T(8,128)S(1)}, u32[]{:S(2)}, u32[]{:S(2)}) collective-permute-start(f32[16,64]{1,0:T(8,128)S(1)} %bitcast.251), channel_id=1, source_target_pairs={{16,0},{32,16},{48,32},{64,48},{80,64},{96,80},{112,96},{17,1},{33... | collective-permute-start | bytes 12296 | tf_op jit(solution)/shard_map/ppermute | solution.py:197
  204.4 6.8 %collective-permute-start.6 = (f32[16,64]{1,0:T(8,128)S(1)}, f32[16,64]{1,0:T(8,128)S(1)}, u32[]{:S(2)}, u32[]{:S(2)}) collective-permute-start(f32[16,64]{1,0:T(8,128)S(1)} %bitcast.249), channel_id=1, source_target_pairs={{0,16},{16,32},{32,48},{48,64},{64,80},{80,96},{96,112},{1,17},{17... | collective-permute-start | bytes 12296 | tf_op jit(solution)/shard_map/ppermute | solution.py:196
  (4 other events, 8.8 us)

commit v10 on v9

--- a/solution.py
+++ b/solution.py
@@ -45,10 +45,13 @@
     return [harmonic(center, other) for other in neighbours(center, strips)]
 
 
-def framed_kernel(
-    framed_ref, active_ref, residual_ref, adjoint_ref, x_low_ref, x_high_ref, y_low_ref, y_high_ref, *refs
-):
-    face_refs, residual_out, adjoint_out = refs[:-2], refs[-2], refs[-1]
+def framed_kernel(framed_ref, active_ref, residual_ref, *refs):
+    if len(refs) == 12:
+        adjoint_ref = None
+    else:
+        adjoint_ref, refs = refs[0], refs[1:]
+    x_low_ref, x_high_ref, y_low_ref, y_high_ref = refs[:4]
+    face_refs, residual_out, adjoint_out = refs[4:-2], refs[-2], refs[-1]
     planes, rows, cols = active_ref.shape
     row = lax.broadcasted_iota(jnp.int32, (rows, cols), 0)
     col = lax.broadcasted_iota(jnp.int32, (rows, cols), 1)
@@ -81,19 +84,21 @@
             result = result + face_ref[z] * (center - other)
         update = updates[z]
         residual_out[z] = residual_ref[z] - (result + (1.0 - active_ref[z]) * update)
-        adjoint_out[z] = adjoint_ref[z] + update
+        adjoint_out[z] = update if adjoint_ref is None else adjoint_ref[z] + update
 
 
 def framed_stencil(framed, active, residual, adjoint, x_strips, y_strips, faces):
     vmem = pl.BlockSpec(memory_space=pltpu.VMEM)
     shape = jax.ShapeDtypeStruct(active.shape, active.dtype)
     y_low, y_high = (jnp.broadcast_to(strip[:, :, None], active.shape) for strip in y_strips)
+    carried = [] if adjoint is None else [adjoint]
+    operands = [framed, active, residual, *carried, x_strips[0], x_strips[1], y_low, y_high, *faces]
     return pl.pallas_call(
         framed_kernel,
         out_shape=(shape, shape),
-        in_specs=[vmem] * (8 + len(faces)),
+        in_specs=[vmem] * len(operands),
         out_specs=(vmem, vmem),
-    )(framed, active, residual, adjoint, x_strips[0], x_strips[1], y_low, y_high, *faces)
+    )(*operands)
 
 
 def solve_kernel(diag_ref, coup_ref, shifts_ref, rhs_ref, out_ref, ratio_ref):
@@ -165,7 +170,7 @@
     mode_start = (lax.axis_index("gx") * lax.axis_size("gy") + lax.axis_index("gy")) * local_modes
     local_values = lax.dynamic_slice_in_dim(values_x, mode_start, local_modes, 0)
     shifts = local_values[:, None] + values_y[None, :]
-    adjoint = jnp.zeros_like(right_side)
+    adjoint = None
     residual = right_side
     everyone = ("gx", "gy")
     blocks_y = lax.axis_size("gx")

time: 235 us -> 234 us (level)
  transfers between devices with their start and end apart: 12 -> 12, of which waited for: 5 -> 5; matrix products, arithmetic and copies ran while one was open for 20% -> 21% of each run, Pallas kernels for 1% -> 1%
where the time goes in v10:
time: 234 us; the launch traced here: 233 us
  blocking collectives  65.6 us (28%)
  starting transfers between devices  56.1 us (24%)
  waiting for transfers between devices  29.5 us (13%)
  matrix products  26.9 us (11%)
  other arithmetic  21 us (9%)
  local copies, waits for them, and re-layouts  20.4 us (9%)
  Pallas kernels  12.5 us (5%)
    all_to_all x2, blocking collectives, shards(): lax.all_to_all(chunks, everyone, split_axis=0, concat_axis=0, tiled=True)  35.4 us
    dot_general x24, matrix products, product(): return jnp.einsum(spec, first, second, preferred_element_type=jnp.float32)  26.9 us
    all_to_all x2, waiting for transfers between devices, shards(): lax.all_to_all(chunks, everyone, split_axis=0, concat_axis=0, tiled=True)  18.1 us
    all_to_all x2, starting transfers between devices, shards(): lax.all_to_all(chunks, everyone, split_axis=0, concat_axis=0, tiled=True)  17.1 us
    all_to_all x1, blocking collectives, shards(): lax.all_to_all(framed, 'gy', split_axis=0, concat_axis=0, tiled=True)  16.5 us
    all_to_all x1, blocking collectives, shards(): lax.all_to_all(scaled, 'gy', split_axis=0, concat_axis=1, tiled=True)  13.7 us
    convert_element_type x2, other arithmetic, split_bf16(): rounded.astype(jnp.bfloat16)  8.92 us
    pallas_call x2, Pallas kernels, framed_stencil(): pl.pallas_call(framed_kernel, out_shape=(shape, shape), in_specs=[vmem] *...  8.35 us
  transfers between devices with their start and end apart: 12, of which 5 were waited for; matrix products, arithmetic and copies ran while one was open for 21% of the time, Pallas kernels for 1%

profile of v10, /device:TPU:3, one launch (start us, length us, event | category | flops | bytes accessed | tf_op | source)
XLA Modules:
  0.0 233.2 jit_solution(10798504648790400017)
XLA Ops:
  2.7 6.5 %all-to-all-start = ((f32[16,64,128]{2,1,0:T(8,128)}), f32[16,64,128]{2,1,0:T(8,128)S(1)}, u32[]{:S(2)}, u32[]{:S(2)}) async-start(f32[16,64,128]{2,1,0:T(8,128)} %multiply_multiply_fusion.1), calls=%async_computation | async-start | bytes 1048576 | tf_op jit(solution)/shard_map/all_to_all | solution.py:187
  10.2 3.5 %collective-permute-start.2 = (f32[2,16,128]{2,1,0:T(8,128)S(1)}, f32[2,16,128]{2,1,0:T(8,128)S(1)}, u32[]{:S(2)}, u32[]{:S(2)}) collective-permute-start(f32[2,16,128]{2,1,0:T(8,128)S(1)} %bitcast.247), channel_id=1, source_target_pairs={{0,1},{1,2},{2,3},{3,4},{4,5},{5,6},{6,7},{7,8},{8,9},{9,10},{10,1... | collective-permute-start | bytes 49160 | tf_op jit(solution)/shard_map/ppermute | solution.py:20
  16.6 5.2 %collective-permute-start.5 = (f32[2,16,64]{2,1,0:T(8,128)S(1)}, f32[2,16,64]{2,1,0:T(8,128)S(1)}, u32[]{:S(2)}, u32[]{:S(2)}) collective-permute-start(f32[2,16,64]{2,1,0:T(8,128)S(1)} %get-tuple-element.10), channel_id=1, source_target_pairs={{16,0},{32,16},{48,32},{64,48},{80,64},{96,80},{112,96},{17,1},{33... | collective-permute-start | bytes 24584 | tf_op jit(solution)/shard_map/ppermute | solution.py:20
  27.8 4.4 %reduce-precision_convert_fusion.1 = (bf16[1024,1024]{1,0:T(8,128)(2,1)S(1)}, bf16[1024,1024]{1,0:T(8,128)(2,1)}) fusion(f32[1024,1024]{1,0:T(8,128)} %param.14), kind=kLoop, calls=%fused_computation.3 | loop fusion | flops 4194304 | bytes 8388608 | tf_op jit(solution)/shard_map/convert_element_type | solution.py:139
  37.1 12.2 %all-to-all-start.1 = ((f32[128,8,128]{2,1,0:T(8,128)}), f32[128,8,128]{2,1,0:T(8,128)S(1)}, u32[]{:S(2)}, u32[]{:S(2)}) async-start(f32[128,8,128]{2,1,0:T(8,128)} %bitcast.3), calls=%async_computation.1 | async-start | bytes 1048576 | tf_op jit(solution)/shard_map/all_to_all | solution.py:191
  49.9 4.5 %reduce-precision_convert_fusion = (bf16[1024,1024]{1,0:T(8,128)(2,1)S(1)}, bf16[1024,1024]{1,0:T(8,128)(2,1)}) fusion(f32[1024,1024]{1,0:T(8,128)} %param.17), kind=kLoop, calls=%fused_computation.1 | loop fusion | flops 4194304 | bytes 8388608 | tf_op jit(solution)/shard_map/convert_element_type | solution.py:139
  54.4 7.8 %all-to-all-done.1 = f32[128,8,128]{2,1,0:T(8,128)S(1)} async-done(((f32[128,8,128]{2,1,0:T(8,128)}), f32[128,8,128]{2,1,0:T(8,128)S(1)}, u32[]{:S(2)}, u32[]{:S(2)}) %all-to-all-start.1) | async-done | bytes 524320 | tf_op jit(solution)/shard_map/all_to_all | solution.py:191
  73.2 4.9 %all-to-all-start.2 = ((f32[128,8,128]{2,1,0:T(8,128)}), f32[128,8,128]{2,1,0:T(8,128)S(1)}, u32[]{:S(2)}, u32[]{:S(2)}) async-start(f32[128,8,128]{2,1,0:T(8,128)} %bitcast.233), calls=%async_computation.2 | async-start | bytes 1048576 | tf_op jit(solution)/shard_map/all_to_all | solution.py:197
  80.8 10.3 %all-to-all-done.2 = f32[128,8,128]{2,1,0:T(8,128)S(1)} async-done(((f32[128,8,128]{2,1,0:T(8,128)}), f32[128,8,128]{2,1,0:T(8,128)S(1)}, u32[]{:S(2)}, u32[]{:S(2)}) %all-to-all-start.2) | async-done | bytes 524320 | tf_op jit(solution)/shard_map/all_to_all | solution.py:197
  101.1 3.3 %collective-permute-start.1 = (f32[16,64]{1,0:T(8,128)S(1)}, f32[16,64]{1,0:T(8,128)S(1)}, u32[]{:S(2)}, u32[]{:S(2)}) collective-permute-start(f32[16,64]{1,0:T(8,128)S(1)} %bitcast.250), channel_id=1, source_target_pairs={{16,0},{32,16},{48,32},{64,48},{80,64},{96,80},{112,96},{17,1},{33... | collective-permute-start | bytes 12296 | tf_op jit(solution)/shard_map/ppermute | solution.py:202
  104.4 3.5 %collective-permute-start = (f32[16,64]{1,0:T(8,128)S(1)}, f32[16,64]{1,0:T(8,128)S(1)}, u32[]{:S(2)}, u32[]{:S(2)}) collective-permute-start(f32[16,64]{1,0:T(8,128)S(1)} %bitcast.248), channel_id=1, source_target_pairs={{0,16},{16,32},{32,48},{48,64},{64,80},{80,96},{96,112},{1,17},{17... | collective-permute-start | bytes 12296 | tf_op jit(solution)/shard_map/ppermute | solution.py:201
  107.9 3.2 %collective-permute-done = f32[16,64]{1,0:T(8,128)S(1)} collective-permute-done((f32[16,64]{1,0:T(8,128)S(1)}, f32[16,64]{1,0:T(8,128)S(1)}, u32[]{:S(2)}, u32[]{:S(2)}) %collective-permute-start) | collective-permute-done | bytes 4128 | tf_op jit(solution)/shard_map/ppermute | solution.py:201
  112.2 6.3 %all-to-all-start.3 = ((f32[16,67,128]{2,1,0:T(8,128)}), f32[16,67,128]{2,1,0:T(8,128)S(1)}, u32[]{:S(2)}, u32[]{:S(2)}) async-start(f32[16,67,128]{2,1,0:T(8,128)} %fusion.23), calls=%async_computation.3 | async-start | bytes 1179648 | tf_op jit(solution)/shard_map/all_to_all | solution.py:208
  119.1 4.7 %add_divide_fusion = (f32[16,64,128]{2,1,0:T(8,128)}, f32[16,64,128]{2,1,0:T(8,128)}, f32[16,64,128]{2,1,0:T(8,128)}, f32[16,64,128]{2,1,0:T(8,128)}, f32[16,64,128]{2,1,0:T(8,128)}, /*index=5*/f32[16,64,128]{2,1,0:T(8,128)}) fusion(f32[16,64,128]{2,1,0:T(8,128)S(1)} %copy-done.6, f32[16,64,127]{2,1,0:T(8,128)} %get-tuple-element.36, ...), kind=kLoop, calls=%fused_computation.85 | loop fusion | flops 3014656 | bytes 6750208 | tf_op jit(solution)/shard_map/div | solution.py:28
  123.7 4.9 %all-to-all-done.3.framed_ref = f32[16,67,128]{2,1,0:T(8,128)S(1)} async-done(((f32[16,67,128]{2,1,0:T(8,128)}), f32[16,67,128]{2,1,0:T(8,128)S(1)}, u32[]{:S(2)}, u32[]{:S(2)}) %all-to-all-start.3) | async-done | bytes 548896 | tf_op jit(solution)/shard_map/all_to_all | solution.py:208
  130.8 4.1 %shard_map.123 = (f32[16,64,128]{2,1,0:T(8,128)}, f32[16,64,128]{2,1,0:T(8,128)}) custom-call(f32[16,67,128]{2,1,0:T(8,128)} %copy-done.11, f32[16,64,128]{2,1,0:T(8,128)} %get-tuple-element.43.active_ref, f32[16,64,128]{2,1,0:T(8,128)} %residual_ref.1, f32[16,128]{1,0:T(8,128)} %get-tuple-element.53.refs_0_.refs_1_, ...), custom_call_target="tpu_custom_call" | custom-call | tf_op jit(solution)/shard_map/pallas_call | solution.py:96
  136.2 13.7 %all_to_all.54 = f32[16,64,128]{2,1,0:T(8,128)S(1)} all-to-all(f32[16,64,128]{2,1,0:T(8,128)S(1)} %multiply_multiply_fusion), channel_id=1, replica_groups=mesh['gx'=8,'gy'=16] {'gy'}, dimensions={0} | all-to-all | bytes 1048576 | tf_op jit(solution)/shard_map/all_to_all | solution.py:187
  152.7 17.9 %all_to_all.55 = f32[128,8,128]{2,1,0:T(8,128)S(1)} all-to-all(f32[128,8,128]{2,1,0:T(8,128)S(1)} %bitcast.234), channel_id=1, replica_groups=mesh['gx'=8,'gy'=16] {'gx','gy'}, dimensions={0} | all-to-all | bytes 1048576 | tf_op jit(solution)/shard_map/all_to_all | solution.py:191
  179.2 17.5 %all_to_all.56 = f32[128,8,128]{2,1,0:T(8,128)S(1)} all-to-all(f32[128,8,128]{2,1,0:T(8,128)S(1)} %bitcast.235), channel_id=1, replica_groups=mesh['gx'=8,'gy'=16] {'gx','gy'}, dimensions={0} | all-to-all | bytes 1048576 | tf_op jit(solution)/shard_map/all_to_all | solution.py:197
  200.1 3.3 %collective-permute-start.7 = (f32[16,64]{1,0:T(8,128)S(1)}, f32[16,64]{1,0:T(8,128)S(1)}, u32[]{:S(2)}, u32[]{:S(2)}) collective-permute-start(f32[16,64]{1,0:T(8,128)S(1)} %bitcast.251), channel_id=1, source_target_pairs={{16,0},{32,16},{48,32},{64,48},{80,64},{96,80},{112,96},{17,1},{33... | collective-permute-start | bytes 12296 | tf_op jit(solution)/shard_map/ppermute | solution.py:202
  203.4 3.5 %collective-permute-start.6 = (f32[16,64]{1,0:T(8,128)S(1)}, f32[16,64]{1,0:T(8,128)S(1)}, u32[]{:S(2)}, u32[]{:S(2)}) collective-permute-start(f32[16,64]{1,0:T(8,128)S(1)} %bitcast.249), channel_id=1, source_target_pairs={{0,16},{16,32},{32,48},{48,64},{64,80},{80,96},{96,112},{1,17},{17... | collective-permute-start | bytes 12296 | tf_op jit(solution)/shard_map/ppermute | solution.py:201
  206.9 3.2 %collective-permute-done.6 = f32[16,64]{1,0:T(8,128)S(1)} collective-permute-done((f32[16,64]{1,0:T(8,128)S(1)}, f32[16,64]{1,0:T(8,128)S(1)}, u32[]{:S(2)}, u32[]{:S(2)}) %collective-permute-start.6) | collective-permute-done | bytes 4128 | tf_op jit(solution)/shard_map/ppermute | solution.py:201
  210.3 16.5 %all_to_all.57.framed_ref = f32[16,67,128]{2,1,0:T(8,128)S(1)} all-to-all(f32[16,67,128]{2,1,0:T(8,128)S(1)} %fusion.19), channel_id=1, replica_groups=mesh['gx'=8,'gy'=16] {'gy'}, dimensions={0} | all-to-all | bytes 1097728 | tf_op jit(solution)/shard_map/all_to_all | solution.py:208
  229.0 4.2 %shard_map.125 = (f32[16,64,128]{2,1,0:T(8,128)}, f32[16,64,128]{2,1,0:T(8,128)}) custom-call(f32[16,67,128]{2,1,0:T(8,128)} %copy-done.10, f32[16,64,128]{2,1,0:T(8,128)} %get-tuple-element.43.active_ref, f32[16,64,128]{2,1,0:T(8,128)} %get-tuple-element.6.residual_ref, f32[16,64,128]{2,1,0:T(8,128)} %get-tuple-element.7.refs_0_, ...), custom_call_target="tpu_custom_call" | custom-call | tf_op jit(solution)/shard_map/pallas_call | solution.py:96
  (115 shorter events, 62.8 us)
Async XLA Ops:
  0.6 8.6 %copy-start.12 = (s32[16,64,128]{2,1,0:T(8,128)S(1)}, s32[16,64,128]{2,1,0:T(8,128)}, u32[]{:S(2)}) copy-start(s32[16,64,128]{2,1,0:T(8,128)} %param.13) | copy-start | bytes 1572868
  0.6 9.5 %copy-start.6 = (f32[16,64,128]{2,1,0:T(8,128)S(1)}, f32[16,64,128]{2,1,0:T(8,128)}, u32[]{:S(2)}) copy-start(f32[16,64,128]{2,1,0:T(8,128)} %param.12) | copy-start | bytes 1572868
  2.7 29.5 %all-to-all-start = ((f32[16,64,128]{2,1,0:T(8,128)}), f32[16,64,128]{2,1,0:T(8,128)S(1)}, u32[]{:S(2)}, u32[]{:S(2)}) async-start(f32[16,64,128]{2,1,0:T(8,128)} %multiply_multiply_fusion.1), calls=%async_computation | async-start | bytes 1048576 | tf_op jit(solution)/shard_map/all_to_all | solution.py:187
  10.2 70.0 %collective-permute-start.2 = (f32[2,16,128]{2,1,0:T(8,128)S(1)}, f32[2,16,128]{2,1,0:T(8,128)S(1)}, u32[]{:S(2)}, u32[]{:S(2)}) collective-permute-start(f32[2,16,128]{2,1,0:T(8,128)S(1)} %bitcast.247), channel_id=1, source_target_pairs={{0,1},{1,2},{2,3},{3,4},{4,5},{5,6},{6,7},{7,8},{8,9},{9,10},{10,1... | collective-permute-start | bytes 49160 | tf_op jit(solution)/shard_map/ppermute | solution.py:20
  13.8 104.7 %collective-permute-start.3 = (f32[2,16,128]{2,1,0:T(8,128)S(1)}, f32[2,16,128]{2,1,0:T(8,128)S(1)}, u32[]{:S(2)}, u32[]{:S(2)}) collective-permute-start(f32[2,16,128]{2,1,0:T(8,128)S(1)} %bitcast.246), channel_id=1, source_target_pairs={{1,0},{2,1},{3,2},{4,3},{5,4},{6,5},{7,6},{8,7},{9,8},{10,9},{11,1... | collective-permute-start | bytes 49160 | tf_op jit(solution)/shard_map/ppermute | solution.py:20
  16.6 61.5 %collective-permute-start.5 = (f32[2,16,64]{2,1,0:T(8,128)S(1)}, f32[2,16,64]{2,1,0:T(8,128)S(1)}, u32[]{:S(2)}, u32[]{:S(2)}) collective-permute-start(f32[2,16,64]{2,1,0:T(8,128)S(1)} %get-tuple-element.10), channel_id=1, source_target_pairs={{16,0},{32,16},{48,32},{64,48},{80,64},{96,80},{112,96},{17,1},{33... | collective-permute-start | bytes 24584 | tf_op jit(solution)/shard_map/ppermute | solution.py:20
  21.8 56.4 %collective-permute-start.4 = (f32[2,16,64]{2,1,0:T(8,128)S(1)}, f32[2,16,64]{2,1,0:T(8,128)S(1)}, u32[]{:S(2)}, u32[]{:S(2)}) collective-permute-start(f32[2,16,64]{2,1,0:T(8,128)S(1)} %get-tuple-element.11), channel_id=1, source_target_pairs={{0,16},{16,32},{32,48},{48,64},{64,80},{80,96},{96,112},{1,17},{17... | collective-permute-start | bytes 24584 | tf_op jit(solution)/shard_map/ppermute | solution.py:20
  32.2 3.3 %copy-start = (bf16[1024,1024]{1,0:T(8,128)(2,1)}, bf16[1024,1024]{1,0:T(8,128)(2,1)S(1)}, u32[]{:S(2)}) copy-start(bf16[1024,1024]{1,0:T(8,128)(2,1)S(1)} %get-tuple-element.14) | copy-start | bytes 6291460
  35.6 13.7 %copy-start.13 = (f32[1024]{0:T(1024)S(1)}, f32[1024]{0:T(1024)}, u32[]{:S(2)}) copy-start(f32[1024]{0:T(1024)} %param.19) | copy-start | bytes 12292
  37.1 25.1 %all-to-all-start.1 = ((f32[128,8,128]{2,1,0:T(8,128)}), f32[128,8,128]{2,1,0:T(8,128)S(1)}, u32[]{:S(2)}, u32[]{:S(2)}) async-start(f32[128,8,128]{2,1,0:T(8,128)} %bitcast.3), calls=%async_computation.1 | async-start | bytes 1048576 | tf_op jit(solution)/shard_map/all_to_all | solution.py:191
  73.2 18.0 %all-to-all-start.2 = ((f32[128,8,128]{2,1,0:T(8,128)}), f32[128,8,128]{2,1,0:T(8,128)S(1)}, u32[]{:S(2)}, u32[]{:S(2)}) async-start(f32[128,8,128]{2,1,0:T(8,128)} %bitcast.233), calls=%async_computation.2 | async-start | bytes 1048576 | tf_op jit(solution)/shard_map/all_to_all | solution.py:197
  91.2 2.6 %copy-start.1 = (bf16[1024,1024]{1,0:T(8,128)(2,1)S(1)}, bf16[1024,1024]{1,0:T(8,128)(2,1)}, u32[]{:S(2)}) copy-start(bf16[1024,1024]{1,0:T(8,128)(2,1)} %copy-done) | copy-start | bytes 6291460
  101.1 6.8 %collective-permute-start.1 = (f32[16,64]{1,0:T(8,128)S(1)}, f32[16,64]{1,0:T(8,128)S(1)}, u32[]{:S(2)}, u32[]{:S(2)}) collective-permute-start(f32[16,64]{1,0:T(8,128)S(1)} %bitcast.250), channel_id=1, source_target_pairs={{16,0},{32,16},{48,32},{64,48},{80,64},{96,80},{112,96},{17,1},{33... | collective-permute-start | bytes 12296 | tf_op jit(solution)/shard_map/ppermute | solution.py:202
  104.4 6.8 %collective-permute-start = (f32[16,64]{1,0:T(8,128)S(1)}, f32[16,64]{1,0:T(8,128)S(1)}, u32[]{:S(2)}, u32[]{:S(2)}) collective-permute-start(f32[16,64]{1,0:T(8,128)S(1)} %bitcast.248), channel_id=1, source_target_pairs={{0,16},{16,32},{32,48},{48,64},{64,80},{80,96},{96,112},{1,17},{17... | collective-permute-start | bytes 12296 | tf_op jit(solution)/shard_map/ppermute | solution.py:201
  112.2 16.5 %all-to-all-start.3 = ((f32[16,67,128]{2,1,0:T(8,128)}), f32[16,67,128]{2,1,0:T(8,128)S(1)}, u32[]{:S(2)}, u32[]{:S(2)}) async-start(f32[16,67,128]{2,1,0:T(8,128)} %fusion.23), calls=%async_computation.3 | async-start | bytes 1179648 | tf_op jit(solution)/shard_map/all_to_all | solution.py:208
  130.8 4.1 %copy-start.14 = (f32[128]{0:T(128)S(1)}, f32[128]{0:T(128)}, u32[]{:S(2)}) copy-start(f32[128]{0:T(128)} %param.18) | copy-start | bytes 1540
  130.8 4.1 %copy-start.15 = (f32[64]{0:T(128)S(1)}, f32[64]{0:T(128)}, u32[]{:S(2)}) copy-start(f32[64]{0:T(128)} %param.15) | copy-start | bytes 772
  134.9 15.1 %copy-start.4 = (bf16[1024,1024]{1,0:T(8,128)(2,1)S(1)}, bf16[1024,1024]{1,0:T(8,128)(2,1)}, u32[]{:S(2)}) copy-start(bf16[1024,1024]{1,0:T(8,128)(2,1)} %get-tuple-element.15) | copy-start | bytes 6291460
  152.7 18.0 %copy-start.7 = (bf16[1024,1024]{1,0:T(8,128)(2,1)S(1)}, bf16[1024,1024]{1,0:T(8,128)(2,1)}, u32[]{:S(2)}) copy-start(bf16[1024,1024]{1,0:T(8,128)(2,1)} %get-tuple-element.13) | copy-start | bytes 6291460
  174.9 2.6 %copy-start.8 = (f32[16,8,1024]{2,1,0:T(8,128)S(1)}, f32[16,8,1024]{2,1,0:T(8,128)}, u32[]{:S(2)}) copy-start(f32[16,8,1024]{2,1,0:T(8,128)} %shard_map.124) | copy-start | bytes 1572868
  178.3 18.4 %copy-start.5 = (bf16[1024,1024]{1,0:T(8,128)(2,1)S(1)}, bf16[1024,1024]{1,0:T(8,128)(2,1)}, u32[]{:S(2)}) copy-start(bf16[1024,1024]{1,0:T(8,128)(2,1)} %get-tuple-element.15) | copy-start | bytes 6291460
  179.2 18.4 %copy-start.3 = (bf16[1024,1024]{1,0:T(8,128)(2,1)S(1)}, bf16[1024,1024]{1,0:T(8,128)(2,1)}, u32[]{:S(2)}) copy-start(bf16[1024,1024]{1,0:T(8,128)(2,1)} %copy-done) | copy-start | bytes 6291460
  200.1 6.8 %collective-permute-start.7 = (f32[16,64]{1,0:T(8,128)S(1)}, f32[16,64]{1,0:T(8,128)S(1)}, u32[]{:S(2)}, u32[]{:S(2)}) collective-permute-start(f32[16,64]{1,0:T(8,128)S(1)} %bitcast.251), channel_id=1, source_target_pairs={{16,0},{32,16},{48,32},{64,48},{80,64},{96,80},{112,96},{17,1},{33... | collective-permute-start | bytes 12296 | tf_op jit(solution)/shard_map/ppermute | solution.py:202
  203.4 6.8 %collective-permute-start.6 = (f32[16,64]{1,0:T(8,128)S(1)}, f32[16,64]{1,0:T(8,128)S(1)}, u32[]{:S(2)}, u32[]{:S(2)}) collective-permute-start(f32[16,64]{1,0:T(8,128)S(1)} %bitcast.249), channel_id=1, source_target_pairs={{0,16},{16,32},{32,48},{48,64},{64,80},{80,96},{96,112},{1,17},{17... | collective-permute-start | bytes 12296 | tf_op jit(solution)/shard_map/ppermute | solution.py:201
  (4 other events, 8.4 us)

commit v11 on v10

--- a/solution.py
+++ b/solution.py
@@ -177,6 +177,7 @@
     basis_x = split_bf16(vectors_x)
     rows = right_side.shape[1]
     count_y = lax.axis_size("gx")
+    block_y = lax.axis_index("gx")
     forward_y = [(i, i + 1) for i in range(count_y - 1)]
     backward_y = [(target, source) for source, target in forward_y]
     basis_y = tuple(piece.reshape(blocks_y, -1, vectors_y.shape[1]) for piece in split_bf16(vectors_y))
@@ -198,8 +199,11 @@
         solved = chunks.reshape(-1, chunks.shape[2])
         plane = transform("iy,xi->xy", solved, basis_x)
         blocks = plane.reshape(-1, rows, plane.shape[1])
-        from_left = lax.ppermute(blocks[:, :, -1], "gx", forward_y)
-        from_right = lax.ppermute(blocks[:, :, 0], "gx", backward_y)
+        gathered = lax.all_gather(jnp.concatenate([blocks[:, :, 0], blocks[:, :, -1]], axis=1), "gx")
+        from_left = lax.dynamic_index_in_dim(gathered, jnp.maximum(block_y - 1, 0), keepdims=False)[:, rows:]
+        from_left = jnp.where(block_y > 0, from_left, 0.0)
+        from_right = lax.dynamic_index_in_dim(gathered, jnp.minimum(block_y + 1, count_y - 1), keepdims=False)
+        from_right = jnp.where(block_y < count_y - 1, from_right[:, :rows], 0.0)
         zero = jnp.zeros_like(blocks[:1, :1])
         below = jnp.concatenate([zero, blocks[:-1, -1:]], axis=0)
         above = jnp.concatenate([blocks[1:, :1], zero], axis=0)

time: 234 us -> 278 us (1.19); the launches traced: 233 us -> 274 us
  blocking collectives: 65.6 us -> 125 us
  starting transfers between devices: 56.1 us -> 46.6 us
  waiting for transfers between devices: 29.5 us -> 23 us
  local copies, waits for them, and re-layouts: 20.4 us -> 17.1 us
    all_gather x0 -> x2, blocking collectives: none -> 53.1 us  [shards(): lax.all_gather(jnp.concatenate([blocks[:, :, 0], blocks[:, :, -1]], axis=...]
    ppermute x4 -> x0, starting transfers between devices: 13.6 us -> none  [the longest x2 7.03 us: shards(): from_left = lax.ppermute(blocks[:, :, -1], 'gx', forward_y)]
    ppermute x4 -> x0, waiting for transfers between devices: 6.49 us -> none  [the longest x2 6.48 us: shards(): from_left = lax.ppermute(blocks[:, :, -1], 'gx', forward_y)]
    all_to_all x1, blocking collectives: 16.5 us -> 20.7 us  [shards(): lax.all_to_all(framed, 'gy', split_axis=0, concat_axis=0, tiled=True)]
    all_to_all x1, starting transfers between devices: 6.32 us -> 10.4 us  [shards(): lax.all_to_all(framed, 'gy', split_axis=0, concat_axis=0, tiled=True)]
    unnamed x36 -> x32, local copies, waits for them, and re-layouts: 4.08 us -> 1.15 us
  transfers between devices with their start and end apart: 12 -> 8, of which waited for: 5 -> 3; matrix products, arithmetic and copies ran while one was open for 21% -> 16% of each run, Pallas kernels for 1% -> 1%
where the time goes in v11:
time: 278 us; the launch traced here: 274 us
  blocking collectives  125 us (45%)
  starting transfers between devices  46.6 us (17%)
  matrix products  26.9 us (10%)
  waiting for transfers between devices  23 us (8%)
  other arithmetic  21.3 us (8%)
  local copies, waits for them, and re-layouts  17.1 us (6%)
  Pallas kernels  12.5 us (4%)
    all_gather x2, blocking collectives, shards(): lax.all_gather(jnp.concatenate([blocks[:, :, 0], blocks[:, :, -1]], axis=...  53.1 us
    all_to_all x2, blocking collectives, shards(): lax.all_to_all(chunks, everyone, split_axis=0, concat_axis=0, tiled=True)  37.5 us
    dot_general x24, matrix products, product(): return jnp.einsum(spec, first, second, preferred_element_type=jnp.float32)  26.9 us
    all_to_all x1, blocking collectives, shards(): lax.all_to_all(framed, 'gy', split_axis=0, concat_axis=0, tiled=True)  20.7 us
    all_to_all x2, waiting for transfers between devices, shards(): lax.all_to_all(chunks, everyone, split_axis=0, concat_axis=0, tiled=True)  18.1 us
    all_to_all x2, starting transfers between devices, shards(): lax.all_to_all(chunks, everyone, split_axis=0, concat_axis=0, tiled=True)  17.1 us
    all_to_all x1, blocking collectives, shards(): lax.all_to_all(scaled, 'gy', split_axis=0, concat_axis=1, tiled=True)  13.7 us
    all_to_all x1, starting transfers between devices, shards(): lax.all_to_all(framed, 'gy', split_axis=0, concat_axis=0, tiled=True)  10.4 us
  transfers between devices with their start and end apart: 8, of which 3 were waited for; matrix products, arithmetic and copies ran while one was open for 16% of the time, Pallas kernels for 1%

profile of v11, /device:TPU:3, one launch (start us, length us, event | category | flops | bytes accessed | tf_op | source)
XLA Modules:
  0.0 273.6 jit_solution(3096658122184665806)
XLA Ops:
  2.7 6.5 %all-to-all-start = ((f32[16,64,128]{2,1,0:T(8,128)}), f32[16,64,128]{2,1,0:T(8,128)S(1)}, u32[]{:S(2)}, u32[]{:S(2)}) async-start(f32[16,64,128]{2,1,0:T(8,128)} %multiply_multiply_fusion.1), calls=%async_computation | async-start | bytes 1048576 | tf_op jit(solution)/shard_map/all_to_all | solution.py:188
  10.2 3.5 %collective-permute-start = (f32[2,16,128]{2,1,0:T(8,128)S(1)}, f32[2,16,128]{2,1,0:T(8,128)S(1)}, u32[]{:S(2)}, u32[]{:S(2)}) collective-permute-start(f32[2,16,128]{2,1,0:T(8,128)S(1)} %bitcast.257), channel_id=1, source_target_pairs={{0,1},{1,2},{2,3},{3,4},{4,5},{5,6},{6,7},{7,8},{8,9},{9,10},{10,1... | collective-permute-start | bytes 49160 | tf_op jit(solution)/shard_map/ppermute | solution.py:20
  16.6 5.2 %collective-permute-start.3 = (f32[2,16,64]{2,1,0:T(8,128)S(1)}, f32[2,16,64]{2,1,0:T(8,128)S(1)}, u32[]{:S(2)}, u32[]{:S(2)}) collective-permute-start(f32[2,16,64]{2,1,0:T(8,128)S(1)} %get-tuple-element.10), channel_id=1, source_target_pairs={{16,0},{32,16},{48,32},{64,48},{80,64},{96,80},{112,96},{17,1},{33... | collective-permute-start | bytes 24584 | tf_op jit(solution)/shard_map/ppermute | solution.py:20
  27.8 4.5 %reduce-precision_convert_fusion.1 = (bf16[1024,1024]{1,0:T(8,128)(2,1)S(1)}, bf16[1024,1024]{1,0:T(8,128)(2,1)}) fusion(f32[1024,1024]{1,0:T(8,128)} %param.14), kind=kLoop, calls=%fused_computation.3 | loop fusion | flops 4194304 | bytes 8388608 | tf_op jit(solution)/shard_map/convert_element_type | solution.py:139
  32.3 2.8 %fusion.60 = f32[1024,128]{0,1:T(8,128)S(1)} fusion(bf16[1024,1024]{1,0:T(8,128)(2,1)} %get-tuple-element.19, bf16[1024,128]{1,0:T(8,128)(2,1)S(1)} %get-tuple-element.51), kind=kOutput, calls=%fused_computation.137 | convolution fusion | flops 268435456 | bytes 2883584 | tf_op jit(solution)/shard_map/zxy,xi->ziy/dot_general | solution.py:147
  37.0 12.2 %all-to-all-start.1 = ((f32[128,8,128]{2,1,0:T(8,128)}), f32[128,8,128]{2,1,0:T(8,128)S(1)}, u32[]{:S(2)}, u32[]{:S(2)}) async-start(f32[128,8,128]{2,1,0:T(8,128)} %bitcast.3), calls=%async_computation.1 | async-start | bytes 1048576 | tf_op jit(solution)/shard_map/all_to_all | solution.py:192
  49.9 4.5 %reduce-precision_convert_fusion = (bf16[1024,1024]{1,0:T(8,128)(2,1)S(1)}, bf16[1024,1024]{1,0:T(8,128)(2,1)}) fusion(f32[1024,1024]{1,0:T(8,128)} %param.17), kind=kLoop, calls=%fused_computation.1 | loop fusion | flops 4194304 | bytes 8388608 | tf_op jit(solution)/shard_map/convert_element_type | solution.py:139
  54.4 7.7 %all-to-all-done.1 = f32[128,8,128]{2,1,0:T(8,128)S(1)} async-done(((f32[128,8,128]{2,1,0:T(8,128)}), f32[128,8,128]{2,1,0:T(8,128)S(1)}, u32[]{:S(2)}, u32[]{:S(2)}) %all-to-all-start.1) | async-done | bytes 524320 | tf_op jit(solution)/shard_map/all_to_all | solution.py:192
  68.1 2.5 convolution_bitcast_fusion.12
  73.1 4.9 %all-to-all-start.2 = ((f32[128,8,128]{2,1,0:T(8,128)}), f32[128,8,128]{2,1,0:T(8,128)S(1)}, u32[]{:S(2)}, u32[]{:S(2)}) async-start(f32[128,8,128]{2,1,0:T(8,128)} %bitcast.241), calls=%async_computation.2 | async-start | bytes 1048576 | tf_op jit(solution)/shard_map/all_to_all | solution.py:198
  80.8 10.3 %all-to-all-done.2 = f32[128,8,128]{2,1,0:T(8,128)S(1)} async-done(((f32[128,8,128]{2,1,0:T(8,128)}), f32[128,8,128]{2,1,0:T(8,128)S(1)}, u32[]{:S(2)}, u32[]{:S(2)}) %all-to-all-start.2) | async-done | bytes 524320 | tf_op jit(solution)/shard_map/all_to_all | solution.py:198
  91.2 2.6 fusion.41
  98.1 26.6 %all-gather = f32[128,128]{1,0:T(8,128)S(1)} all-gather(f32[16,128]{1,0:T(8,128)S(1)} %pad_maximum_fusion.7), channel_id=2, replica_groups=mesh['gx'=8,'gy'=16] {'gx'}, dimensions={0}, use_global_device_ids=true | all-gather | bytes 73728 | tf_op jit(solution)/shard_map/all_gather | solution.py:202
  125.7 10.4 %all-to-all-start.3 = ((f32[16,67,128]{2,1,0:T(8,128)}), f32[16,67,128]{2,1,0:T(8,128)S(1)}, u32[]{:S(2)}, u32[]{:S(2)}) async-start(f32[16,67,128]{2,1,0:T(8,128)} %fusion.23), calls=%async_computation.3 | async-start | bytes 1179648 | tf_op jit(solution)/shard_map/all_to_all | solution.py:212
  136.6 4.7 %add_divide_fusion = (f32[16,64,128]{2,1,0:T(8,128)}, f32[16,64,128]{2,1,0:T(8,128)}, f32[16,64,128]{2,1,0:T(8,128)}, f32[16,64,128]{2,1,0:T(8,128)}, f32[16,64,128]{2,1,0:T(8,128)}, /*index=5*/f32[16,64,128]{2,1,0:T(8,128)}) fusion(f32[16,64,128]{2,1,0:T(8,128)S(1)} %copy-done.6, f32[16,64,127]{2,1,0:T(8,128)} %get-tuple-element.38, ...), kind=kLoop, calls=%fused_computation.89 | loop fusion | flops 3014656 | bytes 6750208 | tf_op jit(solution)/shard_map/div | solution.py:28
  141.3 4.9 %all-to-all-done.3.framed_ref = f32[16,67,128]{2,1,0:T(8,128)S(1)} async-done(((f32[16,67,128]{2,1,0:T(8,128)}), f32[16,67,128]{2,1,0:T(8,128)S(1)}, u32[]{:S(2)}, u32[]{:S(2)}) %all-to-all-start.3) | async-done | bytes 548896 | tf_op jit(solution)/shard_map/all_to_all | solution.py:212
  148.3 4.1 %shard_map.123 = (f32[16,64,128]{2,1,0:T(8,128)}, f32[16,64,128]{2,1,0:T(8,128)}) custom-call(f32[16,67,128]{2,1,0:T(8,128)} %copy-done.11, f32[16,64,128]{2,1,0:T(8,128)} %get-tuple-element.45.active_ref, f32[16,64,128]{2,1,0:T(8,128)} %residual_ref.1, f32[16,128]{1,0:T(8,128)} %get-tuple-element.57.refs_0_.refs_1_, ...), custom_call_target="tpu_custom_call" | custom-call | tf_op jit(solution)/shard_map/pallas_call | solution.py:96
  153.8 13.7 %all_to_all.54 = f32[16,64,128]{2,1,0:T(8,128)S(1)} all-to-all(f32[16,64,128]{2,1,0:T(8,128)S(1)} %multiply_multiply_fusion), channel_id=1, replica_groups=mesh['gx'=8,'gy'=16] {'gy'}, dimensions={0} | all-to-all | bytes 1048576 | tf_op jit(solution)/shard_map/all_to_all | solution.py:188
  170.3 19.9 %all_to_all.55 = f32[128,8,128]{2,1,0:T(8,128)S(1)} all-to-all(f32[128,8,128]{2,1,0:T(8,128)S(1)} %bitcast.242), channel_id=1, replica_groups=mesh['gx'=8,'gy'=16] {'gx','gy'}, dimensions={0} | all-to-all | bytes 1048576 | tf_op jit(solution)/shard_map/all_to_all | solution.py:192
  194.5 2.5 convolution_bitcast_fusion.2
  198.8 17.5 %all_to_all.56 = f32[128,8,128]{2,1,0:T(8,128)S(1)} all-to-all(f32[128,8,128]{2,1,0:T(8,128)S(1)} %bitcast.243), channel_id=1, replica_groups=mesh['gx'=8,'gy'=16] {'gx','gy'}, dimensions={0} | all-to-all | bytes 1048576 | tf_op jit(solution)/shard_map/all_to_all | solution.py:198
  219.7 26.6 %all-gather.1 = f32[128,128]{1,0:T(8,128)S(1)} all-gather(f32[16,128]{1,0:T(8,128)S(1)} %pad_maximum_fusion.9), channel_id=3, replica_groups=mesh['gx'=8,'gy'=16] {'gx'}, dimensions={0}, use_global_device_ids=true | all-gather | bytes 73728 | tf_op jit(solution)/shard_map/all_gather | solution.py:202
  246.5 20.7 %all_to_all.57.framed_ref = f32[16,67,128]{2,1,0:T(8,128)S(1)} all-to-all(f32[16,67,128]{2,1,0:T(8,128)S(1)} %fusion.19), channel_id=1, replica_groups=mesh['gx'=8,'gy'=16] {'gy'}, dimensions={0} | all-to-all | bytes 1097728 | tf_op jit(solution)/shard_map/all_to_all | solution.py:212
  269.4 4.2 %shard_map.125 = (f32[16,64,128]{2,1,0:T(8,128)}, f32[16,64,128]{2,1,0:T(8,128)}) custom-call(f32[16,67,128]{2,1,0:T(8,128)} %copy-done.10, f32[16,64,128]{2,1,0:T(8,128)} %get-tuple-element.45.active_ref, f32[16,64,128]{2,1,0:T(8,128)} %get-tuple-element.6.residual_ref, f32[16,64,128]{2,1,0:T(8,128)} %get-tuple-element.7.refs_0_, ...), custom_call_target="tpu_custom_call" | custom-call | tf_op jit(solution)/shard_map/pallas_call | solution.py:96
  (112 shorter events, 49.4 us)
Async XLA Ops:
  0.6 8.6 %copy-start.12 = (s32[16,64,128]{2,1,0:T(8,128)S(1)}, s32[16,64,128]{2,1,0:T(8,128)}, u32[]{:S(2)}) copy-start(s32[16,64,128]{2,1,0:T(8,128)} %param.13) | copy-start | bytes 1572868
  0.6 9.5 %copy-start.6 = (f32[16,64,128]{2,1,0:T(8,128)S(1)}, f32[16,64,128]{2,1,0:T(8,128)}, u32[]{:S(2)}) copy-start(f32[16,64,128]{2,1,0:T(8,128)} %param.12) | copy-start | bytes 1572868
  2.7 29.5 %all-to-all-start = ((f32[16,64,128]{2,1,0:T(8,128)}), f32[16,64,128]{2,1,0:T(8,128)S(1)}, u32[]{:S(2)}, u32[]{:S(2)}) async-start(f32[16,64,128]{2,1,0:T(8,128)} %multiply_multiply_fusion.1), calls=%async_computation | async-start | bytes 1048576 | tf_op jit(solution)/shard_map/all_to_all | solution.py:188
  10.2 70.1 %collective-permute-start = (f32[2,16,128]{2,1,0:T(8,128)S(1)}, f32[2,16,128]{2,1,0:T(8,128)S(1)}, u32[]{:S(2)}, u32[]{:S(2)}) collective-permute-start(f32[2,16,128]{2,1,0:T(8,128)S(1)} %bitcast.257), channel_id=1, source_target_pairs={{0,1},{1,2},{2,3},{3,4},{4,5},{5,6},{6,7},{7,8},{8,9},{9,10},{10,1... | collective-permute-start | bytes 49160 | tf_op jit(solution)/shard_map/ppermute | solution.py:20
  13.7 122.3 %collective-permute-start.1 = (f32[2,16,128]{2,1,0:T(8,128)S(1)}, f32[2,16,128]{2,1,0:T(8,128)S(1)}, u32[]{:S(2)}, u32[]{:S(2)}) collective-permute-start(f32[2,16,128]{2,1,0:T(8,128)S(1)} %bitcast.256), channel_id=1, source_target_pairs={{1,0},{2,1},{3,2},{4,3},{5,4},{6,5},{7,6},{8,7},{9,8},{10,9},{11,1... | collective-permute-start | bytes 49160 | tf_op jit(solution)/shard_map/ppermute | solution.py:20
  16.6 61.5 %collective-permute-start.3 = (f32[2,16,64]{2,1,0:T(8,128)S(1)}, f32[2,16,64]{2,1,0:T(8,128)S(1)}, u32[]{:S(2)}, u32[]{:S(2)}) collective-permute-start(f32[2,16,64]{2,1,0:T(8,128)S(1)} %get-tuple-element.10), channel_id=1, source_target_pairs={{16,0},{32,16},{48,32},{64,48},{80,64},{96,80},{112,96},{17,1},{33... | collective-permute-start | bytes 24584 | tf_op jit(solution)/shard_map/ppermute | solution.py:20
  21.8 56.4 %collective-permute-start.2 = (f32[2,16,64]{2,1,0:T(8,128)S(1)}, f32[2,16,64]{2,1,0:T(8,128)S(1)}, u32[]{:S(2)}, u32[]{:S(2)}) collective-permute-start(f32[2,16,64]{2,1,0:T(8,128)S(1)} %get-tuple-element.11), channel_id=1, source_target_pairs={{0,16},{16,32},{32,48},{48,64},{64,80},{80,96},{96,112},{1,17},{17... | collective-permute-start | bytes 24584 | tf_op jit(solution)/shard_map/ppermute | solution.py:20
  32.2 3.3 %copy-start = (bf16[1024,1024]{1,0:T(8,128)(2,1)}, bf16[1024,1024]{1,0:T(8,128)(2,1)S(1)}, u32[]{:S(2)}) copy-start(bf16[1024,1024]{1,0:T(8,128)(2,1)S(1)} %get-tuple-element.18) | copy-start | bytes 6291460
  35.6 13.7 %copy-start.13 = (f32[1024]{0:T(1024)S(1)}, f32[1024]{0:T(1024)}, u32[]{:S(2)}) copy-start(f32[1024]{0:T(1024)} %param.19) | copy-start | bytes 12292
  37.0 25.1 %all-to-all-start.1 = ((f32[128,8,128]{2,1,0:T(8,128)}), f32[128,8,128]{2,1,0:T(8,128)S(1)}, u32[]{:S(2)}, u32[]{:S(2)}) async-start(f32[128,8,128]{2,1,0:T(8,128)} %bitcast.3), calls=%async_computation.1 | async-start | bytes 1048576 | tf_op jit(solution)/shard_map/all_to_all | solution.py:192
  68.1 2.6 copy-start.9
  73.1 18.0 %all-to-all-start.2 = ((f32[128,8,128]{2,1,0:T(8,128)}), f32[128,8,128]{2,1,0:T(8,128)S(1)}, u32[]{:S(2)}, u32[]{:S(2)}) async-start(f32[128,8,128]{2,1,0:T(8,128)} %bitcast.241), calls=%async_computation.2 | async-start | bytes 1048576 | tf_op jit(solution)/shard_map/all_to_all | solution.py:198
  91.1 2.6 copy-start.1
  125.7 20.6 %all-to-all-start.3 = ((f32[16,67,128]{2,1,0:T(8,128)}), f32[16,67,128]{2,1,0:T(8,128)S(1)}, u32[]{:S(2)}, u32[]{:S(2)}) async-start(f32[16,67,128]{2,1,0:T(8,128)} %fusion.23), calls=%async_computation.3 | async-start | bytes 1179648 | tf_op jit(solution)/shard_map/all_to_all | solution.py:212
  146.3 2.1 copy-start.11
  148.3 4.1 %copy-start.14 = (f32[128]{0:T(128)S(1)}, f32[128]{0:T(128)}, u32[]{:S(2)}) copy-start(f32[128]{0:T(128)} %param.18) | copy-start | bytes 1540
  148.3 4.1 %copy-start.15 = (f32[64]{0:T(128)S(1)}, f32[64]{0:T(128)}, u32[]{:S(2)}) copy-start(f32[64]{0:T(128)} %param.15) | copy-start | bytes 772
  152.4 15.1 %copy-start.4 = (bf16[1024,1024]{1,0:T(8,128)(2,1)S(1)}, bf16[1024,1024]{1,0:T(8,128)(2,1)}, u32[]{:S(2)}) copy-start(bf16[1024,1024]{1,0:T(8,128)(2,1)} %get-tuple-element.19) | copy-start | bytes 6291460
  167.5 1.6 copy-start.2
  170.3 20.0 %copy-start.7 = (bf16[1024,1024]{1,0:T(8,128)(2,1)S(1)}, bf16[1024,1024]{1,0:T(8,128)(2,1)}, u32[]{:S(2)}) copy-start(bf16[1024,1024]{1,0:T(8,128)(2,1)} %get-tuple-element.17) | copy-start | bytes 6291460
  194.5 2.6 copy-start.8
  197.9 18.4 %copy-start.5 = (bf16[1024,1024]{1,0:T(8,128)(2,1)S(1)}, bf16[1024,1024]{1,0:T(8,128)(2,1)}, u32[]{:S(2)}) copy-start(bf16[1024,1024]{1,0:T(8,128)(2,1)} %get-tuple-element.19) | copy-start | bytes 6291460
  198.8 18.4 %copy-start.3 = (bf16[1024,1024]{1,0:T(8,128)(2,1)S(1)}, bf16[1024,1024]{1,0:T(8,128)(2,1)}, u32[]{:S(2)}) copy-start(bf16[1024,1024]{1,0:T(8,128)(2,1)} %copy-done) | copy-start | bytes 6291460
  267.2 2.1 copy-start.10

commit v12 on v10

--- a/solution.py
+++ b/solution.py
@@ -46,13 +46,15 @@
 
 
 def framed_kernel(framed_ref, active_ref, residual_ref, *refs):
-    if len(refs) == 12:
+    if len(refs) == 11:
         adjoint_ref = None
     else:
         adjoint_ref, refs = refs[0], refs[1:]
-    x_low_ref, x_high_ref, y_low_ref, y_high_ref = refs[:4]
-    face_refs, residual_out, adjoint_out = refs[4:-2], refs[-2], refs[-1]
+    x_low_ref, x_high_ref, y_active_ref = refs[:3]
+    face_refs, residual_out, adjoint_out = refs[3:-2], refs[-2], refs[-1]
     planes, rows, cols = active_ref.shape
+    halo_rows = jnp.concatenate([framed_ref[z, pl.ds(rows + 2, 1), :] for z in range(planes)], axis=0)
+    halo_columns = jnp.transpose(halo_rows * y_active_ref[...])
     row = lax.broadcasted_iota(jnp.int32, (rows, cols), 0)
     col = lax.broadcasted_iota(jnp.int32, (rows, cols), 1)
     row_forward = pltpu.roll(row, 1, 0) == jnp.where(row == 0, rows - 1, row - 1)
@@ -76,8 +78,14 @@
             masked[z - 1] if z > 0 else zeros,
             jnp.where(row == rows - 1, jnp.broadcast_to(x_high, (rows, cols)), after(center, 0, rows, row_forward)),
             jnp.where(row == 0, jnp.broadcast_to(x_low, (rows, cols)), before(center, 0, rows, row_forward)),
-            jnp.where(col == cols - 1, y_high_ref[z], after(center, 1, cols, col_forward)),
-            jnp.where(col == 0, y_low_ref[z], before(center, 1, cols, col_forward)),
+            jnp.where(
+                col == cols - 1,
+                jnp.broadcast_to(halo_columns[rows:, z : z + 1], (rows, cols)),
+                after(center, 1, cols, col_forward),
+            ),
+            jnp.where(
+                col == 0, jnp.broadcast_to(halo_columns[:rows, z : z + 1], (rows, cols)), before(center, 1, cols, col_forward)
+            ),
         ]
         result = storage_term * center
         for face_ref, other in zip(face_refs, others):
@@ -87,12 +95,11 @@
         adjoint_out[z] = update if adjoint_ref is None else adjoint_ref[z] + update
 
 
-def framed_stencil(framed, active, residual, adjoint, x_strips, y_strips, faces):
+def framed_stencil(framed, active, residual, adjoint, x_strips, y_active, faces):
     vmem = pl.BlockSpec(memory_space=pltpu.VMEM)
     shape = jax.ShapeDtypeStruct(active.shape, active.dtype)
-    y_low, y_high = (jnp.broadcast_to(strip[:, :, None], active.shape) for strip in y_strips)
     carried = [] if adjoint is None else [adjoint]
-    operands = [framed, active, residual, *carried, x_strips[0], x_strips[1], y_low, y_high, *faces]
+    operands = [framed, active, residual, *carried, x_strips[0], x_strips[1], y_active, *faces]
     return pl.pallas_call(
         framed_kernel,
         out_shape=(shape, shape),
@@ -176,6 +183,7 @@
     blocks_y = lax.axis_size("gx")
     basis_x = split_bf16(vectors_x)
     rows = right_side.shape[1]
+    y_active = jnp.concatenate(active_y, axis=1)
     count_y = lax.axis_size("gx")
     forward_y = [(i, i + 1) for i in range(count_y - 1)]
     backward_y = [(target, source) for source, target in forward_y]
@@ -206,8 +214,7 @@
         halo_row = jnp.concatenate([from_left, from_right], axis=1)[:, None, :]
         framed = jnp.concatenate([below, blocks, above, halo_row], axis=1)
         framed = lax.all_to_all(framed, "gy", split_axis=0, concat_axis=0, tiled=True)
-        y_strips = (active_y[0] * framed[:, -1, :rows], active_y[1] * framed[:, -1, rows:])
-        residual, adjoint = framed_stencil(framed, active, residual, adjoint, active_x, y_strips, faces)
+        residual, adjoint = framed_stencil(framed, active, residual, adjoint, active_x, y_active, faces)
     return (adjoint, residual)
 
 

time: 234 us -> 238 us (1.017)
  local copies, waits for them, and re-layouts: 20.4 us -> 23 us
    broadcast_in_dim x4 -> x0, local copies, waits for them, and re-layouts: 4.01 us -> none  [framed_stencil(): jnp.broadcast_to(strip[:, :, None], active.shape)]
    slice x2, local copies, waits for them, and re-layouts: 0.16 us -> 4.12 us  [the longest x1 2.8 us: edge_pair(): lax.index_in_dim(block, block.shape[dim] - 1, axis=dim, keepdims=False)]
    ppermute x2, starting transfers between devices: 5.49 us -> 9.3 us  [edge_pair(): lax.ppermute(last, axis, forward)]
    ppermute x2, starting transfers between devices: 7.1 us -> 4.39 us  [edge_pair(): lax.ppermute(first, axis, backward)]
    unnamed x36 -> x41, local copies, waits for them, and re-layouts: 4.08 us -> 6.18 us
  transfers between devices with their start and end apart: 12 -> 12, of which waited for: 5 -> 5; matrix products, arithmetic and copies ran while one was open for 21% -> 22% of each run, Pallas kernels for 1% -> 1%
where the time goes in v12:
time: 238 us; the launch traced here: 237 us
  blocking collectives  66.3 us (28%)
  starting transfers between devices  55.3 us (23%)
  waiting for transfers between devices  31.6 us (13%)
  matrix products  26.4 us (11%)
  local copies, waits for them, and re-layouts  23 us (10%)
  other arithmetic  21.1 us (9%)
  Pallas kernels  12.2 us (5%)
    all_to_all x2, blocking collectives, shards(): lax.all_to_all(chunks, everyone, split_axis=0, concat_axis=0, tiled=True)  35.4 us
    dot_general x24, matrix products, product(): return jnp.einsum(spec, first, second, preferred_element_type=jnp.float32)  26.4 us
    all_to_all x2, waiting for transfers between devices, shards(): lax.all_to_all(chunks, everyone, split_axis=0, concat_axis=0, tiled=True)  20.1 us
    all_to_all x1, blocking collectives, shards(): lax.all_to_all(framed, 'gy', split_axis=0, concat_axis=0, tiled=True)  17.2 us
    all_to_all x2, starting transfers between devices, shards(): lax.all_to_all(chunks, everyone, split_axis=0, concat_axis=0, tiled=True)  15.3 us
    all_to_all x1, blocking collectives, shards(): lax.all_to_all(scaled, 'gy', split_axis=0, concat_axis=1, tiled=True)  13.7 us
    ppermute x2, starting transfers between devices, edge_pair(): lax.ppermute(last, axis, forward)  9.3 us
    pallas_call x2, Pallas kernels, framed_stencil(): pl.pallas_call(framed_kernel, out_shape=(shape, shape), in_specs=[vmem] *...  8.09 us
  transfers between devices with their start and end apart: 12, of which 5 were waited for; matrix products, arithmetic and copies ran while one was open for 22% of the time, Pallas kernels for 1%

profile of v12, /device:TPU:3, one launch (start us, length us, event | category | flops | bytes accessed | tf_op | source)
XLA Modules:
  0.0 237.1 jit_solution(10721118160815671088)
XLA Ops:
  2.7 6.6 %all-to-all-start = ((f32[16,64,128]{2,1,0:T(8,128)}), f32[16,64,128]{2,1,0:T(8,128)S(1)}, u32[]{:S(2)}, u32[]{:S(2)}) async-start(f32[16,64,128]{2,1,0:T(8,128)} %multiply_multiply_fusion.1), calls=%async_computation | async-start | bytes 1048576 | tf_op jit(solution)/shard_map/all_to_all | solution.py:195
  11.2 5.2 %collective-permute-start.4 = (f32[2,16,64]{2,1,0:T(8,128)S(1)}, f32[2,16,64]{2,1,0:T(8,128)S(1)}, u32[]{:S(2)}, u32[]{:S(2)}) collective-permute-start(f32[2,16,64]{2,1,0:T(8,128)S(1)} %get-tuple-element.14), channel_id=1, source_target_pairs={{0,16},{16,32},{32,48},{48,64},{64,80},{80,96},{96,112},{1,17},{17... | collective-permute-start | bytes 24584 | tf_op jit(solution)/shard_map/ppermute | solution.py:20
  21.7 2.8 %copy.100 = f32[2,16,1,128]{3,1,0,2:T(8,128)S(1)} copy(f32[2,16,1,128]{2,1,0,3:T(8,128)} %get-tuple-element.17) | data formatting | bytes 32768 | tf_op jit(solution)/shard_map/slice | solution.py:18
  24.5 4.1 %collective-permute-start.2 = (f32[2,16,128]{2,1,0:T(8,128)S(1)}, f32[2,16,128]{2,1,0:T(8,128)S(1)}, u32[]{:S(2)}, u32[]{:S(2)}) collective-permute-start(f32[2,16,128]{2,1,0:T(8,128)S(1)} %bitcast.233), channel_id=1, source_target_pairs={{0,1},{1,2},{2,3},{3,4},{4,5},{5,6},{6,7},{7,8},{8,9},{9,10},{10,1... | collective-permute-start | bytes 49160 | tf_op jit(solution)/shard_map/ppermute | solution.py:20
  32.8 5.3 %reduce-precision_convert_fusion.1 = (bf16[1024,1024]{1,0:T(8,128)(2,1)}, bf16[1024,1024]{1,0:T(8,128)(2,1)}) fusion(f32[1024,1024]{1,0:T(8,128)} %param.14), kind=kLoop, calls=%fused_computation.3 | loop fusion | flops 4194304 | bytes 8388608 | tf_op jit(solution)/shard_map/convert_element_type | solution.py:146
  45.9 10.2 %all-to-all-start.1 = ((f32[128,8,128]{2,1,0:T(8,128)}), f32[128,8,128]{2,1,0:T(8,128)S(1)}, u32[]{:S(2)}, u32[]{:S(2)}) async-start(f32[128,8,128]{2,1,0:T(8,128)} %bitcast.222), calls=%async_computation.1 | async-start | bytes 1048576 | tf_op jit(solution)/shard_map/all_to_all | solution.py:199
  58.5 10.4 %all-to-all-done.1 = f32[128,8,128]{2,1,0:T(8,128)S(1)} async-done(((f32[128,8,128]{2,1,0:T(8,128)}), f32[128,8,128]{2,1,0:T(8,128)S(1)}, u32[]{:S(2)}, u32[]{:S(2)}) %all-to-all-start.1) | async-done | bytes 524320 | tf_op jit(solution)/shard_map/all_to_all | solution.py:199
  79.9 5.1 %all-to-all-start.2 = ((f32[128,8,128]{2,1,0:T(8,128)}), f32[128,8,128]{2,1,0:T(8,128)S(1)}, u32[]{:S(2)}, u32[]{:S(2)}) async-start(f32[128,8,128]{2,1,0:T(8,128)} %bitcast.223), calls=%async_computation.2 | async-start | bytes 1048576 | tf_op jit(solution)/shard_map/all_to_all | solution.py:205
  88.5 9.7 %all-to-all-done.2 = f32[128,8,128]{2,1,0:T(8,128)S(1)} async-done(((f32[128,8,128]{2,1,0:T(8,128)}), f32[128,8,128]{2,1,0:T(8,128)S(1)}, u32[]{:S(2)}, u32[]{:S(2)}) %all-to-all-start.2) | async-done | bytes 524320 | tf_op jit(solution)/shard_map/all_to_all | solution.py:205
  108.1 3.3 %collective-permute-start.1 = (f32[16,64]{1,0:T(8,128)S(1)}, f32[16,64]{1,0:T(8,128)S(1)}, u32[]{:S(2)}, u32[]{:S(2)}) collective-permute-start(f32[16,64]{1,0:T(8,128)S(1)} %bitcast.236), channel_id=1, source_target_pairs={{16,0},{32,16},{48,32},{64,48},{80,64},{96,80},{112,96},{17,1},{33... | collective-permute-start | bytes 12296 | tf_op jit(solution)/shard_map/ppermute | solution.py:210
  111.3 3.5 %collective-permute-start = (f32[16,64]{1,0:T(8,128)S(1)}, f32[16,64]{1,0:T(8,128)S(1)}, u32[]{:S(2)}, u32[]{:S(2)}) collective-permute-start(f32[16,64]{1,0:T(8,128)S(1)} %bitcast.234), channel_id=1, source_target_pairs={{0,16},{16,32},{32,48},{48,64},{64,80},{80,96},{96,112},{1,17},{17... | collective-permute-start | bytes 12296 | tf_op jit(solution)/shard_map/ppermute | solution.py:209
  114.9 3.2 %collective-permute-done = f32[16,64]{1,0:T(8,128)S(1)} collective-permute-done((f32[16,64]{1,0:T(8,128)S(1)}, f32[16,64]{1,0:T(8,128)S(1)}, u32[]{:S(2)}, u32[]{:S(2)}) %collective-permute-start) | collective-permute-done | bytes 4128 | tf_op jit(solution)/shard_map/ppermute | solution.py:209
  119.1 6.1 %all-to-all-start.3 = ((f32[16,67,128]{2,1,0:T(8,128)}), f32[16,67,128]{2,1,0:T(8,128)S(1)}, u32[]{:S(2)}, u32[]{:S(2)}) async-start(f32[16,67,128]{2,1,0:T(8,128)} %fusion.24), calls=%async_computation.3 | async-start | bytes 1179648 | tf_op jit(solution)/shard_map/all_to_all | solution.py:216
  125.9 4.6 %add_divide_fusion = (f32[16,64,128]{2,1,0:T(8,128)}, f32[16,64,128]{2,1,0:T(8,128)}, f32[16,64,128]{2,1,0:T(8,128)}, f32[16,64,128]{2,1,0:T(8,128)}, f32[16,64,128]{2,1,0:T(8,128)}, /*index=5*/f32[16,64,128]{2,1,0:T(8,128)}) fusion(f32[16,64,128]{2,1,0:T(8,128)S(1)} %copy-done.6, f32[16,64,127]{2,1,0:T(8,128)} %get-tuple-element.32, ...), kind=kLoop, calls=%fused_computation.90 | loop fusion | flops 3014656 | bytes 6750208 | tf_op jit(solution)/shard_map/div | solution.py:28
  130.5 5.0 %all-to-all-done.3.framed_ref = f32[16,67,128]{2,1,0:T(8,128)S(1)} async-done(((f32[16,67,128]{2,1,0:T(8,128)}), f32[16,67,128]{2,1,0:T(8,128)S(1)}, u32[]{:S(2)}, u32[]{:S(2)}) %all-to-all-start.3) | async-done | bytes 548896 | tf_op jit(solution)/shard_map/all_to_all | solution.py:216
  136.3 4.0 %shard_map.123 = (f32[16,64,128]{2,1,0:T(8,128)}, f32[16,64,128]{2,1,0:T(8,128)}) custom-call(f32[16,67,128]{2,1,0:T(8,128)} %copy-done.13, f32[16,64,128]{2,1,0:T(8,128)} %copy-done.9, f32[16,64,128]{2,1,0:T(8,128)} %residual_ref.1, f32[16,128]{1,0:T(8,128)} %get-tuple-element.51.refs_0_.refs_1_, f32[16,128]{1,0:T(8,128)} %get-tuple-element.53.refs_1_.refs_2_, ...), custom_call_target="tpu_custom_call" | custom-call | tf_op jit(solution)/shard_map/pallas_call | solution.py:103
  141.6 13.7 %all_to_all.54 = f32[16,64,128]{2,1,0:T(8,128)S(1)} all-to-all(f32[16,64,128]{2,1,0:T(8,128)S(1)} %multiply_multiply_fusion), channel_id=1, replica_groups=mesh['gx'=8,'gy'=16] {'gy'}, dimensions={0} | all-to-all | bytes 1048576 | tf_op jit(solution)/shard_map/all_to_all | solution.py:195
  158.1 17.9 %all_to_all.55 = f32[128,8,128]{2,1,0:T(8,128)S(1)} all-to-all(f32[128,8,128]{2,1,0:T(8,128)S(1)} %bitcast.224), channel_id=1, replica_groups=mesh['gx'=8,'gy'=16] {'gx','gy'}, dimensions={0} | all-to-all | bytes 1048576 | tf_op jit(solution)/shard_map/all_to_all | solution.py:199
  184.6 17.5 %all_to_all.56 = f32[128,8,128]{2,1,0:T(8,128)S(1)} all-to-all(f32[128,8,128]{2,1,0:T(8,128)S(1)} %bitcast.225), channel_id=1, replica_groups=mesh['gx'=8,'gy'=16] {'gx','gy'}, dimensions={0} | all-to-all | bytes 1048576 | tf_op jit(solution)/shard_map/all_to_all | solution.py:205
  205.5 3.3 %collective-permute-start.7 = (f32[16,64]{1,0:T(8,128)S(1)}, f32[16,64]{1,0:T(8,128)S(1)}, u32[]{:S(2)}, u32[]{:S(2)}) collective-permute-start(f32[16,64]{1,0:T(8,128)S(1)} %bitcast.237), channel_id=1, source_target_pairs={{16,0},{32,16},{48,32},{64,48},{80,64},{96,80},{112,96},{17,1},{33... | collective-permute-start | bytes 12296 | tf_op jit(solution)/shard_map/ppermute | solution.py:210
  208.8 3.5 %collective-permute-start.6 = (f32[16,64]{1,0:T(8,128)S(1)}, f32[16,64]{1,0:T(8,128)S(1)}, u32[]{:S(2)}, u32[]{:S(2)}) collective-permute-start(f32[16,64]{1,0:T(8,128)S(1)} %bitcast.235), channel_id=1, source_target_pairs={{0,16},{16,32},{32,48},{48,64},{64,80},{80,96},{96,112},{1,17},{17... | collective-permute-start | bytes 12296 | tf_op jit(solution)/shard_map/ppermute | solution.py:209
  212.3 3.2 %collective-permute-done.6 = f32[16,64]{1,0:T(8,128)S(1)} collective-permute-done((f32[16,64]{1,0:T(8,128)S(1)}, f32[16,64]{1,0:T(8,128)S(1)}, u32[]{:S(2)}, u32[]{:S(2)}) %collective-permute-start.6) | collective-permute-done | bytes 4128 | tf_op jit(solution)/shard_map/ppermute | solution.py:209
  215.7 17.2 %all_to_all.57.framed_ref = f32[16,67,128]{2,1,0:T(8,128)} all-to-all(f32[16,67,128]{2,1,0:T(8,128)S(1)} %fusion.20), channel_id=1, replica_groups=mesh['gx'=8,'gy'=16] {'gy'}, dimensions={0} | all-to-all | bytes 1097728 | tf_op jit(solution)/shard_map/all_to_all | solution.py:216
  232.9 4.1 %shard_map.125 = (f32[16,64,128]{2,1,0:T(8,128)}, f32[16,64,128]{2,1,0:T(8,128)}) custom-call(f32[16,67,128]{2,1,0:T(8,128)} %all_to_all.57.framed_ref, f32[16,64,128]{2,1,0:T(8,128)} %copy-done.9, f32[16,64,128]{2,1,0:T(8,128)} %get-tuple-element.6.residual_ref, f32[16,64,128]{2,1,0:T(8,128)} %get-tuple-element.7.refs_0_, ...), custom_call_target="tpu_custom_call" | custom-call | tf_op jit(solution)/shard_map/pallas_call | solution.py:103
  (114 shorter events, 66.4 us)
Async XLA Ops:
  0.6 8.7 %copy-start.14 = (s32[16,64,128]{2,1,0:T(8,128)S(1)}, s32[16,64,128]{2,1,0:T(8,128)}, u32[]{:S(2)}) copy-start(s32[16,64,128]{2,1,0:T(8,128)} %param.13) | copy-start | bytes 1572868
  2.7 8.0 %copy-start.6 = (f32[16,64,128]{2,1,0:T(8,128)S(1)}, f32[16,64,128]{2,1,0:T(8,128)}, u32[]{:S(2)}) copy-start(f32[16,64,128]{2,1,0:T(8,128)} %param.12) | copy-start | bytes 1572868
  2.7 38.9 %all-to-all-start = ((f32[16,64,128]{2,1,0:T(8,128)}), f32[16,64,128]{2,1,0:T(8,128)S(1)}, u32[]{:S(2)}, u32[]{:S(2)}) async-start(f32[16,64,128]{2,1,0:T(8,128)} %multiply_multiply_fusion.1), calls=%async_computation | async-start | bytes 1048576 | tf_op jit(solution)/shard_map/all_to_all | solution.py:195
  11.2 47.3 %collective-permute-start.4 = (f32[2,16,64]{2,1,0:T(8,128)S(1)}, f32[2,16,64]{2,1,0:T(8,128)S(1)}, u32[]{:S(2)}, u32[]{:S(2)}) collective-permute-start(f32[2,16,64]{2,1,0:T(8,128)S(1)} %get-tuple-element.14), channel_id=1, source_target_pairs={{0,16},{16,32},{32,48},{48,64},{64,80},{80,96},{96,112},{1,17},{17... | collective-permute-start | bytes 24584 | tf_op jit(solution)/shard_map/ppermute | solution.py:20
  16.5 68.6 %collective-permute-start.5 = (f32[2,16,64]{2,1,0:T(8,128)S(1)}, f32[2,16,64]{2,1,0:T(8,128)S(1)}, u32[]{:S(2)}, u32[]{:S(2)}) collective-permute-start(f32[2,16,64]{2,1,0:T(8,128)S(1)} %get-tuple-element.15), channel_id=1, source_target_pairs={{16,0},{32,16},{48,32},{64,48},{80,64},{96,80},{112,96},{17,1},{33... | collective-permute-start | bytes 24584 | tf_op jit(solution)/shard_map/ppermute | solution.py:20
  21.6 6.9 %copy-start.8 = (f32[2,16,1,128]{2,1,0,3:T(8,128)S(1)}, f32[2,16,1,128]{2,1,0,3:T(8,128)}, u32[]{:S(2)}) copy-start(f32[2,16,1,128]{2,1,0,3:T(8,128)} %get-tuple-element.16) | copy-start | bytes 49156
  24.5 63.4 %collective-permute-start.2 = (f32[2,16,128]{2,1,0:T(8,128)S(1)}, f32[2,16,128]{2,1,0:T(8,128)S(1)}, u32[]{:S(2)}, u32[]{:S(2)}) collective-permute-start(f32[2,16,128]{2,1,0:T(8,128)S(1)} %bitcast.233), channel_id=1, source_target_pairs={{0,1},{1,2},{2,3},{3,4},{4,5},{5,6},{6,7},{7,8},{8,9},{9,10},{10,1... | collective-permute-start | bytes 49160 | tf_op jit(solution)/shard_map/ppermute | solution.py:20
  29.9 95.4 %collective-permute-start.3 = (f32[2,16,128]{2,1,0:T(8,128)S(1)}, f32[2,16,128]{2,1,0:T(8,128)S(1)}, u32[]{:S(2)}, u32[]{:S(2)}) collective-permute-start(f32[2,16,128]{2,1,0:T(8,128)S(1)} %bitcast.232), channel_id=1, source_target_pairs={{1,0},{2,1},{3,2},{4,3},{5,4},{6,5},{7,6},{8,7},{9,8},{10,9},{11,1... | collective-permute-start | bytes 49160 | tf_op jit(solution)/shard_map/ppermute | solution.py:20
  32.8 6.4 %copy-start.12 = (f32[1024,1024]{1,0:T(8,128)S(1)}, f32[1024,1024]{1,0:T(8,128)}, u32[]{:S(2)}) copy-start(f32[1024,1024]{1,0:T(8,128)} %param.17) | copy-start | bytes 12582916
  44.9 13.0 %copy-start.15 = (f32[1024]{0:T(1024)S(1)}, f32[1024]{0:T(1024)}, u32[]{:S(2)}) copy-start(f32[1024]{0:T(1024)} %param.19) | copy-start | bytes 12292
  45.9 23.1 %all-to-all-start.1 = ((f32[128,8,128]{2,1,0:T(8,128)}), f32[128,8,128]{2,1,0:T(8,128)S(1)}, u32[]{:S(2)}, u32[]{:S(2)}) async-start(f32[128,8,128]{2,1,0:T(8,128)} %bitcast.222), calls=%async_computation.1 | async-start | bytes 1048576 | tf_op jit(solution)/shard_map/all_to_all | solution.py:199
  79.9 18.2 %all-to-all-start.2 = ((f32[128,8,128]{2,1,0:T(8,128)}), f32[128,8,128]{2,1,0:T(8,128)S(1)}, u32[]{:S(2)}, u32[]{:S(2)}) async-start(f32[128,8,128]{2,1,0:T(8,128)} %bitcast.223), calls=%async_computation.2 | async-start | bytes 1048576 | tf_op jit(solution)/shard_map/all_to_all | solution.py:205
  98.1 2.6 %copy-start.1 = (bf16[1024,1024]{1,0:T(8,128)(2,1)S(1)}, bf16[1024,1024]{1,0:T(8,128)(2,1)}, u32[]{:S(2)}) copy-start(bf16[1024,1024]{1,0:T(8,128)(2,1)} %get-tuple-element.12) | copy-start | bytes 6291460
  108.1 6.8 %collective-permute-start.1 = (f32[16,64]{1,0:T(8,128)S(1)}, f32[16,64]{1,0:T(8,128)S(1)}, u32[]{:S(2)}, u32[]{:S(2)}) collective-permute-start(f32[16,64]{1,0:T(8,128)S(1)} %bitcast.236), channel_id=1, source_target_pairs={{16,0},{32,16},{48,32},{64,48},{80,64},{96,80},{112,96},{17,1},{33... | collective-permute-start | bytes 12296 | tf_op jit(solution)/shard_map/ppermute | solution.py:210
  111.3 6.8 %collective-permute-start = (f32[16,64]{1,0:T(8,128)S(1)}, f32[16,64]{1,0:T(8,128)S(1)}, u32[]{:S(2)}, u32[]{:S(2)}) collective-permute-start(f32[16,64]{1,0:T(8,128)S(1)} %bitcast.234), channel_id=1, source_target_pairs={{0,16},{16,32},{32,48},{48,64},{64,80},{80,96},{96,112},{1,17},{17... | collective-permute-start | bytes 12296 | tf_op jit(solution)/shard_map/ppermute | solution.py:209
  119.1 16.4 %all-to-all-start.3 = ((f32[16,67,128]{2,1,0:T(8,128)}), f32[16,67,128]{2,1,0:T(8,128)S(1)}, u32[]{:S(2)}, u32[]{:S(2)}) async-start(f32[16,67,128]{2,1,0:T(8,128)} %fusion.24), calls=%async_computation.3 | async-start | bytes 1179648 | tf_op jit(solution)/shard_map/all_to_all | solution.py:216
  136.3 4.0 %copy-start.16 = (f32[128]{0:T(128)S(1)}, f32[128]{0:T(128)}, u32[]{:S(2)}) copy-start(f32[128]{0:T(128)} %param.18) | copy-start | bytes 1540
  136.3 4.0 %copy-start.17 = (f32[64]{0:T(128)S(1)}, f32[64]{0:T(128)}, u32[]{:S(2)}) copy-start(f32[64]{0:T(128)} %param.15) | copy-start | bytes 772
  140.2 15.1 %copy-start.4 = (bf16[1024,1024]{1,0:T(8,128)(2,1)S(1)}, bf16[1024,1024]{1,0:T(8,128)(2,1)}, u32[]{:S(2)}) copy-start(bf16[1024,1024]{1,0:T(8,128)(2,1)} %get-tuple-element.13) | copy-start | bytes 6291460
  158.1 18.0 %copy-start.7 = (bf16[1024,1024]{1,0:T(8,128)(2,1)S(1)}, bf16[1024,1024]{1,0:T(8,128)(2,1)}, u32[]{:S(2)}) copy-start(bf16[1024,1024]{1,0:T(8,128)(2,1)} %get-tuple-element.11) | copy-start | bytes 6291460
  183.7 18.4 %copy-start.5 = (bf16[1024,1024]{1,0:T(8,128)(2,1)S(1)}, bf16[1024,1024]{1,0:T(8,128)(2,1)}, u32[]{:S(2)}) copy-start(bf16[1024,1024]{1,0:T(8,128)(2,1)} %get-tuple-element.13) | copy-start | bytes 6291460
  184.6 18.4 %copy-start.3 = (bf16[1024,1024]{1,0:T(8,128)(2,1)S(1)}, bf16[1024,1024]{1,0:T(8,128)(2,1)}, u32[]{:S(2)}) copy-start(bf16[1024,1024]{1,0:T(8,128)(2,1)} %get-tuple-element.12) | copy-start | bytes 6291460
  205.5 6.8 %collective-permute-start.7 = (f32[16,64]{1,0:T(8,128)S(1)}, f32[16,64]{1,0:T(8,128)S(1)}, u32[]{:S(2)}, u32[]{:S(2)}) collective-permute-start(f32[16,64]{1,0:T(8,128)S(1)} %bitcast.237), channel_id=1, source_target_pairs={{16,0},{32,16},{48,32},{64,48},{80,64},{96,80},{112,96},{17,1},{33... | collective-permute-start | bytes 12296 | tf_op jit(solution)/shard_map/ppermute | solution.py:210
  208.8 6.8 %collective-permute-start.6 = (f32[16,64]{1,0:T(8,128)S(1)}, f32[16,64]{1,0:T(8,128)S(1)}, u32[]{:S(2)}, u32[]{:S(2)}) collective-permute-start(f32[16,64]{1,0:T(8,128)S(1)} %bitcast.235), channel_id=1, source_target_pairs={{0,16},{16,32},{32,48},{48,64},{64,80},{80,96},{96,112},{1,17},{17... | collective-permute-start | bytes 12296 | tf_op jit(solution)/shard_map/ppermute | solution.py:209
  (6 other events, 10.6 us)

commit v13 on v10

--- a/solution.py
+++ b/solution.py
@@ -1,3 +1,5 @@
+import functools
+
 import jax
 import jax.numpy as jnp
 from jax import lax
@@ -45,13 +47,14 @@
     return [harmonic(center, other) for other in neighbours(center, strips)]
 
 
-def framed_kernel(framed_ref, active_ref, residual_ref, *refs):
-    if len(refs) == 12:
-        adjoint_ref = None
-    else:
-        adjoint_ref, refs = refs[0], refs[1:]
+def framed_kernel(has_adjoint, has_scale, framed_ref, active_ref, residual_ref, *refs):
+    refs = list(refs)
+    adjoint_ref = refs.pop(0) if has_adjoint else None
     x_low_ref, x_high_ref, y_low_ref, y_high_ref = refs[:4]
-    face_refs, residual_out, adjoint_out = refs[4:-2], refs[-2], refs[-1]
+    refs = refs[4:]
+    mass_x_ref, mass_y_ref = (refs.pop(0), refs.pop(0)) if has_scale else (None, None)
+    scaled_out = refs.pop() if has_scale else None
+    face_refs, residual_out, adjoint_out = refs[:-2], refs[-2], refs[-1]
     planes, rows, cols = active_ref.shape
     row = lax.broadcasted_iota(jnp.int32, (rows, cols), 0)
     col = lax.broadcasted_iota(jnp.int32, (rows, cols), 1)
@@ -83,21 +86,26 @@
         for face_ref, other in zip(face_refs, others):
             result = result + face_ref[z] * (center - other)
         update = updates[z]
-        residual_out[z] = residual_ref[z] - (result + (1.0 - active_ref[z]) * update)
+        residual = residual_ref[z] - (result + (1.0 - active_ref[z]) * update)
+        residual_out[z] = residual
+        if has_scale:
+            scaled_out[z] = residual * mass_x_ref[...] * mass_y_ref[...]
         adjoint_out[z] = update if adjoint_ref is None else adjoint_ref[z] + update
 
 
-def framed_stencil(framed, active, residual, adjoint, x_strips, y_strips, faces):
+def framed_stencil(framed, active, residual, adjoint, x_strips, y_strips, faces, masses=None):
     vmem = pl.BlockSpec(memory_space=pltpu.VMEM)
     shape = jax.ShapeDtypeStruct(active.shape, active.dtype)
     y_low, y_high = (jnp.broadcast_to(strip[:, :, None], active.shape) for strip in y_strips)
     carried = [] if adjoint is None else [adjoint]
-    operands = [framed, active, residual, *carried, x_strips[0], x_strips[1], y_low, y_high, *faces]
+    scales = [] if masses is None else list(masses)
+    operands = [framed, active, residual, *carried, x_strips[0], x_strips[1], y_low, y_high, *scales, *faces]
+    outputs = 2 if masses is None else 3
     return pl.pallas_call(
-        framed_kernel,
-        out_shape=(shape, shape),
+        functools.partial(framed_kernel, adjoint is not None, masses is not None),
+        out_shape=(shape,) * outputs,
         in_specs=[vmem] * len(operands),
-        out_specs=(vmem, vmem),
+        out_specs=(vmem,) * outputs,
     )(*operands)
 
 
@@ -180,8 +188,13 @@
     forward_y = [(i, i + 1) for i in range(count_y - 1)]
     backward_y = [(target, source) for source, target in forward_y]
     basis_y = tuple(piece.reshape(blocks_y, -1, vectors_y.shape[1]) for piece in split_bf16(vectors_y))
+    rows_of, cols_of = right_side.shape[1], right_side.shape[2]
+    masses = (
+        jnp.broadcast_to(mass_x[:, None], (rows_of, cols_of)),
+        jnp.broadcast_to(mass_y[None, :], (rows_of, cols_of)),
+    )
+    scaled = residual * mass_x[None, :, None] * mass_y[None, None, :]
     for iteration in range(ITERS):
-        scaled = residual * mass_x[None, :, None] * mass_y[None, None, :]
         modes = transform(
             "zxy,xi->ziy",
             lax.all_to_all(scaled, "gy", split_axis=0, concat_axis=1, tiled=True),
@@ -207,7 +220,12 @@
         framed = jnp.concatenate([below, blocks, above, halo_row], axis=1)
         framed = lax.all_to_all(framed, "gy", split_axis=0, concat_axis=0, tiled=True)
         y_strips = (active_y[0] * framed[:, -1, :rows], active_y[1] * framed[:, -1, rows:])
-        residual, adjoint = framed_stencil(framed, active, residual, adjoint, active_x, y_strips, faces)
+        if iteration + 1 < ITERS:
+            residual, adjoint, scaled = framed_stencil(
+                framed, active, residual, adjoint, active_x, y_strips, faces, masses
+            )
+        else:
+            residual, adjoint = framed_stencil(framed, active, residual, adjoint, active_x, y_strips, faces)
     return (adjoint, residual)
 
 

time: 234 us -> 236 us (level)
  transfers between devices with their start and end apart: 12 -> 12, of which waited for: 5 -> 5; matrix products, arithmetic and copies ran while one was open for 21% -> 20% of each run, Pallas kernels for 1% -> 1%
where the time goes in v13:
time: 236 us; the launch traced here: 235 us
  blocking collectives  66.6 us (28%)
  starting transfers between devices  56.1 us (24%)
  waiting for transfers between devices  29.5 us (12%)
  matrix products  26.9 us (11%)
  local copies, waits for them, and re-layouts  21.8 us (9%)
  other arithmetic  19.7 us (8%)
  Pallas kernels  12.7 us (5%)
    all_to_all x2, blocking collectives, shards(): lax.all_to_all(chunks, everyone, split_axis=0, concat_axis=0, tiled=True)  35.4 us
    dot_general x24, matrix products, product(): return jnp.einsum(spec, first, second, preferred_element_type=jnp.float32)  26.9 us
    all_to_all x2, waiting for transfers between devices, shards(): lax.all_to_all(chunks, everyone, split_axis=0, concat_axis=0, tiled=True)  18.1 us
    all_to_all x2, starting transfers between devices, shards(): lax.all_to_all(chunks, everyone, split_axis=0, concat_axis=0, tiled=True)  17.1 us
    all_to_all x1, blocking collectives, shards(): lax.all_to_all(framed, 'gy', split_axis=0, concat_axis=0, tiled=True)  16.5 us
    all_to_all x1, blocking collectives, shards(): lax.all_to_all(scaled, 'gy', split_axis=0, concat_axis=1, tiled=True)  14.7 us
    convert_element_type x2, other arithmetic, split_bf16(): rounded.astype(jnp.bfloat16)  8.92 us
    pallas_call x2, Pallas kernels, framed_stencil(): pl.pallas_call(functools.partial(framed_kernel, adjoint is not None, mass...  8.59 us
  transfers between devices with their start and end apart: 12, of which 5 were waited for; matrix products, arithmetic and copies ran while one was open for 20% of the time, Pallas kernels for 1%

profile of v13, /device:TPU:3, one launch (start us, length us, event | category | flops | bytes accessed | tf_op | source)
XLA Modules:
  0.0 234.5 jit_solution(12402739222384201146)
XLA Ops:
  2.7 6.5 %all-to-all-start = ((f32[16,64,128]{2,1,0:T(8,128)}), f32[16,64,128]{2,1,0:T(8,128)S(1)}, u32[]{:S(2)}, u32[]{:S(2)}) async-start(f32[16,64,128]{2,1,0:T(8,128)} %multiply_multiply_fusion), calls=%async_computation | async-start | bytes 1048576 | tf_op jit(solution)/shard_map/all_to_all | solution.py:200
  10.2 3.5 %collective-permute-start.2 = (f32[2,16,128]{2,1,0:T(8,128)S(1)}, f32[2,16,128]{2,1,0:T(8,128)S(1)}, u32[]{:S(2)}, u32[]{:S(2)}) collective-permute-start(f32[2,16,128]{2,1,0:T(8,128)S(1)} %bitcast.247), channel_id=1, source_target_pairs={{0,1},{1,2},{2,3},{3,4},{4,5},{5,6},{6,7},{7,8},{8,9},{9,10},{10,1... | collective-permute-start | bytes 49160 | tf_op jit(solution)/shard_map/ppermute | solution.py:22
  16.6 5.2 %collective-permute-start.5 = (f32[2,16,64]{2,1,0:T(8,128)S(1)}, f32[2,16,64]{2,1,0:T(8,128)S(1)}, u32[]{:S(2)}, u32[]{:S(2)}) collective-permute-start(f32[2,16,64]{2,1,0:T(8,128)S(1)} %get-tuple-element.12), channel_id=1, source_target_pairs={{16,0},{32,16},{48,32},{64,48},{80,64},{96,80},{112,96},{17,1},{33... | collective-permute-start | bytes 24584 | tf_op jit(solution)/shard_map/ppermute | solution.py:22
  27.8 4.4 %reduce-precision_convert_fusion.1 = (bf16[1024,1024]{1,0:T(8,128)(2,1)S(1)}, bf16[1024,1024]{1,0:T(8,128)(2,1)}) fusion(f32[1024,1024]{1,0:T(8,128)} %param.14), kind=kLoop, calls=%fused_computation.3 | loop fusion | flops 4194304 | bytes 8388608 | tf_op jit(solution)/shard_map/convert_element_type | solution.py:147
  37.1 12.2 %all-to-all-start.1 = ((f32[128,8,128]{2,1,0:T(8,128)}), f32[128,8,128]{2,1,0:T(8,128)S(1)}, u32[]{:S(2)}, u32[]{:S(2)}) async-start(f32[128,8,128]{2,1,0:T(8,128)} %bitcast.3), calls=%async_computation.1 | async-start | bytes 1048576 | tf_op jit(solution)/shard_map/all_to_all | solution.py:204
  49.9 4.5 %reduce-precision_convert_fusion = (bf16[1024,1024]{1,0:T(8,128)(2,1)S(1)}, bf16[1024,1024]{1,0:T(8,128)(2,1)}) fusion(f32[1024,1024]{1,0:T(8,128)} %param.17), kind=kLoop, calls=%fused_computation.1 | loop fusion | flops 4194304 | bytes 8388608 | tf_op jit(solution)/shard_map/convert_element_type | solution.py:147
  54.4 7.8 %all-to-all-done.1 = f32[128,8,128]{2,1,0:T(8,128)S(1)} async-done(((f32[128,8,128]{2,1,0:T(8,128)}), f32[128,8,128]{2,1,0:T(8,128)S(1)}, u32[]{:S(2)}, u32[]{:S(2)}) %all-to-all-start.1) | async-done | bytes 524320 | tf_op jit(solution)/shard_map/all_to_all | solution.py:204
  73.2 4.9 %all-to-all-start.2 = ((f32[128,8,128]{2,1,0:T(8,128)}), f32[128,8,128]{2,1,0:T(8,128)S(1)}, u32[]{:S(2)}, u32[]{:S(2)}) async-start(f32[128,8,128]{2,1,0:T(8,128)} %bitcast.233), calls=%async_computation.2 | async-start | bytes 1048576 | tf_op jit(solution)/shard_map/all_to_all | solution.py:210
  80.8 10.3 %all-to-all-done.2 = f32[128,8,128]{2,1,0:T(8,128)S(1)} async-done(((f32[128,8,128]{2,1,0:T(8,128)}), f32[128,8,128]{2,1,0:T(8,128)S(1)}, u32[]{:S(2)}, u32[]{:S(2)}) %all-to-all-start.2) | async-done | bytes 524320 | tf_op jit(solution)/shard_map/all_to_all | solution.py:210
  101.1 3.3 %collective-permute-start.1 = (f32[16,64]{1,0:T(8,128)S(1)}, f32[16,64]{1,0:T(8,128)S(1)}, u32[]{:S(2)}, u32[]{:S(2)}) collective-permute-start(f32[16,64]{1,0:T(8,128)S(1)} %bitcast.250), channel_id=1, source_target_pairs={{16,0},{32,16},{48,32},{64,48},{80,64},{96,80},{112,96},{17,1},{33... | collective-permute-start | bytes 12296 | tf_op jit(solution)/shard_map/ppermute | solution.py:215
  104.4 3.5 %collective-permute-start = (f32[16,64]{1,0:T(8,128)S(1)}, f32[16,64]{1,0:T(8,128)S(1)}, u32[]{:S(2)}, u32[]{:S(2)}) collective-permute-start(f32[16,64]{1,0:T(8,128)S(1)} %bitcast.248), channel_id=1, source_target_pairs={{0,16},{16,32},{32,48},{48,64},{64,80},{80,96},{96,112},{1,17},{17... | collective-permute-start | bytes 12296 | tf_op jit(solution)/shard_map/ppermute | solution.py:214
  107.9 3.2 %collective-permute-done = f32[16,64]{1,0:T(8,128)S(1)} collective-permute-done((f32[16,64]{1,0:T(8,128)S(1)}, f32[16,64]{1,0:T(8,128)S(1)}, u32[]{:S(2)}, u32[]{:S(2)}) %collective-permute-start) | collective-permute-done | bytes 4128 | tf_op jit(solution)/shard_map/ppermute | solution.py:214
  112.2 6.3 %all-to-all-start.3 = ((f32[16,67,128]{2,1,0:T(8,128)}), f32[16,67,128]{2,1,0:T(8,128)S(1)}, u32[]{:S(2)}, u32[]{:S(2)}) async-start(f32[16,67,128]{2,1,0:T(8,128)} %fusion.23), calls=%async_computation.3 | async-start | bytes 1179648 | tf_op jit(solution)/shard_map/all_to_all | solution.py:221
  119.1 4.7 %add_divide_fusion = (f32[16,64,128]{2,1,0:T(8,128)}, f32[16,64,128]{2,1,0:T(8,128)}, f32[16,64,128]{2,1,0:T(8,128)}, f32[16,64,128]{2,1,0:T(8,128)}, f32[16,64,128]{2,1,0:T(8,128)}, /*index=5*/f32[16,64,128]{2,1,0:T(8,128)}) fusion(f32[16,64,128]{2,1,0:T(8,128)S(1)} %copy-done.6, f32[16,64,127]{2,1,0:T(8,128)} %get-tuple-element.38, ...), kind=kLoop, calls=%fused_computation.84 | loop fusion | flops 3014656 | bytes 6750208 | tf_op jit(solution)/shard_map/div | solution.py:30
  123.8 4.9 %all-to-all-done.3.framed_ref = f32[16,67,128]{2,1,0:T(8,128)S(1)} async-done(((f32[16,67,128]{2,1,0:T(8,128)}), f32[16,67,128]{2,1,0:T(8,128)S(1)}, u32[]{:S(2)}, u32[]{:S(2)}) %all-to-all-start.3) | async-done | bytes 548896 | tf_op jit(solution)/shard_map/all_to_all | solution.py:221
  132.1 4.3 %shard_map.123 = (f32[16,64,128]{2,1,0:T(8,128)}, f32[16,64,128]{2,1,0:T(8,128)}, f32[16,64,128]{2,1,0:T(8,128)}) custom-call(f32[16,67,128]{2,1,0:T(8,128)} %copy-done.10, f32[16,64,128]{2,1,0:T(8,128)} %get-tuple-element.45.active_ref, f32[16,64,128]{2,1,0:T(8,128)} %residual_ref.1, f32[16,128]{1,0:T(8,128)} %get-tuple-element.55.refs_0_.refs_1_, ...), custom_call_target="tpu_custom_call" | custom-call | tf_op jit(solution)/shard_map/pallas_call | solution.py:104
  136.5 14.7 %all_to_all.54 = f32[16,64,128]{2,1,0:T(8,128)S(1)} all-to-all(f32[16,64,128]{2,1,0:T(8,128)} %get-tuple-element.7), channel_id=1, replica_groups=mesh['gx'=8,'gy'=16] {'gy'}, dimensions={0} | all-to-all | bytes 1048576 | tf_op jit(solution)/shard_map/all_to_all | solution.py:200
  154.0 17.9 %all_to_all.55 = f32[128,8,128]{2,1,0:T(8,128)S(1)} all-to-all(f32[128,8,128]{2,1,0:T(8,128)S(1)} %bitcast.234), channel_id=1, replica_groups=mesh['gx'=8,'gy'=16] {'gx','gy'}, dimensions={0} | all-to-all | bytes 1048576 | tf_op jit(solution)/shard_map/all_to_all | solution.py:204
  180.5 17.5 %all_to_all.56 = f32[128,8,128]{2,1,0:T(8,128)S(1)} all-to-all(f32[128,8,128]{2,1,0:T(8,128)S(1)} %bitcast.235), channel_id=1, replica_groups=mesh['gx'=8,'gy'=16] {'gx','gy'}, dimensions={0} | all-to-all | bytes 1048576 | tf_op jit(solution)/shard_map/all_to_all | solution.py:210
  201.4 3.3 %collective-permute-start.7 = (f32[16,64]{1,0:T(8,128)S(1)}, f32[16,64]{1,0:T(8,128)S(1)}, u32[]{:S(2)}, u32[]{:S(2)}) collective-permute-start(f32[16,64]{1,0:T(8,128)S(1)} %bitcast.251), channel_id=1, source_target_pairs={{16,0},{32,16},{48,32},{64,48},{80,64},{96,80},{112,96},{17,1},{33... | collective-permute-start | bytes 12296 | tf_op jit(solution)/shard_map/ppermute | solution.py:215
  204.7 3.5 %collective-permute-start.6 = (f32[16,64]{1,0:T(8,128)S(1)}, f32[16,64]{1,0:T(8,128)S(1)}, u32[]{:S(2)}, u32[]{:S(2)}) collective-permute-start(f32[16,64]{1,0:T(8,128)S(1)} %bitcast.249), channel_id=1, source_target_pairs={{0,16},{16,32},{32,48},{48,64},{64,80},{80,96},{96,112},{1,17},{17... | collective-permute-start | bytes 12296 | tf_op jit(solution)/shard_map/ppermute | solution.py:214
  208.2 3.2 %collective-permute-done.6 = f32[16,64]{1,0:T(8,128)S(1)} collective-permute-done((f32[16,64]{1,0:T(8,128)S(1)}, f32[16,64]{1,0:T(8,128)S(1)}, u32[]{:S(2)}, u32[]{:S(2)}) %collective-permute-start.6) | collective-permute-done | bytes 4128 | tf_op jit(solution)/shard_map/ppermute | solution.py:214
  211.6 16.5 %all_to_all.57.framed_ref = f32[16,67,128]{2,1,0:T(8,128)S(1)} all-to-all(f32[16,67,128]{2,1,0:T(8,128)S(1)} %fusion.19), channel_id=1, replica_groups=mesh['gx'=8,'gy'=16] {'gy'}, dimensions={0} | all-to-all | bytes 1097728 | tf_op jit(solution)/shard_map/all_to_all | solution.py:221
  230.3 4.2 %shard_map.125 = (f32[16,64,128]{2,1,0:T(8,128)}, f32[16,64,128]{2,1,0:T(8,128)}) custom-call(f32[16,67,128]{2,1,0:T(8,128)} %copy-done.11, f32[16,64,128]{2,1,0:T(8,128)} %get-tuple-element.45.active_ref, f32[16,64,128]{2,1,0:T(8,128)} %get-tuple-element.8.residual_ref, f32[16,64,128]{2,1,0:T(8,128)} %get-tuple-element.9.refs_0_, ...), custom_call_target="tpu_custom_call" | custom-call | tf_op jit(solution)/shard_map/pallas_call | solution.py:104
  (116 shorter events, 62.8 us)
Async XLA Ops:
  0.6 8.6 %copy-start.12 = (s32[16,64,128]{2,1,0:T(8,128)S(1)}, s32[16,64,128]{2,1,0:T(8,128)}, u32[]{:S(2)}) copy-start(s32[16,64,128]{2,1,0:T(8,128)} %param.13) | copy-start | bytes 1572868
  0.6 9.5 %copy-start.6 = (f32[16,64,128]{2,1,0:T(8,128)S(1)}, f32[16,64,128]{2,1,0:T(8,128)}, u32[]{:S(2)}) copy-start(f32[16,64,128]{2,1,0:T(8,128)} %param.12) | copy-start | bytes 1572868
  2.7 29.5 %all-to-all-start = ((f32[16,64,128]{2,1,0:T(8,128)}), f32[16,64,128]{2,1,0:T(8,128)S(1)}, u32[]{:S(2)}, u32[]{:S(2)}) async-start(f32[16,64,128]{2,1,0:T(8,128)} %multiply_multiply_fusion), calls=%async_computation | async-start | bytes 1048576 | tf_op jit(solution)/shard_map/all_to_all | solution.py:200
  10.2 70.0 %collective-permute-start.2 = (f32[2,16,128]{2,1,0:T(8,128)S(1)}, f32[2,16,128]{2,1,0:T(8,128)S(1)}, u32[]{:S(2)}, u32[]{:S(2)}) collective-permute-start(f32[2,16,128]{2,1,0:T(8,128)S(1)} %bitcast.247), channel_id=1, source_target_pairs={{0,1},{1,2},{2,3},{3,4},{4,5},{5,6},{6,7},{7,8},{8,9},{9,10},{10,1... | collective-permute-start | bytes 49160 | tf_op jit(solution)/shard_map/ppermute | solution.py:22
  13.8 104.7 %collective-permute-start.3 = (f32[2,16,128]{2,1,0:T(8,128)S(1)}, f32[2,16,128]{2,1,0:T(8,128)S(1)}, u32[]{:S(2)}, u32[]{:S(2)}) collective-permute-start(f32[2,16,128]{2,1,0:T(8,128)S(1)} %bitcast.246), channel_id=1, source_target_pairs={{1,0},{2,1},{3,2},{4,3},{5,4},{6,5},{7,6},{8,7},{9,8},{10,9},{11,1... | collective-permute-start | bytes 49160 | tf_op jit(solution)/shard_map/ppermute | solution.py:22
  16.6 61.5 %collective-permute-start.5 = (f32[2,16,64]{2,1,0:T(8,128)S(1)}, f32[2,16,64]{2,1,0:T(8,128)S(1)}, u32[]{:S(2)}, u32[]{:S(2)}) collective-permute-start(f32[2,16,64]{2,1,0:T(8,128)S(1)} %get-tuple-element.12), channel_id=1, source_target_pairs={{16,0},{32,16},{48,32},{64,48},{80,64},{96,80},{112,96},{17,1},{33... | collective-permute-start | bytes 24584 | tf_op jit(solution)/shard_map/ppermute | solution.py:22
  21.8 56.4 %collective-permute-start.4 = (f32[2,16,64]{2,1,0:T(8,128)S(1)}, f32[2,16,64]{2,1,0:T(8,128)S(1)}, u32[]{:S(2)}, u32[]{:S(2)}) collective-permute-start(f32[2,16,64]{2,1,0:T(8,128)S(1)} %get-tuple-element.13), channel_id=1, source_target_pairs={{0,16},{16,32},{32,48},{48,64},{64,80},{80,96},{96,112},{1,17},{17... | collective-permute-start | bytes 24584 | tf_op jit(solution)/shard_map/ppermute | solution.py:22
  32.2 3.3 %copy-start = (bf16[1024,1024]{1,0:T(8,128)(2,1)}, bf16[1024,1024]{1,0:T(8,128)(2,1)S(1)}, u32[]{:S(2)}) copy-start(bf16[1024,1024]{1,0:T(8,128)(2,1)S(1)} %get-tuple-element.16) | copy-start | bytes 6291460
  35.6 13.7 %copy-start.13 = (f32[1024]{0:T(1024)S(1)}, f32[1024]{0:T(1024)}, u32[]{:S(2)}) copy-start(f32[1024]{0:T(1024)} %param.19) | copy-start | bytes 12292
  37.1 25.1 %all-to-all-start.1 = ((f32[128,8,128]{2,1,0:T(8,128)}), f32[128,8,128]{2,1,0:T(8,128)S(1)}, u32[]{:S(2)}, u32[]{:S(2)}) async-start(f32[128,8,128]{2,1,0:T(8,128)} %bitcast.3), calls=%async_computation.1 | async-start | bytes 1048576 | tf_op jit(solution)/shard_map/all_to_all | solution.py:204
  73.2 18.0 %all-to-all-start.2 = ((f32[128,8,128]{2,1,0:T(8,128)}), f32[128,8,128]{2,1,0:T(8,128)S(1)}, u32[]{:S(2)}, u32[]{:S(2)}) async-start(f32[128,8,128]{2,1,0:T(8,128)} %bitcast.233), calls=%async_computation.2 | async-start | bytes 1048576 | tf_op jit(solution)/shard_map/all_to_all | solution.py:210
  91.2 2.6 %copy-start.1 = (bf16[1024,1024]{1,0:T(8,128)(2,1)S(1)}, bf16[1024,1024]{1,0:T(8,128)(2,1)}, u32[]{:S(2)}) copy-start(bf16[1024,1024]{1,0:T(8,128)(2,1)} %copy-done) | copy-start | bytes 6291460
  101.1 6.8 %collective-permute-start.1 = (f32[16,64]{1,0:T(8,128)S(1)}, f32[16,64]{1,0:T(8,128)S(1)}, u32[]{:S(2)}, u32[]{:S(2)}) collective-permute-start(f32[16,64]{1,0:T(8,128)S(1)} %bitcast.250), channel_id=1, source_target_pairs={{16,0},{32,16},{48,32},{64,48},{80,64},{96,80},{112,96},{17,1},{33... | collective-permute-start | bytes 12296 | tf_op jit(solution)/shard_map/ppermute | solution.py:215
  104.4 6.8 %collective-permute-start = (f32[16,64]{1,0:T(8,128)S(1)}, f32[16,64]{1,0:T(8,128)S(1)}, u32[]{:S(2)}, u32[]{:S(2)}) collective-permute-start(f32[16,64]{1,0:T(8,128)S(1)} %bitcast.248), channel_id=1, source_target_pairs={{0,16},{16,32},{32,48},{48,64},{64,80},{80,96},{96,112},{1,17},{17... | collective-permute-start | bytes 12296 | tf_op jit(solution)/shard_map/ppermute | solution.py:214
  112.2 16.5 %all-to-all-start.3 = ((f32[16,67,128]{2,1,0:T(8,128)}), f32[16,67,128]{2,1,0:T(8,128)S(1)}, u32[]{:S(2)}, u32[]{:S(2)}) async-start(f32[16,67,128]{2,1,0:T(8,128)} %fusion.23), calls=%async_computation.3 | async-start | bytes 1179648 | tf_op jit(solution)/shard_map/all_to_all | solution.py:221
  119.1 9.7 %copy-start.14 = (f32[64]{0:T(128)S(1)}, f32[64]{0:T(128)}, u32[]{:S(2)}) copy-start(f32[64]{0:T(128)} %param.15) | copy-start | bytes 772
  119.1 10.4 %copy-start.15 = (f32[128]{0:T(128)S(1)}, f32[128]{0:T(128)}, u32[]{:S(2)}) copy-start(f32[128]{0:T(128)} %param.18) | copy-start | bytes 1540
  128.7 3.4 %copy-start.10 = (f32[16,67,128]{2,1,0:T(8,128)}, f32[16,67,128]{2,1,0:T(8,128)S(1)}, u32[]{:S(2)}) copy-start(f32[16,67,128]{2,1,0:T(8,128)S(1)} %all-to-all-done.3.framed_ref) | copy-start | bytes 1646596
  136.5 14.8 %copy-start.4 = (bf16[1024,1024]{1,0:T(8,128)(2,1)S(1)}, bf16[1024,1024]{1,0:T(8,128)(2,1)}, u32[]{:S(2)}) copy-start(bf16[1024,1024]{1,0:T(8,128)(2,1)} %get-tuple-element.17) | copy-start | bytes 6291460
  154.0 18.0 %copy-start.7 = (bf16[1024,1024]{1,0:T(8,128)(2,1)S(1)}, bf16[1024,1024]{1,0:T(8,128)(2,1)}, u32[]{:S(2)}) copy-start(bf16[1024,1024]{1,0:T(8,128)(2,1)} %get-tuple-element.15) | copy-start | bytes 6291460
  179.6 18.4 %copy-start.5 = (bf16[1024,1024]{1,0:T(8,128)(2,1)S(1)}, bf16[1024,1024]{1,0:T(8,128)(2,1)}, u32[]{:S(2)}) copy-start(bf16[1024,1024]{1,0:T(8,128)(2,1)} %get-tuple-element.17) | copy-start | bytes 6291460
  180.5 18.4 %copy-start.3 = (bf16[1024,1024]{1,0:T(8,128)(2,1)S(1)}, bf16[1024,1024]{1,0:T(8,128)(2,1)}, u32[]{:S(2)}) copy-start(bf16[1024,1024]{1,0:T(8,128)(2,1)} %copy-done) | copy-start | bytes 6291460
  201.4 6.8 %collective-permute-start.7 = (f32[16,64]{1,0:T(8,128)S(1)}, f32[16,64]{1,0:T(8,128)S(1)}, u32[]{:S(2)}, u32[]{:S(2)}) collective-permute-start(f32[16,64]{1,0:T(8,128)S(1)} %bitcast.251), channel_id=1, source_target_pairs={{16,0},{32,16},{48,32},{64,48},{80,64},{96,80},{112,96},{17,1},{33... | collective-permute-start | bytes 12296 | tf_op jit(solution)/shard_map/ppermute | solution.py:215
  204.7 6.8 %collective-permute-start.6 = (f32[16,64]{1,0:T(8,128)S(1)}, f32[16,64]{1,0:T(8,128)S(1)}, u32[]{:S(2)}, u32[]{:S(2)}) collective-permute-start(f32[16,64]{1,0:T(8,128)S(1)} %bitcast.249), channel_id=1, source_target_pairs={{0,16},{16,32},{32,48},{48,64},{64,80},{80,96},{96,112},{1,17},{17... | collective-permute-start | bytes 12296 | tf_op jit(solution)/shard_map/ppermute | solution.py:214
  (4 other events, 8.8 us)

commit v14 on v13

--- a/solution.py
+++ b/solution.py
@@ -189,10 +189,7 @@
     backward_y = [(target, source) for source, target in forward_y]
     basis_y = tuple(piece.reshape(blocks_y, -1, vectors_y.shape[1]) for piece in split_bf16(vectors_y))
     rows_of, cols_of = right_side.shape[1], right_side.shape[2]
-    masses = (
-        jnp.broadcast_to(mass_x[:, None], (rows_of, cols_of)),
-        jnp.broadcast_to(mass_y[None, :], (rows_of, cols_of)),
-    )
+    masses = (mass_x.reshape(rows_of, 1), mass_y.reshape(1, cols_of))
     scaled = residual * mass_x[None, :, None] * mass_y[None, None, :]
     for iteration in range(ITERS):
         modes = transform(

time: 236 us -> 234 us (level)
  transfers between devices with their start and end apart: 12 -> 12, of which waited for: 5 -> 5; matrix products, arithmetic and copies ran while one was open for 20% -> 21% of each run, Pallas kernels for 1% -> 1%
where the time goes in v14:
time: 234 us; the launch traced here: 233 us
  blocking collectives  66.6 us (28%)
  starting transfers between devices  56.1 us (24%)
  waiting for transfers between devices  28.8 us (12%)
  matrix products  26.9 us (11%)
  local copies, waits for them, and re-layouts  21.2 us (9%)
  other arithmetic  19.7 us (8%)
  Pallas kernels  12.7 us (5%)
    all_to_all x2, blocking collectives, shards(): lax.all_to_all(chunks, everyone, split_axis=0, concat_axis=0, tiled=True)  35.4 us
    dot_general x24, matrix products, product(): return jnp.einsum(spec, first, second, preferred_element_type=jnp.float32)  26.9 us
    all_to_all x2, waiting for transfers between devices, shards(): lax.all_to_all(chunks, everyone, split_axis=0, concat_axis=0, tiled=True)  17.3 us
    all_to_all x2, starting transfers between devices, shards(): lax.all_to_all(chunks, everyone, split_axis=0, concat_axis=0, tiled=True)  17.1 us
    all_to_all x1, blocking collectives, shards(): lax.all_to_all(framed, 'gy', split_axis=0, concat_axis=0, tiled=True)  16.5 us
    all_to_all x1, blocking collectives, shards(): lax.all_to_all(scaled, 'gy', split_axis=0, concat_axis=1, tiled=True)  14.7 us
    convert_element_type x2, other arithmetic, split_bf16(): rounded.astype(jnp.bfloat16)  8.93 us
    pallas_call x2, Pallas kernels, framed_stencil(): pl.pallas_call(functools.partial(framed_kernel, adjoint is not None, mass...  8.59 us
  transfers between devices with their start and end apart: 12, of which 5 were waited for; matrix products, arithmetic and copies ran while one was open for 21% of the time, Pallas kernels for 1%

profile of v14, /device:TPU:3, one launch (start us, length us, event | category | flops | bytes accessed | tf_op | source)
XLA Modules:
  0.0 233.2 jit_solution(16961817551343764899)
XLA Ops:
  2.7 6.5 %all-to-all-start = ((f32[16,64,128]{2,1,0:T(8,128)}), f32[16,64,128]{2,1,0:T(8,128)S(1)}, u32[]{:S(2)}, u32[]{:S(2)}) async-start(f32[16,64,128]{2,1,0:T(8,128)} %multiply_multiply_fusion), calls=%async_computation | async-start | bytes 1048576 | tf_op jit(solution)/shard_map/all_to_all | solution.py:197
  10.2 3.5 %collective-permute-start.2 = (f32[2,16,128]{2,1,0:T(8,128)S(1)}, f32[2,16,128]{2,1,0:T(8,128)S(1)}, u32[]{:S(2)}, u32[]{:S(2)}) collective-permute-start(f32[2,16,128]{2,1,0:T(8,128)S(1)} %bitcast.249), channel_id=1, source_target_pairs={{0,1},{1,2},{2,3},{3,4},{4,5},{5,6},{6,7},{7,8},{8,9},{9,10},{10,1... | collective-permute-start | bytes 49160 | tf_op jit(solution)/shard_map/ppermute | solution.py:22
  16.6 5.2 %collective-permute-start.5 = (f32[2,16,64]{2,1,0:T(8,128)S(1)}, f32[2,16,64]{2,1,0:T(8,128)S(1)}, u32[]{:S(2)}, u32[]{:S(2)}) collective-permute-start(f32[2,16,64]{2,1,0:T(8,128)S(1)} %get-tuple-element.12), channel_id=1, source_target_pairs={{16,0},{32,16},{48,32},{64,48},{80,64},{96,80},{112,96},{17,1},{33... | collective-permute-start | bytes 24584 | tf_op jit(solution)/shard_map/ppermute | solution.py:22
  27.8 4.5 %reduce-precision_convert_fusion.1 = (bf16[1024,1024]{1,0:T(8,128)(2,1)S(1)}, bf16[1024,1024]{1,0:T(8,128)(2,1)}) fusion(f32[1024,1024]{1,0:T(8,128)} %param.14), kind=kLoop, calls=%fused_computation.3 | loop fusion | flops 4194304 | bytes 8388608 | tf_op jit(solution)/shard_map/convert_element_type | solution.py:147
  37.1 12.2 %all-to-all-start.1 = ((f32[128,8,128]{2,1,0:T(8,128)}), f32[128,8,128]{2,1,0:T(8,128)S(1)}, u32[]{:S(2)}, u32[]{:S(2)}) async-start(f32[128,8,128]{2,1,0:T(8,128)} %bitcast.3), calls=%async_computation.1 | async-start | bytes 1048576 | tf_op jit(solution)/shard_map/all_to_all | solution.py:201
  50.6 4.5 %reduce-precision_convert_fusion = (bf16[1024,1024]{1,0:T(8,128)(2,1)S(1)}, bf16[1024,1024]{1,0:T(8,128)(2,1)}) fusion(f32[1024,1024]{1,0:T(8,128)} %param.17), kind=kLoop, calls=%fused_computation.1 | loop fusion | flops 4194304 | bytes 8388608 | tf_op jit(solution)/shard_map/convert_element_type | solution.py:147
  55.1 7.1 %all-to-all-done.1 = f32[128,8,128]{2,1,0:T(8,128)S(1)} async-done(((f32[128,8,128]{2,1,0:T(8,128)}), f32[128,8,128]{2,1,0:T(8,128)S(1)}, u32[]{:S(2)}, u32[]{:S(2)}) %all-to-all-start.1) | async-done | bytes 524320 | tf_op jit(solution)/shard_map/all_to_all | solution.py:201
  73.2 4.9 %all-to-all-start.2 = ((f32[128,8,128]{2,1,0:T(8,128)}), f32[128,8,128]{2,1,0:T(8,128)S(1)}, u32[]{:S(2)}, u32[]{:S(2)}) async-start(f32[128,8,128]{2,1,0:T(8,128)} %bitcast.235), calls=%async_computation.2 | async-start | bytes 1048576 | tf_op jit(solution)/shard_map/all_to_all | solution.py:207
  80.9 10.3 %all-to-all-done.2 = f32[128,8,128]{2,1,0:T(8,128)S(1)} async-done(((f32[128,8,128]{2,1,0:T(8,128)}), f32[128,8,128]{2,1,0:T(8,128)S(1)}, u32[]{:S(2)}, u32[]{:S(2)}) %all-to-all-start.2) | async-done | bytes 524320 | tf_op jit(solution)/shard_map/all_to_all | solution.py:207
  101.1 3.3 %collective-permute-start.1 = (f32[16,64]{1,0:T(8,128)S(1)}, f32[16,64]{1,0:T(8,128)S(1)}, u32[]{:S(2)}, u32[]{:S(2)}) collective-permute-start(f32[16,64]{1,0:T(8,128)S(1)} %bitcast.252), channel_id=1, source_target_pairs={{16,0},{32,16},{48,32},{64,48},{80,64},{96,80},{112,96},{17,1},{33... | collective-permute-start | bytes 12296 | tf_op jit(solution)/shard_map/ppermute | solution.py:212
  104.4 3.5 %collective-permute-start = (f32[16,64]{1,0:T(8,128)S(1)}, f32[16,64]{1,0:T(8,128)S(1)}, u32[]{:S(2)}, u32[]{:S(2)}) collective-permute-start(f32[16,64]{1,0:T(8,128)S(1)} %bitcast.250), channel_id=1, source_target_pairs={{0,16},{16,32},{32,48},{48,64},{64,80},{80,96},{96,112},{1,17},{17... | collective-permute-start | bytes 12296 | tf_op jit(solution)/shard_map/ppermute | solution.py:211
  108.0 3.2 %collective-permute-done = f32[16,64]{1,0:T(8,128)S(1)} collective-permute-done((f32[16,64]{1,0:T(8,128)S(1)}, f32[16,64]{1,0:T(8,128)S(1)}, u32[]{:S(2)}, u32[]{:S(2)}) %collective-permute-start) | collective-permute-done | bytes 4128 | tf_op jit(solution)/shard_map/ppermute | solution.py:211
  112.2 6.3 %all-to-all-start.3 = ((f32[16,67,128]{2,1,0:T(8,128)}), f32[16,67,128]{2,1,0:T(8,128)S(1)}, u32[]{:S(2)}, u32[]{:S(2)}) async-start(f32[16,67,128]{2,1,0:T(8,128)} %fusion.23), calls=%async_computation.3 | async-start | bytes 1179648 | tf_op jit(solution)/shard_map/all_to_all | solution.py:218
  119.1 4.6 %add_divide_fusion = (f32[16,64,128]{2,1,0:T(8,128)}, f32[16,64,128]{2,1,0:T(8,128)}, f32[16,64,128]{2,1,0:T(8,128)}, f32[16,64,128]{2,1,0:T(8,128)}, f32[16,64,128]{2,1,0:T(8,128)}, /*index=5*/f32[16,64,128]{2,1,0:T(8,128)}) fusion(f32[16,64,128]{2,1,0:T(8,128)S(1)} %copy-done.6, f32[16,64,127]{2,1,0:T(8,128)} %get-tuple-element.38, ...), kind=kLoop, calls=%fused_computation.84 | loop fusion | flops 3014656 | bytes 6750208 | tf_op jit(solution)/shard_map/div | solution.py:30
  123.7 5.0 %all-to-all-done.3.framed_ref = f32[16,67,128]{2,1,0:T(8,128)S(1)} async-done(((f32[16,67,128]{2,1,0:T(8,128)}), f32[16,67,128]{2,1,0:T(8,128)S(1)}, u32[]{:S(2)}, u32[]{:S(2)}) %all-to-all-start.3) | async-done | bytes 548896 | tf_op jit(solution)/shard_map/all_to_all | solution.py:218
  130.8 4.3 %shard_map.123 = (f32[16,64,128]{2,1,0:T(8,128)}, f32[16,64,128]{2,1,0:T(8,128)}, f32[16,64,128]{2,1,0:T(8,128)}) custom-call(f32[16,67,128]{2,1,0:T(8,128)} %copy-done.10, f32[16,64,128]{2,1,0:T(8,128)} %get-tuple-element.45.active_ref, f32[16,64,128]{2,1,0:T(8,128)} %residual_ref.1, f32[16,128]{1,0:T(8,128)} %get-tuple-element.55.refs_0_.refs_1_, ...), custom_call_target="tpu_custom_call" | custom-call | tf_op jit(solution)/shard_map/pallas_call | solution.py:104
  135.1 14.7 %all_to_all.54 = f32[16,64,128]{2,1,0:T(8,128)S(1)} all-to-all(f32[16,64,128]{2,1,0:T(8,128)} %get-tuple-element.7), channel_id=1, replica_groups=mesh['gx'=8,'gy'=16] {'gy'}, dimensions={0} | all-to-all | bytes 1048576 | tf_op jit(solution)/shard_map/all_to_all | solution.py:197
  152.7 17.9 %all_to_all.55 = f32[128,8,128]{2,1,0:T(8,128)S(1)} all-to-all(f32[128,8,128]{2,1,0:T(8,128)S(1)} %bitcast.236), channel_id=1, replica_groups=mesh['gx'=8,'gy'=16] {'gx','gy'}, dimensions={0} | all-to-all | bytes 1048576 | tf_op jit(solution)/shard_map/all_to_all | solution.py:201
  179.2 17.5 %all_to_all.56 = f32[128,8,128]{2,1,0:T(8,128)S(1)} all-to-all(f32[128,8,128]{2,1,0:T(8,128)S(1)} %bitcast.237), channel_id=1, replica_groups=mesh['gx'=8,'gy'=16] {'gx','gy'}, dimensions={0} | all-to-all | bytes 1048576 | tf_op jit(solution)/shard_map/all_to_all | solution.py:207
  200.0 3.3 %collective-permute-start.7 = (f32[16,64]{1,0:T(8,128)S(1)}, f32[16,64]{1,0:T(8,128)S(1)}, u32[]{:S(2)}, u32[]{:S(2)}) collective-permute-start(f32[16,64]{1,0:T(8,128)S(1)} %bitcast.253), channel_id=1, source_target_pairs={{16,0},{32,16},{48,32},{64,48},{80,64},{96,80},{112,96},{17,1},{33... | collective-permute-start | bytes 12296 | tf_op jit(solution)/shard_map/ppermute | solution.py:212
  203.3 3.5 %collective-permute-start.6 = (f32[16,64]{1,0:T(8,128)S(1)}, f32[16,64]{1,0:T(8,128)S(1)}, u32[]{:S(2)}, u32[]{:S(2)}) collective-permute-start(f32[16,64]{1,0:T(8,128)S(1)} %bitcast.251), channel_id=1, source_target_pairs={{0,16},{16,32},{32,48},{48,64},{64,80},{80,96},{96,112},{1,17},{17... | collective-permute-start | bytes 12296 | tf_op jit(solution)/shard_map/ppermute | solution.py:211
  206.9 3.2 %collective-permute-done.6 = f32[16,64]{1,0:T(8,128)S(1)} collective-permute-done((f32[16,64]{1,0:T(8,128)S(1)}, f32[16,64]{1,0:T(8,128)S(1)}, u32[]{:S(2)}, u32[]{:S(2)}) %collective-permute-start.6) | collective-permute-done | bytes 4128 | tf_op jit(solution)/shard_map/ppermute | solution.py:211
  210.3 16.5 %all_to_all.57.framed_ref = f32[16,67,128]{2,1,0:T(8,128)S(1)} all-to-all(f32[16,67,128]{2,1,0:T(8,128)S(1)} %fusion.19), channel_id=1, replica_groups=mesh['gx'=8,'gy'=16] {'gy'}, dimensions={0} | all-to-all | bytes 1097728 | tf_op jit(solution)/shard_map/all_to_all | solution.py:218
  228.9 4.2 %shard_map.125 = (f32[16,64,128]{2,1,0:T(8,128)}, f32[16,64,128]{2,1,0:T(8,128)}) custom-call(f32[16,67,128]{2,1,0:T(8,128)} %copy-done.11, f32[16,64,128]{2,1,0:T(8,128)} %get-tuple-element.45.active_ref, f32[16,64,128]{2,1,0:T(8,128)} %get-tuple-element.8.residual_ref, f32[16,64,128]{2,1,0:T(8,128)} %get-tuple-element.9.refs_0_, ...), custom_call_target="tpu_custom_call" | custom-call | tf_op jit(solution)/shard_map/pallas_call | solution.py:104
  (113 shorter events, 62.2 us)
Async XLA Ops:
  0.6 8.6 %copy-start.12 = (s32[16,64,128]{2,1,0:T(8,128)S(1)}, s32[16,64,128]{2,1,0:T(8,128)}, u32[]{:S(2)}) copy-start(s32[16,64,128]{2,1,0:T(8,128)} %param.13) | copy-start | bytes 1572868
  0.6 9.5 %copy-start.6 = (f32[16,64,128]{2,1,0:T(8,128)S(1)}, f32[16,64,128]{2,1,0:T(8,128)}, u32[]{:S(2)}) copy-start(f32[16,64,128]{2,1,0:T(8,128)} %param.12) | copy-start | bytes 1572868
  2.7 29.5 %all-to-all-start = ((f32[16,64,128]{2,1,0:T(8,128)}), f32[16,64,128]{2,1,0:T(8,128)S(1)}, u32[]{:S(2)}, u32[]{:S(2)}) async-start(f32[16,64,128]{2,1,0:T(8,128)} %multiply_multiply_fusion), calls=%async_computation | async-start | bytes 1048576 | tf_op jit(solution)/shard_map/all_to_all | solution.py:197
  10.2 70.1 %collective-permute-start.2 = (f32[2,16,128]{2,1,0:T(8,128)S(1)}, f32[2,16,128]{2,1,0:T(8,128)S(1)}, u32[]{:S(2)}, u32[]{:S(2)}) collective-permute-start(f32[2,16,128]{2,1,0:T(8,128)S(1)} %bitcast.249), channel_id=1, source_target_pairs={{0,1},{1,2},{2,3},{3,4},{4,5},{5,6},{6,7},{7,8},{8,9},{9,10},{10,1... | collective-permute-start | bytes 49160 | tf_op jit(solution)/shard_map/ppermute | solution.py:22
  13.8 104.7 %collective-permute-start.3 = (f32[2,16,128]{2,1,0:T(8,128)S(1)}, f32[2,16,128]{2,1,0:T(8,128)S(1)}, u32[]{:S(2)}, u32[]{:S(2)}) collective-permute-start(f32[2,16,128]{2,1,0:T(8,128)S(1)} %bitcast.248), channel_id=1, source_target_pairs={{1,0},{2,1},{3,2},{4,3},{5,4},{6,5},{7,6},{8,7},{9,8},{10,9},{11,1... | collective-permute-start | bytes 49160 | tf_op jit(solution)/shard_map/ppermute | solution.py:22
  16.6 61.5 %collective-permute-start.5 = (f32[2,16,64]{2,1,0:T(8,128)S(1)}, f32[2,16,64]{2,1,0:T(8,128)S(1)}, u32[]{:S(2)}, u32[]{:S(2)}) collective-permute-start(f32[2,16,64]{2,1,0:T(8,128)S(1)} %get-tuple-element.12), channel_id=1, source_target_pairs={{16,0},{32,16},{48,32},{64,48},{80,64},{96,80},{112,96},{17,1},{33... | collective-permute-start | bytes 24584 | tf_op jit(solution)/shard_map/ppermute | solution.py:22
  21.8 56.4 %collective-permute-start.4 = (f32[2,16,64]{2,1,0:T(8,128)S(1)}, f32[2,16,64]{2,1,0:T(8,128)S(1)}, u32[]{:S(2)}, u32[]{:S(2)}) collective-permute-start(f32[2,16,64]{2,1,0:T(8,128)S(1)} %get-tuple-element.13), channel_id=1, source_target_pairs={{0,16},{16,32},{32,48},{48,64},{64,80},{80,96},{96,112},{1,17},{17... | collective-permute-start | bytes 24584 | tf_op jit(solution)/shard_map/ppermute | solution.py:22
  32.2 3.3 %copy-start = (bf16[1024,1024]{1,0:T(8,128)(2,1)}, bf16[1024,1024]{1,0:T(8,128)(2,1)S(1)}, u32[]{:S(2)}) copy-start(bf16[1024,1024]{1,0:T(8,128)(2,1)S(1)} %get-tuple-element.16) | copy-start | bytes 6291460
  35.6 13.7 %copy-start.13 = (f32[1024]{0:T(1024)S(1)}, f32[1024]{0:T(1024)}, u32[]{:S(2)}) copy-start(f32[1024]{0:T(1024)} %param.19) | copy-start | bytes 12292
  35.6 14.4 %copy-start.14 = (f32[64]{0:T(128)S(1)}, f32[64]{0:T(128)}, u32[]{:S(2)}) copy-start(f32[64]{0:T(128)} %param.15) | copy-start | bytes 772
  37.1 25.1 %all-to-all-start.1 = ((f32[128,8,128]{2,1,0:T(8,128)}), f32[128,8,128]{2,1,0:T(8,128)S(1)}, u32[]{:S(2)}, u32[]{:S(2)}) async-start(f32[128,8,128]{2,1,0:T(8,128)} %bitcast.3), calls=%async_computation.1 | async-start | bytes 1048576 | tf_op jit(solution)/shard_map/all_to_all | solution.py:201
  68.1 2.6 %copy-start.9 = (f32[16,8,1024]{2,1,0:T(8,128)S(1)}, f32[16,8,1024]{2,1,0:T(8,128)}, u32[]{:S(2)}) copy-start(f32[16,8,1024]{2,1,0:T(8,128)} %shard_map.122) | copy-start | bytes 1572868
  73.2 18.0 %all-to-all-start.2 = ((f32[128,8,128]{2,1,0:T(8,128)}), f32[128,8,128]{2,1,0:T(8,128)S(1)}, u32[]{:S(2)}, u32[]{:S(2)}) async-start(f32[128,8,128]{2,1,0:T(8,128)} %bitcast.235), calls=%async_computation.2 | async-start | bytes 1048576 | tf_op jit(solution)/shard_map/all_to_all | solution.py:207
  91.2 2.6 %copy-start.1 = (bf16[1024,1024]{1,0:T(8,128)(2,1)S(1)}, bf16[1024,1024]{1,0:T(8,128)(2,1)}, u32[]{:S(2)}) copy-start(bf16[1024,1024]{1,0:T(8,128)(2,1)} %copy-done) | copy-start | bytes 6291460
  101.1 6.8 %collective-permute-start.1 = (f32[16,64]{1,0:T(8,128)S(1)}, f32[16,64]{1,0:T(8,128)S(1)}, u32[]{:S(2)}, u32[]{:S(2)}) collective-permute-start(f32[16,64]{1,0:T(8,128)S(1)} %bitcast.252), channel_id=1, source_target_pairs={{16,0},{32,16},{48,32},{64,48},{80,64},{96,80},{112,96},{17,1},{33... | collective-permute-start | bytes 12296 | tf_op jit(solution)/shard_map/ppermute | solution.py:212
  104.4 6.8 %collective-permute-start = (f32[16,64]{1,0:T(8,128)S(1)}, f32[16,64]{1,0:T(8,128)S(1)}, u32[]{:S(2)}, u32[]{:S(2)}) collective-permute-start(f32[16,64]{1,0:T(8,128)S(1)} %bitcast.250), channel_id=1, source_target_pairs={{0,16},{16,32},{32,48},{48,64},{64,80},{80,96},{96,112},{1,17},{17... | collective-permute-start | bytes 12296 | tf_op jit(solution)/shard_map/ppermute | solution.py:211
  112.2 16.5 %all-to-all-start.3 = ((f32[16,67,128]{2,1,0:T(8,128)}), f32[16,67,128]{2,1,0:T(8,128)S(1)}, u32[]{:S(2)}, u32[]{:S(2)}) async-start(f32[16,67,128]{2,1,0:T(8,128)} %fusion.23), calls=%async_computation.3 | async-start | bytes 1179648 | tf_op jit(solution)/shard_map/all_to_all | solution.py:218
  135.1 14.8 %copy-start.4 = (bf16[1024,1024]{1,0:T(8,128)(2,1)S(1)}, bf16[1024,1024]{1,0:T(8,128)(2,1)}, u32[]{:S(2)}) copy-start(bf16[1024,1024]{1,0:T(8,128)(2,1)} %get-tuple-element.17) | copy-start | bytes 6291460
  152.7 18.0 %copy-start.7 = (bf16[1024,1024]{1,0:T(8,128)(2,1)S(1)}, bf16[1024,1024]{1,0:T(8,128)(2,1)}, u32[]{:S(2)}) copy-start(bf16[1024,1024]{1,0:T(8,128)(2,1)} %get-tuple-element.15) | copy-start | bytes 6291460
  174.9 2.6 %copy-start.8 = (f32[16,8,1024]{2,1,0:T(8,128)S(1)}, f32[16,8,1024]{2,1,0:T(8,128)}, u32[]{:S(2)}) copy-start(f32[16,8,1024]{2,1,0:T(8,128)} %shard_map.124) | copy-start | bytes 1572868
  178.3 18.4 %copy-start.5 = (bf16[1024,1024]{1,0:T(8,128)(2,1)S(1)}, bf16[1024,1024]{1,0:T(8,128)(2,1)}, u32[]{:S(2)}) copy-start(bf16[1024,1024]{1,0:T(8,128)(2,1)} %get-tuple-element.17) | copy-start | bytes 6291460
  179.1 18.4 %copy-start.3 = (bf16[1024,1024]{1,0:T(8,128)(2,1)S(1)}, bf16[1024,1024]{1,0:T(8,128)(2,1)}, u32[]{:S(2)}) copy-start(bf16[1024,1024]{1,0:T(8,128)(2,1)} %copy-done) | copy-start | bytes 6291460
  200.0 6.8 %collective-permute-start.7 = (f32[16,64]{1,0:T(8,128)S(1)}, f32[16,64]{1,0:T(8,128)S(1)}, u32[]{:S(2)}, u32[]{:S(2)}) collective-permute-start(f32[16,64]{1,0:T(8,128)S(1)} %bitcast.253), channel_id=1, source_target_pairs={{16,0},{32,16},{48,32},{64,48},{80,64},{96,80},{112,96},{17,1},{33... | collective-permute-start | bytes 12296 | tf_op jit(solution)/shard_map/ppermute | solution.py:212
  203.3 6.8 %collective-permute-start.6 = (f32[16,64]{1,0:T(8,128)S(1)}, f32[16,64]{1,0:T(8,128)S(1)}, u32[]{:S(2)}, u32[]{:S(2)}) collective-permute-start(f32[16,64]{1,0:T(8,128)S(1)} %bitcast.251), channel_id=1, source_target_pairs={{0,16},{16,32},{32,48},{48,64},{64,80},{80,96},{96,112},{1,17},{17... | collective-permute-start | bytes 12296 | tf_op jit(solution)/shard_map/ppermute | solution.py:211
  (3 other events, 5.8 us)

commit v15 on v14

--- a/solution.py
+++ b/solution.py
@@ -50,8 +50,8 @@
 def framed_kernel(has_adjoint, has_scale, framed_ref, active_ref, residual_ref, *refs):
     refs = list(refs)
     adjoint_ref = refs.pop(0) if has_adjoint else None
-    x_low_ref, x_high_ref, y_low_ref, y_high_ref = refs[:4]
-    refs = refs[4:]
+    x_low_ref, x_high_ref, y_halo_ref = refs[:3]
+    refs = refs[3:]
     mass_x_ref, mass_y_ref = (refs.pop(0), refs.pop(0)) if has_scale else (None, None)
     scaled_out = refs.pop() if has_scale else None
     face_refs, residual_out, adjoint_out = refs[:-2], refs[-2], refs[-1]
@@ -79,8 +79,8 @@
             masked[z - 1] if z > 0 else zeros,
             jnp.where(row == rows - 1, jnp.broadcast_to(x_high, (rows, cols)), after(center, 0, rows, row_forward)),
             jnp.where(row == 0, jnp.broadcast_to(x_low, (rows, cols)), before(center, 0, rows, row_forward)),
-            jnp.where(col == cols - 1, y_high_ref[z], after(center, 1, cols, col_forward)),
-            jnp.where(col == 0, y_low_ref[z], before(center, 1, cols, col_forward)),
+            jnp.where(col == cols - 1, y_halo_ref[z], after(center, 1, cols, col_forward)),
+            jnp.where(col == 0, y_halo_ref[z], before(center, 1, cols, col_forward)),
         ]
         result = storage_term * center
         for face_ref, other in zip(face_refs, others):
@@ -96,10 +96,11 @@
 def framed_stencil(framed, active, residual, adjoint, x_strips, y_strips, faces, masses=None):
     vmem = pl.BlockSpec(memory_space=pltpu.VMEM)
     shape = jax.ShapeDtypeStruct(active.shape, active.dtype)
-    y_low, y_high = (jnp.broadcast_to(strip[:, :, None], active.shape) for strip in y_strips)
+    lane = lax.broadcasted_iota(jnp.int32, active.shape, 2)
+    y_halo = jnp.where(lane == 0, y_strips[0][:, :, None], y_strips[1][:, :, None])
     carried = [] if adjoint is None else [adjoint]
     scales = [] if masses is None else list(masses)
-    operands = [framed, active, residual, *carried, x_strips[0], x_strips[1], y_low, y_high, *scales, *faces]
+    operands = [framed, active, residual, *carried, x_strips[0], x_strips[1], y_halo, *scales, *faces]
     outputs = 2 if masses is None else 3
     return pl.pallas_call(
         functools.partial(framed_kernel, adjoint is not None, masses is not None),

time: 234 us -> 233 us (level)
  local copies, waits for them, and re-layouts: 21.2 us -> 17.1 us
    broadcast_in_dim x4 -> x0, local copies, waits for them, and re-layouts: 4.03 us -> none  [framed_stencil(): jnp.broadcast_to(strip[:, :, None], active.shape)]
    ppermute x2, starting transfers between devices: 5.49 us -> 8.75 us  [edge_pair(): lax.ppermute(last, axis, forward)]
    ppermute x2, starting transfers between devices: 7.1 us -> 4.4 us  [edge_pair(): lax.ppermute(first, axis, backward)]
where the time goes in v15:
time: 233 us; the launch traced here: 232 us
  blocking collectives  66.6 us (29%)
  starting transfers between devices  55.2 us (24%)
  waiting for transfers between devices  30.3 us (13%)
  matrix products  27 us (12%)
  other arithmetic  21.9 us (9%)
  local copies, waits for them, and re-layouts  17.1 us (7%)
  Pallas kernels  12.4 us (5%)
    all_to_all x2, blocking collectives, shards(): lax.all_to_all(chunks, everyone, split_axis=0, concat_axis=0, tiled=True)  35.4 us
    dot_general x24, matrix products, product(): return jnp.einsum(spec, first, second, preferred_element_type=jnp.float32)  27 us
    all_to_all x2, waiting for transfers between devices, shards(): lax.all_to_all(chunks, everyone, split_axis=0, concat_axis=0, tiled=True)  18.8 us
    all_to_all x1, blocking collectives, shards(): lax.all_to_all(framed, 'gy', split_axis=0, concat_axis=0, tiled=True)  16.5 us
    all_to_all x2, starting transfers between devices, shards(): lax.all_to_all(chunks, everyone, split_axis=0, concat_axis=0, tiled=True)  15.7 us
    all_to_all x1, blocking collectives, shards(): lax.all_to_all(scaled, 'gy', split_axis=0, concat_axis=1, tiled=True)  14.7 us
    convert_element_type x2, other arithmetic, split_bf16(): rounded.astype(jnp.bfloat16)  8.93 us
    ppermute x2, starting transfers between devices, edge_pair(): lax.ppermute(last, axis, forward)  8.75 us
  transfers between devices with their start and end apart: 12, of which 5 were waited for; matrix products, arithmetic and copies ran while one was open for 21% of the time, Pallas kernels for 1%

profile of v15, /device:TPU:3, one launch (start us, length us, event | category | flops | bytes accessed | tf_op | source)
XLA Modules:
  0.0 231.6 jit_solution(8537137888224139324)
XLA Ops:
  2.7 6.5 %all-to-all-start = ((f32[16,64,128]{2,1,0:T(8,128)}), f32[16,64,128]{2,1,0:T(8,128)S(1)}, u32[]{:S(2)}, u32[]{:S(2)}) async-start(f32[16,64,128]{2,1,0:T(8,128)} %multiply_multiply_fusion), calls=%async_computation | async-start | bytes 1048576 | tf_op jit(solution)/shard_map/all_to_all | solution.py:198
  10.2 3.5 %collective-permute-start.2 = (f32[2,16,128]{2,1,0:T(8,128)S(1)}, f32[2,16,128]{2,1,0:T(8,128)S(1)}, u32[]{:S(2)}, u32[]{:S(2)}) collective-permute-start(f32[2,16,128]{2,1,0:T(8,128)S(1)} %bitcast.249), channel_id=1, source_target_pairs={{0,1},{1,2},{2,3},{3,4},{4,5},{5,6},{6,7},{7,8},{8,9},{9,10},{10,1... | collective-permute-start | bytes 49160 | tf_op jit(solution)/shard_map/ppermute | solution.py:22
  16.6 5.2 %collective-permute-start.4 = (f32[2,16,64]{2,1,0:T(8,128)S(1)}, f32[2,16,64]{2,1,0:T(8,128)S(1)}, u32[]{:S(2)}, u32[]{:S(2)}) collective-permute-start(f32[2,16,64]{2,1,0:T(8,128)S(1)} %get-tuple-element.12), channel_id=1, source_target_pairs={{0,16},{16,32},{32,48},{48,64},{64,80},{80,96},{96,112},{1,17},{17... | collective-permute-start | bytes 24584 | tf_op jit(solution)/shard_map/ppermute | solution.py:22
  29.7 4.4 %reduce-precision_convert_fusion.1 = (bf16[1024,1024]{1,0:T(8,128)(2,1)S(1)}, bf16[1024,1024]{1,0:T(8,128)(2,1)}) fusion(f32[1024,1024]{1,0:T(8,128)} %param.14), kind=kLoop, calls=%fused_computation.3 | loop fusion | flops 4194304 | bytes 8388608 | tf_op jit(solution)/shard_map/convert_element_type | solution.py:148
  39.0 10.7 %all-to-all-start.1 = ((f32[128,8,128]{2,1,0:T(8,128)}), f32[128,8,128]{2,1,0:T(8,128)S(1)}, u32[]{:S(2)}, u32[]{:S(2)}) async-start(f32[128,8,128]{2,1,0:T(8,128)} %bitcast.3), calls=%async_computation.1 | async-start | bytes 1048576 | tf_op jit(solution)/shard_map/all_to_all | solution.py:202
  49.7 4.5 %reduce-precision_convert_fusion = (bf16[1024,1024]{1,0:T(8,128)(2,1)S(1)}, bf16[1024,1024]{1,0:T(8,128)(2,1)}) fusion(f32[1024,1024]{1,0:T(8,128)} %param.17), kind=kLoop, calls=%fused_computation.1 | loop fusion | flops 4194304 | bytes 8388608 | tf_op jit(solution)/shard_map/convert_element_type | solution.py:148
  54.2 8.4 %all-to-all-done.1 = f32[128,8,128]{2,1,0:T(8,128)S(1)} async-done(((f32[128,8,128]{2,1,0:T(8,128)}), f32[128,8,128]{2,1,0:T(8,128)S(1)}, u32[]{:S(2)}, u32[]{:S(2)}) %all-to-all-start.1) | async-done | bytes 524320 | tf_op jit(solution)/shard_map/all_to_all | solution.py:202
  73.6 4.9 %all-to-all-start.2 = ((f32[128,8,128]{2,1,0:T(8,128)}), f32[128,8,128]{2,1,0:T(8,128)S(1)}, u32[]{:S(2)}, u32[]{:S(2)}) async-start(f32[128,8,128]{2,1,0:T(8,128)} %bitcast.235), calls=%async_computation.2 | async-start | bytes 1048576 | tf_op jit(solution)/shard_map/all_to_all | solution.py:208
  81.3 10.3 %all-to-all-done.2 = f32[128,8,128]{2,1,0:T(8,128)S(1)} async-done(((f32[128,8,128]{2,1,0:T(8,128)}), f32[128,8,128]{2,1,0:T(8,128)S(1)}, u32[]{:S(2)}, u32[]{:S(2)}) %all-to-all-start.2) | async-done | bytes 524320 | tf_op jit(solution)/shard_map/all_to_all | solution.py:208
  101.5 3.3 %collective-permute-start.1 = (f32[16,64]{1,0:T(8,128)S(1)}, f32[16,64]{1,0:T(8,128)S(1)}, u32[]{:S(2)}, u32[]{:S(2)}) collective-permute-start(f32[16,64]{1,0:T(8,128)S(1)} %bitcast.252), channel_id=1, source_target_pairs={{16,0},{32,16},{48,32},{64,48},{80,64},{96,80},{112,96},{17,1},{33... | collective-permute-start | bytes 12296 | tf_op jit(solution)/shard_map/ppermute | solution.py:213
  104.8 3.5 %collective-permute-start = (f32[16,64]{1,0:T(8,128)S(1)}, f32[16,64]{1,0:T(8,128)S(1)}, u32[]{:S(2)}, u32[]{:S(2)}) collective-permute-start(f32[16,64]{1,0:T(8,128)S(1)} %bitcast.250), channel_id=1, source_target_pairs={{0,16},{16,32},{32,48},{48,64},{64,80},{80,96},{96,112},{1,17},{17... | collective-permute-start | bytes 12296 | tf_op jit(solution)/shard_map/ppermute | solution.py:212
  108.4 3.2 %collective-permute-done = f32[16,64]{1,0:T(8,128)S(1)} collective-permute-done((f32[16,64]{1,0:T(8,128)S(1)}, f32[16,64]{1,0:T(8,128)S(1)}, u32[]{:S(2)}, u32[]{:S(2)}) %collective-permute-start) | collective-permute-done | bytes 4128 | tf_op jit(solution)/shard_map/ppermute | solution.py:212
  112.6 6.3 %all-to-all-start.3 = ((f32[16,67,128]{2,1,0:T(8,128)}), f32[16,67,128]{2,1,0:T(8,128)S(1)}, u32[]{:S(2)}, u32[]{:S(2)}) async-start(f32[16,67,128]{2,1,0:T(8,128)} %fusion.23), calls=%async_computation.3 | async-start | bytes 1179648 | tf_op jit(solution)/shard_map/all_to_all | solution.py:219
  119.5 4.6 %add_divide_fusion = (f32[16,64,128]{2,1,0:T(8,128)}, f32[16,64,128]{2,1,0:T(8,128)}, f32[16,64,128]{2,1,0:T(8,128)}, f32[16,64,128]{2,1,0:T(8,128)}, f32[16,64,128]{2,1,0:T(8,128)}, /*index=5*/f32[16,64,128]{2,1,0:T(8,128)}) fusion(f32[16,64,128]{2,1,0:T(8,128)S(1)} %copy-done.6, f32[16,64,127]{2,1,0:T(8,128)} %get-tuple-element.38, ...), kind=kLoop, calls=%fused_computation.84 | loop fusion | flops 3014656 | bytes 6750208 | tf_op jit(solution)/shard_map/div | solution.py:30
  124.1 5.0 %all-to-all-done.3.framed_ref = f32[16,67,128]{2,1,0:T(8,128)S(1)} async-done(((f32[16,67,128]{2,1,0:T(8,128)}), f32[16,67,128]{2,1,0:T(8,128)S(1)}, u32[]{:S(2)}, u32[]{:S(2)}) %all-to-all-start.3) | async-done | bytes 548896 | tf_op jit(solution)/shard_map/all_to_all | solution.py:219
  130.4 4.2 %shard_map.123 = (f32[16,64,128]{2,1,0:T(8,128)}, f32[16,64,128]{2,1,0:T(8,128)}, f32[16,64,128]{2,1,0:T(8,128)}) custom-call(f32[16,67,128]{2,1,0:T(8,128)} %copy-done.10, f32[16,64,128]{2,1,0:T(8,128)} %get-tuple-element.45.active_ref, f32[16,64,128]{2,1,0:T(8,128)} %residual_ref.1, f32[16,128]{1,0:T(8,128)} %get-tuple-element.55.refs_0_.refs_1_, ...), custom_call_target="tpu_custom_call" | custom-call | tf_op jit(solution)/shard_map/pallas_call | solution.py:105
  134.5 14.7 %all_to_all.54 = f32[16,64,128]{2,1,0:T(8,128)S(1)} all-to-all(f32[16,64,128]{2,1,0:T(8,128)} %get-tuple-element.7), channel_id=1, replica_groups=mesh['gx'=8,'gy'=16] {'gy'}, dimensions={0} | all-to-all | bytes 1048576 | tf_op jit(solution)/shard_map/all_to_all | solution.py:198
  152.1 17.9 %all_to_all.55 = f32[128,8,128]{2,1,0:T(8,128)S(1)} all-to-all(f32[128,8,128]{2,1,0:T(8,128)S(1)} %bitcast.236), channel_id=1, replica_groups=mesh['gx'=8,'gy'=16] {'gx','gy'}, dimensions={0} | all-to-all | bytes 1048576 | tf_op jit(solution)/shard_map/all_to_all | solution.py:202
  178.6 17.5 %all_to_all.56 = f32[128,8,128]{2,1,0:T(8,128)S(1)} all-to-all(f32[128,8,128]{2,1,0:T(8,128)S(1)} %bitcast.237), channel_id=1, replica_groups=mesh['gx'=8,'gy'=16] {'gx','gy'}, dimensions={0} | all-to-all | bytes 1048576 | tf_op jit(solution)/shard_map/all_to_all | solution.py:208
  199.5 3.3 %collective-permute-start.7 = (f32[16,64]{1,0:T(8,128)S(1)}, f32[16,64]{1,0:T(8,128)S(1)}, u32[]{:S(2)}, u32[]{:S(2)}) collective-permute-start(f32[16,64]{1,0:T(8,128)S(1)} %bitcast.253), channel_id=1, source_target_pairs={{16,0},{32,16},{48,32},{64,48},{80,64},{96,80},{112,96},{17,1},{33... | collective-permute-start | bytes 12296 | tf_op jit(solution)/shard_map/ppermute | solution.py:213
  202.8 3.5 %collective-permute-start.6 = (f32[16,64]{1,0:T(8,128)S(1)}, f32[16,64]{1,0:T(8,128)S(1)}, u32[]{:S(2)}, u32[]{:S(2)}) collective-permute-start(f32[16,64]{1,0:T(8,128)S(1)} %bitcast.251), channel_id=1, source_target_pairs={{0,16},{16,32},{32,48},{48,64},{64,80},{80,96},{96,112},{1,17},{17... | collective-permute-start | bytes 12296 | tf_op jit(solution)/shard_map/ppermute | solution.py:212
  206.3 3.2 %collective-permute-done.6 = f32[16,64]{1,0:T(8,128)S(1)} collective-permute-done((f32[16,64]{1,0:T(8,128)S(1)}, f32[16,64]{1,0:T(8,128)S(1)}, u32[]{:S(2)}, u32[]{:S(2)}) %collective-permute-start.6) | collective-permute-done | bytes 4128 | tf_op jit(solution)/shard_map/ppermute | solution.py:212
  209.7 16.5 %all_to_all.57.framed_ref = f32[16,67,128]{2,1,0:T(8,128)S(1)} all-to-all(f32[16,67,128]{2,1,0:T(8,128)S(1)} %fusion.19), channel_id=1, replica_groups=mesh['gx'=8,'gy'=16] {'gy'}, dimensions={0} | all-to-all | bytes 1097728 | tf_op jit(solution)/shard_map/all_to_all | solution.py:219
  227.5 4.1 %shard_map.125 = (f32[16,64,128]{2,1,0:T(8,128)}, f32[16,64,128]{2,1,0:T(8,128)}) custom-call(f32[16,67,128]{2,1,0:T(8,128)} %copy-done.11, f32[16,64,128]{2,1,0:T(8,128)} %get-tuple-element.45.active_ref, f32[16,64,128]{2,1,0:T(8,128)} %get-tuple-element.8.residual_ref, f32[16,64,128]{2,1,0:T(8,128)} %get-tuple-element.9.refs_0_, ...), custom_call_target="tpu_custom_call" | custom-call | tf_op jit(solution)/shard_map/pallas_call | solution.py:105
  (111 shorter events, 60.9 us)
Async XLA Ops:
  0.6 8.6 %copy-start.12 = (s32[16,64,128]{2,1,0:T(8,128)S(1)}, s32[16,64,128]{2,1,0:T(8,128)}, u32[]{:S(2)}) copy-start(s32[16,64,128]{2,1,0:T(8,128)} %param.13) | copy-start | bytes 1572868
  0.6 9.5 %copy-start.6 = (f32[16,64,128]{2,1,0:T(8,128)S(1)}, f32[16,64,128]{2,1,0:T(8,128)}, u32[]{:S(2)}) copy-start(f32[16,64,128]{2,1,0:T(8,128)} %param.12) | copy-start | bytes 1572868
  2.7 31.4 %all-to-all-start = ((f32[16,64,128]{2,1,0:T(8,128)}), f32[16,64,128]{2,1,0:T(8,128)S(1)}, u32[]{:S(2)}, u32[]{:S(2)}) async-start(f32[16,64,128]{2,1,0:T(8,128)} %multiply_multiply_fusion), calls=%async_computation | async-start | bytes 1048576 | tf_op jit(solution)/shard_map/all_to_all | solution.py:198
  10.2 70.5 %collective-permute-start.2 = (f32[2,16,128]{2,1,0:T(8,128)S(1)}, f32[2,16,128]{2,1,0:T(8,128)S(1)}, u32[]{:S(2)}, u32[]{:S(2)}) collective-permute-start(f32[2,16,128]{2,1,0:T(8,128)S(1)} %bitcast.249), channel_id=1, source_target_pairs={{0,1},{1,2},{2,3},{3,4},{4,5},{5,6},{6,7},{7,8},{8,9},{9,10},{10,1... | collective-permute-start | bytes 49160 | tf_op jit(solution)/shard_map/ppermute | solution.py:22
  13.7 105.2 %collective-permute-start.3 = (f32[2,16,128]{2,1,0:T(8,128)S(1)}, f32[2,16,128]{2,1,0:T(8,128)S(1)}, u32[]{:S(2)}, u32[]{:S(2)}) collective-permute-start(f32[2,16,128]{2,1,0:T(8,128)S(1)} %bitcast.248), channel_id=1, source_target_pairs={{1,0},{2,1},{3,2},{4,3},{5,4},{6,5},{7,6},{8,7},{9,8},{10,9},{11,1... | collective-permute-start | bytes 49160 | tf_op jit(solution)/shard_map/ppermute | solution.py:22
  16.6 62.0 %collective-permute-start.4 = (f32[2,16,64]{2,1,0:T(8,128)S(1)}, f32[2,16,64]{2,1,0:T(8,128)S(1)}, u32[]{:S(2)}, u32[]{:S(2)}) collective-permute-start(f32[2,16,64]{2,1,0:T(8,128)S(1)} %get-tuple-element.12), channel_id=1, source_target_pairs={{0,16},{16,32},{32,48},{48,64},{64,80},{80,96},{96,112},{1,17},{17... | collective-permute-start | bytes 24584 | tf_op jit(solution)/shard_map/ppermute | solution.py:22
  21.8 56.8 %collective-permute-start.5 = (f32[2,16,64]{2,1,0:T(8,128)S(1)}, f32[2,16,64]{2,1,0:T(8,128)S(1)}, u32[]{:S(2)}, u32[]{:S(2)}) collective-permute-start(f32[2,16,64]{2,1,0:T(8,128)S(1)} %get-tuple-element.13), channel_id=1, source_target_pairs={{16,0},{32,16},{48,32},{64,48},{80,64},{96,80},{112,96},{17,1},{33... | collective-permute-start | bytes 24584 | tf_op jit(solution)/shard_map/ppermute | solution.py:22
  25.3 3.0 %copy-start.13 = (f32[1024]{0:T(1024)S(1)}, f32[1024]{0:T(1024)}, u32[]{:S(2)}) copy-start(f32[1024]{0:T(1024)} %param.19) | copy-start | bytes 12292
  25.3 3.7 %copy-start.14 = (f32[64]{0:T(128)S(1)}, f32[64]{0:T(128)}, u32[]{:S(2)}) copy-start(f32[64]{0:T(128)} %param.15) | copy-start | bytes 772
  34.1 3.3 %copy-start = (bf16[1024,1024]{1,0:T(8,128)(2,1)}, bf16[1024,1024]{1,0:T(8,128)(2,1)S(1)}, u32[]{:S(2)}) copy-start(bf16[1024,1024]{1,0:T(8,128)(2,1)S(1)} %get-tuple-element.16) | copy-start | bytes 6291460
  39.0 23.6 %all-to-all-start.1 = ((f32[128,8,128]{2,1,0:T(8,128)}), f32[128,8,128]{2,1,0:T(8,128)S(1)}, u32[]{:S(2)}, u32[]{:S(2)}) async-start(f32[128,8,128]{2,1,0:T(8,128)} %bitcast.3), calls=%async_computation.1 | async-start | bytes 1048576 | tf_op jit(solution)/shard_map/all_to_all | solution.py:202
  68.5 2.6 %copy-start.9 = (f32[16,8,1024]{2,1,0:T(8,128)S(1)}, f32[16,8,1024]{2,1,0:T(8,128)}, u32[]{:S(2)}) copy-start(f32[16,8,1024]{2,1,0:T(8,128)} %shard_map.122) | copy-start | bytes 1572868
  73.6 18.0 %all-to-all-start.2 = ((f32[128,8,128]{2,1,0:T(8,128)}), f32[128,8,128]{2,1,0:T(8,128)S(1)}, u32[]{:S(2)}, u32[]{:S(2)}) async-start(f32[128,8,128]{2,1,0:T(8,128)} %bitcast.235), calls=%async_computation.2 | async-start | bytes 1048576 | tf_op jit(solution)/shard_map/all_to_all | solution.py:208
  91.6 2.6 %copy-start.1 = (bf16[1024,1024]{1,0:T(8,128)(2,1)S(1)}, bf16[1024,1024]{1,0:T(8,128)(2,1)}, u32[]{:S(2)}) copy-start(bf16[1024,1024]{1,0:T(8,128)(2,1)} %copy-done) | copy-start | bytes 6291460
  101.5 6.8 %collective-permute-start.1 = (f32[16,64]{1,0:T(8,128)S(1)}, f32[16,64]{1,0:T(8,128)S(1)}, u32[]{:S(2)}, u32[]{:S(2)}) collective-permute-start(f32[16,64]{1,0:T(8,128)S(1)} %bitcast.252), channel_id=1, source_target_pairs={{16,0},{32,16},{48,32},{64,48},{80,64},{96,80},{112,96},{17,1},{33... | collective-permute-start | bytes 12296 | tf_op jit(solution)/shard_map/ppermute | solution.py:213
  104.8 6.8 %collective-permute-start = (f32[16,64]{1,0:T(8,128)S(1)}, f32[16,64]{1,0:T(8,128)S(1)}, u32[]{:S(2)}, u32[]{:S(2)}) collective-permute-start(f32[16,64]{1,0:T(8,128)S(1)} %bitcast.250), channel_id=1, source_target_pairs={{0,16},{16,32},{32,48},{48,64},{64,80},{80,96},{96,112},{1,17},{17... | collective-permute-start | bytes 12296 | tf_op jit(solution)/shard_map/ppermute | solution.py:212
  112.6 16.5 %all-to-all-start.3 = ((f32[16,67,128]{2,1,0:T(8,128)}), f32[16,67,128]{2,1,0:T(8,128)S(1)}, u32[]{:S(2)}, u32[]{:S(2)}) async-start(f32[16,67,128]{2,1,0:T(8,128)} %fusion.23), calls=%async_computation.3 | async-start | bytes 1179648 | tf_op jit(solution)/shard_map/all_to_all | solution.py:219
  134.5 14.8 %copy-start.4 = (bf16[1024,1024]{1,0:T(8,128)(2,1)S(1)}, bf16[1024,1024]{1,0:T(8,128)(2,1)}, u32[]{:S(2)}) copy-start(bf16[1024,1024]{1,0:T(8,128)(2,1)} %get-tuple-element.17) | copy-start | bytes 6291460
  152.1 18.0 %copy-start.7 = (bf16[1024,1024]{1,0:T(8,128)(2,1)S(1)}, bf16[1024,1024]{1,0:T(8,128)(2,1)}, u32[]{:S(2)}) copy-start(bf16[1024,1024]{1,0:T(8,128)(2,1)} %get-tuple-element.15) | copy-start | bytes 6291460
  174.3 2.6 %copy-start.8 = (f32[16,8,1024]{2,1,0:T(8,128)S(1)}, f32[16,8,1024]{2,1,0:T(8,128)}, u32[]{:S(2)}) copy-start(f32[16,8,1024]{2,1,0:T(8,128)} %shard_map.124) | copy-start | bytes 1572868
  177.7 18.5 %copy-start.5 = (bf16[1024,1024]{1,0:T(8,128)(2,1)S(1)}, bf16[1024,1024]{1,0:T(8,128)(2,1)}, u32[]{:S(2)}) copy-start(bf16[1024,1024]{1,0:T(8,128)(2,1)} %get-tuple-element.17) | copy-start | bytes 6291460
  178.6 18.4 %copy-start.3 = (bf16[1024,1024]{1,0:T(8,128)(2,1)S(1)}, bf16[1024,1024]{1,0:T(8,128)(2,1)}, u32[]{:S(2)}) copy-start(bf16[1024,1024]{1,0:T(8,128)(2,1)} %copy-done) | copy-start | bytes 6291460
  199.5 6.8 %collective-permute-start.7 = (f32[16,64]{1,0:T(8,128)S(1)}, f32[16,64]{1,0:T(8,128)S(1)}, u32[]{:S(2)}, u32[]{:S(2)}) collective-permute-start(f32[16,64]{1,0:T(8,128)S(1)} %bitcast.253), channel_id=1, source_target_pairs={{16,0},{32,16},{48,32},{64,48},{80,64},{96,80},{112,96},{17,1},{33... | collective-permute-start | bytes 12296 | tf_op jit(solution)/shard_map/ppermute | solution.py:213
  202.8 6.8 %collective-permute-start.6 = (f32[16,64]{1,0:T(8,128)S(1)}, f32[16,64]{1,0:T(8,128)S(1)}, u32[]{:S(2)}, u32[]{:S(2)}) collective-permute-start(f32[16,64]{1,0:T(8,128)S(1)} %bitcast.251), channel_id=1, source_target_pairs={{0,16},{16,32},{32,48},{48,64},{64,80},{80,96},{96,112},{1,17},{17... | collective-permute-start | bytes 12296 | tf_op jit(solution)/shard_map/ppermute | solution.py:212
  (3 other events, 4.1 us)

commit v16 on v15

--- a/solution.py
+++ b/solution.py
@@ -83,8 +83,10 @@
             jnp.where(col == 0, y_halo_ref[z], before(center, 1, cols, col_forward)),
         ]
         result = storage_term * center
-        for face_ref, other in zip(face_refs, others):
-            result = result + face_ref[z] * (center - other)
+        below = face_refs[0][z - 1] if z > 0 else zeros
+        plane_faces = [face_refs[0][z], below] + [face_ref[z] for face_ref in face_refs[1:]]
+        for face, other in zip(plane_faces, others):
+            result = result + face * (center - other)
         update = updates[z]
         residual = residual_ref[z] - (result + (1.0 - active_ref[z]) * update)
         residual_out[z] = residual
@@ -220,10 +222,10 @@
         y_strips = (active_y[0] * framed[:, -1, :rows], active_y[1] * framed[:, -1, rows:])
         if iteration + 1 < ITERS:
             residual, adjoint, scaled = framed_stencil(
-                framed, active, residual, adjoint, active_x, y_strips, faces, masses
+                framed, active, residual, adjoint, active_x, y_strips, [faces[0], *faces[2:]], masses
             )
         else:
-            residual, adjoint = framed_stencil(framed, active, residual, adjoint, active_x, y_strips, faces)
+            residual, adjoint = framed_stencil(framed, active, residual, adjoint, active_x, y_strips, [faces[0], *faces[2:]])
     return (adjoint, residual)
 
 

time: 233 us -> 232 us (level)
  no operation moved by 1% of the time
where the time goes in v16:
time: 232 us; the launch traced here: 231 us
  blocking collectives  66.6 us (29%)
  starting transfers between devices  55.2 us (24%)
  waiting for transfers between devices  30.6 us (13%)
  matrix products  27 us (12%)
  other arithmetic  21.5 us (9%)
  local copies, waits for them, and re-layouts  16.9 us (7%)
  Pallas kernels  12.1 us (5%)
    all_to_all x2, blocking collectives, shards(): lax.all_to_all(chunks, everyone, split_axis=0, concat_axis=0, tiled=True)  35.4 us
    dot_general x24, matrix products, product(): return jnp.einsum(spec, first, second, preferred_element_type=jnp.float32)  27 us
    all_to_all x2, waiting for transfers between devices, shards(): lax.all_to_all(chunks, everyone, split_axis=0, concat_axis=0, tiled=True)  18.7 us
    all_to_all x1, blocking collectives, shards(): lax.all_to_all(framed, 'gy', split_axis=0, concat_axis=0, tiled=True)  16.5 us
    all_to_all x2, starting transfers between devices, shards(): lax.all_to_all(chunks, everyone, split_axis=0, concat_axis=0, tiled=True)  15.7 us
    all_to_all x1, blocking collectives, shards(): lax.all_to_all(scaled, 'gy', split_axis=0, concat_axis=1, tiled=True)  14.7 us
    convert_element_type x2, other arithmetic, split_bf16(): rounded.astype(jnp.bfloat16)  8.94 us
    ppermute x2, starting transfers between devices, edge_pair(): lax.ppermute(last, axis, forward)  8.75 us
  transfers between devices with their start and end apart: 12, of which 5 were waited for; matrix products, arithmetic and copies ran while one was open for 21% of the time, Pallas kernels for 1%

profile of v16, /device:TPU:3, one launch (start us, length us, event | category | flops | bytes accessed | tf_op | source)
XLA Modules:
  0.0 231.1 jit_solution(7966565140903974794)
XLA Ops:
  2.7 6.5 %all-to-all-start = ((f32[16,64,128]{2,1,0:T(8,128)}), f32[16,64,128]{2,1,0:T(8,128)S(1)}, u32[]{:S(2)}, u32[]{:S(2)}) async-start(f32[16,64,128]{2,1,0:T(8,128)} %multiply_multiply_fusion), calls=%async_computation | async-start | bytes 1048576 | tf_op jit(solution)/shard_map/all_to_all | solution.py:200
  10.2 3.5 %collective-permute-start.2 = (f32[2,16,128]{2,1,0:T(8,128)S(1)}, f32[2,16,128]{2,1,0:T(8,128)S(1)}, u32[]{:S(2)}, u32[]{:S(2)}) collective-permute-start(f32[2,16,128]{2,1,0:T(8,128)S(1)} %bitcast.249), channel_id=1, source_target_pairs={{0,1},{1,2},{2,3},{3,4},{4,5},{5,6},{6,7},{7,8},{8,9},{9,10},{10,1... | collective-permute-start | bytes 49160 | tf_op jit(solution)/shard_map/ppermute | solution.py:22
  16.6 5.2 %collective-permute-start.4 = (f32[2,16,64]{2,1,0:T(8,128)S(1)}, f32[2,16,64]{2,1,0:T(8,128)S(1)}, u32[]{:S(2)}, u32[]{:S(2)}) collective-permute-start(f32[2,16,64]{2,1,0:T(8,128)S(1)} %get-tuple-element.12), channel_id=1, source_target_pairs={{0,16},{16,32},{32,48},{48,64},{64,80},{80,96},{96,112},{1,17},{17... | collective-permute-start | bytes 24584 | tf_op jit(solution)/shard_map/ppermute | solution.py:22
  29.5 4.5 %reduce-precision_convert_fusion.1 = (bf16[1024,1024]{1,0:T(8,128)(2,1)S(1)}, bf16[1024,1024]{1,0:T(8,128)(2,1)}) fusion(f32[1024,1024]{1,0:T(8,128)} %param.14), kind=kLoop, calls=%fused_computation.3 | loop fusion | flops 4194304 | bytes 8388608 | tf_op jit(solution)/shard_map/convert_element_type | solution.py:150
  38.8 10.7 %all-to-all-start.1 = ((f32[128,8,128]{2,1,0:T(8,128)}), f32[128,8,128]{2,1,0:T(8,128)S(1)}, u32[]{:S(2)}, u32[]{:S(2)}) async-start(f32[128,8,128]{2,1,0:T(8,128)} %bitcast.3), calls=%async_computation.1 | async-start | bytes 1048576 | tf_op jit(solution)/shard_map/all_to_all | solution.py:204
  49.5 4.5 %reduce-precision_convert_fusion = (bf16[1024,1024]{1,0:T(8,128)(2,1)S(1)}, bf16[1024,1024]{1,0:T(8,128)(2,1)}) fusion(f32[1024,1024]{1,0:T(8,128)} %param.17), kind=kLoop, calls=%fused_computation.1 | loop fusion | flops 4194304 | bytes 8388608 | tf_op jit(solution)/shard_map/convert_element_type | solution.py:150
  54.0 8.4 %all-to-all-done.1 = f32[128,8,128]{2,1,0:T(8,128)S(1)} async-done(((f32[128,8,128]{2,1,0:T(8,128)}), f32[128,8,128]{2,1,0:T(8,128)S(1)}, u32[]{:S(2)}, u32[]{:S(2)}) %all-to-all-start.1) | async-done | bytes 524320 | tf_op jit(solution)/shard_map/all_to_all | solution.py:204
  73.4 4.9 %all-to-all-start.2 = ((f32[128,8,128]{2,1,0:T(8,128)}), f32[128,8,128]{2,1,0:T(8,128)S(1)}, u32[]{:S(2)}, u32[]{:S(2)}) async-start(f32[128,8,128]{2,1,0:T(8,128)} %bitcast.235), calls=%async_computation.2 | async-start | bytes 1048576 | tf_op jit(solution)/shard_map/all_to_all | solution.py:210
  81.1 10.3 %all-to-all-done.2 = f32[128,8,128]{2,1,0:T(8,128)S(1)} async-done(((f32[128,8,128]{2,1,0:T(8,128)}), f32[128,8,128]{2,1,0:T(8,128)S(1)}, u32[]{:S(2)}, u32[]{:S(2)}) %all-to-all-start.2) | async-done | bytes 524320 | tf_op jit(solution)/shard_map/all_to_all | solution.py:210
  101.3 3.3 %collective-permute-start.1 = (f32[16,64]{1,0:T(8,128)S(1)}, f32[16,64]{1,0:T(8,128)S(1)}, u32[]{:S(2)}, u32[]{:S(2)}) collective-permute-start(f32[16,64]{1,0:T(8,128)S(1)} %bitcast.252), channel_id=1, source_target_pairs={{16,0},{32,16},{48,32},{64,48},{80,64},{96,80},{112,96},{17,1},{33... | collective-permute-start | bytes 12296 | tf_op jit(solution)/shard_map/ppermute | solution.py:215
  104.6 3.5 %collective-permute-start = (f32[16,64]{1,0:T(8,128)S(1)}, f32[16,64]{1,0:T(8,128)S(1)}, u32[]{:S(2)}, u32[]{:S(2)}) collective-permute-start(f32[16,64]{1,0:T(8,128)S(1)} %bitcast.250), channel_id=1, source_target_pairs={{0,16},{16,32},{32,48},{48,64},{64,80},{80,96},{96,112},{1,17},{17... | collective-permute-start | bytes 12296 | tf_op jit(solution)/shard_map/ppermute | solution.py:214
  108.2 3.2 %collective-permute-done = f32[16,64]{1,0:T(8,128)S(1)} collective-permute-done((f32[16,64]{1,0:T(8,128)S(1)}, f32[16,64]{1,0:T(8,128)S(1)}, u32[]{:S(2)}, u32[]{:S(2)}) %collective-permute-start) | collective-permute-done | bytes 4128 | tf_op jit(solution)/shard_map/ppermute | solution.py:214
  112.4 6.3 %all-to-all-start.3 = ((f32[16,67,128]{2,1,0:T(8,128)}), f32[16,67,128]{2,1,0:T(8,128)S(1)}, u32[]{:S(2)}, u32[]{:S(2)}) async-start(f32[16,67,128]{2,1,0:T(8,128)} %fusion.23), calls=%async_computation.3 | async-start | bytes 1179648 | tf_op jit(solution)/shard_map/all_to_all | solution.py:221
  119.3 4.2 %add_divide_fusion = (f32[16,64,128]{2,1,0:T(8,128)}, f32[16,64,128]{2,1,0:T(8,128)}, f32[16,64,128]{2,1,0:T(8,128)}, f32[16,64,128]{2,1,0:T(8,128)}, f32[16,64,128]{2,1,0:T(8,128)}) fusion(f32[16,64,128]{2,1,0:T(8,128)S(1)} %copy-done.6, f32[16,64,127]{2,1,0:T(8,128)} %get-tuple-element.37, f32[16,64,1]{2,1,0:T(8,128)} %copy.164, ...), kind=kLoop, calls=%fused_computation.84 | loop fusion | flops 2621440 | bytes 5734400 | tf_op jit(solution)/shard_map/div | solution.py:30
  123.5 5.5 %all-to-all-done.3.framed_ref = f32[16,67,128]{2,1,0:T(8,128)S(1)} async-done(((f32[16,67,128]{2,1,0:T(8,128)}), f32[16,67,128]{2,1,0:T(8,128)S(1)}, u32[]{:S(2)}, u32[]{:S(2)}) %all-to-all-start.3) | async-done | bytes 548896 | tf_op jit(solution)/shard_map/all_to_all | solution.py:221
  130.2 4.0 %shard_map.123 = (f32[16,64,128]{2,1,0:T(8,128)}, f32[16,64,128]{2,1,0:T(8,128)}, f32[16,64,128]{2,1,0:T(8,128)}) custom-call(f32[16,67,128]{2,1,0:T(8,128)} %copy-done.10, f32[16,64,128]{2,1,0:T(8,128)} %get-tuple-element.42.active_ref, f32[16,64,128]{2,1,0:T(8,128)} %residual_ref.1, f32[16,128]{1,0:T(8,128)} %get-tuple-element.52.refs_0_.refs_1_, ...), custom_call_target="tpu_custom_call" | custom-call | tf_op jit(solution)/shard_map/pallas_call | solution.py:107
  134.2 14.7 %all_to_all.54 = f32[16,64,128]{2,1,0:T(8,128)S(1)} all-to-all(f32[16,64,128]{2,1,0:T(8,128)} %get-tuple-element.7), channel_id=1, replica_groups=mesh['gx'=8,'gy'=16] {'gy'}, dimensions={0} | all-to-all | bytes 1048576 | tf_op jit(solution)/shard_map/all_to_all | solution.py:200
  151.7 17.9 %all_to_all.55 = f32[128,8,128]{2,1,0:T(8,128)S(1)} all-to-all(f32[128,8,128]{2,1,0:T(8,128)S(1)} %bitcast.236), channel_id=1, replica_groups=mesh['gx'=8,'gy'=16] {'gx','gy'}, dimensions={0} | all-to-all | bytes 1048576 | tf_op jit(solution)/shard_map/all_to_all | solution.py:204
  178.2 17.5 %all_to_all.56 = f32[128,8,128]{2,1,0:T(8,128)S(1)} all-to-all(f32[128,8,128]{2,1,0:T(8,128)S(1)} %bitcast.237), channel_id=1, replica_groups=mesh['gx'=8,'gy'=16] {'gx','gy'}, dimensions={0} | all-to-all | bytes 1048576 | tf_op jit(solution)/shard_map/all_to_all | solution.py:210
  199.1 3.3 %collective-permute-start.7 = (f32[16,64]{1,0:T(8,128)S(1)}, f32[16,64]{1,0:T(8,128)S(1)}, u32[]{:S(2)}, u32[]{:S(2)}) collective-permute-start(f32[16,64]{1,0:T(8,128)S(1)} %bitcast.253), channel_id=1, source_target_pairs={{16,0},{32,16},{48,32},{64,48},{80,64},{96,80},{112,96},{17,1},{33... | collective-permute-start | bytes 12296 | tf_op jit(solution)/shard_map/ppermute | solution.py:215
  202.4 3.5 %collective-permute-start.6 = (f32[16,64]{1,0:T(8,128)S(1)}, f32[16,64]{1,0:T(8,128)S(1)}, u32[]{:S(2)}, u32[]{:S(2)}) collective-permute-start(f32[16,64]{1,0:T(8,128)S(1)} %bitcast.251), channel_id=1, source_target_pairs={{0,16},{16,32},{32,48},{48,64},{64,80},{80,96},{96,112},{1,17},{17... | collective-permute-start | bytes 12296 | tf_op jit(solution)/shard_map/ppermute | solution.py:214
  206.0 3.2 %collective-permute-done.6 = f32[16,64]{1,0:T(8,128)S(1)} collective-permute-done((f32[16,64]{1,0:T(8,128)S(1)}, f32[16,64]{1,0:T(8,128)S(1)}, u32[]{:S(2)}, u32[]{:S(2)}) %collective-permute-start.6) | collective-permute-done | bytes 4128 | tf_op jit(solution)/shard_map/ppermute | solution.py:214
  209.4 16.5 %all_to_all.57.framed_ref = f32[16,67,128]{2,1,0:T(8,128)S(1)} all-to-all(f32[16,67,128]{2,1,0:T(8,128)S(1)} %fusion.19), channel_id=1, replica_groups=mesh['gx'=8,'gy'=16] {'gy'}, dimensions={0} | all-to-all | bytes 1097728 | tf_op jit(solution)/shard_map/all_to_all | solution.py:221
  227.1 4.0 %shard_map.125 = (f32[16,64,128]{2,1,0:T(8,128)}, f32[16,64,128]{2,1,0:T(8,128)}) custom-call(f32[16,67,128]{2,1,0:T(8,128)} %copy-done.11, f32[16,64,128]{2,1,0:T(8,128)} %get-tuple-element.42.active_ref, f32[16,64,128]{2,1,0:T(8,128)} %get-tuple-element.8.residual_ref, f32[16,64,128]{2,1,0:T(8,128)} %get-tuple-element.9.refs_0_, ...), custom_call_target="tpu_custom_call" | custom-call | tf_op jit(solution)/shard_map/pallas_call | solution.py:107
  (111 shorter events, 60.8 us)
Async XLA Ops:
  0.6 8.6 %copy-start.12 = (s32[16,64,128]{2,1,0:T(8,128)S(1)}, s32[16,64,128]{2,1,0:T(8,128)}, u32[]{:S(2)}) copy-start(s32[16,64,128]{2,1,0:T(8,128)} %param.13) | copy-start | bytes 1572868
  0.6 9.5 %copy-start.6 = (f32[16,64,128]{2,1,0:T(8,128)S(1)}, f32[16,64,128]{2,1,0:T(8,128)}, u32[]{:S(2)}) copy-start(f32[16,64,128]{2,1,0:T(8,128)} %param.12) | copy-start | bytes 1572868
  2.7 31.2 %all-to-all-start = ((f32[16,64,128]{2,1,0:T(8,128)}), f32[16,64,128]{2,1,0:T(8,128)S(1)}, u32[]{:S(2)}, u32[]{:S(2)}) async-start(f32[16,64,128]{2,1,0:T(8,128)} %multiply_multiply_fusion), calls=%async_computation | async-start | bytes 1048576 | tf_op jit(solution)/shard_map/all_to_all | solution.py:200
  10.2 70.4 %collective-permute-start.2 = (f32[2,16,128]{2,1,0:T(8,128)S(1)}, f32[2,16,128]{2,1,0:T(8,128)S(1)}, u32[]{:S(2)}, u32[]{:S(2)}) collective-permute-start(f32[2,16,128]{2,1,0:T(8,128)S(1)} %bitcast.249), channel_id=1, source_target_pairs={{0,1},{1,2},{2,3},{3,4},{4,5},{5,6},{6,7},{7,8},{8,9},{9,10},{10,1... | collective-permute-start | bytes 49160 | tf_op jit(solution)/shard_map/ppermute | solution.py:22
  13.7 105.0 %collective-permute-start.3 = (f32[2,16,128]{2,1,0:T(8,128)S(1)}, f32[2,16,128]{2,1,0:T(8,128)S(1)}, u32[]{:S(2)}, u32[]{:S(2)}) collective-permute-start(f32[2,16,128]{2,1,0:T(8,128)S(1)} %bitcast.248), channel_id=1, source_target_pairs={{1,0},{2,1},{3,2},{4,3},{5,4},{6,5},{7,6},{8,7},{9,8},{10,9},{11,1... | collective-permute-start | bytes 49160 | tf_op jit(solution)/shard_map/ppermute | solution.py:22
  16.6 61.8 %collective-permute-start.4 = (f32[2,16,64]{2,1,0:T(8,128)S(1)}, f32[2,16,64]{2,1,0:T(8,128)S(1)}, u32[]{:S(2)}, u32[]{:S(2)}) collective-permute-start(f32[2,16,64]{2,1,0:T(8,128)S(1)} %get-tuple-element.12), channel_id=1, source_target_pairs={{0,16},{16,32},{32,48},{48,64},{64,80},{80,96},{96,112},{1,17},{17... | collective-permute-start | bytes 24584 | tf_op jit(solution)/shard_map/ppermute | solution.py:22
  21.8 56.6 %collective-permute-start.5 = (f32[2,16,64]{2,1,0:T(8,128)S(1)}, f32[2,16,64]{2,1,0:T(8,128)S(1)}, u32[]{:S(2)}, u32[]{:S(2)}) collective-permute-start(f32[2,16,64]{2,1,0:T(8,128)S(1)} %get-tuple-element.13), channel_id=1, source_target_pairs={{16,0},{32,16},{48,32},{64,48},{80,64},{96,80},{112,96},{17,1},{33... | collective-permute-start | bytes 24584 | tf_op jit(solution)/shard_map/ppermute | solution.py:22
  24.3 3.0 %copy-start.13 = (f32[1024]{0:T(1024)S(1)}, f32[1024]{0:T(1024)}, u32[]{:S(2)}) copy-start(f32[1024]{0:T(1024)} %param.19) | copy-start | bytes 12292
  24.3 4.5 %copy-start.14 = (f32[64]{0:T(128)S(1)}, f32[64]{0:T(128)}, u32[]{:S(2)}) copy-start(f32[64]{0:T(128)} %param.15) | copy-start | bytes 772
  33.9 3.3 %copy-start = (bf16[1024,1024]{1,0:T(8,128)(2,1)}, bf16[1024,1024]{1,0:T(8,128)(2,1)S(1)}, u32[]{:S(2)}) copy-start(bf16[1024,1024]{1,0:T(8,128)(2,1)S(1)} %get-tuple-element.16) | copy-start | bytes 6291460
  38.8 23.6 %all-to-all-start.1 = ((f32[128,8,128]{2,1,0:T(8,128)}), f32[128,8,128]{2,1,0:T(8,128)S(1)}, u32[]{:S(2)}, u32[]{:S(2)}) async-start(f32[128,8,128]{2,1,0:T(8,128)} %bitcast.3), calls=%async_computation.1 | async-start | bytes 1048576 | tf_op jit(solution)/shard_map/all_to_all | solution.py:204
  68.3 2.6 %copy-start.9 = (f32[16,8,1024]{2,1,0:T(8,128)S(1)}, f32[16,8,1024]{2,1,0:T(8,128)}, u32[]{:S(2)}) copy-start(f32[16,8,1024]{2,1,0:T(8,128)} %shard_map.122) | copy-start | bytes 1572868
  73.4 18.0 %all-to-all-start.2 = ((f32[128,8,128]{2,1,0:T(8,128)}), f32[128,8,128]{2,1,0:T(8,128)S(1)}, u32[]{:S(2)}, u32[]{:S(2)}) async-start(f32[128,8,128]{2,1,0:T(8,128)} %bitcast.235), calls=%async_computation.2 | async-start | bytes 1048576 | tf_op jit(solution)/shard_map/all_to_all | solution.py:210
  91.4 2.6 %copy-start.1 = (bf16[1024,1024]{1,0:T(8,128)(2,1)S(1)}, bf16[1024,1024]{1,0:T(8,128)(2,1)}, u32[]{:S(2)}) copy-start(bf16[1024,1024]{1,0:T(8,128)(2,1)} %copy-done) | copy-start | bytes 6291460
  101.3 6.8 %collective-permute-start.1 = (f32[16,64]{1,0:T(8,128)S(1)}, f32[16,64]{1,0:T(8,128)S(1)}, u32[]{:S(2)}, u32[]{:S(2)}) collective-permute-start(f32[16,64]{1,0:T(8,128)S(1)} %bitcast.252), channel_id=1, source_target_pairs={{16,0},{32,16},{48,32},{64,48},{80,64},{96,80},{112,96},{17,1},{33... | collective-permute-start | bytes 12296 | tf_op jit(solution)/shard_map/ppermute | solution.py:215
  104.6 6.8 %collective-permute-start = (f32[16,64]{1,0:T(8,128)S(1)}, f32[16,64]{1,0:T(8,128)S(1)}, u32[]{:S(2)}, u32[]{:S(2)}) collective-permute-start(f32[16,64]{1,0:T(8,128)S(1)} %bitcast.250), channel_id=1, source_target_pairs={{0,16},{16,32},{32,48},{48,64},{64,80},{80,96},{96,112},{1,17},{17... | collective-permute-start | bytes 12296 | tf_op jit(solution)/shard_map/ppermute | solution.py:214
  112.4 16.5 %all-to-all-start.3 = ((f32[16,67,128]{2,1,0:T(8,128)}), f32[16,67,128]{2,1,0:T(8,128)S(1)}, u32[]{:S(2)}, u32[]{:S(2)}) async-start(f32[16,67,128]{2,1,0:T(8,128)} %fusion.23), calls=%async_computation.3 | async-start | bytes 1179648 | tf_op jit(solution)/shard_map/all_to_all | solution.py:221
  134.2 14.8 %copy-start.4 = (bf16[1024,1024]{1,0:T(8,128)(2,1)S(1)}, bf16[1024,1024]{1,0:T(8,128)(2,1)}, u32[]{:S(2)}) copy-start(bf16[1024,1024]{1,0:T(8,128)(2,1)} %get-tuple-element.17) | copy-start | bytes 6291460
  151.7 18.0 %copy-start.7 = (bf16[1024,1024]{1,0:T(8,128)(2,1)S(1)}, bf16[1024,1024]{1,0:T(8,128)(2,1)}, u32[]{:S(2)}) copy-start(bf16[1024,1024]{1,0:T(8,128)(2,1)} %get-tuple-element.15) | copy-start | bytes 6291460
  173.9 2.6 %copy-start.8 = (f32[16,8,1024]{2,1,0:T(8,128)S(1)}, f32[16,8,1024]{2,1,0:T(8,128)}, u32[]{:S(2)}) copy-start(f32[16,8,1024]{2,1,0:T(8,128)} %shard_map.124) | copy-start | bytes 1572868
  177.3 18.5 %copy-start.5 = (bf16[1024,1024]{1,0:T(8,128)(2,1)S(1)}, bf16[1024,1024]{1,0:T(8,128)(2,1)}, u32[]{:S(2)}) copy-start(bf16[1024,1024]{1,0:T(8,128)(2,1)} %get-tuple-element.17) | copy-start | bytes 6291460
  178.2 18.4 %copy-start.3 = (bf16[1024,1024]{1,0:T(8,128)(2,1)S(1)}, bf16[1024,1024]{1,0:T(8,128)(2,1)}, u32[]{:S(2)}) copy-start(bf16[1024,1024]{1,0:T(8,128)(2,1)} %copy-done) | copy-start | bytes 6291460
  199.1 6.8 %collective-permute-start.7 = (f32[16,64]{1,0:T(8,128)S(1)}, f32[16,64]{1,0:T(8,128)S(1)}, u32[]{:S(2)}, u32[]{:S(2)}) collective-permute-start(f32[16,64]{1,0:T(8,128)S(1)} %bitcast.253), channel_id=1, source_target_pairs={{16,0},{32,16},{48,32},{64,48},{80,64},{96,80},{112,96},{17,1},{33... | collective-permute-start | bytes 12296 | tf_op jit(solution)/shard_map/ppermute | solution.py:215
  202.4 6.8 %collective-permute-start.6 = (f32[16,64]{1,0:T(8,128)S(1)}, f32[16,64]{1,0:T(8,128)S(1)}, u32[]{:S(2)}, u32[]{:S(2)}) collective-permute-start(f32[16,64]{1,0:T(8,128)S(1)} %bitcast.251), channel_id=1, source_target_pairs={{0,16},{16,32},{32,48},{48,64},{64,80},{80,96},{96,112},{1,17},{17... | collective-permute-start | bytes 12296 | tf_op jit(solution)/shard_map/ppermute | solution.py:214
  (3 other events, 4.1 us)

commit v17 on v16

--- a/solution.py
+++ b/solution.py
@@ -50,8 +50,8 @@
 def framed_kernel(has_adjoint, has_scale, framed_ref, active_ref, residual_ref, *refs):
     refs = list(refs)
     adjoint_ref = refs.pop(0) if has_adjoint else None
-    x_low_ref, x_high_ref, y_halo_ref = refs[:3]
-    refs = refs[3:]
+    x_low_ref, x_high_ref, y_halo_ref, x_face_ref = refs[:4]
+    refs = refs[4:]
     mass_x_ref, mass_y_ref = (refs.pop(0), refs.pop(0)) if has_scale else (None, None)
     scaled_out = refs.pop() if has_scale else None
     face_refs, residual_out, adjoint_out = refs[:-2], refs[-2], refs[-1]
@@ -84,7 +84,10 @@
         ]
         result = storage_term * center
         below = face_refs[0][z - 1] if z > 0 else zeros
-        plane_faces = [face_refs[0][z], below] + [face_ref[z] for face_ref in face_refs[1:]]
+        x_plus = face_refs[1][z]
+        x_edge = jnp.broadcast_to(x_face_ref[pl.ds(z, 1), :], (rows, cols))
+        x_minus = jnp.where(row == 0, x_edge, before(x_plus, 0, rows, row_forward))
+        plane_faces = [face_refs[0][z], below, x_plus, x_minus] + [face_ref[z] for face_ref in face_refs[2:]]
         for face, other in zip(plane_faces, others):
             result = result + face * (center - other)
         update = updates[z]
@@ -102,7 +105,7 @@
     y_halo = jnp.where(lane == 0, y_strips[0][:, :, None], y_strips[1][:, :, None])
     carried = [] if adjoint is None else [adjoint]
     scales = [] if masses is None else list(masses)
-    operands = [framed, active, residual, *carried, x_strips[0], x_strips[1], y_halo, *scales, *faces]
+    operands = [framed, active, residual, *carried, x_strips[0], x_strips[1], y_halo, faces[3][:, 0, :], *scales, faces[0], faces[2], *faces[4:]]
     outputs = 2 if masses is None else 3
     return pl.pallas_call(
         functools.partial(framed_kernel, adjoint is not None, masses is not None),
@@ -222,10 +225,10 @@
         y_strips = (active_y[0] * framed[:, -1, :rows], active_y[1] * framed[:, -1, rows:])
         if iteration + 1 < ITERS:
             residual, adjoint, scaled = framed_stencil(
-                framed, active, residual, adjoint, active_x, y_strips, [faces[0], *faces[2:]], masses
+                framed, active, residual, adjoint, active_x, y_strips, faces, masses
             )
         else:
-            residual, adjoint = framed_stencil(framed, active, residual, adjoint, active_x, y_strips, [faces[0], *faces[2:]])
+            residual, adjoint = framed_stencil(framed, active, residual, adjoint, active_x, y_strips, faces)
     return (adjoint, residual)
 
 

time: 232 us -> 232 us (level)
  no operation moved by 1% of the time
where the time goes in v17:
time: 232 us; the launch traced here: 231 us
  blocking collectives  66.6 us (29%)
  starting transfers between devices  55.2 us (24%)
  waiting for transfers between devices  30.4 us (13%)
  matrix products  26.9 us (12%)
  other arithmetic  21.7 us (9%)
  local copies, waits for them, and re-layouts  16.9 us (7%)
  Pallas kernels  12 us (5%)
    all_to_all x2, blocking collectives, shards(): lax.all_to_all(chunks, everyone, split_axis=0, concat_axis=0, tiled=True)  35.4 us
    dot_general x24, matrix products, product(): return jnp.einsum(spec, first, second, preferred_element_type=jnp.float32)  26.9 us
    all_to_all x2, waiting for transfers between devices, shards(): lax.all_to_all(chunks, everyone, split_axis=0, concat_axis=0, tiled=True)  18.7 us
    all_to_all x1, blocking collectives, shards(): lax.all_to_all(framed, 'gy', split_axis=0, concat_axis=0, tiled=True)  16.5 us
    all_to_all x2, starting transfers between devices, shards(): lax.all_to_all(chunks, everyone, split_axis=0, concat_axis=0, tiled=True)  15.7 us
    all_to_all x1, blocking collectives, shards(): lax.all_to_all(scaled, 'gy', split_axis=0, concat_axis=1, tiled=True)  14.7 us
    convert_element_type x2, other arithmetic, split_bf16(): rounded.astype(jnp.bfloat16)  8.92 us
    ppermute x2, starting transfers between devices, edge_pair(): lax.ppermute(last, axis, forward)  8.75 us
  transfers between devices with their start and end apart: 12, of which 5 were waited for; matrix products, arithmetic and copies ran while one was open for 21% of the time, Pallas kernels for 1%

profile of v17, /device:TPU:3, one launch (start us, length us, event | category | flops | bytes accessed | tf_op | source)
XLA Modules:
  0.0 230.9 jit_solution(13009491331961620157)
XLA Ops:
  2.7 6.5 %all-to-all-start = ((f32[16,64,128]{2,1,0:T(8,128)}), f32[16,64,128]{2,1,0:T(8,128)S(1)}, u32[]{:S(2)}, u32[]{:S(2)}) async-start(f32[16,64,128]{2,1,0:T(8,128)} %multiply_multiply_fusion), calls=%async_computation | async-start | bytes 1048576 | tf_op jit(solution)/shard_map/all_to_all | solution.py:203
  10.2 3.5 %collective-permute-start.2 = (f32[2,16,128]{2,1,0:T(8,128)S(1)}, f32[2,16,128]{2,1,0:T(8,128)S(1)}, u32[]{:S(2)}, u32[]{:S(2)}) collective-permute-start(f32[2,16,128]{2,1,0:T(8,128)S(1)} %bitcast.251), channel_id=1, source_target_pairs={{0,1},{1,2},{2,3},{3,4},{4,5},{5,6},{6,7},{7,8},{8,9},{9,10},{10,1... | collective-permute-start | bytes 49160 | tf_op jit(solution)/shard_map/ppermute | solution.py:22
  16.6 5.2 %collective-permute-start.4 = (f32[2,16,64]{2,1,0:T(8,128)S(1)}, f32[2,16,64]{2,1,0:T(8,128)S(1)}, u32[]{:S(2)}, u32[]{:S(2)}) collective-permute-start(f32[2,16,64]{2,1,0:T(8,128)S(1)} %get-tuple-element.12), channel_id=1, source_target_pairs={{0,16},{16,32},{32,48},{48,64},{64,80},{80,96},{96,112},{1,17},{17... | collective-permute-start | bytes 24584 | tf_op jit(solution)/shard_map/ppermute | solution.py:22
  29.4 4.4 %reduce-precision_convert_fusion.1 = (bf16[1024,1024]{1,0:T(8,128)(2,1)S(1)}, bf16[1024,1024]{1,0:T(8,128)(2,1)}) fusion(f32[1024,1024]{1,0:T(8,128)} %param.14), kind=kLoop, calls=%fused_computation.3 | loop fusion | flops 4194304 | bytes 8388608 | tf_op jit(solution)/shard_map/convert_element_type | solution.py:153
  38.7 10.7 %all-to-all-start.1 = ((f32[128,8,128]{2,1,0:T(8,128)}), f32[128,8,128]{2,1,0:T(8,128)S(1)}, u32[]{:S(2)}, u32[]{:S(2)}) async-start(f32[128,8,128]{2,1,0:T(8,128)} %bitcast.3), calls=%async_computation.1 | async-start | bytes 1048576 | tf_op jit(solution)/shard_map/all_to_all | solution.py:207
  49.4 4.5 %reduce-precision_convert_fusion = (bf16[1024,1024]{1,0:T(8,128)(2,1)S(1)}, bf16[1024,1024]{1,0:T(8,128)(2,1)}) fusion(f32[1024,1024]{1,0:T(8,128)} %param.17), kind=kLoop, calls=%fused_computation.1 | loop fusion | flops 4194304 | bytes 8388608 | tf_op jit(solution)/shard_map/convert_element_type | solution.py:153
  53.9 8.4 %all-to-all-done.1 = f32[128,8,128]{2,1,0:T(8,128)S(1)} async-done(((f32[128,8,128]{2,1,0:T(8,128)}), f32[128,8,128]{2,1,0:T(8,128)S(1)}, u32[]{:S(2)}, u32[]{:S(2)}) %all-to-all-start.1) | async-done | bytes 524320 | tf_op jit(solution)/shard_map/all_to_all | solution.py:207
  73.3 4.9 %all-to-all-start.2 = ((f32[128,8,128]{2,1,0:T(8,128)}), f32[128,8,128]{2,1,0:T(8,128)S(1)}, u32[]{:S(2)}, u32[]{:S(2)}) async-start(f32[128,8,128]{2,1,0:T(8,128)} %bitcast.236), calls=%async_computation.2 | async-start | bytes 1048576 | tf_op jit(solution)/shard_map/all_to_all | solution.py:213
  81.1 10.3 %all-to-all-done.2 = f32[128,8,128]{2,1,0:T(8,128)S(1)} async-done(((f32[128,8,128]{2,1,0:T(8,128)}), f32[128,8,128]{2,1,0:T(8,128)S(1)}, u32[]{:S(2)}, u32[]{:S(2)}) %all-to-all-start.2) | async-done | bytes 524320 | tf_op jit(solution)/shard_map/all_to_all | solution.py:213
  101.3 3.3 %collective-permute-start.1 = (f32[16,64]{1,0:T(8,128)S(1)}, f32[16,64]{1,0:T(8,128)S(1)}, u32[]{:S(2)}, u32[]{:S(2)}) collective-permute-start(f32[16,64]{1,0:T(8,128)S(1)} %bitcast.255), channel_id=1, source_target_pairs={{16,0},{32,16},{48,32},{64,48},{80,64},{96,80},{112,96},{17,1},{33... | collective-permute-start | bytes 12296 | tf_op jit(solution)/shard_map/ppermute | solution.py:218
  104.6 3.5 %collective-permute-start = (f32[16,64]{1,0:T(8,128)S(1)}, f32[16,64]{1,0:T(8,128)S(1)}, u32[]{:S(2)}, u32[]{:S(2)}) collective-permute-start(f32[16,64]{1,0:T(8,128)S(1)} %bitcast.253), channel_id=1, source_target_pairs={{0,16},{16,32},{32,48},{48,64},{64,80},{80,96},{96,112},{1,17},{17... | collective-permute-start | bytes 12296 | tf_op jit(solution)/shard_map/ppermute | solution.py:217
  108.1 3.2 %collective-permute-done = f32[16,64]{1,0:T(8,128)S(1)} collective-permute-done((f32[16,64]{1,0:T(8,128)S(1)}, f32[16,64]{1,0:T(8,128)S(1)}, u32[]{:S(2)}, u32[]{:S(2)}) %collective-permute-start) | collective-permute-done | bytes 4128 | tf_op jit(solution)/shard_map/ppermute | solution.py:217
  112.3 6.3 %all-to-all-start.3 = ((f32[16,67,128]{2,1,0:T(8,128)}), f32[16,67,128]{2,1,0:T(8,128)S(1)}, u32[]{:S(2)}, u32[]{:S(2)}) async-start(f32[16,67,128]{2,1,0:T(8,128)} %fusion.23), calls=%async_computation.3 | async-start | bytes 1179648 | tf_op jit(solution)/shard_map/all_to_all | solution.py:224
  118.7 3.8 %add_divide_fusion = (f32[16,64,128]{2,1,0:T(8,128)}, f32[16,64,128]{2,1,0:T(8,128)}, f32[16,64,128]{2,1,0:T(8,128)}, f32[16,64,128]{2,1,0:T(8,128)}, f32[16,64,128]{2,1,0:T(8,128)S(1)}) fusion(f32[16,64,128]{2,1,0:T(8,128)S(1)} %copy-done.6, f32[16,64,127]{2,1,0:T(8,128)} %get-tuple-element.37, f32[16,64,1]{2,1,0:T(8,128)} %copy.164, ...), kind=kLoop, calls=%fused_computation.83 | loop fusion | flops 2097152 | bytes 5210112 | tf_op jit(solution)/shard_map/div | solution.py:30
  123.7 5.2 %all-to-all-done.3.framed_ref = f32[16,67,128]{2,1,0:T(8,128)S(1)} async-done(((f32[16,67,128]{2,1,0:T(8,128)}), f32[16,67,128]{2,1,0:T(8,128)S(1)}, u32[]{:S(2)}, u32[]{:S(2)}) %all-to-all-start.3) | async-done | bytes 548896 | tf_op jit(solution)/shard_map/all_to_all | solution.py:224
  130.1 4.0 %shard_map.123 = (f32[16,64,128]{2,1,0:T(8,128)}, f32[16,64,128]{2,1,0:T(8,128)}, f32[16,64,128]{2,1,0:T(8,128)}) custom-call(f32[16,67,128]{2,1,0:T(8,128)} %copy-done.10, f32[16,64,128]{2,1,0:T(8,128)} %get-tuple-element.42.active_ref, f32[16,64,128]{2,1,0:T(8,128)} %residual_ref.1, f32[16,128]{1,0:T(8,128)} %get-tuple-element.54.refs_0_.refs_1_, ...), custom_call_target="tpu_custom_call" | custom-call | tf_op jit(solution)/shard_map/pallas_call | solution.py:110
  134.1 14.7 %all_to_all.54 = f32[16,64,128]{2,1,0:T(8,128)S(1)} all-to-all(f32[16,64,128]{2,1,0:T(8,128)} %get-tuple-element.7), channel_id=1, replica_groups=mesh['gx'=8,'gy'=16] {'gy'}, dimensions={0} | all-to-all | bytes 1048576 | tf_op jit(solution)/shard_map/all_to_all | solution.py:203
  151.6 17.9 %all_to_all.55 = f32[128,8,128]{2,1,0:T(8,128)S(1)} all-to-all(f32[128,8,128]{2,1,0:T(8,128)S(1)} %bitcast.237), channel_id=1, replica_groups=mesh['gx'=8,'gy'=16] {'gx','gy'}, dimensions={0} | all-to-all | bytes 1048576 | tf_op jit(solution)/shard_map/all_to_all | solution.py:207
  178.1 17.5 %all_to_all.56 = f32[128,8,128]{2,1,0:T(8,128)S(1)} all-to-all(f32[128,8,128]{2,1,0:T(8,128)S(1)} %bitcast.238), channel_id=1, replica_groups=mesh['gx'=8,'gy'=16] {'gx','gy'}, dimensions={0} | all-to-all | bytes 1048576 | tf_op jit(solution)/shard_map/all_to_all | solution.py:213
  199.0 3.3 %collective-permute-start.7 = (f32[16,64]{1,0:T(8,128)S(1)}, f32[16,64]{1,0:T(8,128)S(1)}, u32[]{:S(2)}, u32[]{:S(2)}) collective-permute-start(f32[16,64]{1,0:T(8,128)S(1)} %bitcast.256), channel_id=1, source_target_pairs={{16,0},{32,16},{48,32},{64,48},{80,64},{96,80},{112,96},{17,1},{33... | collective-permute-start | bytes 12296 | tf_op jit(solution)/shard_map/ppermute | solution.py:218
  202.3 3.5 %collective-permute-start.6 = (f32[16,64]{1,0:T(8,128)S(1)}, f32[16,64]{1,0:T(8,128)S(1)}, u32[]{:S(2)}, u32[]{:S(2)}) collective-permute-start(f32[16,64]{1,0:T(8,128)S(1)} %bitcast.254), channel_id=1, source_target_pairs={{0,16},{16,32},{32,48},{48,64},{64,80},{80,96},{96,112},{1,17},{17... | collective-permute-start | bytes 12296 | tf_op jit(solution)/shard_map/ppermute | solution.py:217
  205.8 3.2 %collective-permute-done.6 = f32[16,64]{1,0:T(8,128)S(1)} collective-permute-done((f32[16,64]{1,0:T(8,128)S(1)}, f32[16,64]{1,0:T(8,128)S(1)}, u32[]{:S(2)}, u32[]{:S(2)}) %collective-permute-start.6) | collective-permute-done | bytes 4128 | tf_op jit(solution)/shard_map/ppermute | solution.py:217
  209.2 16.5 %all_to_all.57.framed_ref = f32[16,67,128]{2,1,0:T(8,128)S(1)} all-to-all(f32[16,67,128]{2,1,0:T(8,128)S(1)} %fusion.19), channel_id=1, replica_groups=mesh['gx'=8,'gy'=16] {'gy'}, dimensions={0} | all-to-all | bytes 1097728 | tf_op jit(solution)/shard_map/all_to_all | solution.py:224
  227.0 3.9 %shard_map.125 = (f32[16,64,128]{2,1,0:T(8,128)}, f32[16,64,128]{2,1,0:T(8,128)}) custom-call(f32[16,67,128]{2,1,0:T(8,128)} %copy-done.11, f32[16,64,128]{2,1,0:T(8,128)} %get-tuple-element.42.active_ref, f32[16,64,128]{2,1,0:T(8,128)} %get-tuple-element.8.residual_ref, f32[16,64,128]{2,1,0:T(8,128)} %get-tuple-element.9.refs_0_, ...), custom_call_target="tpu_custom_call" | custom-call | tf_op jit(solution)/shard_map/pallas_call | solution.py:110
  (114 shorter events, 61.3 us)
Async XLA Ops:
  0.6 8.6 %copy-start.13 = (s32[16,64,128]{2,1,0:T(8,128)S(1)}, s32[16,64,128]{2,1,0:T(8,128)}, u32[]{:S(2)}) copy-start(s32[16,64,128]{2,1,0:T(8,128)} %param.13) | copy-start | bytes 1572868
  0.6 9.5 %copy-start.6 = (f32[16,64,128]{2,1,0:T(8,128)S(1)}, f32[16,64,128]{2,1,0:T(8,128)}, u32[]{:S(2)}) copy-start(f32[16,64,128]{2,1,0:T(8,128)} %param.12) | copy-start | bytes 1572868
  2.7 31.2 %all-to-all-start = ((f32[16,64,128]{2,1,0:T(8,128)}), f32[16,64,128]{2,1,0:T(8,128)S(1)}, u32[]{:S(2)}, u32[]{:S(2)}) async-start(f32[16,64,128]{2,1,0:T(8,128)} %multiply_multiply_fusion), calls=%async_computation | async-start | bytes 1048576 | tf_op jit(solution)/shard_map/all_to_all | solution.py:203
  10.2 112.2 %collective-permute-start.2 = (f32[2,16,128]{2,1,0:T(8,128)S(1)}, f32[2,16,128]{2,1,0:T(8,128)S(1)}, u32[]{:S(2)}, u32[]{:S(2)}) collective-permute-start(f32[2,16,128]{2,1,0:T(8,128)S(1)} %bitcast.251), channel_id=1, source_target_pairs={{0,1},{1,2},{2,3},{3,4},{4,5},{5,6},{6,7},{7,8},{8,9},{9,10},{10,1... | collective-permute-start | bytes 49160 | tf_op jit(solution)/shard_map/ppermute | solution.py:22
  13.8 66.7 %collective-permute-start.3 = (f32[2,16,128]{2,1,0:T(8,128)S(1)}, f32[2,16,128]{2,1,0:T(8,128)S(1)}, u32[]{:S(2)}, u32[]{:S(2)}) collective-permute-start(f32[2,16,128]{2,1,0:T(8,128)S(1)} %bitcast.252), channel_id=1, source_target_pairs={{1,0},{2,1},{3,2},{4,3},{5,4},{6,5},{7,6},{8,7},{9,8},{10,9},{11,1... | collective-permute-start | bytes 49160 | tf_op jit(solution)/shard_map/ppermute | solution.py:22
  16.6 61.7 %collective-permute-start.4 = (f32[2,16,64]{2,1,0:T(8,128)S(1)}, f32[2,16,64]{2,1,0:T(8,128)S(1)}, u32[]{:S(2)}, u32[]{:S(2)}) collective-permute-start(f32[2,16,64]{2,1,0:T(8,128)S(1)} %get-tuple-element.12), channel_id=1, source_target_pairs={{0,16},{16,32},{32,48},{48,64},{64,80},{80,96},{96,112},{1,17},{17... | collective-permute-start | bytes 24584 | tf_op jit(solution)/shard_map/ppermute | solution.py:22
  21.8 56.5 %collective-permute-start.5 = (f32[2,16,64]{2,1,0:T(8,128)S(1)}, f32[2,16,64]{2,1,0:T(8,128)S(1)}, u32[]{:S(2)}, u32[]{:S(2)}) collective-permute-start(f32[2,16,64]{2,1,0:T(8,128)S(1)} %get-tuple-element.13), channel_id=1, source_target_pairs={{16,0},{32,16},{48,32},{64,48},{80,64},{96,80},{112,96},{17,1},{33... | collective-permute-start | bytes 24584 | tf_op jit(solution)/shard_map/ppermute | solution.py:22
  24.3 2.9 %copy-start.14 = (f32[1024]{0:T(1024)S(1)}, f32[1024]{0:T(1024)}, u32[]{:S(2)}) copy-start(f32[1024]{0:T(1024)} %param.19) | copy-start | bytes 12292
  24.3 4.4 %copy-start.15 = (f32[64]{0:T(128)S(1)}, f32[64]{0:T(128)}, u32[]{:S(2)}) copy-start(f32[64]{0:T(128)} %param.15) | copy-start | bytes 772
  33.9 3.3 %copy-start = (bf16[1024,1024]{1,0:T(8,128)(2,1)}, bf16[1024,1024]{1,0:T(8,128)(2,1)S(1)}, u32[]{:S(2)}) copy-start(bf16[1024,1024]{1,0:T(8,128)(2,1)S(1)} %get-tuple-element.16) | copy-start | bytes 6291460
  38.7 23.7 %all-to-all-start.1 = ((f32[128,8,128]{2,1,0:T(8,128)}), f32[128,8,128]{2,1,0:T(8,128)S(1)}, u32[]{:S(2)}, u32[]{:S(2)}) async-start(f32[128,8,128]{2,1,0:T(8,128)} %bitcast.3), calls=%async_computation.1 | async-start | bytes 1048576 | tf_op jit(solution)/shard_map/all_to_all | solution.py:207
  68.3 2.6 %copy-start.9 = (f32[16,8,1024]{2,1,0:T(8,128)S(1)}, f32[16,8,1024]{2,1,0:T(8,128)}, u32[]{:S(2)}) copy-start(f32[16,8,1024]{2,1,0:T(8,128)} %shard_map.122) | copy-start | bytes 1572868
  73.3 18.0 %all-to-all-start.2 = ((f32[128,8,128]{2,1,0:T(8,128)}), f32[128,8,128]{2,1,0:T(8,128)S(1)}, u32[]{:S(2)}, u32[]{:S(2)}) async-start(f32[128,8,128]{2,1,0:T(8,128)} %bitcast.236), calls=%async_computation.2 | async-start | bytes 1048576 | tf_op jit(solution)/shard_map/all_to_all | solution.py:213
  91.4 2.6 %copy-start.1 = (bf16[1024,1024]{1,0:T(8,128)(2,1)S(1)}, bf16[1024,1024]{1,0:T(8,128)(2,1)}, u32[]{:S(2)}) copy-start(bf16[1024,1024]{1,0:T(8,128)(2,1)} %copy-done) | copy-start | bytes 6291460
  101.3 6.8 %collective-permute-start.1 = (f32[16,64]{1,0:T(8,128)S(1)}, f32[16,64]{1,0:T(8,128)S(1)}, u32[]{:S(2)}, u32[]{:S(2)}) collective-permute-start(f32[16,64]{1,0:T(8,128)S(1)} %bitcast.255), channel_id=1, source_target_pairs={{16,0},{32,16},{48,32},{64,48},{80,64},{96,80},{112,96},{17,1},{33... | collective-permute-start | bytes 12296 | tf_op jit(solution)/shard_map/ppermute | solution.py:218
  104.6 6.8 %collective-permute-start = (f32[16,64]{1,0:T(8,128)S(1)}, f32[16,64]{1,0:T(8,128)S(1)}, u32[]{:S(2)}, u32[]{:S(2)}) collective-permute-start(f32[16,64]{1,0:T(8,128)S(1)} %bitcast.253), channel_id=1, source_target_pairs={{0,16},{16,32},{32,48},{48,64},{64,80},{80,96},{96,112},{1,17},{17... | collective-permute-start | bytes 12296 | tf_op jit(solution)/shard_map/ppermute | solution.py:217
  112.3 16.5 %all-to-all-start.3 = ((f32[16,67,128]{2,1,0:T(8,128)}), f32[16,67,128]{2,1,0:T(8,128)S(1)}, u32[]{:S(2)}, u32[]{:S(2)}) async-start(f32[16,67,128]{2,1,0:T(8,128)} %fusion.23), calls=%async_computation.3 | async-start | bytes 1179648 | tf_op jit(solution)/shard_map/all_to_all | solution.py:224
  118.7 4.4 %copy-start.12 = (f32[16,63,128]{2,1,0:T(8,128)S(1)}, f32[16,63,128]{2,1,0:T(8,128)}, u32[]{:S(2)}) copy-start(f32[16,63,128]{2,1,0:T(8,128)} %get-tuple-element.40) | copy-start | bytes 1548292
  134.1 14.8 %copy-start.4 = (bf16[1024,1024]{1,0:T(8,128)(2,1)S(1)}, bf16[1024,1024]{1,0:T(8,128)(2,1)}, u32[]{:S(2)}) copy-start(bf16[1024,1024]{1,0:T(8,128)(2,1)} %get-tuple-element.17) | copy-start | bytes 6291460
  151.6 18.0 %copy-start.7 = (bf16[1024,1024]{1,0:T(8,128)(2,1)S(1)}, bf16[1024,1024]{1,0:T(8,128)(2,1)}, u32[]{:S(2)}) copy-start(bf16[1024,1024]{1,0:T(8,128)(2,1)} %get-tuple-element.15) | copy-start | bytes 6291460
  177.2 18.4 %copy-start.5 = (bf16[1024,1024]{1,0:T(8,128)(2,1)S(1)}, bf16[1024,1024]{1,0:T(8,128)(2,1)}, u32[]{:S(2)}) copy-start(bf16[1024,1024]{1,0:T(8,128)(2,1)} %get-tuple-element.17) | copy-start | bytes 6291460
  178.1 18.4 %copy-start.3 = (bf16[1024,1024]{1,0:T(8,128)(2,1)S(1)}, bf16[1024,1024]{1,0:T(8,128)(2,1)}, u32[]{:S(2)}) copy-start(bf16[1024,1024]{1,0:T(8,128)(2,1)} %copy-done) | copy-start | bytes 6291460
  199.0 6.8 %collective-permute-start.7 = (f32[16,64]{1,0:T(8,128)S(1)}, f32[16,64]{1,0:T(8,128)S(1)}, u32[]{:S(2)}, u32[]{:S(2)}) collective-permute-start(f32[16,64]{1,0:T(8,128)S(1)} %bitcast.256), channel_id=1, source_target_pairs={{16,0},{32,16},{48,32},{64,48},{80,64},{96,80},{112,96},{17,1},{33... | collective-permute-start | bytes 12296 | tf_op jit(solution)/shard_map/ppermute | solution.py:218
  202.3 6.8 %collective-permute-start.6 = (f32[16,64]{1,0:T(8,128)S(1)}, f32[16,64]{1,0:T(8,128)S(1)}, u32[]{:S(2)}, u32[]{:S(2)}) collective-permute-start(f32[16,64]{1,0:T(8,128)S(1)} %bitcast.254), channel_id=1, source_target_pairs={{0,16},{16,32},{32,48},{48,64},{64,80},{80,96},{96,112},{1,17},{17... | collective-permute-start | bytes 12296 | tf_op jit(solution)/shard_map/ppermute | solution.py:217
  (4 other events, 6.6 us)
